TPU v7x, 128 devices: a whole 4x4x4 slice. The times are simulated.
128 devices in a mesh: section: 4 (over x), seq: 32 (over z, y, core).
Axes of the slice: x: 4, y: 4, z: 4, core: 2. Of those that a mesh axis runs over, the one named last changes fastest.
Arguments:
- section_inputs: bfloat16 [4, 2, 16384, 256], P('section', None, 'seq'), may hold values from -6 to 6
- cotangent: bfloat16 [2, 16384, 256], P(None, 'seq'), may hold values from -6 to 6
- conv_weight: bfloat16 [4, 2, 3, 256, 512], P('section'), may hold values from -0.21875 to 0.21875
- out_weight: bfloat16 [4, 2, 256, 256], P('section'), may hold values from -0.375 to 0.375
Outputs:
- input_grads: float32 [4, 2, 16384, 256], P('section', None, 'seq')
- conv_grads: float32 [4, 2, 768, 512], P('section', None, 'seq')
- out_grads: float32 [4, 2, 256, 256], P('section', None, 'seq')
All inputs are finite; a program needn't handle non-finite values.
Results may differ from a plain program's by a relative error of at most 0.019.
Values may be sent and summed in bfloat16 or wider, within the bound.
No kernel may reach another device: no remote copies, remote signals or barrier semaphores. Data moves between devices by JAX's collectives and lax.ppermute only.
A program may use at most 128 MiB of HBM per device.

v0:
```python
import math

import jax
import jax.numpy as jnp
from jax import lax
from jax.sharding import PartitionSpec as P

NEAR = 128
FAR = 1024


def shifted(value, axis, steps):
    count = lax.axis_size(axis)
    leading, last = (max(0, -steps), min(count, count - steps))
    return lax.ppermute(value, axis, [(source, source + steps) for source in range(leading, last)])


def halo_sides(block, width):
    rows = block.shape[1]
    from_low = shifted(block[:, rows - width :], "seq", 1)
    from_high = shifted(block[:, :width], "seq", -1)
    earlier = jnp.concatenate([from_low, block[:, : rows - width]], axis=1)
    following = jnp.concatenate([block[:, width:], from_high], axis=1)
    return earlier, following


def far_sides(block, hops):
    return shifted(block, "seq", hops), shifted(block, "seq", -hops)


def mm(a, b):
    return jnp.einsum("mpc,cd->mpd", a, b, preferred_element_type=jnp.float32)


def forward_layer(hidden, earlier, following, conv, out_mat, last):
    chans = hidden.shape[2]
    preact = mm(earlier, conv[0])
    preact = preact + mm(hidden, conv[1])
    preact = preact + mm(following, conv[2])
    tanh_part = jnp.tanh(preact[..., :chans])
    sig_part = jax.nn.sigmoid(preact[..., chans:])
    gated = (tanh_part * sig_part).astype(jnp.bfloat16)
    factor_a = (1.0 - tanh_part * tanh_part) * sig_part
    factor_b = tanh_part * sig_part * (1.0 - sig_part)
    taps = jnp.concatenate([earlier, hidden, following], axis=2)
    saved = (taps, gated, factor_a, factor_b)
    if last:
        return None, saved
    nxt = (hidden.astype(jnp.float32) + mm(gated, out_mat)).astype(jnp.bfloat16)
    return nxt, saved


def backward_layer(flowing, saved, conv, out_mat, layer, far_hops):
    taps, gated, factor_a, factor_b = saved
    chans = flowing.shape[2]
    grad_half = flowing.astype(jnp.bfloat16)
    out_term = jnp.einsum("mpc,mpd->cd", gated, grad_half, preferred_element_type=jnp.float32)
    grad_gated = jnp.einsum("mpd,cd->mpc", grad_half, out_mat, preferred_element_type=jnp.float32)
    grad_pre = jnp.concatenate([grad_gated * factor_a, grad_gated * factor_b], axis=2).astype(
        jnp.bfloat16
    )
    conv_term = jnp.einsum("mpc,mpd->cd", taps, grad_pre, preferred_element_type=jnp.float32)
    weights = conv.reshape(3 * chans, 2 * chans)
    back = jnp.einsum("mpd,cd->mpc", grad_pre, weights, preferred_element_type=jnp.float32)
    grad_first = back[..., :chans].astype(jnp.bfloat16)
    middle = back[..., chans : 2 * chans]
    grad_third = back[..., 2 * chans :].astype(jnp.bfloat16)
    if layer == 0:
        third_earlier, first_following = halo_sides_pair(grad_first, grad_third, NEAR)
    else:
        third_earlier = shifted(grad_third, "seq", far_hops)
        first_following = shifted(grad_first, "seq", -far_hops)
    grad_conv = middle + first_following.astype(jnp.float32) + third_earlier.astype(jnp.float32)
    return flowing + grad_conv, conv_term, out_term


def halo_sides_pair(grad_first, grad_third, width):
    rows = grad_first.shape[1]
    from_low = shifted(grad_third[:, rows - width :], "seq", 1)
    from_high = shifted(grad_first[:, :width], "seq", -1)
    third_earlier = jnp.concatenate([from_low, grad_third[:, : rows - width]], axis=1)
    first_following = jnp.concatenate([grad_first[:, width:], from_high], axis=1)
    return third_earlier, first_following


def halving_scatter(parts):
    count = parts[0].shape[0]
    rank = lax.axis_index("seq")
    bit = 0
    while (1 << bit) < count:
        own = ((rank >> bit) & 1) == 1
        pairs = [(j, j ^ (1 << bit)) for j in range(count)]
        halves = [p.reshape(p.shape[0] // 2, 2, *p.shape[1:]) for p in parts]
        sends = tuple(jnp.where(own, h[:, 0], h[:, 1]).astype(jnp.bfloat16) for h in halves)
        got = lax.ppermute(sends, "seq", pairs)
        parts = [jnp.where(own, h[:, 1], h[:, 0]) + g.astype(jnp.float32) for h, g in zip(halves, got)]
        bit += 1
    return [p[0] for p in parts]


def shards(section_inputs, cotangent, conv_weight, out_weight):
    batch_count = cotangent.shape[0]
    positions = cotangent.shape[1]
    channels = cotangent.shape[2]
    far_hops = FAR // positions
    seq_count = lax.axis_size("seq")
    section_count = lax.axis_size("section")
    section_rank = lax.axis_index("section")
    conv_mat = conv_weight[0]
    out_mat = out_weight[0]
    depth = conv_mat.shape[0]
    grad_scale = 1.0 / math.sqrt(batch_count * positions * seq_count)

    hidden = section_inputs[0]
    stored = []
    for layer in range(depth):
        if layer == 0:
            earlier, following = halo_sides(hidden, NEAR)
        else:
            earlier, following = far_sides(hidden, far_hops)
        hidden, saved = forward_layer(
            hidden, earlier, following, conv_mat[layer], out_mat[layer], layer + 1 == depth
        )
        stored.append(saved)

    top = jnp.where(section_rank == section_count - 1, 1.0, 0.0).astype(jnp.float32)
    flowing = cotangent.astype(jnp.float32) * top
    input_grads = None
    conv_acc = [None] * depth
    out_acc = [None] * depth
    for step in range(section_count):
        for layer in reversed(range(depth)):
            flowing, conv_term, out_term = backward_layer(
                flowing, stored[layer], conv_mat[layer], out_mat[layer], layer, far_hops
            )
            conv_acc[layer] = conv_term if step == 0 else conv_acc[layer] + conv_term
            out_acc[layer] = out_term if step == 0 else out_acc[layer] + out_term
        input_grads = flowing if step == 0 else input_grads + flowing
        if step + 1 < section_count:
            flowing = shifted(flowing.astype(jnp.bfloat16), "section", -1).astype(jnp.float32)

    conv_rows = 3 * channels // seq_count
    out_rows = channels // seq_count
    conv_parts = []
    out_parts = []
    for layer in range(depth):
        conv_mine, out_mine = halving_scatter(
            [
                conv_acc[layer].reshape(seq_count, conv_rows, 2 * channels),
                out_acc[layer].reshape(seq_count, out_rows, channels),
            ]
        )
        conv_parts.append(conv_mine)
        out_parts.append(out_mine)
    conv_grads = jnp.stack(conv_parts)[None] * grad_scale
    out_grads = jnp.stack(out_parts)[None] * grad_scale
    return (input_grads[None], conv_grads, out_grads)


def solution(mesh):
    return jax.shard_map(
        shards,
        mesh=mesh,
        in_specs=(
            P("section", None, "seq", None),
            P(None, "seq", None),
            P("section", None, None, None, None),
            P("section", None, None, None),
        ),
        out_specs=(
            P("section", None, "seq", None),
            P("section", None, "seq", None),
            P("section", None, "seq", None),
        ),
        check_vma=False,
    )
```

profile of v0, /device:TPU:24, one launch (start us, length us, event | category | flops | bytes accessed | tf_op | source)
XLA Modules:
  0.0 275.7 jit_solution(493345194602499104)
XLA Ops:
  1.7 1.9 collective-permute-start
  3.6 3.6 %collective-permute-start.1 = (bf16[2,128,256]{2,1,0:T(8,128)(2,1)S(1)}, bf16[2,128,256]{2,1,0:T(8,128)(2,1)S(1)}, u32[]{:S(2)}, u32[]{:S(2)}) collective-permute-start(bf16[2,128,256]{2,1,0:T(8,128)(2,1)S(1)} %get-tuple-element.56), channel_id=1, source_target_pairs={{1,0},{2,1},{3,2},{4,3},{5,4},{6,5},{7,6},{8,7},{9,8},{10,9},{11,1... | collective-permute-start | bytes 393224 | tf_op jit(solution)/shard_map/ppermute | solution.py:15
  7.3 1.6 fusion.76
  9.0 1.8 fusion.50
  12.8 5.6 %collective-permute-start.2 = (bf16[2,512,256]{2,1,0:T(8,128)(2,1)S(1)}, bf16[2,512,256]{2,1,0:T(8,128)(2,1)S(1)}, u32[]{:S(2)}, u32[]{:S(2)}) collective-permute-start(bf16[2,512,256]{2,1,0:T(8,128)(2,1)S(1)} %fusion), channel_id=1, source_target_pairs={{0,2},{1,3},{2,4},{3,5},{4,6},{5,7},{6,8},{7,9},{8,10},{9,11},{10,... | collective-permute-start | bytes 1572872 | tf_op jit(solution)/shard_map/ppermute | solution.py:15
  18.5 1.9 collective-permute-start.3
  20.9 8.2 %collective-permute-done.2 = bf16[2,512,256]{2,1,0:T(8,128)(2,1)S(1)} collective-permute-done((bf16[2,512,256]{2,1,0:T(8,128)(2,1)S(1)}, bf16[2,512,256]{2,1,0:T(8,128)(2,1)S(1)}, u32[]{:S(2)}, u32[]{:S(2)}) %collective-permute-start.2) | collective-permute-done | bytes 524320 | tf_op jit(solution)/shard_map/ppermute | solution.py:15
  30.0 5.5 %collective-permute-done.3 = bf16[2,512,256]{2,1,0:T(8,128)(2,1)S(1)} collective-permute-done((bf16[2,512,256]{2,1,0:T(8,128)(2,1)S(1)}, bf16[2,512,256]{2,1,0:T(8,128)(2,1)S(1)}, u32[]{:S(2)}, u32[]{:S(2)}) %collective-permute-start.3) | collective-permute-done | bytes 524320 | tf_op jit(solution)/shard_map/ppermute | solution.py:15
  36.1 1.6 multiply_convert_fusion.15
  38.8 1.9 collective-permute-start.5
  40.7 3.9 %collective-permute-start.4 = (bf16[2,512,256]{2,1,0:T(8,128)(2,1)S(1)}, bf16[2,512,256]{2,1,0:T(8,128)(2,1)S(1)}, u32[]{:S(2)}, u32[]{:S(2)}) collective-permute-start(bf16[2,512,256]{2,1,0:T(8,128)(2,1)S(1)} %get-tuple-element.40), channel_id=1, source_target_pairs={{2,0},{3,1},{4,2},{5,3},{6,4},{7,5},{8,6},{9,7},{10,8},{11,9},{12,... | collective-permute-start | bytes 1572872 | tf_op jit(solution)/shard_map/ppermute | solution.py:15
  44.6 8.2 %collective-permute-done.5 = bf16[2,512,256]{2,1,0:T(8,128)(2,1)S(1)} collective-permute-done((bf16[2,512,256]{2,1,0:T(8,128)(2,1)S(1)}, bf16[2,512,256]{2,1,0:T(8,128)(2,1)S(1)}, u32[]{:S(2)}, u32[]{:S(2)}) %collective-permute-start.5) | collective-permute-done | bytes 524320 | tf_op jit(solution)/shard_map/ppermute | solution.py:15
  52.8 4.0 %collective-permute-done.4 = bf16[2,512,256]{2,1,0:T(8,128)(2,1)S(1)} collective-permute-done((bf16[2,512,256]{2,1,0:T(8,128)(2,1)S(1)}, bf16[2,512,256]{2,1,0:T(8,128)(2,1)S(1)}, u32[]{:S(2)}, u32[]{:S(2)}) %collective-permute-start.4) | collective-permute-done | bytes 524320 | tf_op jit(solution)/shard_map/ppermute | solution.py:15
  57.1 2.0 multiply_convert_fusion.13
  60.2 1.9 collective-permute-start.7
  62.1 3.6 %collective-permute-start.6 = (bf16[2,128,256]{2,1,0:T(8,128)(2,1)S(1)}, bf16[2,128,256]{2,1,0:T(8,128)(2,1)S(1)}, u32[]{:S(2)}, u32[]{:S(2)}) collective-permute-start(bf16[2,128,256]{2,1,0:T(8,128)(2,1)S(1)} %get-tuple-element.36), channel_id=1, source_target_pairs={{1,0},{2,1},{3,2},{4,3},{5,4},{6,5},{7,6},{8,7},{9,8},{10,9},{11,1... | collective-permute-start | bytes 393224 | tf_op jit(solution)/shard_map/ppermute | solution.py:15
  66.5 1.8 collective-permute-done.6
  70.0 12.8 %collective-permute-done.8 = bf16[2,512,256]{2,1,0:T(8,128)(2,1)S(1)} collective-permute-done((bf16[2,512,256]{2,1,0:T(8,128)(2,1)S(1)}, bf16[2,512,256]{2,1,0:T(8,128)(2,1)S(1)}, u32[]{:S(2)}, u32[]{:S(2)}) %collective-permute-start.8) | collective-permute-done | bytes 524320 | tf_op jit(solution)/shard_map/ppermute | solution.py:15
  83.6 2.7 fusion.193
  87.3 6.7 %collective-permute-start.10 = (bf16[2,512,256]{2,1,0:T(8,128)(2,1)}, bf16[2,512,256]{2,1,0:T(8,128)(2,1)}, u32[]{:S(2)}, u32[]{:S(2)}) collective-permute-start(bf16[2,512,256]{2,1,0:T(8,128)(2,1)} %get-tuple-element.33), channel_id=1, source_target_pairs={{0,2},{1,3},{2,4},{3,5},{4,6},{5,7},{6,8},{7,9},{8,10},{9,11},{10,... | collective-permute-start | bytes 1572872 | tf_op jit(solution)/shard_map/ppermute | solution.py:15
  94.0 2.1 collective-permute-start.9
  96.1 2.8 fusion.48
  98.9 5.7 %collective-permute-done.10 = bf16[2,512,256]{2,1,0:T(8,128)(2,1)} collective-permute-done((bf16[2,512,256]{2,1,0:T(8,128)(2,1)}, bf16[2,512,256]{2,1,0:T(8,128)(2,1)}, u32[]{:S(2)}, u32[]{:S(2)}) %collective-permute-start.10) | collective-permute-done | bytes 524320 | tf_op jit(solution)/shard_map/ppermute | solution.py:15
  104.6 6.2 %collective-permute-done.9 = bf16[2,512,256]{2,1,0:T(8,128)(2,1)} collective-permute-done((bf16[2,512,256]{2,1,0:T(8,128)(2,1)}, bf16[2,512,256]{2,1,0:T(8,128)(2,1)}, u32[]{:S(2)}, u32[]{:S(2)}) %collective-permute-start.9) | collective-permute-done | bytes 524320 | tf_op jit(solution)/shard_map/ppermute | solution.py:15
  110.8 1.8 fusion.20
  114.1 1.9 collective-permute-start.12
  116.0 3.6 %collective-permute-start.11 = (bf16[2,128,256]{2,1,0:T(8,128)(2,1)S(1)}, bf16[2,128,256]{2,1,0:T(8,128)(2,1)S(1)}, u32[]{:S(2)}, u32[]{:S(2)}) collective-permute-start(bf16[2,128,256]{2,1,0:T(8,128)(2,1)S(1)} %get-tuple-element.30), channel_id=1, source_target_pairs={{1,0},{2,1},{3,2},{4,3},{5,4},{6,5},{7,6},{8,7},{9,8},{10,9},{11,1... | collective-permute-start | bytes 393224 | tf_op jit(solution)/shard_map/ppermute | solution.py:15
  120.4 1.8 collective-permute-done.11
  127.0 11.2 %collective-permute-done.13 = bf16[2,512,256]{2,1,0:T(8,128)(2,1)S(1)} collective-permute-done((bf16[2,512,256]{2,1,0:T(8,128)(2,1)S(1)}, bf16[2,512,256]{2,1,0:T(8,128)(2,1)S(1)}, u32[]{:S(2)}, u32[]{:S(2)}) %collective-permute-start.13) | collective-permute-done | bytes 524320 | tf_op jit(solution)/shard_map/ppermute | solution.py:15
  139.7 3.0 %collective-permute-start.15 = (bf16[2,512,256]{2,1,0:T(8,128)(2,1)S(1)}, bf16[2,512,256]{2,1,0:T(8,128)(2,1)S(1)}, u32[]{:S(2)}, u32[]{:S(2)}) collective-permute-start(bf16[2,512,256]{2,1,0:T(8,128)(2,1)S(1)} %get-tuple-element.27), channel_id=1, source_target_pairs={{0,2},{1,3},{2,4},{3,5},{4,6},{5,7},{6,8},{7,9},{8,10},{9,11},{10,... | collective-permute-start | bytes 1572872 | tf_op jit(solution)/shard_map/ppermute | solution.py:15
  142.7 2.8 %collective-permute-start.14 = (bf16[2,512,256]{2,1,0:T(8,128)(2,1)S(1)}, bf16[2,512,256]{2,1,0:T(8,128)(2,1)S(1)}, u32[]{:S(2)}, u32[]{:S(2)}) collective-permute-start(bf16[2,512,256]{2,1,0:T(8,128)(2,1)S(1)} %get-tuple-element.26), channel_id=1, source_target_pairs={{2,0},{3,1},{4,2},{5,3},{6,4},{7,5},{8,6},{9,7},{10,8},{11,9},{12,... | collective-permute-start | bytes 1572872 | tf_op jit(solution)/shard_map/ppermute | solution.py:15
  147.9 8.3 %collective-permute-done.15 = bf16[2,512,256]{2,1,0:T(8,128)(2,1)S(1)} collective-permute-done((bf16[2,512,256]{2,1,0:T(8,128)(2,1)S(1)}, bf16[2,512,256]{2,1,0:T(8,128)(2,1)S(1)}, u32[]{:S(2)}, u32[]{:S(2)}) %collective-permute-start.15) | collective-permute-done | bytes 524320 | tf_op jit(solution)/shard_map/ppermute | solution.py:15
  156.3 4.0 %collective-permute-done.14 = bf16[2,512,256]{2,1,0:T(8,128)(2,1)S(1)} collective-permute-done((bf16[2,512,256]{2,1,0:T(8,128)(2,1)S(1)}, bf16[2,512,256]{2,1,0:T(8,128)(2,1)S(1)}, u32[]{:S(2)}, u32[]{:S(2)}) %collective-permute-start.14) | collective-permute-done | bytes 524320 | tf_op jit(solution)/shard_map/ppermute | solution.py:15
  162.0 1.9 collective-permute-start.17
  164.0 3.6 %collective-permute-start.16 = (bf16[2,128,256]{2,1,0:T(8,128)(2,1)S(1)}, bf16[2,128,256]{2,1,0:T(8,128)(2,1)S(1)}, u32[]{:S(2)}, u32[]{:S(2)}) collective-permute-start(bf16[2,128,256]{2,1,0:T(8,128)(2,1)S(1)} %get-tuple-element.24), channel_id=1, source_target_pairs={{1,0},{2,1},{3,2},{4,3},{5,4},{6,5},{7,6},{8,7},{9,8},{10,9},{11,1... | collective-permute-start | bytes 393224 | tf_op jit(solution)/shard_map/ppermute | solution.py:15
  168.3 1.8 collective-permute-done.16
  170.3 1.5 collective-permute-start.18
  173.5 12.6 %collective-permute-done.18 = bf16[2,512,256]{2,1,0:T(8,128)(2,1)S(1)} collective-permute-done((bf16[2,512,256]{2,1,0:T(8,128)(2,1)S(1)}, bf16[2,512,256]{2,1,0:T(8,128)(2,1)S(1)}, u32[]{:S(2)}, u32[]{:S(2)}) %collective-permute-start.18) | collective-permute-done | bytes 524320 | tf_op jit(solution)/shard_map/ppermute | solution.py:15
  189.7 2.9 %collective-permute-done.39 = bf16[8,8,256]{2,1,0:T(8,128)(2,1)S(1)} collective-permute-done((bf16[8,8,256]{2,1,0:T(8,128)(2,1)S(1)}, bf16[8,8,256]{2,1,0:T(8,128)(2,1)S(1)}, u32[]{:S(2)}, u32[]{:S(2)}) %collective-permute-start.39) | collective-permute-done | bytes 32800 | tf_op jit(solution)/shard_map/ppermute | solution.py:95
  193.7 4.2 %collective-permute-done.40 = bf16[4,8,256]{2,1,0:T(8,128)(2,1)S(1)} collective-permute-done((bf16[4,8,256]{2,1,0:T(8,128)(2,1)S(1)}, bf16[4,8,256]{2,1,0:T(8,128)(2,1)S(1)}, u32[]{:S(2)}, u32[]{:S(2)}) %collective-permute-start.40) | collective-permute-done | bytes 16416 | tf_op jit(solution)/shard_map/ppermute | solution.py:95
  197.9 1.7 collective-permute-start.41
  199.8 1.9 collective-permute-done.41
  201.6 2.6 collective-permute-start.42
  204.3 1.9 collective-permute-start.20
  206.2 3.9 %collective-permute-start.19 = (bf16[2,512,256]{2,1,0:T(8,128)(2,1)S(1)}, bf16[2,512,256]{2,1,0:T(8,128)(2,1)S(1)}, u32[]{:S(2)}, u32[]{:S(2)}) collective-permute-start(bf16[2,512,256]{2,1,0:T(8,128)(2,1)S(1)} %get-tuple-element.20), channel_id=1, source_target_pairs={{2,0},{3,1},{4,2},{5,3},{6,4},{7,5},{8,6},{9,7},{10,8},{11,9},{12,... | collective-permute-start | bytes 1572872 | tf_op jit(solution)/shard_map/ppermute | solution.py:15
  210.5 8.4 %collective-permute-done.20 = bf16[2,512,256]{2,1,0:T(8,128)(2,1)S(1)} collective-permute-done((bf16[2,512,256]{2,1,0:T(8,128)(2,1)S(1)}, bf16[2,512,256]{2,1,0:T(8,128)(2,1)S(1)}, u32[]{:S(2)}, u32[]{:S(2)}) %collective-permute-start.20) | collective-permute-done | bytes 524320 | tf_op jit(solution)/shard_map/ppermute | solution.py:15
  218.9 2.7 collective-permute-done.19
  223.7 1.9 collective-permute-start.21
  225.6 2.4 collective-permute-start.22
  231.3 2.4 collective-permute-done.34
  233.8 2.4 collective-permute-start.35
  236.4 2.7 collective-permute-done.35
  239.2 2.0 collective-permute-start.36
  241.3 1.6 collective-permute-done.36
  242.9 2.4 collective-permute-start.37
  245.3 3.0 %collective-permute-start.30 = (bf16[4,24,512]{2,1,0:T(8,128)(2,1)S(1)}, bf16[4,24,512]{2,1,0:T(8,128)(2,1)S(1)}, u32[]{:S(2)}, u32[]{:S(2)}) collective-permute-start(bf16[4,24,512]{2,1,0:T(8,128)(2,1)S(1)} %fusion.114), channel_id=1, source_target_pairs={{0,4},{1,5},{2,6},{3,7},{4,0},{5,1},{6,2},{7,3},{8,12},{9,13},{10,... | collective-permute-start | bytes 294920 | tf_op jit(solution)/shard_map/ppermute | solution.py:95
  249.0 3.0 %fusion.10 = f32[1,2,512,256]{3,2,1,0:T(8,128)} fusion(f32[2,512,256]{2,1,0:T(8,128)S(1)} %fusion.12, f32[2,512,768]{2,1,0:T(8,128)S(1)} %get-tuple-element.73, bf16[2,128,256]{2,1,0:T(8,128)(2,1)S(1)} %collective-permute-done.21, bf16[2,384,256]{2,1,0:T(8,128)(2,1)S(1)} %get-tuple-element.19, bf16[2,384,256]{2,1,0:T(8,128)(2,1)S(1)} %get-tuple-element.18, ...), kind=kLoop, calls=%fused_computation.30 | loop fusion | flops 12320768 | bytes 13631488 | tf_op jit(solution)/shard_map/broadcast_in_dim | solution.py:157
  252.3 1.6 collective-permute-start.24
  254.8 4.2 %collective-permute-done.24 = bf16[8,24,512]{2,1,0:T(8,128)(2,1)S(1)} collective-permute-done((bf16[8,24,512]{2,1,0:T(8,128)(2,1)S(1)}, bf16[8,24,512]{2,1,0:T(8,128)(2,1)S(1)}, u32[]{:S(2)}, u32[]{:S(2)}) %collective-permute-start.24) | collective-permute-done | bytes 196640 | tf_op jit(solution)/shard_map/ppermute | solution.py:95
  259.2 3.6 %collective-permute-start.25 = (bf16[4,24,512]{2,1,0:T(8,128)(2,1)S(1)}, bf16[4,24,512]{2,1,0:T(8,128)(2,1)S(1)}, u32[]{:S(2)}, u32[]{:S(2)}) collective-permute-start(bf16[4,24,512]{2,1,0:T(8,128)(2,1)S(1)} %fusion.113), channel_id=1, source_target_pairs={{0,4},{1,5},{2,6},{3,7},{4,0},{5,1},{6,2},{7,3},{8,12},{9,13},{10,... | collective-permute-start | bytes 294920 | tf_op jit(solution)/shard_map/ppermute | solution.py:95
  262.8 2.6 collective-permute-done.25
  266.3 3.1 %collective-permute-start.32 = (bf16[1,24,512]{2,1,0:T(8,128)(2,1)S(1)}, bf16[1,24,512]{2,1,0:T(8,128)(2,1)S(1)}, u32[]{:S(2)}, u32[]{:S(2)}) collective-permute-start(bf16[1,24,512]{2,1,0:T(8,128)(2,1)S(1)} %fusion.141), channel_id=1, source_target_pairs={{0,16},{1,17},{2,18},{3,19},{4,20},{5,21},{6,22},{7,23},{8,24},{9,... | collective-permute-start | bytes 73736 | tf_op jit(solution)/shard_map/ppermute | solution.py:95
  269.7 2.1 collective-permute-start.27
  271.8 3.3 %collective-permute-done.27 = bf16[1,24,512]{2,1,0:T(8,128)(2,1)S(1)} collective-permute-done((bf16[1,24,512]{2,1,0:T(8,128)(2,1)S(1)}, bf16[1,24,512]{2,1,0:T(8,128)(2,1)S(1)}, u32[]{:S(2)}, u32[]{:S(2)}) %collective-permute-start.27) | collective-permute-done | bytes 24608 | tf_op jit(solution)/shard_map/ppermute | solution.py:95
  (221 shorter events, 40.9 us)
Async XLA Ops:
  0.6 8.3 %copy-start.7 = (bf16[1,2,512,256]{3,2,1,0:T(8,128)(2,1)S(1)}, bf16[1,2,512,256]{3,2,1,0:T(8,128)(2,1)}, u32[]{:S(2)}) copy-start(bf16[1,2,512,256]{3,2,1,0:T(8,128)(2,1)} %param.4) | copy-start | bytes 1572868
  1.7 7.3 %collective-permute-start = (bf16[2,128,256]{2,1,0:T(8,128)(2,1)S(1)}, bf16[2,128,256]{2,1,0:T(8,128)(2,1)S(1)}, u32[]{:S(2)}, u32[]{:S(2)}) collective-permute-start(bf16[2,128,256]{2,1,0:T(8,128)(2,1)S(1)} %get-tuple-element.57), channel_id=1, source_target_pairs={{0,1},{1,2},{2,3},{3,4},{4,5},{5,6},{6,7},{7,8},{8,9},{9,10},{10,1... | collective-permute-start | bytes 393224 | tf_op jit(solution)/shard_map/ppermute | solution.py:15
  3.6 7.2 %collective-permute-start.1 = (bf16[2,128,256]{2,1,0:T(8,128)(2,1)S(1)}, bf16[2,128,256]{2,1,0:T(8,128)(2,1)S(1)}, u32[]{:S(2)}, u32[]{:S(2)}) collective-permute-start(bf16[2,128,256]{2,1,0:T(8,128)(2,1)S(1)} %get-tuple-element.56), channel_id=1, source_target_pairs={{1,0},{2,1},{3,2},{4,3},{5,4},{6,5},{7,6},{8,7},{9,8},{10,9},{11,1... | collective-permute-start | bytes 393224 | tf_op jit(solution)/shard_map/ppermute | solution.py:15
  12.8 16.9 %copy-start.19 = (bf16[2,512,256]{2,1,0:T(8,128)(2,1)}, bf16[2,512,256]{2,1,0:T(8,128)(2,1)S(1)}, u32[]{:S(2)}) copy-start(bf16[2,512,256]{2,1,0:T(8,128)(2,1)S(1)} %fusion) | copy-start | bytes 1572868
  12.8 16.4 %collective-permute-start.2 = (bf16[2,512,256]{2,1,0:T(8,128)(2,1)S(1)}, bf16[2,512,256]{2,1,0:T(8,128)(2,1)S(1)}, u32[]{:S(2)}, u32[]{:S(2)}) collective-permute-start(bf16[2,512,256]{2,1,0:T(8,128)(2,1)S(1)} %fusion), channel_id=1, source_target_pairs={{0,2},{1,3},{2,4},{3,5},{4,6},{5,7},{6,8},{7,9},{8,10},{9,11},{10,... | collective-permute-start | bytes 1572872 | tf_op jit(solution)/shard_map/ppermute | solution.py:15
  18.5 17.0 %collective-permute-start.3 = (bf16[2,512,256]{2,1,0:T(8,128)(2,1)S(1)}, bf16[2,512,256]{2,1,0:T(8,128)(2,1)S(1)}, u32[]{:S(2)}, u32[]{:S(2)}) collective-permute-start(bf16[2,512,256]{2,1,0:T(8,128)(2,1)S(1)} %fusion), channel_id=1, source_target_pairs={{2,0},{3,1},{4,2},{5,3},{6,4},{7,5},{8,6},{9,7},{10,8},{11,9},{12,... | collective-permute-start | bytes 1572872 | tf_op jit(solution)/shard_map/ppermute | solution.py:15
  30.0 6.1 %copy-start.17 = (bf16[2,512,256]{2,1,0:T(8,128)(2,1)S(1)}, bf16[2,512,256]{2,1,0:T(8,128)(2,1)}, u32[]{:S(2)}) copy-start(bf16[2,512,256]{2,1,0:T(8,128)(2,1)} %param.5) | copy-start | bytes 1572868
  37.6 21.5 %copy-start.35 = (bf16[2,512,256]{1,2,0:T(8,128)(2,1)}, bf16[2,512,256]{1,2,0:T(8,128)(2,1)S(1)}, u32[]{:S(2)}) copy-start(bf16[2,512,256]{1,2,0:T(8,128)(2,1)S(1)} %get-tuple-element.7) | copy-start | bytes 1572868
  37.6 45.1 %copy-start.2 = (f32[2,512,256]{1,2,0:T(8,128)}, f32[2,512,256]{1,2,0:T(8,128)S(1)}, u32[]{:S(2)}) copy-start(f32[2,512,256]{1,2,0:T(8,128)S(1)} %get-tuple-element.8) | copy-start | bytes 3145732
  37.6 45.1 %copy-start.4 = (f32[2,512,256]{1,2,0:T(8,128)}, f32[2,512,256]{1,2,0:T(8,128)S(1)}, u32[]{:S(2)}) copy-start(f32[2,512,256]{1,2,0:T(8,128)S(1)} %get-tuple-element.14) | copy-start | bytes 3145732
  38.8 14.0 %collective-permute-start.5 = (bf16[2,512,256]{2,1,0:T(8,128)(2,1)S(1)}, bf16[2,512,256]{2,1,0:T(8,128)(2,1)S(1)}, u32[]{:S(2)}, u32[]{:S(2)}) collective-permute-start(bf16[2,512,256]{2,1,0:T(8,128)(2,1)S(1)} %get-tuple-element.41), channel_id=1, source_target_pairs={{0,2},{1,3},{2,4},{3,5},{4,6},{5,7},{6,8},{7,9},{8,10},{9,11},{10,... | collective-permute-start | bytes 1572872 | tf_op jit(solution)/shard_map/ppermute | solution.py:15
  40.7 16.1 %collective-permute-start.4 = (bf16[2,512,256]{2,1,0:T(8,128)(2,1)S(1)}, bf16[2,512,256]{2,1,0:T(8,128)(2,1)S(1)}, u32[]{:S(2)}, u32[]{:S(2)}) collective-permute-start(bf16[2,512,256]{2,1,0:T(8,128)(2,1)S(1)} %get-tuple-element.40), channel_id=1, source_target_pairs={{2,0},{3,1},{4,2},{5,3},{6,4},{7,5},{8,6},{9,7},{10,8},{11,9},{12,... | collective-permute-start | bytes 1572872 | tf_op jit(solution)/shard_map/ppermute | solution.py:15
  60.2 8.5 %copy-start.6 = (f32[2,512,768]{2,1,0:T(8,128)}, f32[2,512,768]{2,1,0:T(8,128)S(1)}, u32[]{:S(2)}) copy-start(f32[2,512,768]{2,1,0:T(8,128)S(1)} %get-tuple-element.61) | copy-start | bytes 9437188
  60.2 6.3 %collective-permute-start.7 = (bf16[2,128,256]{2,1,0:T(8,128)(2,1)S(1)}, bf16[2,128,256]{2,1,0:T(8,128)(2,1)S(1)}, u32[]{:S(2)}, u32[]{:S(2)}) collective-permute-start(bf16[2,128,256]{2,1,0:T(8,128)(2,1)S(1)} %get-tuple-element.37), channel_id=1, source_target_pairs={{0,1},{1,2},{2,3},{3,4},{4,5},{5,6},{6,7},{7,8},{8,9},{9,10},{10,1... | collective-permute-start | bytes 393224 | tf_op jit(solution)/shard_map/ppermute | solution.py:15
  62.1 6.1 %collective-permute-start.6 = (bf16[2,128,256]{2,1,0:T(8,128)(2,1)S(1)}, bf16[2,128,256]{2,1,0:T(8,128)(2,1)S(1)}, u32[]{:S(2)}, u32[]{:S(2)}) collective-permute-start(bf16[2,128,256]{2,1,0:T(8,128)(2,1)S(1)} %get-tuple-element.36), channel_id=1, source_target_pairs={{1,0},{2,1},{3,2},{4,3},{5,4},{6,5},{7,6},{8,7},{9,8},{10,9},{11,1... | collective-permute-start | bytes 393224 | tf_op jit(solution)/shard_map/ppermute | solution.py:15
  65.9 17.3 %copy-start.13 = (bf16[2,384,256]{2,1,0:T(8,128)(2,1)}, bf16[2,384,256]{2,1,0:T(8,128)(2,1)S(1)}, u32[]{:S(2)}) copy-start(bf16[2,384,256]{2,1,0:T(8,128)(2,1)S(1)} %get-tuple-element.35) | copy-start | bytes 1179652
  66.5 16.6 %copy-start.39 = (bf16[2,128,256]{2,1,0:T(8,128)(2,1)}, bf16[2,128,256]{2,1,0:T(8,128)(2,1)S(1)}, u32[]{:S(2)}) copy-start(bf16[2,128,256]{2,1,0:T(8,128)(2,1)S(1)} %collective-permute-done.7) | copy-start | bytes 393220
  68.3 14.8 %copy-start.41 = (bf16[2,128,256]{2,1,0:T(8,128)(2,1)}, bf16[2,128,256]{2,1,0:T(8,128)(2,1)S(1)}, u32[]{:S(2)}) copy-start(bf16[2,128,256]{2,1,0:T(8,128)(2,1)S(1)} %collective-permute-done.6) | copy-start | bytes 393220
  68.7 14.1 %collective-permute-start.8 = (bf16[2,512,256]{2,1,0:T(8,128)(2,1)S(1)}, bf16[2,512,256]{2,1,0:T(8,128)(2,1)S(1)}, u32[]{:S(2)}, u32[]{:S(2)}) collective-permute-start(bf16[2,512,256]{2,1,0:T(8,128)(2,1)S(1)} %fusion.173), channel_id=1, source_target_pairs={{32,0},{64,32},{96,64},{33,1},{65,33},{97,65},{34,2},{66,34},{98,6... | collective-permute-start | bytes 1572872 | tf_op jit(solution)/shard_map/ppermute | solution.py:15
  87.3 17.3 %collective-permute-start.10 = (bf16[2,512,256]{2,1,0:T(8,128)(2,1)}, bf16[2,512,256]{2,1,0:T(8,128)(2,1)}, u32[]{:S(2)}, u32[]{:S(2)}) collective-permute-start(bf16[2,512,256]{2,1,0:T(8,128)(2,1)} %get-tuple-element.33), channel_id=1, source_target_pairs={{0,2},{1,3},{2,4},{3,5},{4,6},{5,7},{6,8},{7,9},{8,10},{9,11},{10,... | collective-permute-start | bytes 1572872 | tf_op jit(solution)/shard_map/ppermute | solution.py:15
  94.0 16.9 %collective-permute-start.9 = (bf16[2,512,256]{2,1,0:T(8,128)(2,1)}, bf16[2,512,256]{2,1,0:T(8,128)(2,1)}, u32[]{:S(2)}, u32[]{:S(2)}) collective-permute-start(bf16[2,512,256]{2,1,0:T(8,128)(2,1)} %get-tuple-element.32), channel_id=1, source_target_pairs={{2,0},{3,1},{4,2},{5,3},{6,4},{7,5},{8,6},{9,7},{10,8},{11,9},{12,... | collective-permute-start | bytes 1572872 | tf_op jit(solution)/shard_map/ppermute | solution.py:15
  96.1 14.8 %copy-start.12 = (bf16[2,512,256]{2,1,0:T(8,128)(2,1)S(1)}, bf16[2,512,256]{2,1,0:T(8,128)(2,1)}, u32[]{:S(2)}) copy-start(bf16[2,512,256]{2,1,0:T(8,128)(2,1)} %copy-done.11) | copy-start | bytes 1572868
  98.9 13.8 %copy-start = (f32[2,512,256]{1,2,0:T(8,128)S(1)}, f32[2,512,256]{1,2,0:T(8,128)}, u32[]{:S(2)}) copy-start(f32[2,512,256]{1,2,0:T(8,128)} %get-tuple-element.4) | copy-start | bytes 3145732
  98.9 13.8 %copy-start.1 = (f32[2,512,256]{1,2,0:T(8,128)S(1)}, f32[2,512,256]{1,2,0:T(8,128)}, u32[]{:S(2)}) copy-start(f32[2,512,256]{1,2,0:T(8,128)} %get-tuple-element.12) | copy-start | bytes 3145732
  98.9 13.8 %copy-start.16 = (bf16[1,2,256,256]{3,2,1,0:T(8,128)(2,1)S(1)}, bf16[1,2,256,256]{3,2,1,0:T(8,128)(2,1)}, u32[]{:S(2)}) copy-start(bf16[1,2,256,256]{3,2,1,0:T(8,128)(2,1)} %param.7) | copy-start | bytes 786436
  114.1 6.3 %collective-permute-start.12 = (bf16[2,128,256]{2,1,0:T(8,128)(2,1)S(1)}, bf16[2,128,256]{2,1,0:T(8,128)(2,1)S(1)}, u32[]{:S(2)}, u32[]{:S(2)}) collective-permute-start(bf16[2,128,256]{2,1,0:T(8,128)(2,1)S(1)} %get-tuple-element.31), channel_id=1, source_target_pairs={{0,1},{1,2},{2,3},{3,4},{4,5},{5,6},{6,7},{7,8},{8,9},{9,10},{10,1... | collective-permute-start | bytes 393224 | tf_op jit(solution)/shard_map/ppermute | solution.py:15
  116.0 6.1 %collective-permute-start.11 = (bf16[2,128,256]{2,1,0:T(8,128)(2,1)S(1)}, bf16[2,128,256]{2,1,0:T(8,128)(2,1)S(1)}, u32[]{:S(2)}, u32[]{:S(2)}) collective-permute-start(bf16[2,128,256]{2,1,0:T(8,128)(2,1)S(1)} %get-tuple-element.30), channel_id=1, source_target_pairs={{1,0},{2,1},{3,2},{4,3},{5,4},{6,5},{7,6},{8,7},{9,8},{10,9},{11,1... | collective-permute-start | bytes 393224 | tf_op jit(solution)/shard_map/ppermute | solution.py:15
  119.7 4.1 %copy-start.9 = (bf16[2,512,256]{1,2,0:T(8,128)(2,1)S(1)}, bf16[2,512,256]{1,2,0:T(8,128)(2,1)}, u32[]{:S(2)}) copy-start(bf16[2,512,256]{1,2,0:T(8,128)(2,1)} %get-tuple-element.15) | copy-start | bytes 1572868
  119.7 4.1 %copy-start.18 = (bf16[2,512,256]{2,1,0:T(8,128)(2,1)S(1)}, bf16[2,512,256]{2,1,0:T(8,128)(2,1)}, u32[]{:S(2)}) copy-start(bf16[2,512,256]{2,1,0:T(8,128)(2,1)} %param.5) | copy-start | bytes 1572868
  122.4 15.8 %collective-permute-start.13 = (bf16[2,512,256]{2,1,0:T(8,128)(2,1)S(1)}, bf16[2,512,256]{2,1,0:T(8,128)(2,1)S(1)}, u32[]{:S(2)}, u32[]{:S(2)}) collective-permute-start(bf16[2,512,256]{2,1,0:T(8,128)(2,1)S(1)} %fusion.174), channel_id=1, source_target_pairs={{32,0},{64,32},{96,64},{33,1},{65,33},{97,65},{34,2},{66,34},{98,6... | collective-permute-start | bytes 1572872 | tf_op jit(solution)/shard_map/ppermute | solution.py:15
  126.0 12.3 %copy-start.3 = (f32[2,512,256]{1,2,0:T(8,128)S(1)}, f32[2,512,256]{1,2,0:T(8,128)}, u32[]{:S(2)}) copy-start(f32[2,512,256]{1,2,0:T(8,128)} %copy-done.2) | copy-start | bytes 3145732
  126.0 12.3 %copy-start.5 = (f32[2,512,256]{1,2,0:T(8,128)S(1)}, f32[2,512,256]{1,2,0:T(8,128)}, u32[]{:S(2)}) copy-start(f32[2,512,256]{1,2,0:T(8,128)} %copy-done.4) | copy-start | bytes 3145732
  139.7 16.6 %collective-permute-start.15 = (bf16[2,512,256]{2,1,0:T(8,128)(2,1)S(1)}, bf16[2,512,256]{2,1,0:T(8,128)(2,1)S(1)}, u32[]{:S(2)}, u32[]{:S(2)}) collective-permute-start(bf16[2,512,256]{2,1,0:T(8,128)(2,1)S(1)} %get-tuple-element.27), channel_id=1, source_target_pairs={{0,2},{1,3},{2,4},{3,5},{4,6},{5,7},{6,8},{7,9},{8,10},{9,11},{10,... | collective-permute-start | bytes 1572872 | tf_op jit(solution)/shard_map/ppermute | solution.py:15
  142.7 17.6 %collective-permute-start.14 = (bf16[2,512,256]{2,1,0:T(8,128)(2,1)S(1)}, bf16[2,512,256]{2,1,0:T(8,128)(2,1)S(1)}, u32[]{:S(2)}, u32[]{:S(2)}) collective-permute-start(bf16[2,512,256]{2,1,0:T(8,128)(2,1)S(1)} %get-tuple-element.26), channel_id=1, source_target_pairs={{2,0},{3,1},{4,2},{5,3},{6,4},{7,5},{8,6},{9,7},{10,8},{11,9},{12,... | collective-permute-start | bytes 1572872 | tf_op jit(solution)/shard_map/ppermute | solution.py:15
  162.0 6.3 %collective-permute-start.17 = (bf16[2,128,256]{2,1,0:T(8,128)(2,1)S(1)}, bf16[2,128,256]{2,1,0:T(8,128)(2,1)S(1)}, u32[]{:S(2)}, u32[]{:S(2)}) collective-permute-start(bf16[2,128,256]{2,1,0:T(8,128)(2,1)S(1)} %get-tuple-element.25), channel_id=1, source_target_pairs={{0,1},{1,2},{2,3},{3,4},{4,5},{5,6},{6,7},{7,8},{8,9},{9,10},{10,1... | collective-permute-start | bytes 393224 | tf_op jit(solution)/shard_map/ppermute | solution.py:15
  164.0 6.1 %collective-permute-start.16 = (bf16[2,128,256]{2,1,0:T(8,128)(2,1)S(1)}, bf16[2,128,256]{2,1,0:T(8,128)(2,1)S(1)}, u32[]{:S(2)}, u32[]{:S(2)}) collective-permute-start(bf16[2,128,256]{2,1,0:T(8,128)(2,1)S(1)} %get-tuple-element.24), channel_id=1, source_target_pairs={{1,0},{2,1},{3,2},{4,3},{5,4},{6,5},{7,6},{8,7},{9,8},{10,9},{11,1... | collective-permute-start | bytes 393224 | tf_op jit(solution)/shard_map/ppermute | solution.py:15
  170.3 15.8 %collective-permute-start.18 = (bf16[2,512,256]{2,1,0:T(8,128)(2,1)S(1)}, bf16[2,512,256]{2,1,0:T(8,128)(2,1)S(1)}, u32[]{:S(2)}, u32[]{:S(2)}) collective-permute-start(bf16[2,512,256]{2,1,0:T(8,128)(2,1)S(1)} %fusion.175), channel_id=1, source_target_pairs={{32,0},{64,32},{96,64},{33,1},{65,33},{97,65},{34,2},{66,34},{98,6... | collective-permute-start | bytes 1572872 | tf_op jit(solution)/shard_map/ppermute | solution.py:15
  186.8 1.7 collective-permute-start.38
  188.5 4.0 %collective-permute-start.39 = (bf16[8,8,256]{2,1,0:T(8,128)(2,1)S(1)}, bf16[8,8,256]{2,1,0:T(8,128)(2,1)S(1)}, u32[]{:S(2)}, u32[]{:S(2)}) collective-permute-start(bf16[8,8,256]{2,1,0:T(8,128)(2,1)S(1)} %fusion.137), channel_id=1, source_target_pairs={{0,2},{1,3},{2,0},{3,1},{4,6},{5,7},{6,4},{7,5},{8,10},{9,11},{10,... | collective-permute-start | bytes 98312 | tf_op jit(solution)/shard_map/ppermute | solution.py:95
  192.6 5.3 %collective-permute-start.40 = (bf16[4,8,256]{2,1,0:T(8,128)(2,1)S(1)}, bf16[4,8,256]{2,1,0:T(8,128)(2,1)S(1)}, u32[]{:S(2)}, u32[]{:S(2)}) collective-permute-start(bf16[4,8,256]{2,1,0:T(8,128)(2,1)S(1)} %fusion.143), channel_id=1, source_target_pairs={{0,4},{1,5},{2,6},{3,7},{4,0},{5,1},{6,2},{7,3},{8,12},{9,13},{10,... | collective-permute-start | bytes 49160 | tf_op jit(solution)/shard_map/ppermute | solution.py:95
  197.9 3.7 %collective-permute-start.41 = (bf16[2,8,256]{2,1,0:T(8,128)(2,1)S(1)}, bf16[2,8,256]{2,1,0:T(8,128)(2,1)S(1)}, u32[]{:S(2)}, u32[]{:S(2)}) collective-permute-start(bf16[2,8,256]{2,1,0:T(8,128)(2,1)S(1)} %fusion.149), channel_id=1, source_target_pairs={{0,8},{1,9},{2,10},{3,11},{4,12},{5,13},{6,14},{7,15},{8,0},{9,1},... | collective-permute-start | bytes 24584 | tf_op jit(solution)/shard_map/ppermute | solution.py:95
  199.7 10.5 %collective-permute-start.28 = (bf16[16,24,512]{2,1,0:T(8,128)(2,1)S(1)}, bf16[16,24,512]{2,1,0:T(8,128)(2,1)S(1)}, u32[]{:S(2)}, u32[]{:S(2)}) collective-permute-start(bf16[16,24,512]{2,1,0:T(8,128)(2,1)S(1)} %fusion.64), channel_id=1, source_target_pairs={{0,1},{1,0},{2,3},{3,2},{4,5},{5,4},{6,7},{7,6},{8,9},{9,8},{10,11... | collective-permute-start | bytes 1179656 | tf_op jit(solution)/shard_map/ppermute | solution.py:95
  201.6 8.5 %collective-permute-start.42 = (bf16[1,8,256]{2,1,0:T(8,128)(2,1)S(1)}, bf16[1,8,256]{2,1,0:T(8,128)(2,1)S(1)}, u32[]{:S(2)}, u32[]{:S(2)}) collective-permute-start(bf16[1,8,256]{2,1,0:T(8,128)(2,1)S(1)} %fusion.153), channel_id=1, source_target_pairs={{0,16},{1,17},{2,18},{3,19},{4,20},{5,21},{6,22},{7,23},{8,24},{9,... | collective-permute-start | bytes 12296 | tf_op jit(solution)/shard_map/ppermute | solution.py:95
  204.3 14.6 %collective-permute-start.20 = (bf16[2,512,256]{2,1,0:T(8,128)(2,1)S(1)}, bf16[2,512,256]{2,1,0:T(8,128)(2,1)S(1)}, u32[]{:S(2)}, u32[]{:S(2)}) collective-permute-start(bf16[2,512,256]{2,1,0:T(8,128)(2,1)S(1)} %get-tuple-element.21), channel_id=1, source_target_pairs={{0,2},{1,3},{2,4},{3,5},{4,6},{5,7},{6,8},{7,9},{8,10},{9,11},{10,... | collective-permute-start | bytes 1572872 | tf_op jit(solution)/shard_map/ppermute | solution.py:15
  206.2 15.4 %collective-permute-start.19 = (bf16[2,512,256]{2,1,0:T(8,128)(2,1)S(1)}, bf16[2,512,256]{2,1,0:T(8,128)(2,1)S(1)}, u32[]{:S(2)}, u32[]{:S(2)}) collective-permute-start(bf16[2,512,256]{2,1,0:T(8,128)(2,1)S(1)} %get-tuple-element.20), channel_id=1, source_target_pairs={{2,0},{3,1},{4,2},{5,3},{6,4},{7,5},{8,6},{9,7},{10,8},{11,9},{12,... | collective-permute-start | bytes 1572872 | tf_op jit(solution)/shard_map/ppermute | solution.py:15
  210.4 30.8 %collective-permute-start.29 = (bf16[8,24,512]{2,1,0:T(8,128)(2,1)S(1)}, bf16[8,24,512]{2,1,0:T(8,128)(2,1)S(1)}, u32[]{:S(2)}, u32[]{:S(2)}) collective-permute-start(bf16[8,24,512]{2,1,0:T(8,128)(2,1)S(1)} %fusion.98), channel_id=1, source_target_pairs={{0,2},{1,3},{2,0},{3,1},{4,6},{5,7},{6,4},{7,5},{8,10},{9,11},{10,... | collective-permute-start | bytes 589832 | tf_op jit(solution)/shard_map/ppermute | solution.py:95
  223.7 25.3 %collective-permute-start.21 = (bf16[2,128,256]{2,1,0:T(8,128)(2,1)S(1)}, bf16[2,128,256]{2,1,0:T(8,128)(2,1)S(1)}, u32[]{:S(2)}, u32[]{:S(2)}) collective-permute-start(bf16[2,128,256]{2,1,0:T(8,128)(2,1)S(1)} %get-tuple-element.17), channel_id=1, source_target_pairs={{1,0},{2,1},{3,2},{4,3},{5,4},{6,5},{7,6},{8,7},{9,8},{10,9},{11,1... | collective-permute-start | bytes 393224 | tf_op jit(solution)/shard_map/ppermute | solution.py:15
  225.6 23.3 %collective-permute-start.22 = (bf16[2,128,256]{2,1,0:T(8,128)(2,1)S(1)}, bf16[2,128,256]{2,1,0:T(8,128)(2,1)S(1)}, u32[]{:S(2)}, u32[]{:S(2)}) collective-permute-start(bf16[2,128,256]{2,1,0:T(8,128)(2,1)S(1)} %get-tuple-element.16), channel_id=1, source_target_pairs={{0,1},{1,2},{2,3},{3,4},{4,5},{5,6},{6,7},{7,8},{8,9},{9,10},{10,1... | collective-permute-start | bytes 393224 | tf_op jit(solution)/shard_map/ppermute | solution.py:15
  228.4 1.4 collective-permute-start.33
  229.8 4.0 %collective-permute-start.34 = (bf16[8,8,256]{2,1,0:T(8,128)(2,1)S(1)}, bf16[8,8,256]{2,1,0:T(8,128)(2,1)S(1)}, u32[]{:S(2)}, u32[]{:S(2)}) collective-permute-start(bf16[8,8,256]{2,1,0:T(8,128)(2,1)S(1)} %fusion.136), channel_id=1, source_target_pairs={{0,2},{1,3},{2,0},{3,1},{4,6},{5,7},{6,4},{7,5},{8,10},{9,11},{10,... | collective-permute-start | bytes 98312 | tf_op jit(solution)/shard_map/ppermute | solution.py:95
  231.3 17.6 %copy-start.14 = (bf16[2,384,256]{2,1,0:T(8,128)(2,1)S(1)}, bf16[2,384,256]{2,1,0:T(8,128)(2,1)}, u32[]{:S(2)}) copy-start(bf16[2,384,256]{2,1,0:T(8,128)(2,1)} %copy-done.13) | copy-start | bytes 1179652
  231.3 17.6 %copy-start.40 = (bf16[2,128,256]{2,1,0:T(8,128)(2,1)S(1)}, bf16[2,128,256]{2,1,0:T(8,128)(2,1)}, u32[]{:S(2)}) copy-start(bf16[2,128,256]{2,1,0:T(8,128)(2,1)} %copy-done.39) | copy-start | bytes 393220
  231.3 17.6 %copy-start.42 = (bf16[2,128,256]{2,1,0:T(8,128)(2,1)S(1)}, bf16[2,128,256]{2,1,0:T(8,128)(2,1)}, u32[]{:S(2)}) copy-start(bf16[2,128,256]{2,1,0:T(8,128)(2,1)} %copy-done.41) | copy-start | bytes 393220
  233.8 5.3 %collective-permute-start.35 = (bf16[4,8,256]{2,1,0:T(8,128)(2,1)S(1)}, bf16[4,8,256]{2,1,0:T(8,128)(2,1)S(1)}, u32[]{:S(2)}, u32[]{:S(2)}) collective-permute-start(bf16[4,8,256]{2,1,0:T(8,128)(2,1)S(1)} %fusion.142), channel_id=1, source_target_pairs={{0,4},{1,5},{2,6},{3,7},{4,0},{5,1},{6,2},{7,3},{8,12},{9,13},{10,... | collective-permute-start | bytes 49160 | tf_op jit(solution)/shard_map/ppermute | solution.py:95
  236.3 15.7 %collective-permute-start.23 = (bf16[16,24,512]{2,1,0:T(8,128)(2,1)S(1)}, bf16[16,24,512]{2,1,0:T(8,128)(2,1)S(1)}, u32[]{:S(2)}, u32[]{:S(2)}) collective-permute-start(bf16[16,24,512]{2,1,0:T(8,128)(2,1)S(1)} %fusion.63), channel_id=1, source_target_pairs={{0,1},{1,0},{2,3},{3,2},{4,5},{5,4},{6,7},{7,6},{8,9},{9,8},{10,11... | collective-permute-start | bytes 1179656 | tf_op jit(solution)/shard_map/ppermute | solution.py:95
  239.2 3.7 %collective-permute-start.36 = (bf16[2,8,256]{2,1,0:T(8,128)(2,1)S(1)}, bf16[2,8,256]{2,1,0:T(8,128)(2,1)S(1)}, u32[]{:S(2)}, u32[]{:S(2)}) collective-permute-start(bf16[2,8,256]{2,1,0:T(8,128)(2,1)S(1)} %fusion.148), channel_id=1, source_target_pairs={{0,8},{1,9},{2,10},{3,11},{4,12},{5,13},{6,14},{7,15},{8,0},{9,1},... | collective-permute-start | bytes 24584 | tf_op jit(solution)/shard_map/ppermute | solution.py:95
  242.9 5.4 %collective-permute-start.37 = (bf16[1,8,256]{2,1,0:T(8,128)(2,1)S(1)}, bf16[1,8,256]{2,1,0:T(8,128)(2,1)S(1)}, u32[]{:S(2)}, u32[]{:S(2)}) collective-permute-start(bf16[1,8,256]{2,1,0:T(8,128)(2,1)S(1)} %fusion.152), channel_id=1, source_target_pairs={{0,16},{1,17},{2,18},{3,19},{4,20},{5,21},{6,22},{7,23},{8,24},{9,... | collective-permute-start | bytes 12296 | tf_op jit(solution)/shard_map/ppermute | solution.py:95
  245.3 6.7 %collective-permute-start.30 = (bf16[4,24,512]{2,1,0:T(8,128)(2,1)S(1)}, bf16[4,24,512]{2,1,0:T(8,128)(2,1)S(1)}, u32[]{:S(2)}, u32[]{:S(2)}) collective-permute-start(bf16[4,24,512]{2,1,0:T(8,128)(2,1)S(1)} %fusion.114), channel_id=1, source_target_pairs={{0,4},{1,5},{2,6},{3,7},{4,0},{5,1},{6,2},{7,3},{8,12},{9,13},{10,... | collective-permute-start | bytes 294920 | tf_op jit(solution)/shard_map/ppermute | solution.py:95
  252.3 6.8 %collective-permute-start.24 = (bf16[8,24,512]{2,1,0:T(8,128)(2,1)S(1)}, bf16[8,24,512]{2,1,0:T(8,128)(2,1)S(1)}, u32[]{:S(2)}, u32[]{:S(2)}) collective-permute-start(bf16[8,24,512]{2,1,0:T(8,128)(2,1)S(1)} %fusion.97), channel_id=1, source_target_pairs={{0,2},{1,3},{2,0},{3,1},{4,6},{5,7},{6,4},{7,5},{8,10},{9,11},{10,... | collective-permute-start | bytes 589832 | tf_op jit(solution)/shard_map/ppermute | solution.py:95
  253.9 8.9 %collective-permute-start.31 = (bf16[2,24,512]{2,1,0:T(8,128)(2,1)S(1)}, bf16[2,24,512]{2,1,0:T(8,128)(2,1)S(1)}, u32[]{:S(2)}, u32[]{:S(2)}) collective-permute-start(bf16[2,24,512]{2,1,0:T(8,128)(2,1)S(1)} %fusion.133), channel_id=1, source_target_pairs={{0,8},{1,9},{2,10},{3,11},{4,12},{5,13},{6,14},{7,15},{8,0},{9,1},... | collective-permute-start | bytes 147464 | tf_op jit(solution)/shard_map/ppermute | solution.py:95
  259.2 6.2 %collective-permute-start.25 = (bf16[4,24,512]{2,1,0:T(8,128)(2,1)S(1)}, bf16[4,24,512]{2,1,0:T(8,128)(2,1)S(1)}, u32[]{:S(2)}, u32[]{:S(2)}) collective-permute-start(bf16[4,24,512]{2,1,0:T(8,128)(2,1)S(1)} %fusion.113), channel_id=1, source_target_pairs={{0,4},{1,5},{2,6},{3,7},{4,0},{5,1},{6,2},{7,3},{8,12},{9,13},{10,... | collective-permute-start | bytes 294920 | tf_op jit(solution)/shard_map/ppermute | solution.py:95
  265.5 4.2 %collective-permute-start.26 = (bf16[2,24,512]{2,1,0:T(8,128)(2,1)S(1)}, bf16[2,24,512]{2,1,0:T(8,128)(2,1)S(1)}, u32[]{:S(2)}, u32[]{:S(2)}) collective-permute-start(bf16[2,24,512]{2,1,0:T(8,128)(2,1)S(1)} %fusion.132), channel_id=1, source_target_pairs={{0,8},{1,9},{2,10},{3,11},{4,12},{5,13},{6,14},{7,15},{8,0},{9,1},... | collective-permute-start | bytes 147464 | tf_op jit(solution)/shard_map/ppermute | solution.py:95
  266.3 5.5 %collective-permute-start.32 = (bf16[1,24,512]{2,1,0:T(8,128)(2,1)S(1)}, bf16[1,24,512]{2,1,0:T(8,128)(2,1)S(1)}, u32[]{:S(2)}, u32[]{:S(2)}) collective-permute-start(bf16[1,24,512]{2,1,0:T(8,128)(2,1)S(1)} %fusion.141), channel_id=1, source_target_pairs={{0,16},{1,17},{2,18},{3,19},{4,20},{5,21},{6,22},{7,23},{8,24},{9,... | collective-permute-start | bytes 73736 | tf_op jit(solution)/shard_map/ppermute | solution.py:95
  269.7 5.4 %collective-permute-start.27 = (bf16[1,24,512]{2,1,0:T(8,128)(2,1)S(1)}, bf16[1,24,512]{2,1,0:T(8,128)(2,1)S(1)}, u32[]{:S(2)}, u32[]{:S(2)}) collective-permute-start(bf16[1,24,512]{2,1,0:T(8,128)(2,1)S(1)} %fusion.140), channel_id=1, source_target_pairs={{0,16},{1,17},{2,18},{3,19},{4,20},{5,21},{6,22},{7,23},{8,24},{9,... | collective-permute-start | bytes 73736 | tf_op jit(solution)/shard_map/ppermute | solution.py:95
  (26 other events, 43.7 us)
where the time goes:
time: 279 us; the launch traced here: 276 us
  waiting for transfers between devices  132 us (47%)
  starting transfers between devices  94.1 us (34%)
  matrix products  33.7 us (12%)
  other arithmetic  9.23 us (3%)
  local copies, waits for them, and re-layouts  4.83 us (2%)
    ppermute x23, waiting for transfers between devices, shifted(): lax.ppermute(value, axis, [(source, source + steps) for source in range(l...  105 us
    ppermute x23, starting transfers between devices, shifted(): lax.ppermute(value, axis, [(source, source + steps) for source in range(l...  64.6 us
    ppermute x20, starting transfers between devices, halving_scatter(): got = lax.ppermute(sends, 'seq', pairs)  29.4 us
    ppermute x20, waiting for transfers between devices, halving_scatter(): got = lax.ppermute(sends, 'seq', pairs)  26.5 us
    dot_general x8, matrix products, backward_layer(): jnp.einsum('mpc,mpd->cd', taps, grad_pre, preferred_element_type=jnp.floa...  9.91 us
    dot_general x8, matrix products, backward_layer(): jnp.einsum('mpd,cd->mpc', grad_pre, weights, preferred_element_type=jnp.f...  9.87 us
    dot_general x8, matrix products, backward_layer(): jnp.einsum('mpd,cd->mpc', grad_half, out_mat, preferred_element_type=jnp....  5.76 us
    dot_general x7, matrix products, mm(): return jnp.einsum('mpc,cd->mpd', a, b, preferred_element_type=jnp.float32)  5.75 us
  transfers between devices with their start and end apart: 43, of which 30 were waited for; matrix products, arithmetic and copies ran while one was open for 9% of the time, Pallas kernels for 0%

commit v1 on v0

--- a/solution.py
+++ b/solution.py
@@ -141,19 +141,15 @@
 
     conv_rows = 3 * channels // seq_count
     out_rows = channels // seq_count
-    conv_parts = []
-    out_parts = []
-    for layer in range(depth):
-        conv_mine, out_mine = halving_scatter(
-            [
-                conv_acc[layer].reshape(seq_count, conv_rows, 2 * channels),
-                out_acc[layer].reshape(seq_count, out_rows, channels),
-            ]
-        )
-        conv_parts.append(conv_mine)
-        out_parts.append(out_mine)
-    conv_grads = jnp.stack(conv_parts)[None] * grad_scale
-    out_grads = jnp.stack(out_parts)[None] * grad_scale
+    conv_all = jnp.concatenate(
+        [acc.reshape(seq_count, conv_rows, 2 * channels) for acc in conv_acc], axis=1
+    )
+    out_all = jnp.concatenate(
+        [acc.reshape(seq_count, out_rows, channels) for acc in out_acc], axis=1
+    ).reshape(seq_count, depth * out_rows * channels // (2 * channels), 2 * channels)
+    (mine,) = halving_scatter([jnp.concatenate([conv_all, out_all], axis=1)])
+    conv_grads = mine[: depth * conv_rows].reshape(1, depth, conv_rows, 2 * channels) * grad_scale
+    out_grads = mine[depth * conv_rows :].reshape(1, depth, out_rows, channels) * grad_scale
     return (input_grads[None], conv_grads, out_grads)
 
 

time: 279 us -> 271 us (0.971)
  starting transfers between devices: 94.1 us -> 67.7 us
  matrix products: 33.7 us -> 43.3 us
  local copies, waits for them, and re-layouts: 4.83 us -> 11.1 us
  other arithmetic: 9.23 us -> 15.4 us
  waiting for transfers between devices: 132 us -> 127 us
    ppermute x20 -> x5, starting transfers between devices: 29.4 us -> 3.1 us  [halving_scatter(): got = lax.ppermute(sends, 'seq', pairs)]
    dot_general x8, matrix products: 9.91 us -> 17.4 us  [backward_layer(): jnp.einsum('mpc,mpd->cd', taps, grad_pre, preferred_element_type=jnp.floa...]
    ppermute x20 -> x5, waiting for transfers between devices: 26.5 us -> 21.6 us  [halving_scatter(): got = lax.ppermute(sends, 'seq', pairs)]
    unnamed x94 -> x162, local copies, waits for them, and re-layouts: 2.08 us -> 5.69 us
    add x12 -> x4, other arithmetic: 0.71 us -> 4.22 us  [halving_scatter(): jnp.where(own, h[:, 1], h[:, 0]) + g.astype(jnp.float32)]
  transfers between devices with their start and end apart: 43 -> 28, of which waited for: 30 -> 23; matrix products, arithmetic and copies ran while one was open for 9% -> 9% of each run, Pallas kernels for 0% -> 0%
where the time goes in v1:
time: 271 us; the launch traced here: 267 us
  waiting for transfers between devices  127 us (47%)
  starting transfers between devices  67.7 us (25%)
  matrix products  43.3 us (16%)
  other arithmetic  15.4 us (6%)
  local copies, waits for them, and re-layouts  11.1 us (4%)
    ppermute x23, waiting for transfers between devices, shifted(): lax.ppermute(value, axis, [(source, source + steps) for source in range(l...  106 us
    ppermute x23, starting transfers between devices, shifted(): lax.ppermute(value, axis, [(source, source + steps) for source in range(l...  64.6 us
    ppermute x5, waiting for transfers between devices, halving_scatter(): got = lax.ppermute(sends, 'seq', pairs)  21.6 us
    dot_general x8, matrix products, backward_layer(): jnp.einsum('mpc,mpd->cd', taps, grad_pre, preferred_element_type=jnp.floa...  17.4 us
    dot_general x8, matrix products, backward_layer(): jnp.einsum('mpd,cd->mpc', grad_pre, weights, preferred_element_type=jnp.f...  11.1 us
    dot_general x8, matrix products, backward_layer(): jnp.einsum('mpd,cd->mpc', grad_half, out_mat, preferred_element_type=jnp....  6.57 us
    dot_general x7, matrix products, mm(): return jnp.einsum('mpc,cd->mpd', a, b, preferred_element_type=jnp.float32)  5.77 us
    unnamed x162, local copies, waits for them, and re-layouts  5.69 us
  transfers between devices with their start and end apart: 28, of which 23 were waited for; matrix products, arithmetic and copies ran while one was open for 9% of the time, Pallas kernels for 0%

profile of v1, /device:TPU:24, one launch (start us, length us, event | category | flops | bytes accessed | tf_op | source)
XLA Modules:
  0.0 267.0 jit_solution(6039316135187077539)
XLA Ops:
  1.7 1.9 collective-permute-start
  3.6 3.6 %collective-permute-start.1 = (bf16[2,128,256]{2,1,0:T(8,128)(2,1)S(1)}, bf16[2,128,256]{2,1,0:T(8,128)(2,1)S(1)}, u32[]{:S(2)}, u32[]{:S(2)}) collective-permute-start(bf16[2,128,256]{2,1,0:T(8,128)(2,1)S(1)} %get-tuple-element.56), channel_id=1, source_target_pairs={{1,0},{2,1},{3,2},{4,3},{5,4},{6,5},{7,6},{8,7},{9,8},{10,9},{11,1... | collective-permute-start | bytes 393224 | tf_op jit(solution)/shard_map/ppermute | solution.py:15
  7.3 1.6 fusion.80
  9.0 1.8 fusion.55
  12.8 5.6 %collective-permute-start.2 = (bf16[2,512,256]{2,1,0:T(8,128)(2,1)S(1)}, bf16[2,512,256]{2,1,0:T(8,128)(2,1)S(1)}, u32[]{:S(2)}, u32[]{:S(2)}) collective-permute-start(bf16[2,512,256]{2,1,0:T(8,128)(2,1)S(1)} %fusion), channel_id=1, source_target_pairs={{0,2},{1,3},{2,4},{3,5},{4,6},{5,7},{6,8},{7,9},{8,10},{9,11},{10,... | collective-permute-start | bytes 1572872 | tf_op jit(solution)/shard_map/ppermute | solution.py:15
  18.5 1.9 collective-permute-start.3
  21.0 8.2 %collective-permute-done.2 = bf16[2,512,256]{2,1,0:T(8,128)(2,1)S(1)} collective-permute-done((bf16[2,512,256]{2,1,0:T(8,128)(2,1)S(1)}, bf16[2,512,256]{2,1,0:T(8,128)(2,1)S(1)}, u32[]{:S(2)}, u32[]{:S(2)}) %collective-permute-start.2) | collective-permute-done | bytes 524320 | tf_op jit(solution)/shard_map/ppermute | solution.py:15
  30.0 5.5 %collective-permute-done.3 = bf16[2,512,256]{2,1,0:T(8,128)(2,1)S(1)} collective-permute-done((bf16[2,512,256]{2,1,0:T(8,128)(2,1)S(1)}, bf16[2,512,256]{2,1,0:T(8,128)(2,1)S(1)}, u32[]{:S(2)}, u32[]{:S(2)}) %collective-permute-start.3) | collective-permute-done | bytes 524320 | tf_op jit(solution)/shard_map/ppermute | solution.py:15
  36.4 1.5 multiply_convert_fusion.15
  39.0 1.9 collective-permute-start.5
  41.0 3.9 %collective-permute-start.4 = (bf16[2,512,256]{2,1,0:T(8,128)(2,1)S(1)}, bf16[2,512,256]{2,1,0:T(8,128)(2,1)S(1)}, u32[]{:S(2)}, u32[]{:S(2)}) collective-permute-start(bf16[2,512,256]{2,1,0:T(8,128)(2,1)S(1)} %get-tuple-element.40), channel_id=1, source_target_pairs={{2,0},{3,1},{4,2},{5,3},{6,4},{7,5},{8,6},{9,7},{10,8},{11,9},{12,... | collective-permute-start | bytes 1572872 | tf_op jit(solution)/shard_map/ppermute | solution.py:15
  44.9 8.2 %collective-permute-done.5 = bf16[2,512,256]{2,1,0:T(8,128)(2,1)S(1)} collective-permute-done((bf16[2,512,256]{2,1,0:T(8,128)(2,1)S(1)}, bf16[2,512,256]{2,1,0:T(8,128)(2,1)S(1)}, u32[]{:S(2)}, u32[]{:S(2)}) %collective-permute-start.5) | collective-permute-done | bytes 524320 | tf_op jit(solution)/shard_map/ppermute | solution.py:15
  53.1 4.0 %collective-permute-done.4 = bf16[2,512,256]{2,1,0:T(8,128)(2,1)S(1)} collective-permute-done((bf16[2,512,256]{2,1,0:T(8,128)(2,1)S(1)}, bf16[2,512,256]{2,1,0:T(8,128)(2,1)S(1)}, u32[]{:S(2)}, u32[]{:S(2)}) %collective-permute-start.4) | collective-permute-done | bytes 524320 | tf_op jit(solution)/shard_map/ppermute | solution.py:15
  57.3 2.0 multiply_convert_fusion.13
  60.5 1.9 collective-permute-start.7
  62.4 3.6 %collective-permute-start.6 = (bf16[2,128,256]{2,1,0:T(8,128)(2,1)S(1)}, bf16[2,128,256]{2,1,0:T(8,128)(2,1)S(1)}, u32[]{:S(2)}, u32[]{:S(2)}) collective-permute-start(bf16[2,128,256]{2,1,0:T(8,128)(2,1)S(1)} %get-tuple-element.36), channel_id=1, source_target_pairs={{1,0},{2,1},{3,2},{4,3},{5,4},{6,5},{7,6},{8,7},{9,8},{10,9},{11,1... | collective-permute-start | bytes 393224 | tf_op jit(solution)/shard_map/ppermute | solution.py:15
  66.8 1.8 collective-permute-done.6
  68.9 1.3 collective-permute-start.8
  70.2 12.8 %collective-permute-done.8 = bf16[2,512,256]{2,1,0:T(8,128)(2,1)S(1)} collective-permute-done((bf16[2,512,256]{2,1,0:T(8,128)(2,1)S(1)}, bf16[2,512,256]{2,1,0:T(8,128)(2,1)S(1)}, u32[]{:S(2)}, u32[]{:S(2)}) %collective-permute-start.8) | collective-permute-done | bytes 524320 | tf_op jit(solution)/shard_map/ppermute | solution.py:15
  84.2 2.7 %fusion.167 = (bf16[2,512,768]{2,1,0:T(8,128)(2,1)S(1)}, f32[2,512,768]{2,1,0:T(8,128)}) fusion(bf16[768,512,1]{1,0,2:T(8,128)(2,1)S(1)} %bitcast.286, bf16[2,512,256]{1,2,0:T(8,128)(2,1)S(1)} %get-tuple-element.53, bf16[2,512,256]{1,2,0:T(8,128)(2,1)S(1)} %get-tuple-element.52), kind=kOutput, calls=%fused_computation.237 | convolution fusion | flops 808189952 | bytes 6553600 | tf_op jit(solution)/shard_map/mpd,cd->mpc/dot_general | solution.py:64
  88.0 6.7 %collective-permute-start.10 = (bf16[2,512,256]{2,1,0:T(8,128)(2,1)}, bf16[2,512,256]{2,1,0:T(8,128)(2,1)}, u32[]{:S(2)}, u32[]{:S(2)}) collective-permute-start(bf16[2,512,256]{2,1,0:T(8,128)(2,1)} %get-tuple-element.33), channel_id=1, source_target_pairs={{0,2},{1,3},{2,4},{3,5},{4,6},{5,7},{6,8},{7,9},{8,10},{9,11},{10,... | collective-permute-start | bytes 1572872 | tf_op jit(solution)/shard_map/ppermute | solution.py:15
  94.7 2.1 collective-permute-start.9
  96.8 2.4 fusion.53
  99.3 6.0 %collective-permute-done.10 = bf16[2,512,256]{2,1,0:T(8,128)(2,1)} collective-permute-done((bf16[2,512,256]{2,1,0:T(8,128)(2,1)}, bf16[2,512,256]{2,1,0:T(8,128)(2,1)}, u32[]{:S(2)}, u32[]{:S(2)}) %collective-permute-start.10) | collective-permute-done | bytes 524320 | tf_op jit(solution)/shard_map/ppermute | solution.py:15
  105.3 6.2 %collective-permute-done.9 = bf16[2,512,256]{2,1,0:T(8,128)(2,1)} collective-permute-done((bf16[2,512,256]{2,1,0:T(8,128)(2,1)}, bf16[2,512,256]{2,1,0:T(8,128)(2,1)}, u32[]{:S(2)}, u32[]{:S(2)}) %collective-permute-start.9) | collective-permute-done | bytes 524320 | tf_op jit(solution)/shard_map/ppermute | solution.py:15
  111.5 1.8 fusion.22
  114.7 1.9 collective-permute-start.12
  116.7 3.6 %collective-permute-start.11 = (bf16[2,128,256]{2,1,0:T(8,128)(2,1)S(1)}, bf16[2,128,256]{2,1,0:T(8,128)(2,1)S(1)}, u32[]{:S(2)}, u32[]{:S(2)}) collective-permute-start(bf16[2,128,256]{2,1,0:T(8,128)(2,1)S(1)} %get-tuple-element.30), channel_id=1, source_target_pairs={{1,0},{2,1},{3,2},{4,3},{5,4},{6,5},{7,6},{8,7},{9,8},{10,9},{11,1... | collective-permute-start | bytes 393224 | tf_op jit(solution)/shard_map/ppermute | solution.py:15
  121.0 1.8 collective-permute-done.11
  123.2 1.4 collective-permute-start.13
  125.1 2.2 fusion.51
  128.4 10.6 %collective-permute-done.13 = bf16[2,512,256]{2,1,0:T(8,128)(2,1)S(1)} collective-permute-done((bf16[2,512,256]{2,1,0:T(8,128)(2,1)S(1)}, bf16[2,512,256]{2,1,0:T(8,128)(2,1)S(1)}, u32[]{:S(2)}, u32[]{:S(2)}) %collective-permute-start.13) | collective-permute-done | bytes 524320 | tf_op jit(solution)/shard_map/ppermute | solution.py:15
  140.5 3.0 %collective-permute-start.15 = (bf16[2,512,256]{2,1,0:T(8,128)(2,1)S(1)}, bf16[2,512,256]{2,1,0:T(8,128)(2,1)S(1)}, u32[]{:S(2)}, u32[]{:S(2)}) collective-permute-start(bf16[2,512,256]{2,1,0:T(8,128)(2,1)S(1)} %get-tuple-element.27), channel_id=1, source_target_pairs={{0,2},{1,3},{2,4},{3,5},{4,6},{5,7},{6,8},{7,9},{8,10},{9,11},{10,... | collective-permute-start | bytes 1572872 | tf_op jit(solution)/shard_map/ppermute | solution.py:15
  143.5 2.8 %collective-permute-start.14 = (bf16[2,512,256]{2,1,0:T(8,128)(2,1)S(1)}, bf16[2,512,256]{2,1,0:T(8,128)(2,1)S(1)}, u32[]{:S(2)}, u32[]{:S(2)}) collective-permute-start(bf16[2,512,256]{2,1,0:T(8,128)(2,1)S(1)} %get-tuple-element.26), channel_id=1, source_target_pairs={{2,0},{3,1},{4,2},{5,3},{6,4},{7,5},{8,6},{9,7},{10,8},{11,9},{12,... | collective-permute-start | bytes 1572872 | tf_op jit(solution)/shard_map/ppermute | solution.py:15
  146.7 2.2 fusion.47
  149.9 7.2 %collective-permute-done.15 = bf16[2,512,256]{2,1,0:T(8,128)(2,1)S(1)} collective-permute-done((bf16[2,512,256]{2,1,0:T(8,128)(2,1)S(1)}, bf16[2,512,256]{2,1,0:T(8,128)(2,1)S(1)}, u32[]{:S(2)}, u32[]{:S(2)}) %collective-permute-start.15) | collective-permute-done | bytes 524320 | tf_op jit(solution)/shard_map/ppermute | solution.py:15
  157.1 4.0 %collective-permute-done.14 = bf16[2,512,256]{2,1,0:T(8,128)(2,1)S(1)} collective-permute-done((bf16[2,512,256]{2,1,0:T(8,128)(2,1)S(1)}, bf16[2,512,256]{2,1,0:T(8,128)(2,1)S(1)}, u32[]{:S(2)}, u32[]{:S(2)}) %collective-permute-start.14) | collective-permute-done | bytes 524320 | tf_op jit(solution)/shard_map/ppermute | solution.py:15
  162.8 1.9 collective-permute-start.17
  164.7 3.6 %collective-permute-start.16 = (bf16[2,128,256]{2,1,0:T(8,128)(2,1)S(1)}, bf16[2,128,256]{2,1,0:T(8,128)(2,1)S(1)}, u32[]{:S(2)}, u32[]{:S(2)}) collective-permute-start(bf16[2,128,256]{2,1,0:T(8,128)(2,1)S(1)} %get-tuple-element.24), channel_id=1, source_target_pairs={{1,0},{2,1},{3,2},{4,3},{5,4},{6,5},{7,6},{8,7},{9,8},{10,9},{11,1... | collective-permute-start | bytes 393224 | tf_op jit(solution)/shard_map/ppermute | solution.py:15
  169.0 1.8 collective-permute-done.16
  171.1 1.5 collective-permute-start.18
  173.3 2.2 fusion.43
  175.5 11.4 %collective-permute-done.18 = bf16[2,512,256]{2,1,0:T(8,128)(2,1)S(1)} collective-permute-done((bf16[2,512,256]{2,1,0:T(8,128)(2,1)S(1)}, bf16[2,512,256]{2,1,0:T(8,128)(2,1)S(1)}, u32[]{:S(2)}, u32[]{:S(2)}) %collective-permute-start.18) | collective-permute-done | bytes 524320 | tf_op jit(solution)/shard_map/ppermute | solution.py:15
  188.4 3.7 %collective-permute-start.20 = (bf16[2,512,256]{2,1,0:T(8,128)(2,1)S(1)}, bf16[2,512,256]{2,1,0:T(8,128)(2,1)S(1)}, u32[]{:S(2)}, u32[]{:S(2)}) collective-permute-start(bf16[2,512,256]{2,1,0:T(8,128)(2,1)S(1)} %get-tuple-element.21), channel_id=1, source_target_pairs={{0,2},{1,3},{2,4},{3,5},{4,6},{5,7},{6,8},{7,9},{8,10},{9,11},{10,... | collective-permute-start | bytes 1572872 | tf_op jit(solution)/shard_map/ppermute | solution.py:15
  192.1 2.2 collective-permute-start.19
  194.8 2.2 bitcast_add_fusion.1
  197.0 7.8 %collective-permute-done.20 = bf16[2,512,256]{2,1,0:T(8,128)(2,1)S(1)} collective-permute-done((bf16[2,512,256]{2,1,0:T(8,128)(2,1)S(1)}, bf16[2,512,256]{2,1,0:T(8,128)(2,1)S(1)}, u32[]{:S(2)}, u32[]{:S(2)}) %collective-permute-start.20) | collective-permute-done | bytes 524320 | tf_op jit(solution)/shard_map/ppermute | solution.py:15
  204.8 4.1 %collective-permute-done.19 = bf16[2,512,256]{2,1,0:T(8,128)(2,1)S(1)} collective-permute-done((bf16[2,512,256]{2,1,0:T(8,128)(2,1)S(1)}, bf16[2,512,256]{2,1,0:T(8,128)(2,1)S(1)}, u32[]{:S(2)}, u32[]{:S(2)}) %collective-permute-start.19) | collective-permute-done | bytes 524320 | tf_op jit(solution)/shard_map/ppermute | solution.py:15
  209.2 1.3 multiply_convert_fusion.1
  212.3 2.0 concatenate.104
  214.3 4.2 %bitcast_add_fusion.4 = f32[768,512]{1,0:T(8,128)S(1)} fusion(f32[768,512,1]{1,0,2:T(8,128)} %fusion.43, f32[768,512,1]{1,0,2:T(8,128)} %fusion.47, f32[768,512,1]{1,0,2:T(8,128)} %fusion.51, bf16[2,512,256]{1,2,0:T(8,128)(2,1)} %get-tuple-element.43, bf16[2,512,256]{1,2,0:T(8,128)(2,1)} %get-tuple-element.42, bf16[2,128,256]{2,1,0:T(8,128)(2,1)} %copy-done.77, ...), kind=kOutput, calls=%fused_computation.12 | convolution fusion | flops 816447488 | bytes 8912896 | tf_op jit(solution)/shard_map/mpc,mpd->cd/dot_general | solution.py:62
  219.1 1.8 copy-done
  222.1 2.8 %collective-permute-done.23 = bf16[16,56,512]{2,1,0:T(8,128)(2,1)} collective-permute-done((bf16[16,56,512]{2,1,0:T(8,128)(2,1)}, bf16[16,56,512]{2,1,0:T(8,128)(2,1)}, u32[]{:S(2)}, u32[]{:S(2)}) %collective-permute-start.23) | collective-permute-done | bytes 917536 | tf_op jit(solution)/shard_map/ppermute | solution.py:95
  224.9 2.8 %bitcast_add_fusion = f32[16,56,512]{2,1,0:T(8,128)S(1)} fusion(bf16[16,56,512]{2,1,0:T(8,128)(2,1)} %collective-permute-done.23, f32[16,2,56,512]{3,2,1,0:T(8,128)} %copy-done, pred[]{:T(512)S(6)} %eq.23), kind=kLoop, calls=%fused_computation.5 | loop fusion | flops 1376256 | bytes 6422529 | tf_op jit(solution)/shard_map/add | solution.py:96
  229.8 2.2 fusion.172
  232.0 10.7 %collective-permute-done.24 = bf16[8,56,512]{2,1,0:T(8,128)(2,1)} collective-permute-done((bf16[8,56,512]{2,1,0:T(8,128)(2,1)}, bf16[8,56,512]{2,1,0:T(8,128)(2,1)}, u32[]{:S(2)}, u32[]{:S(2)}) %collective-permute-start.24) | collective-permute-done | bytes 458784 | tf_op jit(solution)/shard_map/ppermute | solution.py:95
  242.7 1.2 fusion.38
  244.3 8.1 %collective-permute-done.25 = bf16[4,56,512]{2,1,0:T(8,128)(2,1)S(1)} collective-permute-done((bf16[4,56,512]{2,1,0:T(8,128)(2,1)S(1)}, bf16[4,56,512]{2,1,0:T(8,128)(2,1)S(1)}, u32[]{:S(2)}, u32[]{:S(2)}) %collective-permute-start.25) | collective-permute-done | bytes 229408 | tf_op jit(solution)/shard_map/ppermute | solution.py:95
  252.5 1.7 collective-permute-start.26
  254.2 1.9 collective-permute-start.21
  256.1 2.4 collective-permute-start.22
  258.6 1.4 collective-permute-start.27
  260.0 2.4 collective-permute-done.22
  262.5 3.2 %fusion.12 = f32[1,2,512,256]{3,2,1,0:T(8,128)} fusion(f32[2,512,256]{2,1,0:T(8,128)S(1)} %copy-done.4, f32[2,512,768]{2,1,0:T(8,128)S(1)} %get-tuple-element.73, bf16[2,128,256]{2,1,0:T(8,128)(2,1)S(1)} %collective-permute-done.21, bf16[2,384,256]{2,1,0:T(8,128)(2,1)S(1)} %get-tuple-element.19, bf16[2,384,256]{2,1,0:T(8,128)(2,1)S(1)} %get-tuple-element.18, ...), kind=kLoop, calls=%fused_computation.37 | loop fusion | flops 12320768 | bytes 13631488 | tf_op jit(solution)/shard_map/broadcast_in_dim | solution.py:153
  (233 shorter events, 30.2 us)
Async XLA Ops:
  0.6 8.3 %copy-start.19 = (bf16[1,2,512,256]{3,2,1,0:T(8,128)(2,1)S(1)}, bf16[1,2,512,256]{3,2,1,0:T(8,128)(2,1)}, u32[]{:S(2)}) copy-start(bf16[1,2,512,256]{3,2,1,0:T(8,128)(2,1)} %param.4) | copy-start | bytes 1572868
  1.7 7.3 %collective-permute-start = (bf16[2,128,256]{2,1,0:T(8,128)(2,1)S(1)}, bf16[2,128,256]{2,1,0:T(8,128)(2,1)S(1)}, u32[]{:S(2)}, u32[]{:S(2)}) collective-permute-start(bf16[2,128,256]{2,1,0:T(8,128)(2,1)S(1)} %get-tuple-element.57), channel_id=1, source_target_pairs={{0,1},{1,2},{2,3},{3,4},{4,5},{5,6},{6,7},{7,8},{8,9},{9,10},{10,1... | collective-permute-start | bytes 393224 | tf_op jit(solution)/shard_map/ppermute | solution.py:15
  3.6 7.2 %collective-permute-start.1 = (bf16[2,128,256]{2,1,0:T(8,128)(2,1)S(1)}, bf16[2,128,256]{2,1,0:T(8,128)(2,1)S(1)}, u32[]{:S(2)}, u32[]{:S(2)}) collective-permute-start(bf16[2,128,256]{2,1,0:T(8,128)(2,1)S(1)} %get-tuple-element.56), channel_id=1, source_target_pairs={{1,0},{2,1},{3,2},{4,3},{5,4},{6,5},{7,6},{8,7},{9,8},{10,9},{11,1... | collective-permute-start | bytes 393224 | tf_op jit(solution)/shard_map/ppermute | solution.py:15
  12.8 8.2 %copy-start.44 = (bf16[2,512,256]{2,1,0:T(8,128)(2,1)}, bf16[2,512,256]{2,1,0:T(8,128)(2,1)S(1)}, u32[]{:S(2)}) copy-start(bf16[2,512,256]{2,1,0:T(8,128)(2,1)S(1)} %fusion) | copy-start | bytes 1572868
  12.8 16.4 %collective-permute-start.2 = (bf16[2,512,256]{2,1,0:T(8,128)(2,1)S(1)}, bf16[2,512,256]{2,1,0:T(8,128)(2,1)S(1)}, u32[]{:S(2)}, u32[]{:S(2)}) collective-permute-start(bf16[2,512,256]{2,1,0:T(8,128)(2,1)S(1)} %fusion), channel_id=1, source_target_pairs={{0,2},{1,3},{2,4},{3,5},{4,6},{5,7},{6,8},{7,9},{8,10},{9,11},{10,... | collective-permute-start | bytes 1572872 | tf_op jit(solution)/shard_map/ppermute | solution.py:15
  18.5 120.8 %copy-start.1 = (bf16[1,1,3,256,512]{4,3,2,1,0:T(8,128)(2,1)}, bf16[1,1,3,256,512]{4,3,2,1,0:T(8,128)(2,1)S(1)}, u32[]{:S(2)}) copy-start(bf16[1,1,3,256,512]{4,3,2,1,0:T(8,128)(2,1)S(1)} %get-tuple-element.39) | copy-start | bytes 2359300
  18.5 17.0 %collective-permute-start.3 = (bf16[2,512,256]{2,1,0:T(8,128)(2,1)S(1)}, bf16[2,512,256]{2,1,0:T(8,128)(2,1)S(1)}, u32[]{:S(2)}, u32[]{:S(2)}) collective-permute-start(bf16[2,512,256]{2,1,0:T(8,128)(2,1)S(1)} %fusion), channel_id=1, source_target_pairs={{2,0},{3,1},{4,2},{5,3},{6,4},{7,5},{8,6},{9,7},{10,8},{11,9},{12,... | collective-permute-start | bytes 1572872 | tf_op jit(solution)/shard_map/ppermute | solution.py:15
  37.9 45.1 %copy-start.12 = (f32[2,512,256]{1,2,0:T(8,128)}, f32[2,512,256]{1,2,0:T(8,128)S(1)}, u32[]{:S(2)}) copy-start(f32[2,512,256]{1,2,0:T(8,128)S(1)} %get-tuple-element.8) | copy-start | bytes 3145732
  37.9 45.1 %copy-start.14 = (f32[2,512,256]{1,2,0:T(8,128)}, f32[2,512,256]{1,2,0:T(8,128)S(1)}, u32[]{:S(2)}) copy-start(f32[2,512,256]{1,2,0:T(8,128)S(1)} %get-tuple-element.14) | copy-start | bytes 3145732
  39.0 14.0 %collective-permute-start.5 = (bf16[2,512,256]{2,1,0:T(8,128)(2,1)S(1)}, bf16[2,512,256]{2,1,0:T(8,128)(2,1)S(1)}, u32[]{:S(2)}, u32[]{:S(2)}) collective-permute-start(bf16[2,512,256]{2,1,0:T(8,128)(2,1)S(1)} %get-tuple-element.41), channel_id=1, source_target_pairs={{0,2},{1,3},{2,4},{3,5},{4,6},{5,7},{6,8},{7,9},{8,10},{9,11},{10,... | collective-permute-start | bytes 1572872 | tf_op jit(solution)/shard_map/ppermute | solution.py:15
  41.0 16.1 %collective-permute-start.4 = (bf16[2,512,256]{2,1,0:T(8,128)(2,1)S(1)}, bf16[2,512,256]{2,1,0:T(8,128)(2,1)S(1)}, u32[]{:S(2)}, u32[]{:S(2)}) collective-permute-start(bf16[2,512,256]{2,1,0:T(8,128)(2,1)S(1)} %get-tuple-element.40), channel_id=1, source_target_pairs={{2,0},{3,1},{4,2},{5,3},{6,4},{7,5},{8,6},{9,7},{10,8},{11,9},{12,... | collective-permute-start | bytes 1572872 | tf_op jit(solution)/shard_map/ppermute | solution.py:15
  57.3 11.2 %copy-start.5 = (f32[2,512,256]{2,1,0:T(8,128)}, f32[2,512,256]{2,1,0:T(8,128)S(1)}, u32[]{:S(2)}) copy-start(f32[2,512,256]{2,1,0:T(8,128)S(1)} %fusion.26) | copy-start | bytes 3145732
  60.4 8.5 %copy-start.16 = (f32[2,512,768]{2,1,0:T(8,128)}, f32[2,512,768]{2,1,0:T(8,128)S(1)}, u32[]{:S(2)}) copy-start(f32[2,512,768]{2,1,0:T(8,128)S(1)} %get-tuple-element.61) | copy-start | bytes 9437188
  60.5 6.3 %collective-permute-start.7 = (bf16[2,128,256]{2,1,0:T(8,128)(2,1)S(1)}, bf16[2,128,256]{2,1,0:T(8,128)(2,1)S(1)}, u32[]{:S(2)}, u32[]{:S(2)}) collective-permute-start(bf16[2,128,256]{2,1,0:T(8,128)(2,1)S(1)} %get-tuple-element.37), channel_id=1, source_target_pairs={{0,1},{1,2},{2,3},{3,4},{4,5},{5,6},{6,7},{7,8},{8,9},{9,10},{10,1... | collective-permute-start | bytes 393224 | tf_op jit(solution)/shard_map/ppermute | solution.py:15
  62.4 6.1 %collective-permute-start.6 = (bf16[2,128,256]{2,1,0:T(8,128)(2,1)S(1)}, bf16[2,128,256]{2,1,0:T(8,128)(2,1)S(1)}, u32[]{:S(2)}, u32[]{:S(2)}) collective-permute-start(bf16[2,128,256]{2,1,0:T(8,128)(2,1)S(1)} %get-tuple-element.36), channel_id=1, source_target_pairs={{1,0},{2,1},{3,2},{4,3},{5,4},{6,5},{7,6},{8,7},{9,8},{10,9},{11,1... | collective-permute-start | bytes 393224 | tf_op jit(solution)/shard_map/ppermute | solution.py:15
  66.1 17.3 %copy-start.26 = (bf16[2,384,256]{2,1,0:T(8,128)(2,1)}, bf16[2,384,256]{2,1,0:T(8,128)(2,1)S(1)}, u32[]{:S(2)}) copy-start(bf16[2,384,256]{2,1,0:T(8,128)(2,1)S(1)} %get-tuple-element.34) | copy-start | bytes 1179652
  66.1 17.3 %copy-start.28 = (bf16[2,384,256]{2,1,0:T(8,128)(2,1)}, bf16[2,384,256]{2,1,0:T(8,128)(2,1)S(1)}, u32[]{:S(2)}) copy-start(bf16[2,384,256]{2,1,0:T(8,128)(2,1)S(1)} %get-tuple-element.35) | copy-start | bytes 1179652
  68.6 14.8 %copy-start.67 = (bf16[2,128,256]{2,1,0:T(8,128)(2,1)}, bf16[2,128,256]{2,1,0:T(8,128)(2,1)S(1)}, u32[]{:S(2)}) copy-start(bf16[2,128,256]{2,1,0:T(8,128)(2,1)S(1)} %collective-permute-done.6) | copy-start | bytes 393220
  68.9 14.1 %collective-permute-start.8 = (bf16[2,512,256]{2,1,0:T(8,128)(2,1)S(1)}, bf16[2,512,256]{2,1,0:T(8,128)(2,1)S(1)}, u32[]{:S(2)}, u32[]{:S(2)}) collective-permute-start(bf16[2,512,256]{2,1,0:T(8,128)(2,1)S(1)} %fusion.147), channel_id=1, source_target_pairs={{32,0},{64,32},{96,64},{33,1},{65,33},{97,65},{34,2},{66,34},{98,6... | collective-permute-start | bytes 1572872 | tf_op jit(solution)/shard_map/ppermute | solution.py:15
  86.9 9.9 %copy-start.45 = (bf16[2,512,256]{2,1,0:T(8,128)(2,1)S(1)}, bf16[2,512,256]{2,1,0:T(8,128)(2,1)}, u32[]{:S(2)}) copy-start(bf16[2,512,256]{2,1,0:T(8,128)(2,1)} %copy-done.44) | copy-start | bytes 1572868
  86.9 9.9 %copy-start.57 = (bf16[2,512,256]{2,1,0:T(8,128)(2,1)S(1)}, bf16[2,512,256]{2,1,0:T(8,128)(2,1)}, u32[]{:S(2)}) copy-start(bf16[2,512,256]{2,1,0:T(8,128)(2,1)} %copy-done.56) | copy-start | bytes 1572868
  88.0 17.3 %collective-permute-start.10 = (bf16[2,512,256]{2,1,0:T(8,128)(2,1)}, bf16[2,512,256]{2,1,0:T(8,128)(2,1)}, u32[]{:S(2)}, u32[]{:S(2)}) collective-permute-start(bf16[2,512,256]{2,1,0:T(8,128)(2,1)} %get-tuple-element.33), channel_id=1, source_target_pairs={{0,2},{1,3},{2,4},{3,5},{4,6},{5,7},{6,8},{7,9},{8,10},{9,11},{10,... | collective-permute-start | bytes 1572872 | tf_op jit(solution)/shard_map/ppermute | solution.py:15
  94.7 16.9 %collective-permute-start.9 = (bf16[2,512,256]{2,1,0:T(8,128)(2,1)}, bf16[2,512,256]{2,1,0:T(8,128)(2,1)}, u32[]{:S(2)}, u32[]{:S(2)}) collective-permute-start(bf16[2,512,256]{2,1,0:T(8,128)(2,1)} %get-tuple-element.32), channel_id=1, source_target_pairs={{2,0},{3,1},{4,2},{5,3},{6,4},{7,5},{8,6},{9,7},{10,8},{11,9},{12,... | collective-permute-start | bytes 1572872 | tf_op jit(solution)/shard_map/ppermute | solution.py:15
  96.8 14.7 %copy-start.25 = (bf16[2,512,256]{2,1,0:T(8,128)(2,1)S(1)}, bf16[2,512,256]{2,1,0:T(8,128)(2,1)}, u32[]{:S(2)}) copy-start(bf16[2,512,256]{2,1,0:T(8,128)(2,1)} %copy-done.24) | copy-start | bytes 1572868
  99.2 14.1 %copy-start.10 = (f32[2,512,256]{1,2,0:T(8,128)S(1)}, f32[2,512,256]{1,2,0:T(8,128)}, u32[]{:S(2)}) copy-start(f32[2,512,256]{1,2,0:T(8,128)} %get-tuple-element.4) | copy-start | bytes 3145732
  99.3 14.1 %copy-start.11 = (f32[2,512,256]{1,2,0:T(8,128)S(1)}, f32[2,512,256]{1,2,0:T(8,128)}, u32[]{:S(2)}) copy-start(f32[2,512,256]{1,2,0:T(8,128)} %get-tuple-element.12) | copy-start | bytes 3145732
  114.7 8.5 %copy-start.17 = (f32[2,512,768]{2,1,0:T(8,128)}, f32[2,512,768]{2,1,0:T(8,128)S(1)}, u32[]{:S(2)}) copy-start(f32[2,512,768]{2,1,0:T(8,128)S(1)} %get-tuple-element.65) | copy-start | bytes 9437188
  114.7 6.3 %collective-permute-start.12 = (bf16[2,128,256]{2,1,0:T(8,128)(2,1)S(1)}, bf16[2,128,256]{2,1,0:T(8,128)(2,1)S(1)}, u32[]{:S(2)}, u32[]{:S(2)}) collective-permute-start(bf16[2,128,256]{2,1,0:T(8,128)(2,1)S(1)} %get-tuple-element.31), channel_id=1, source_target_pairs={{0,1},{1,2},{2,3},{3,4},{4,5},{5,6},{6,7},{7,8},{8,9},{9,10},{10,1... | collective-permute-start | bytes 393224 | tf_op jit(solution)/shard_map/ppermute | solution.py:15
  116.7 6.1 %collective-permute-start.11 = (bf16[2,128,256]{2,1,0:T(8,128)(2,1)S(1)}, bf16[2,128,256]{2,1,0:T(8,128)(2,1)S(1)}, u32[]{:S(2)}, u32[]{:S(2)}) collective-permute-start(bf16[2,128,256]{2,1,0:T(8,128)(2,1)S(1)} %get-tuple-element.30), channel_id=1, source_target_pairs={{1,0},{2,1},{3,2},{4,3},{5,4},{6,5},{7,6},{8,7},{9,8},{10,9},{11,1... | collective-permute-start | bytes 393224 | tf_op jit(solution)/shard_map/ppermute | solution.py:15
  123.2 15.8 %collective-permute-start.13 = (bf16[2,512,256]{2,1,0:T(8,128)(2,1)S(1)}, bf16[2,512,256]{2,1,0:T(8,128)(2,1)S(1)}, u32[]{:S(2)}, u32[]{:S(2)}) collective-permute-start(bf16[2,512,256]{2,1,0:T(8,128)(2,1)S(1)} %fusion.148), channel_id=1, source_target_pairs={{32,0},{64,32},{96,64},{33,1},{65,33},{97,65},{34,2},{66,34},{98,6... | collective-permute-start | bytes 1572872 | tf_op jit(solution)/shard_map/ppermute | solution.py:15
  127.4 11.6 %copy-start.13 = (f32[2,512,256]{1,2,0:T(8,128)S(1)}, f32[2,512,256]{1,2,0:T(8,128)}, u32[]{:S(2)}) copy-start(f32[2,512,256]{1,2,0:T(8,128)} %copy-done.12) | copy-start | bytes 3145732
  127.4 11.6 %copy-start.15 = (f32[2,512,256]{1,2,0:T(8,128)S(1)}, f32[2,512,256]{1,2,0:T(8,128)}, u32[]{:S(2)}) copy-start(f32[2,512,256]{1,2,0:T(8,128)} %copy-done.14) | copy-start | bytes 3145732
  140.5 16.6 %collective-permute-start.15 = (bf16[2,512,256]{2,1,0:T(8,128)(2,1)S(1)}, bf16[2,512,256]{2,1,0:T(8,128)(2,1)S(1)}, u32[]{:S(2)}, u32[]{:S(2)}) collective-permute-start(bf16[2,512,256]{2,1,0:T(8,128)(2,1)S(1)} %get-tuple-element.27), channel_id=1, source_target_pairs={{0,2},{1,3},{2,4},{3,5},{4,6},{5,7},{6,8},{7,9},{8,10},{9,11},{10,... | collective-permute-start | bytes 1572872 | tf_op jit(solution)/shard_map/ppermute | solution.py:15
  143.5 17.6 %collective-permute-start.14 = (bf16[2,512,256]{2,1,0:T(8,128)(2,1)S(1)}, bf16[2,512,256]{2,1,0:T(8,128)(2,1)S(1)}, u32[]{:S(2)}, u32[]{:S(2)}) collective-permute-start(bf16[2,512,256]{2,1,0:T(8,128)(2,1)S(1)} %get-tuple-element.26), channel_id=1, source_target_pairs={{2,0},{3,1},{4,2},{5,3},{6,4},{7,5},{8,6},{9,7},{10,8},{11,9},{12,... | collective-permute-start | bytes 1572872 | tf_op jit(solution)/shard_map/ppermute | solution.py:15
  149.9 11.5 %copy-start.39 = (bf16[1,2,256,256]{3,2,1,0:T(8,128)(2,1)S(1)}, bf16[1,2,256,256]{3,2,1,0:T(8,128)(2,1)}, u32[]{:S(2)}) copy-start(bf16[1,2,256,256]{3,2,1,0:T(8,128)(2,1)} %param.7) | copy-start | bytes 786436
  162.7 8.4 %copy-start.18 = (f32[2,512,768]{2,1,0:T(8,128)}, f32[2,512,768]{2,1,0:T(8,128)S(1)}, u32[]{:S(2)}) copy-start(f32[2,512,768]{2,1,0:T(8,128)S(1)} %get-tuple-element.69) | copy-start | bytes 9437188
  162.8 6.3 %collective-permute-start.17 = (bf16[2,128,256]{2,1,0:T(8,128)(2,1)S(1)}, bf16[2,128,256]{2,1,0:T(8,128)(2,1)S(1)}, u32[]{:S(2)}, u32[]{:S(2)}) collective-permute-start(bf16[2,128,256]{2,1,0:T(8,128)(2,1)S(1)} %get-tuple-element.25), channel_id=1, source_target_pairs={{0,1},{1,2},{2,3},{3,4},{4,5},{5,6},{6,7},{7,8},{8,9},{9,10},{10,1... | collective-permute-start | bytes 393224 | tf_op jit(solution)/shard_map/ppermute | solution.py:15
  164.7 6.1 %collective-permute-start.16 = (bf16[2,128,256]{2,1,0:T(8,128)(2,1)S(1)}, bf16[2,128,256]{2,1,0:T(8,128)(2,1)S(1)}, u32[]{:S(2)}, u32[]{:S(2)}) collective-permute-start(bf16[2,128,256]{2,1,0:T(8,128)(2,1)S(1)} %get-tuple-element.24), channel_id=1, source_target_pairs={{1,0},{2,1},{3,2},{4,3},{5,4},{6,5},{7,6},{8,7},{9,8},{10,9},{11,1... | collective-permute-start | bytes 393224 | tf_op jit(solution)/shard_map/ppermute | solution.py:15
  171.1 15.8 %collective-permute-start.18 = (bf16[2,512,256]{2,1,0:T(8,128)(2,1)S(1)}, bf16[2,512,256]{2,1,0:T(8,128)(2,1)S(1)}, u32[]{:S(2)}, u32[]{:S(2)}) collective-permute-start(bf16[2,512,256]{2,1,0:T(8,128)(2,1)S(1)} %fusion.149), channel_id=1, source_target_pairs={{32,0},{64,32},{96,64},{33,1},{65,33},{97,65},{34,2},{66,34},{98,6... | collective-permute-start | bytes 1572872 | tf_op jit(solution)/shard_map/ppermute | solution.py:15
  175.5 11.8 %copy-start.2 = (bf16[1,1,3,256,512]{4,3,2,1,0:T(8,128)(2,1)S(1)}, bf16[1,1,3,256,512]{4,3,2,1,0:T(8,128)(2,1)}, u32[]{:S(2)}) copy-start(bf16[1,1,3,256,512]{4,3,2,1,0:T(8,128)(2,1)} %copy-done.1) | copy-start | bytes 2359300
  188.4 16.5 %collective-permute-start.20 = (bf16[2,512,256]{2,1,0:T(8,128)(2,1)S(1)}, bf16[2,512,256]{2,1,0:T(8,128)(2,1)S(1)}, u32[]{:S(2)}, u32[]{:S(2)}) collective-permute-start(bf16[2,512,256]{2,1,0:T(8,128)(2,1)S(1)} %get-tuple-element.21), channel_id=1, source_target_pairs={{0,2},{1,3},{2,4},{3,5},{4,6},{5,7},{6,8},{7,9},{8,10},{9,11},{10,... | collective-permute-start | bytes 1572872 | tf_op jit(solution)/shard_map/ppermute | solution.py:15
  192.1 16.9 %collective-permute-start.19 = (bf16[2,512,256]{2,1,0:T(8,128)(2,1)S(1)}, bf16[2,512,256]{2,1,0:T(8,128)(2,1)S(1)}, u32[]{:S(2)}, u32[]{:S(2)}) collective-permute-start(bf16[2,512,256]{2,1,0:T(8,128)(2,1)S(1)} %get-tuple-element.20), channel_id=1, source_target_pairs={{2,0},{3,1},{4,2},{5,3},{6,4},{7,5},{8,6},{9,7},{10,8},{11,9},{12,... | collective-permute-start | bytes 1572872 | tf_op jit(solution)/shard_map/ppermute | solution.py:15
  222.1 2.8 %collective-permute-start.23 = (bf16[16,56,512]{2,1,0:T(8,128)(2,1)}, bf16[16,56,512]{2,1,0:T(8,128)(2,1)}, u32[]{:S(2)}, u32[]{:S(2)}) collective-permute-start(bf16[16,56,512]{2,1,0:T(8,128)(2,1)} %fusion.36), channel_id=1, source_target_pairs={{0,1},{1,0},{2,3},{3,2},{4,5},{5,4},{6,7},{7,6},{8,9},{9,8},{10,11... | collective-permute-start | bytes 2752520 | tf_op jit(solution)/shard_map/ppermute | solution.py:95
  222.1 7.7 %copy-start.41 = (bf16[2,512,256]{1,2,0:T(8,128)(2,1)S(1)}, bf16[2,512,256]{1,2,0:T(8,128)(2,1)}, u32[]{:S(2)}) copy-start(bf16[2,512,256]{1,2,0:T(8,128)(2,1)} %get-tuple-element.42) | copy-start | bytes 1572868
  229.8 12.9 %collective-permute-start.24 = (bf16[8,56,512]{2,1,0:T(8,128)(2,1)}, bf16[8,56,512]{2,1,0:T(8,128)(2,1)}, u32[]{:S(2)}, u32[]{:S(2)}) collective-permute-start(bf16[8,56,512]{2,1,0:T(8,128)(2,1)} %fusion.68), channel_id=1, source_target_pairs={{0,2},{1,3},{2,0},{3,1},{4,6},{5,7},{6,4},{7,5},{8,10},{9,11},{10,... | collective-permute-start | bytes 1376264 | tf_op jit(solution)/shard_map/ppermute | solution.py:95
  229.8 12.9 %copy-start.9 = (f32[16,56,512]{2,1,0:T(8,128)S(1)}, f32[16,56,512]{2,1,0:T(8,128)}, u32[]{:S(2)}) copy-start(f32[16,56,512]{2,1,0:T(8,128)} %copy-done.8) | copy-start | bytes 5505028
  243.9 18.5 %copy-start.76 = (bf16[2,128,256]{2,1,0:T(8,128)(2,1)S(1)}, bf16[2,128,256]{2,1,0:T(8,128)(2,1)}, u32[]{:S(2)}) copy-start(bf16[2,128,256]{2,1,0:T(8,128)(2,1)} %copy-done.75) | copy-start | bytes 393220
  244.0 8.4 %collective-permute-start.25 = (bf16[4,56,512]{2,1,0:T(8,128)(2,1)S(1)}, bf16[4,56,512]{2,1,0:T(8,128)(2,1)S(1)}, u32[]{:S(2)}, u32[]{:S(2)}) collective-permute-start(bf16[4,56,512]{2,1,0:T(8,128)(2,1)S(1)} %fusion.101), channel_id=1, source_target_pairs={{0,4},{1,5},{2,6},{3,7},{4,0},{5,1},{6,2},{7,3},{8,12},{9,13},{10,... | collective-permute-start | bytes 688136 | tf_op jit(solution)/shard_map/ppermute | solution.py:95
  244.1 18.3 %copy-start.33 = (bf16[2,384,256]{2,1,0:T(8,128)(2,1)S(1)}, bf16[2,384,256]{2,1,0:T(8,128)(2,1)}, u32[]{:S(2)}) copy-start(bf16[2,384,256]{2,1,0:T(8,128)(2,1)} %copy-done.32) | copy-start | bytes 1179652
  244.1 18.3 %copy-start.35 = (bf16[2,384,256]{2,1,0:T(8,128)(2,1)S(1)}, bf16[2,384,256]{2,1,0:T(8,128)(2,1)}, u32[]{:S(2)}) copy-start(bf16[2,384,256]{2,1,0:T(8,128)(2,1)} %copy-done.34) | copy-start | bytes 1179652
  244.1 18.3 %copy-start.37 = (bf16[2,384,256]{2,1,0:T(8,128)(2,1)S(1)}, bf16[2,384,256]{2,1,0:T(8,128)(2,1)}, u32[]{:S(2)}) copy-start(bf16[2,384,256]{2,1,0:T(8,128)(2,1)} %copy-done.36) | copy-start | bytes 1179652
  244.1 18.3 %copy-start.70 = (bf16[2,128,256]{2,1,0:T(8,128)(2,1)S(1)}, bf16[2,128,256]{2,1,0:T(8,128)(2,1)}, u32[]{:S(2)}) copy-start(bf16[2,128,256]{2,1,0:T(8,128)(2,1)} %copy-done.69) | copy-start | bytes 393220
  244.1 18.3 %copy-start.72 = (bf16[2,128,256]{2,1,0:T(8,128)(2,1)S(1)}, bf16[2,128,256]{2,1,0:T(8,128)(2,1)}, u32[]{:S(2)}) copy-start(bf16[2,128,256]{2,1,0:T(8,128)(2,1)} %copy-done.71) | copy-start | bytes 393220
  244.1 18.3 %copy-start.74 = (bf16[2,128,256]{2,1,0:T(8,128)(2,1)S(1)}, bf16[2,128,256]{2,1,0:T(8,128)(2,1)}, u32[]{:S(2)}) copy-start(bf16[2,128,256]{2,1,0:T(8,128)(2,1)} %copy-done.73) | copy-start | bytes 393220
  244.2 18.3 %copy-start.4 = (f32[2,512,256]{2,1,0:T(8,128)S(1)}, f32[2,512,256]{2,1,0:T(8,128)}, u32[]{:S(2)}) copy-start(f32[2,512,256]{2,1,0:T(8,128)} %copy-done.3) | copy-start | bytes 3145732
  244.2 18.2 %copy-start.7 = (f32[2,512,256]{2,1,0:T(8,128)S(1)}, f32[2,512,256]{2,1,0:T(8,128)}, u32[]{:S(2)}) copy-start(f32[2,512,256]{2,1,0:T(8,128)} %copy-done.5) | copy-start | bytes 3145732
  244.2 18.2 %copy-start.27 = (bf16[2,384,256]{2,1,0:T(8,128)(2,1)S(1)}, bf16[2,384,256]{2,1,0:T(8,128)(2,1)}, u32[]{:S(2)}) copy-start(bf16[2,384,256]{2,1,0:T(8,128)(2,1)} %copy-done.26) | copy-start | bytes 1179652
  244.2 18.2 %copy-start.29 = (bf16[2,384,256]{2,1,0:T(8,128)(2,1)S(1)}, bf16[2,384,256]{2,1,0:T(8,128)(2,1)}, u32[]{:S(2)}) copy-start(bf16[2,384,256]{2,1,0:T(8,128)(2,1)} %copy-done.28) | copy-start | bytes 1179652
  244.2 18.2 %copy-start.31 = (bf16[2,384,256]{2,1,0:T(8,128)(2,1)S(1)}, bf16[2,384,256]{2,1,0:T(8,128)(2,1)}, u32[]{:S(2)}) copy-start(bf16[2,384,256]{2,1,0:T(8,128)(2,1)} %copy-done.30) | copy-start | bytes 1179652
  244.2 18.2 %copy-start.68 = (bf16[2,128,256]{2,1,0:T(8,128)(2,1)S(1)}, bf16[2,128,256]{2,1,0:T(8,128)(2,1)}, u32[]{:S(2)}) copy-start(bf16[2,128,256]{2,1,0:T(8,128)(2,1)} %copy-done.67) | copy-start | bytes 393220
  252.5 6.0 %collective-permute-start.26 = (bf16[2,56,512]{2,1,0:T(8,128)(2,1)S(1)}, bf16[2,56,512]{2,1,0:T(8,128)(2,1)S(1)}, u32[]{:S(2)}, u32[]{:S(2)}) collective-permute-start(bf16[2,56,512]{2,1,0:T(8,128)(2,1)S(1)} %fusion.117), channel_id=1, source_target_pairs={{0,8},{1,9},{2,10},{3,11},{4,12},{5,13},{6,14},{7,15},{8,0},{9,1},... | collective-permute-start | bytes 344072 | tf_op jit(solution)/shard_map/ppermute | solution.py:95
  254.2 5.8 %collective-permute-start.21 = (bf16[2,128,256]{2,1,0:T(8,128)(2,1)S(1)}, bf16[2,128,256]{2,1,0:T(8,128)(2,1)S(1)}, u32[]{:S(2)}, u32[]{:S(2)}) collective-permute-start(bf16[2,128,256]{2,1,0:T(8,128)(2,1)S(1)} %get-tuple-element.17), channel_id=1, source_target_pairs={{1,0},{2,1},{3,2},{4,3},{5,4},{6,5},{7,6},{8,7},{9,8},{10,9},{11,1... | collective-permute-start | bytes 393224 | tf_op jit(solution)/shard_map/ppermute | solution.py:15
  256.1 6.3 %collective-permute-start.22 = (bf16[2,128,256]{2,1,0:T(8,128)(2,1)S(1)}, bf16[2,128,256]{2,1,0:T(8,128)(2,1)S(1)}, u32[]{:S(2)}, u32[]{:S(2)}) collective-permute-start(bf16[2,128,256]{2,1,0:T(8,128)(2,1)S(1)} %get-tuple-element.16), channel_id=1, source_target_pairs={{0,1},{1,2},{2,3},{3,4},{4,5},{5,6},{6,7},{7,8},{8,9},{9,10},{10,1... | collective-permute-start | bytes 393224 | tf_op jit(solution)/shard_map/ppermute | solution.py:15
  258.6 7.1 %collective-permute-start.27 = (bf16[1,56,512]{2,1,0:T(8,128)(2,1)S(1)}, bf16[1,56,512]{2,1,0:T(8,128)(2,1)S(1)}, u32[]{:S(2)}, u32[]{:S(2)}) collective-permute-start(bf16[1,56,512]{2,1,0:T(8,128)(2,1)S(1)} %fusion.127), channel_id=1, source_target_pairs={{0,16},{1,17},{2,18},{3,19},{4,20},{5,21},{6,22},{7,23},{8,24},{9,... | collective-permute-start | bytes 172040 | tf_op jit(solution)/shard_map/ppermute | solution.py:95
  (45 other events, 107.8 us)

commit v2 on v1

--- a/solution.py
+++ b/solution.py
@@ -66,12 +66,33 @@
     middle = back[..., chans : 2 * chans]
     grad_third = back[..., 2 * chans :].astype(jnp.bfloat16)
     if layer == 0:
-        third_earlier, first_following = halo_sides_pair(grad_first, grad_third, NEAR)
+        return split_near(flowing, middle, grad_first, grad_third, NEAR), conv_term, out_term
     else:
         third_earlier = shifted(grad_third, "seq", far_hops)
         first_following = shifted(grad_first, "seq", -far_hops)
     grad_conv = middle + first_following.astype(jnp.float32) + third_earlier.astype(jnp.float32)
     return flowing + grad_conv, conv_term, out_term
+
+
+def split_near(flowing, middle, grad_first, grad_third, width):
+    rows = grad_first.shape[1]
+    low_in = shifted(grad_third[:, rows - width :], "seq", 1)
+    high_in = shifted(grad_first[:, :width], "seq", -1)
+    f32 = jnp.float32
+    inner = flowing[:, width : rows - width] + (
+        middle[:, width : rows - width]
+        + grad_first[:, 2 * width :].astype(f32)
+        + grad_third[:, : rows - 2 * width].astype(f32)
+    )
+    low = flowing[:, :width] + (
+        middle[:, :width] + grad_first[:, width : 2 * width].astype(f32) + low_in.astype(f32)
+    )
+    high = flowing[:, rows - width :] + (
+        middle[:, rows - width :]
+        + high_in.astype(f32)
+        + grad_third[:, rows - 2 * width : rows - width].astype(f32)
+    )
+    return low, inner, high
 
 
 def halo_sides_pair(grad_first, grad_third, width):
@@ -135,9 +156,17 @@
             )
             conv_acc[layer] = conv_term if step == 0 else conv_acc[layer] + conv_term
             out_acc[layer] = out_term if step == 0 else out_acc[layer] + out_term
+        low, inner, high = flowing
+        flowing = jnp.concatenate([low, inner, high], axis=1)
         input_grads = flowing if step == 0 else input_grads + flowing
         if step + 1 < section_count:
-            flowing = shifted(flowing.astype(jnp.bfloat16), "section", -1).astype(jnp.float32)
+            bf16 = jnp.bfloat16
+            inner = shifted(inner.astype(bf16), "section", -1)
+            edges = shifted(jnp.concatenate([low, high], axis=1).astype(bf16), "section", -1)
+            width = low.shape[1]
+            flowing = jnp.concatenate(
+                [edges[:, :width], inner, edges[:, width:]], axis=1
+            ).astype(jnp.float32)
 
     conv_rows = 3 * channels // seq_count
     out_rows = channels // seq_count

time: 271 us -> 256 us (0.945)
  waiting for transfers between devices: 127 us -> 111 us
  starting transfers between devices: 67.7 us -> 73.7 us
  local copies, waits for them, and re-layouts: 11.1 us -> 8.33 us
    ppermute x23 -> x26, waiting for transfers between devices: 106 us -> 88.7 us  [shifted(): lax.ppermute(value, axis, [(source, source + steps) for source in range(l...]
    ppermute x23 -> x26, starting transfers between devices: 64.6 us -> 69.5 us  [shifted(): lax.ppermute(value, axis, [(source, source + steps) for source in range(l...]
    another operation x0 -> x3, other arithmetic: none -> 4.24 us
    broadcast_in_dim x1 -> x0, other arithmetic: 3.25 us -> none  [shards(): return (input_grads[None], conv_grads, out_grads)]
    convert_element_type x3, other arithmetic: 0.95 us -> 4.01 us  [shards(): inner = shifted(inner.astype(bf16), 'section', -1)]
    unnamed x162 -> x102, local copies, waits for them, and re-layouts: 5.69 us -> 3.22 us
  transfers between devices with their start and end apart: 28 -> 31, of which waited for: 23 -> 23; matrix products, arithmetic and copies ran while one was open for 9% -> 11% of each run, Pallas kernels for 0% -> 0%
where the time goes in v2:
time: 256 us; the launch traced here: 255 us
  waiting for transfers between devices  111 us (43%)
  starting transfers between devices  73.7 us (29%)
  matrix products  41.6 us (16%)
  other arithmetic  17.8 us (7%)
  local copies, waits for them, and re-layouts  8.33 us (3%)
    ppermute x26, waiting for transfers between devices, shifted(): lax.ppermute(value, axis, [(source, source + steps) for source in range(l...  88.7 us
    ppermute x26, starting transfers between devices, shifted(): lax.ppermute(value, axis, [(source, source + steps) for source in range(l...  69.5 us
    ppermute x5, waiting for transfers between devices, halving_scatter(): got = lax.ppermute(sends, 'seq', pairs)  22.6 us
    dot_general x8, matrix products, backward_layer(): jnp.einsum('mpc,mpd->cd', taps, grad_pre, preferred_element_type=jnp.floa...  15.8 us
    dot_general x8, matrix products, backward_layer(): jnp.einsum('mpd,cd->mpc', grad_pre, weights, preferred_element_type=jnp.f...  10.4 us
    dot_general x8, matrix products, backward_layer(): jnp.einsum('mpd,cd->mpc', grad_half, out_mat, preferred_element_type=jnp....  7.21 us
    dot_general x7, matrix products, mm(): return jnp.einsum('mpc,cd->mpd', a, b, preferred_element_type=jnp.float32)  5.75 us
  transfers between devices with their start and end apart: 31, of which 23 were waited for; matrix products, arithmetic and copies ran while one was open for 11% of the time, Pallas kernels for 0%

profile of v2, /device:TPU:24, one launch (start us, length us, event | category | flops | bytes accessed | tf_op | source)
XLA Modules:
  0.0 254.6 jit_solution(2705673917577885878)
XLA Ops:
  1.7 1.9 collective-permute-start
  3.6 3.6 %collective-permute-start.1 = (bf16[2,128,256]{2,1,0:T(8,128)(2,1)S(1)}, bf16[2,128,256]{2,1,0:T(8,128)(2,1)S(1)}, u32[]{:S(2)}, u32[]{:S(2)}) collective-permute-start(bf16[2,128,256]{2,1,0:T(8,128)(2,1)S(1)} %get-tuple-element.74), channel_id=1, source_target_pairs={{1,0},{2,1},{3,2},{4,3},{5,4},{6,5},{7,6},{8,7},{9,8},{10,9},{11,1... | collective-permute-start | bytes 393224 | tf_op jit(solution)/shard_map/ppermute | solution.py:15
  7.3 1.6 fusion.99
  9.0 1.8 fusion.56
  12.7 5.6 %collective-permute-start.2 = (bf16[2,512,256]{2,1,0:T(8,128)(2,1)S(1)}, bf16[2,512,256]{2,1,0:T(8,128)(2,1)S(1)}, u32[]{:S(2)}, u32[]{:S(2)}) collective-permute-start(bf16[2,512,256]{2,1,0:T(8,128)(2,1)S(1)} %fusion), channel_id=1, source_target_pairs={{0,2},{1,3},{2,4},{3,5},{4,6},{5,7},{6,8},{7,9},{8,10},{9,11},{10,... | collective-permute-start | bytes 1572872 | tf_op jit(solution)/shard_map/ppermute | solution.py:15
  18.5 1.9 collective-permute-start.3
  20.9 8.2 %collective-permute-done.2 = bf16[2,512,256]{2,1,0:T(8,128)(2,1)S(1)} collective-permute-done((bf16[2,512,256]{2,1,0:T(8,128)(2,1)S(1)}, bf16[2,512,256]{2,1,0:T(8,128)(2,1)S(1)}, u32[]{:S(2)}, u32[]{:S(2)}) %collective-permute-start.2) | collective-permute-done | bytes 524320 | tf_op jit(solution)/shard_map/ppermute | solution.py:15
  29.9 5.5 %collective-permute-done.3 = bf16[2,512,256]{2,1,0:T(8,128)(2,1)S(1)} collective-permute-done((bf16[2,512,256]{2,1,0:T(8,128)(2,1)S(1)}, bf16[2,512,256]{2,1,0:T(8,128)(2,1)S(1)}, u32[]{:S(2)}, u32[]{:S(2)}) %collective-permute-start.3) | collective-permute-done | bytes 524320 | tf_op jit(solution)/shard_map/ppermute | solution.py:15
  36.3 2.2 multiply_convert_fusion.15
  39.6 1.9 collective-permute-start.5
  41.6 3.9 %collective-permute-start.4 = (bf16[2,512,256]{2,1,0:T(8,128)(2,1)S(1)}, bf16[2,512,256]{2,1,0:T(8,128)(2,1)S(1)}, u32[]{:S(2)}, u32[]{:S(2)}) collective-permute-start(bf16[2,512,256]{2,1,0:T(8,128)(2,1)S(1)} %get-tuple-element.56), channel_id=1, source_target_pairs={{2,0},{3,1},{4,2},{5,3},{6,4},{7,5},{8,6},{9,7},{10,8},{11,9},{12,... | collective-permute-start | bytes 1572872 | tf_op jit(solution)/shard_map/ppermute | solution.py:15
  45.5 8.2 %collective-permute-done.5 = bf16[2,512,256]{2,1,0:T(8,128)(2,1)S(1)} collective-permute-done((bf16[2,512,256]{2,1,0:T(8,128)(2,1)S(1)}, bf16[2,512,256]{2,1,0:T(8,128)(2,1)S(1)}, u32[]{:S(2)}, u32[]{:S(2)}) %collective-permute-start.5) | collective-permute-done | bytes 524320 | tf_op jit(solution)/shard_map/ppermute | solution.py:15
  53.7 4.0 %collective-permute-done.4 = bf16[2,512,256]{2,1,0:T(8,128)(2,1)S(1)} collective-permute-done((bf16[2,512,256]{2,1,0:T(8,128)(2,1)S(1)}, bf16[2,512,256]{2,1,0:T(8,128)(2,1)S(1)}, u32[]{:S(2)}, u32[]{:S(2)}) %collective-permute-start.4) | collective-permute-done | bytes 524320 | tf_op jit(solution)/shard_map/ppermute | solution.py:15
  58.0 2.0 multiply_convert_fusion.13
  60.0 3.2 %fusion.199 = (bf16[2,512,768]{2,1,0:T(8,128)(2,1)}, f32[2,512,768]{2,1,0:T(8,128)}) fusion(bf16[768,512,1]{1,0,2:T(8,128)(2,1)S(1)} %bitcast.297, bf16[2,512,256]{1,2,0:T(8,128)(2,1)S(1)} %get-tuple-element.37, bf16[2,512,256]{1,2,0:T(8,128)(2,1)S(1)} %get-tuple-element.3), kind=kOutput, calls=%fused_computation.284 | convolution fusion | flops 808189952 | bytes 6553600 | tf_op jit(solution)/shard_map/mpd,cd->mpc/dot_general | solution.py:64
  63.2 1.7 fusion.190
  64.9 1.9 collective-permute-start.6
  66.8 3.6 %collective-permute-start.7 = (bf16[2,128,256]{2,1,0:T(8,128)(2,1)}, bf16[2,128,256]{2,1,0:T(8,128)(2,1)}, u32[]{:S(2)}, u32[]{:S(2)}) collective-permute-start(bf16[2,128,256]{2,1,0:T(8,128)(2,1)} %get-tuple-element.55), channel_id=1, source_target_pairs={{1,0},{2,1},{3,2},{4,3},{5,4},{6,5},{7,6},{8,7},{9,8},{10,9},{11,1... | collective-permute-start | bytes 393224 | tf_op jit(solution)/shard_map/ppermute | solution.py:15
  71.5 1.8 collective-permute-done.7
  73.3 2.3 fusion.166
  75.7 1.3 collective-permute-start.8
  77.0 2.1 fusion.178
  79.1 1.4 collective-permute-start.9
  81.6 2.5 %collective-permute-done.8 = bf16[2,256,256]{2,1,0:T(8,128)(2,1)S(1)} collective-permute-done((bf16[2,256,256]{2,1,0:T(8,128)(2,1)S(1)}, bf16[2,256,256]{2,1,0:T(8,128)(2,1)S(1)}, u32[]{:S(2)}, u32[]{:S(2)}) %collective-permute-start.8) | collective-permute-done | bytes 262176 | tf_op jit(solution)/shard_map/ppermute | solution.py:15
  84.2 6.8 %collective-permute-done.9 = bf16[2,256,256]{2,1,0:T(8,128)(2,1)S(1)} collective-permute-done((bf16[2,256,256]{2,1,0:T(8,128)(2,1)S(1)}, bf16[2,256,256]{2,1,0:T(8,128)(2,1)S(1)}, u32[]{:S(2)}, u32[]{:S(2)}) %collective-permute-start.9) | collective-permute-done | bytes 262176 | tf_op jit(solution)/shard_map/ppermute | solution.py:15
  92.5 5.7 %collective-permute-start.11 = (bf16[2,512,256]{2,1,0:T(8,128)(2,1)S(1)}, bf16[2,512,256]{2,1,0:T(8,128)(2,1)S(1)}, u32[]{:S(2)}, u32[]{:S(2)}) collective-permute-start(bf16[2,512,256]{2,1,0:T(8,128)(2,1)S(1)} %get-tuple-element.53), channel_id=1, source_target_pairs={{0,2},{1,3},{2,4},{3,5},{4,6},{5,7},{6,8},{7,9},{8,10},{9,11},{10,... | collective-permute-start | bytes 1572872 | tf_op jit(solution)/shard_map/ppermute | solution.py:15
  98.2 2.1 collective-permute-start.10
  100.7 2.2 fusion.43
  103.9 5.1 %collective-permute-done.11 = bf16[2,512,256]{2,1,0:T(8,128)(2,1)S(1)} collective-permute-done((bf16[2,512,256]{2,1,0:T(8,128)(2,1)S(1)}, bf16[2,512,256]{2,1,0:T(8,128)(2,1)S(1)}, u32[]{:S(2)}, u32[]{:S(2)}) %collective-permute-start.11) | collective-permute-done | bytes 524320 | tf_op jit(solution)/shard_map/ppermute | solution.py:15
  109.0 5.7 %collective-permute-done.10 = bf16[2,512,256]{2,1,0:T(8,128)(2,1)S(1)} collective-permute-done((bf16[2,512,256]{2,1,0:T(8,128)(2,1)S(1)}, bf16[2,512,256]{2,1,0:T(8,128)(2,1)S(1)}, u32[]{:S(2)}, u32[]{:S(2)}) %collective-permute-start.10) | collective-permute-done | bytes 524320 | tf_op jit(solution)/shard_map/ppermute | solution.py:15
  116.4 1.9 collective-permute-start.12
  118.3 3.6 %collective-permute-start.13 = (bf16[2,128,256]{2,1,0:T(8,128)(2,1)S(1)}, bf16[2,128,256]{2,1,0:T(8,128)(2,1)S(1)}, u32[]{:S(2)}, u32[]{:S(2)}) collective-permute-start(bf16[2,128,256]{2,1,0:T(8,128)(2,1)S(1)} %get-tuple-element.51), channel_id=1, source_target_pairs={{1,0},{2,1},{3,2},{4,3},{5,4},{6,5},{7,6},{8,7},{9,8},{10,9},{11,1... | collective-permute-start | bytes 393224 | tf_op jit(solution)/shard_map/ppermute | solution.py:15
  122.9 1.3 collective-permute-start.15
  125.4 1.3 collective-permute-start.14
  126.7 2.2 fusion.39
  128.9 8.3 %collective-permute-done.14 = bf16[2,256,256]{2,1,0:T(8,128)(2,1)S(1)} collective-permute-done((bf16[2,256,256]{2,1,0:T(8,128)(2,1)S(1)}, bf16[2,256,256]{2,1,0:T(8,128)(2,1)S(1)}, u32[]{:S(2)}, u32[]{:S(2)}) %collective-permute-start.14) | collective-permute-done | bytes 262176 | tf_op jit(solution)/shard_map/ppermute | solution.py:15
  138.7 3.2 %collective-permute-start.17 = (bf16[2,512,256]{2,1,0:T(8,128)(2,1)S(1)}, bf16[2,512,256]{2,1,0:T(8,128)(2,1)S(1)}, u32[]{:S(2)}, u32[]{:S(2)}) collective-permute-start(bf16[2,512,256]{2,1,0:T(8,128)(2,1)S(1)} %get-tuple-element.49), channel_id=1, source_target_pairs={{0,2},{1,3},{2,4},{3,5},{4,6},{5,7},{6,8},{7,9},{8,10},{9,11},{10,... | collective-permute-start | bytes 1572872 | tf_op jit(solution)/shard_map/ppermute | solution.py:15
  141.9 2.7 %collective-permute-start.16 = (bf16[2,512,256]{2,1,0:T(8,128)(2,1)S(1)}, bf16[2,512,256]{2,1,0:T(8,128)(2,1)S(1)}, u32[]{:S(2)}, u32[]{:S(2)}) collective-permute-start(bf16[2,512,256]{2,1,0:T(8,128)(2,1)S(1)} %get-tuple-element.48), channel_id=1, source_target_pairs={{2,0},{3,1},{4,2},{5,3},{6,4},{7,5},{8,6},{9,7},{10,8},{11,9},{12,... | collective-permute-start | bytes 1572872 | tf_op jit(solution)/shard_map/ppermute | solution.py:15
  146.2 8.3 %collective-permute-done.17 = bf16[2,512,256]{2,1,0:T(8,128)(2,1)S(1)} collective-permute-done((bf16[2,512,256]{2,1,0:T(8,128)(2,1)S(1)}, bf16[2,512,256]{2,1,0:T(8,128)(2,1)S(1)}, u32[]{:S(2)}, u32[]{:S(2)}) %collective-permute-start.17) | collective-permute-done | bytes 524320 | tf_op jit(solution)/shard_map/ppermute | solution.py:15
  154.6 4.0 %collective-permute-done.16 = bf16[2,512,256]{2,1,0:T(8,128)(2,1)S(1)} collective-permute-done((bf16[2,512,256]{2,1,0:T(8,128)(2,1)S(1)}, bf16[2,512,256]{2,1,0:T(8,128)(2,1)S(1)}, u32[]{:S(2)}, u32[]{:S(2)}) %collective-permute-start.16) | collective-permute-done | bytes 524320 | tf_op jit(solution)/shard_map/ppermute | solution.py:15
  160.3 1.9 collective-permute-start.18
  162.2 3.6 %collective-permute-start.19 = (bf16[2,128,256]{2,1,0:T(8,128)(2,1)S(1)}, bf16[2,128,256]{2,1,0:T(8,128)(2,1)S(1)}, u32[]{:S(2)}, u32[]{:S(2)}) collective-permute-start(bf16[2,128,256]{2,1,0:T(8,128)(2,1)S(1)} %get-tuple-element.47), channel_id=1, source_target_pairs={{1,0},{2,1},{3,2},{4,3},{5,4},{6,5},{7,6},{8,7},{9,8},{10,9},{11,1... | collective-permute-start | bytes 393224 | tf_op jit(solution)/shard_map/ppermute | solution.py:15
  166.8 1.3 collective-permute-start.21
  169.4 1.5 collective-permute-start.20
  170.9 2.2 fusion.35
  173.4 7.0 %collective-permute-done.20 = bf16[2,256,256]{2,1,0:T(8,128)(2,1)S(1)} collective-permute-done((bf16[2,256,256]{2,1,0:T(8,128)(2,1)S(1)}, bf16[2,256,256]{2,1,0:T(8,128)(2,1)S(1)}, u32[]{:S(2)}, u32[]{:S(2)}) %collective-permute-start.20) | collective-permute-done | bytes 262176 | tf_op jit(solution)/shard_map/ppermute | solution.py:15
  181.9 4.7 %collective-permute-start.23 = (bf16[2,512,256]{2,1,0:T(8,128)(2,1)S(1)}, bf16[2,512,256]{2,1,0:T(8,128)(2,1)S(1)}, u32[]{:S(2)}, u32[]{:S(2)}) collective-permute-start(bf16[2,512,256]{2,1,0:T(8,128)(2,1)S(1)} %get-tuple-element.45), channel_id=1, source_target_pairs={{0,2},{1,3},{2,4},{3,5},{4,6},{5,7},{6,8},{7,9},{8,10},{9,11},{10,... | collective-permute-start | bytes 1572872 | tf_op jit(solution)/shard_map/ppermute | solution.py:15
  186.6 1.9 collective-permute-start.22
  189.2 2.2 bitcast_add_fusion.1
  191.4 7.0 %collective-permute-done.23 = bf16[2,512,256]{2,1,0:T(8,128)(2,1)S(1)} collective-permute-done((bf16[2,512,256]{2,1,0:T(8,128)(2,1)S(1)}, bf16[2,512,256]{2,1,0:T(8,128)(2,1)S(1)}, u32[]{:S(2)}, u32[]{:S(2)}) %collective-permute-start.23) | collective-permute-done | bytes 524320 | tf_op jit(solution)/shard_map/ppermute | solution.py:15
  198.3 4.6 %collective-permute-done.22 = bf16[2,512,256]{2,1,0:T(8,128)(2,1)S(1)} collective-permute-done((bf16[2,512,256]{2,1,0:T(8,128)(2,1)S(1)}, bf16[2,512,256]{2,1,0:T(8,128)(2,1)S(1)}, u32[]{:S(2)}, u32[]{:S(2)}) %collective-permute-start.22) | collective-permute-done | bytes 524320 | tf_op jit(solution)/shard_map/ppermute | solution.py:15
  203.2 1.3 multiply_convert_fusion.1
  207.3 3.9 %bitcast_add_fusion.4 = f32[768,512]{1,0:T(8,128)S(1)} fusion(f32[768,512,1]{1,0,2:T(8,128)} %fusion.35, f32[768,512,1]{1,0,2:T(8,128)} %fusion.39, f32[768,512,1]{1,0,2:T(8,128)} %fusion.43, bf16[2,512,256]{1,2,0:T(8,128)(2,1)} %get-tuple-element.61, bf16[2,512,256]{1,2,0:T(8,128)(2,1)} %get-tuple-element.60, bf16[2,128,256]{2,1,0:T(8,128)(2,1)S(1)} %copy-done.47, ...), kind=kOutput, calls=%fused_computation.12 | convolution fusion | flops 816447488 | bytes 8912896 | tf_op jit(solution)/shard_map/mpc,mpd->cd/dot_general | solution.py:62
  211.8 1.9 copy-done
  214.7 2.8 %collective-permute-done.26 = bf16[16,56,512]{2,1,0:T(8,128)(2,1)} collective-permute-done((bf16[16,56,512]{2,1,0:T(8,128)(2,1)}, bf16[16,56,512]{2,1,0:T(8,128)(2,1)}, u32[]{:S(2)}, u32[]{:S(2)}) %collective-permute-start.26) | collective-permute-done | bytes 917536 | tf_op jit(solution)/shard_map/ppermute | solution.py:116
  217.5 2.8 %bitcast_add_fusion = f32[16,56,512]{2,1,0:T(8,128)S(1)} fusion(bf16[16,56,512]{2,1,0:T(8,128)(2,1)} %collective-permute-done.26, f32[16,2,56,512]{3,2,1,0:T(8,128)} %copy-done, pred[]{:T(512)S(6)} %eq.23), kind=kLoop, calls=%fused_computation.5 | loop fusion | flops 1376256 | bytes 6422529 | tf_op jit(solution)/shard_map/add | solution.py:117
  221.6 2.0 collective-permute-start.24
  223.7 3.5 %collective-permute-start.25 = (bf16[2,128,256]{2,1,0:T(8,128)(2,1)S(1)}, bf16[2,128,256]{2,1,0:T(8,128)(2,1)S(1)}, u32[]{:S(2)}, u32[]{:S(2)}) collective-permute-start(bf16[2,128,256]{2,1,0:T(8,128)(2,1)S(1)} %get-tuple-element.43), channel_id=1, source_target_pairs={{1,0},{2,1},{3,2},{4,3},{5,4},{6,5},{7,6},{8,7},{9,8},{10,9},{11,1... | collective-permute-start | bytes 393224 | tf_op jit(solution)/shard_map/ppermute | solution.py:15
  227.2 6.7 %collective-permute-done.27 = bf16[8,56,512]{2,1,0:T(8,128)(2,1)S(1)} collective-permute-done((bf16[8,56,512]{2,1,0:T(8,128)(2,1)S(1)}, bf16[8,56,512]{2,1,0:T(8,128)(2,1)S(1)}, u32[]{:S(2)}, u32[]{:S(2)}) %collective-permute-start.27) | collective-permute-done | bytes 458784 | tf_op jit(solution)/shard_map/ppermute | solution.py:116
  235.3 6.5 %collective-permute-done.28 = bf16[4,56,512]{2,1,0:T(8,128)(2,1)S(1)} collective-permute-done((bf16[4,56,512]{2,1,0:T(8,128)(2,1)S(1)}, bf16[4,56,512]{2,1,0:T(8,128)(2,1)S(1)}, u32[]{:S(2)}, u32[]{:S(2)}) %collective-permute-start.28) | collective-permute-done | bytes 229408 | tf_op jit(solution)/shard_map/ppermute | solution.py:116
  242.1 1.6 collective-permute-start.29
  243.8 3.6 %collective-permute-done.29 = bf16[2,56,512]{2,1,0:T(8,128)(2,1)S(1)} collective-permute-done((bf16[2,56,512]{2,1,0:T(8,128)(2,1)S(1)}, bf16[2,56,512]{2,1,0:T(8,128)(2,1)S(1)}, u32[]{:S(2)}, u32[]{:S(2)}) %collective-permute-start.29) | collective-permute-done | bytes 114720 | tf_op jit(solution)/shard_map/ppermute | solution.py:116
  247.5 1.6 collective-permute-start.30
  250.4 2.9 %collective-permute-done.30 = bf16[1,56,512]{2,1,0:T(8,128)(2,1)S(1)} collective-permute-done((bf16[1,56,512]{2,1,0:T(8,128)(2,1)S(1)}, bf16[1,56,512]{2,1,0:T(8,128)(2,1)S(1)}, u32[]{:S(2)}, u32[]{:S(2)}) %collective-permute-start.30) | collective-permute-done | bytes 57376 | tf_op jit(solution)/shard_map/ppermute | solution.py:116
  (186 shorter events, 34.6 us)
Async XLA Ops:
  0.6 8.3 %copy-start.7 = (bf16[1,2,512,256]{3,2,1,0:T(8,128)(2,1)S(1)}, bf16[1,2,512,256]{3,2,1,0:T(8,128)(2,1)}, u32[]{:S(2)}) copy-start(bf16[1,2,512,256]{3,2,1,0:T(8,128)(2,1)} %param.4) | copy-start | bytes 1572868
  1.7 7.3 %collective-permute-start = (bf16[2,128,256]{2,1,0:T(8,128)(2,1)S(1)}, bf16[2,128,256]{2,1,0:T(8,128)(2,1)S(1)}, u32[]{:S(2)}, u32[]{:S(2)}) collective-permute-start(bf16[2,128,256]{2,1,0:T(8,128)(2,1)S(1)} %get-tuple-element.75), channel_id=1, source_target_pairs={{0,1},{1,2},{2,3},{3,4},{4,5},{5,6},{6,7},{7,8},{8,9},{9,10},{10,1... | collective-permute-start | bytes 393224 | tf_op jit(solution)/shard_map/ppermute | solution.py:15
  3.6 7.2 %collective-permute-start.1 = (bf16[2,128,256]{2,1,0:T(8,128)(2,1)S(1)}, bf16[2,128,256]{2,1,0:T(8,128)(2,1)S(1)}, u32[]{:S(2)}, u32[]{:S(2)}) collective-permute-start(bf16[2,128,256]{2,1,0:T(8,128)(2,1)S(1)} %get-tuple-element.74), channel_id=1, source_target_pairs={{1,0},{2,1},{3,2},{4,3},{5,4},{6,5},{7,6},{8,7},{9,8},{10,9},{11,1... | collective-permute-start | bytes 393224 | tf_op jit(solution)/shard_map/ppermute | solution.py:15
  10.9 160.0 %copy-start.46 = (bf16[2,128,256]{2,1,0:T(8,128)(2,1)}, bf16[2,128,256]{2,1,0:T(8,128)(2,1)S(1)}, u32[]{:S(2)}) copy-start(bf16[2,128,256]{2,1,0:T(8,128)(2,1)S(1)} %collective-permute-done.1) | copy-start | bytes 393220
  12.7 8.2 %copy-start.19 = (bf16[2,512,256]{2,1,0:T(8,128)(2,1)}, bf16[2,512,256]{2,1,0:T(8,128)(2,1)S(1)}, u32[]{:S(2)}) copy-start(bf16[2,512,256]{2,1,0:T(8,128)(2,1)S(1)} %fusion) | copy-start | bytes 1572868
  12.7 16.4 %collective-permute-start.2 = (bf16[2,512,256]{2,1,0:T(8,128)(2,1)S(1)}, bf16[2,512,256]{2,1,0:T(8,128)(2,1)S(1)}, u32[]{:S(2)}, u32[]{:S(2)}) collective-permute-start(bf16[2,512,256]{2,1,0:T(8,128)(2,1)S(1)} %fusion), channel_id=1, source_target_pairs={{0,2},{1,3},{2,4},{3,5},{4,6},{5,7},{6,8},{7,9},{8,10},{9,11},{10,... | collective-permute-start | bytes 1572872 | tf_op jit(solution)/shard_map/ppermute | solution.py:15
  18.5 17.0 %collective-permute-start.3 = (bf16[2,512,256]{2,1,0:T(8,128)(2,1)S(1)}, bf16[2,512,256]{2,1,0:T(8,128)(2,1)S(1)}, u32[]{:S(2)}, u32[]{:S(2)}) collective-permute-start(bf16[2,512,256]{2,1,0:T(8,128)(2,1)S(1)} %fusion), channel_id=1, source_target_pairs={{2,0},{3,1},{4,2},{5,3},{6,4},{7,5},{8,6},{9,7},{10,8},{11,9},{12,... | collective-permute-start | bytes 1572872 | tf_op jit(solution)/shard_map/ppermute | solution.py:15
  29.9 6.4 %copy-start.14 = (bf16[2,512,256]{2,1,0:T(8,128)(2,1)S(1)}, bf16[2,512,256]{2,1,0:T(8,128)(2,1)}, u32[]{:S(2)}) copy-start(bf16[2,512,256]{2,1,0:T(8,128)(2,1)} %param.5) | copy-start | bytes 1572868
  39.6 14.0 %collective-permute-start.5 = (bf16[2,512,256]{2,1,0:T(8,128)(2,1)S(1)}, bf16[2,512,256]{2,1,0:T(8,128)(2,1)S(1)}, u32[]{:S(2)}, u32[]{:S(2)}) collective-permute-start(bf16[2,512,256]{2,1,0:T(8,128)(2,1)S(1)} %get-tuple-element.57), channel_id=1, source_target_pairs={{0,2},{1,3},{2,4},{3,5},{4,6},{5,7},{6,8},{7,9},{8,10},{9,11},{10,... | collective-permute-start | bytes 1572872 | tf_op jit(solution)/shard_map/ppermute | solution.py:15
  41.6 16.1 %collective-permute-start.4 = (bf16[2,512,256]{2,1,0:T(8,128)(2,1)S(1)}, bf16[2,512,256]{2,1,0:T(8,128)(2,1)S(1)}, u32[]{:S(2)}, u32[]{:S(2)}) collective-permute-start(bf16[2,512,256]{2,1,0:T(8,128)(2,1)S(1)} %get-tuple-element.56), channel_id=1, source_target_pairs={{2,0},{3,1},{4,2},{5,3},{6,4},{7,5},{8,6},{9,7},{10,8},{11,9},{12,... | collective-permute-start | bytes 1572872 | tf_op jit(solution)/shard_map/ppermute | solution.py:15
  57.9 19.0 %copy-start.1 = (f32[2,512,256]{2,1,0:T(8,128)}, f32[2,512,256]{2,1,0:T(8,128)S(1)}, u32[]{:S(2)}) copy-start(f32[2,512,256]{2,1,0:T(8,128)S(1)} %fusion.16) | copy-start | bytes 3145732
  64.9 6.6 %collective-permute-start.6 = (bf16[2,128,256]{2,1,0:T(8,128)(2,1)}, bf16[2,128,256]{2,1,0:T(8,128)(2,1)}, u32[]{:S(2)}, u32[]{:S(2)}) collective-permute-start(bf16[2,128,256]{2,1,0:T(8,128)(2,1)} %get-tuple-element.54), channel_id=1, source_target_pairs={{0,1},{1,2},{2,3},{3,4},{4,5},{5,6},{6,7},{7,8},{8,9},{9,10},{10,1... | collective-permute-start | bytes 393224 | tf_op jit(solution)/shard_map/ppermute | solution.py:15
  66.8 6.5 %collective-permute-start.7 = (bf16[2,128,256]{2,1,0:T(8,128)(2,1)}, bf16[2,128,256]{2,1,0:T(8,128)(2,1)}, u32[]{:S(2)}, u32[]{:S(2)}) collective-permute-start(bf16[2,128,256]{2,1,0:T(8,128)(2,1)} %get-tuple-element.55), channel_id=1, source_target_pairs={{1,0},{2,1},{3,2},{4,3},{5,4},{6,5},{7,6},{8,7},{9,8},{10,9},{11,1... | collective-permute-start | bytes 393224 | tf_op jit(solution)/shard_map/ppermute | solution.py:15
  73.3 7.3 %copy-start.20 = (bf16[2,512,256]{2,1,0:T(8,128)(2,1)S(1)}, bf16[2,512,256]{2,1,0:T(8,128)(2,1)}, u32[]{:S(2)}) copy-start(bf16[2,512,256]{2,1,0:T(8,128)(2,1)} %copy-done.19) | copy-start | bytes 1572868
  73.3 7.3 %copy-start.34 = (bf16[2,512,256]{2,1,0:T(8,128)(2,1)S(1)}, bf16[2,512,256]{2,1,0:T(8,128)(2,1)}, u32[]{:S(2)}) copy-start(bf16[2,512,256]{2,1,0:T(8,128)(2,1)} %copy-done.33) | copy-start | bytes 1572868
  73.3 7.3 %copy-start.41 = (bf16[2,512,256]{1,2,0:T(8,128)(2,1)S(1)}, bf16[2,512,256]{1,2,0:T(8,128)(2,1)}, u32[]{:S(2)}) copy-start(bf16[2,512,256]{1,2,0:T(8,128)(2,1)} %copy-done.40) | copy-start | bytes 1572868
  73.3 7.3 %copy-start.43 = (bf16[2,512,256]{1,2,0:T(8,128)(2,1)S(1)}, bf16[2,512,256]{1,2,0:T(8,128)(2,1)}, u32[]{:S(2)}) copy-start(bf16[2,512,256]{1,2,0:T(8,128)(2,1)} %copy-done.42) | copy-start | bytes 1572868
  73.3 7.3 %copy-start.45 = (bf16[2,512,256]{2,1,0:T(8,128)(2,1)S(1)}, bf16[2,512,256]{2,1,0:T(8,128)(2,1)}, u32[]{:S(2)}) copy-start(bf16[2,512,256]{2,1,0:T(8,128)(2,1)} %copy-done.44) | copy-start | bytes 1572868
  75.7 8.5 %collective-permute-start.8 = (bf16[2,256,256]{2,1,0:T(8,128)(2,1)S(1)}, bf16[2,256,256]{2,1,0:T(8,128)(2,1)S(1)}, u32[]{:S(2)}, u32[]{:S(2)}) collective-permute-start(bf16[2,256,256]{2,1,0:T(8,128)(2,1)S(1)} %pad_maximum_fusion.30), channel_id=1, source_target_pairs={{32,0},{64,32},{96,64},{33,1},{65,33},{97,65},{34,2},{66,34},{98,6... | collective-permute-start | bytes 786440 | tf_op jit(solution)/shard_map/ppermute | solution.py:15
  79.1 11.8 %copy-start.5 = (f32[2,512,256]{1,2,0:T(8,128)S(1)}, f32[2,512,256]{1,2,0:T(8,128)}, u32[]{:S(2)}) copy-start(f32[2,512,256]{1,2,0:T(8,128)} %get-tuple-element.8) | copy-start | bytes 3145732
  79.1 11.8 %copy-start.6 = (f32[2,512,256]{1,2,0:T(8,128)S(1)}, f32[2,512,256]{1,2,0:T(8,128)}, u32[]{:S(2)}) copy-start(f32[2,512,256]{1,2,0:T(8,128)} %get-tuple-element.40) | copy-start | bytes 3145732
  79.1 11.8 %collective-permute-start.9 = (bf16[2,256,256]{2,1,0:T(8,128)(2,1)S(1)}, bf16[2,256,256]{2,1,0:T(8,128)(2,1)S(1)}, u32[]{:S(2)}, u32[]{:S(2)}) collective-permute-start(bf16[2,256,256]{2,1,0:T(8,128)(2,1)S(1)} %get-tuple-element.33), channel_id=1, source_target_pairs={{32,0},{64,32},{96,64},{33,1},{65,33},{97,65},{34,2},{66,34},{98,6... | collective-permute-start | bytes 786440 | tf_op jit(solution)/shard_map/ppermute | solution.py:15
  91.3 9.0 %copy-start.35 = (bf16[2,512,256]{1,2,0:T(8,128)(2,1)S(1)}, bf16[2,512,256]{1,2,0:T(8,128)(2,1)}, u32[]{:S(2)}) copy-start(bf16[2,512,256]{1,2,0:T(8,128)(2,1)} %get-tuple-element.41) | copy-start | bytes 1572868
  92.3 8.0 %copy-start.15 = (bf16[2,512,256]{2,1,0:T(8,128)(2,1)S(1)}, bf16[2,512,256]{2,1,0:T(8,128)(2,1)}, u32[]{:S(2)}) copy-start(bf16[2,512,256]{2,1,0:T(8,128)(2,1)} %param.5) | copy-start | bytes 1572868
  92.3 8.3 %copy-start.8 = (bf16[1,2,512,256]{3,2,1,0:T(8,128)(2,1)S(1)}, bf16[1,2,512,256]{3,2,1,0:T(8,128)(2,1)}, u32[]{:S(2)}) copy-start(bf16[1,2,512,256]{3,2,1,0:T(8,128)(2,1)} %param.4) | copy-start | bytes 1572868
  92.4 8.3 %copy-start.23 = (bf16[2,384,256]{2,1,0:T(8,128)(2,1)S(1)}, bf16[2,384,256]{2,1,0:T(8,128)(2,1)}, u32[]{:S(2)}) copy-start(bf16[2,384,256]{2,1,0:T(8,128)(2,1)} %copy-done.22) | copy-start | bytes 1179652
  92.4 8.3 %copy-start.26 = (bf16[2,384,256]{2,1,0:T(8,128)(2,1)S(1)}, bf16[2,384,256]{2,1,0:T(8,128)(2,1)}, u32[]{:S(2)}) copy-start(bf16[2,384,256]{2,1,0:T(8,128)(2,1)} %copy-done.25) | copy-start | bytes 1179652
  92.4 8.3 %copy-start.37 = (bf16[2,512,256]{1,2,0:T(8,128)(2,1)S(1)}, bf16[2,512,256]{1,2,0:T(8,128)(2,1)}, u32[]{:S(2)}) copy-start(bf16[2,512,256]{1,2,0:T(8,128)(2,1)} %copy-done.36) | copy-start | bytes 1572868
  92.4 8.3 %copy-start.39 = (bf16[2,512,256]{1,2,0:T(8,128)(2,1)S(1)}, bf16[2,512,256]{1,2,0:T(8,128)(2,1)}, u32[]{:S(2)}) copy-start(bf16[2,512,256]{1,2,0:T(8,128)(2,1)} %copy-done.38) | copy-start | bytes 1572868
  92.4 8.3 %copy-start.49 = (bf16[2,128,256]{2,1,0:T(8,128)(2,1)S(1)}, bf16[2,128,256]{2,1,0:T(8,128)(2,1)}, u32[]{:S(2)}) copy-start(bf16[2,128,256]{2,1,0:T(8,128)(2,1)} %copy-done.48) | copy-start | bytes 393220
  92.5 16.5 %collective-permute-start.11 = (bf16[2,512,256]{2,1,0:T(8,128)(2,1)S(1)}, bf16[2,512,256]{2,1,0:T(8,128)(2,1)S(1)}, u32[]{:S(2)}, u32[]{:S(2)}) collective-permute-start(bf16[2,512,256]{2,1,0:T(8,128)(2,1)S(1)} %get-tuple-element.53), channel_id=1, source_target_pairs={{0,2},{1,3},{2,4},{3,5},{4,6},{5,7},{6,8},{7,9},{8,10},{9,11},{10,... | collective-permute-start | bytes 1572872 | tf_op jit(solution)/shard_map/ppermute | solution.py:15
  98.2 16.6 %collective-permute-start.10 = (bf16[2,512,256]{2,1,0:T(8,128)(2,1)S(1)}, bf16[2,512,256]{2,1,0:T(8,128)(2,1)S(1)}, u32[]{:S(2)}, u32[]{:S(2)}) collective-permute-start(bf16[2,512,256]{2,1,0:T(8,128)(2,1)S(1)} %get-tuple-element.52), channel_id=1, source_target_pairs={{2,0},{3,1},{4,2},{5,3},{6,4},{7,5},{8,6},{9,7},{10,8},{11,9},{12,... | collective-permute-start | bytes 1572872 | tf_op jit(solution)/shard_map/ppermute | solution.py:15
  103.9 11.1 %copy-start.3 = (f32[2,512,256]{1,2,0:T(8,128)S(1)}, f32[2,512,256]{1,2,0:T(8,128)}, u32[]{:S(2)}) copy-start(f32[2,512,256]{1,2,0:T(8,128)} %get-tuple-element.4) | copy-start | bytes 3145732
  103.9 11.1 %copy-start.4 = (f32[2,512,256]{1,2,0:T(8,128)S(1)}, f32[2,512,256]{1,2,0:T(8,128)}, u32[]{:S(2)}) copy-start(f32[2,512,256]{1,2,0:T(8,128)} %get-tuple-element.38) | copy-start | bytes 3145732
  116.4 7.8 %collective-permute-start.12 = (bf16[2,128,256]{2,1,0:T(8,128)(2,1)S(1)}, bf16[2,128,256]{2,1,0:T(8,128)(2,1)S(1)}, u32[]{:S(2)}, u32[]{:S(2)}) collective-permute-start(bf16[2,128,256]{2,1,0:T(8,128)(2,1)S(1)} %get-tuple-element.50), channel_id=1, source_target_pairs={{0,1},{1,2},{2,3},{3,4},{4,5},{5,6},{6,7},{7,8},{8,9},{9,10},{10,1... | collective-permute-start | bytes 393224 | tf_op jit(solution)/shard_map/ppermute | solution.py:15
  118.3 6.1 %collective-permute-start.13 = (bf16[2,128,256]{2,1,0:T(8,128)(2,1)S(1)}, bf16[2,128,256]{2,1,0:T(8,128)(2,1)S(1)}, u32[]{:S(2)}, u32[]{:S(2)}) collective-permute-start(bf16[2,128,256]{2,1,0:T(8,128)(2,1)S(1)} %get-tuple-element.51), channel_id=1, source_target_pairs={{1,0},{2,1},{3,2},{4,3},{5,4},{6,5},{7,6},{8,7},{9,8},{10,9},{11,1... | collective-permute-start | bytes 393224 | tf_op jit(solution)/shard_map/ppermute | solution.py:15
  122.9 14.4 %collective-permute-start.15 = (bf16[2,256,256]{2,1,0:T(8,128)(2,1)S(1)}, bf16[2,256,256]{2,1,0:T(8,128)(2,1)S(1)}, u32[]{:S(2)}, u32[]{:S(2)}) collective-permute-start(bf16[2,256,256]{2,1,0:T(8,128)(2,1)S(1)} %get-tuple-element.29), channel_id=1, source_target_pairs={{32,0},{64,32},{96,64},{33,1},{65,33},{97,65},{34,2},{66,34},{98,6... | collective-permute-start | bytes 786440 | tf_op jit(solution)/shard_map/ppermute | solution.py:15
  125.4 11.8 %collective-permute-start.14 = (bf16[2,256,256]{2,1,0:T(8,128)(2,1)S(1)}, bf16[2,256,256]{2,1,0:T(8,128)(2,1)S(1)}, u32[]{:S(2)}, u32[]{:S(2)}) collective-permute-start(bf16[2,256,256]{2,1,0:T(8,128)(2,1)S(1)} %pad_maximum_fusion.31), channel_id=1, source_target_pairs={{32,0},{64,32},{96,64},{33,1},{65,33},{97,65},{34,2},{66,34},{98,6... | collective-permute-start | bytes 786440 | tf_op jit(solution)/shard_map/ppermute | solution.py:15
  138.7 15.8 %collective-permute-start.17 = (bf16[2,512,256]{2,1,0:T(8,128)(2,1)S(1)}, bf16[2,512,256]{2,1,0:T(8,128)(2,1)S(1)}, u32[]{:S(2)}, u32[]{:S(2)}) collective-permute-start(bf16[2,512,256]{2,1,0:T(8,128)(2,1)S(1)} %get-tuple-element.49), channel_id=1, source_target_pairs={{0,2},{1,3},{2,4},{3,5},{4,6},{5,7},{6,8},{7,9},{8,10},{9,11},{10,... | collective-permute-start | bytes 1572872 | tf_op jit(solution)/shard_map/ppermute | solution.py:15
  141.9 16.7 %collective-permute-start.16 = (bf16[2,512,256]{2,1,0:T(8,128)(2,1)S(1)}, bf16[2,512,256]{2,1,0:T(8,128)(2,1)S(1)}, u32[]{:S(2)}, u32[]{:S(2)}) collective-permute-start(bf16[2,512,256]{2,1,0:T(8,128)(2,1)S(1)} %get-tuple-element.48), channel_id=1, source_target_pairs={{2,0},{3,1},{4,2},{5,3},{6,4},{7,5},{8,6},{9,7},{10,8},{11,9},{12,... | collective-permute-start | bytes 1572872 | tf_op jit(solution)/shard_map/ppermute | solution.py:15
  160.3 7.8 %collective-permute-start.18 = (bf16[2,128,256]{2,1,0:T(8,128)(2,1)S(1)}, bf16[2,128,256]{2,1,0:T(8,128)(2,1)S(1)}, u32[]{:S(2)}, u32[]{:S(2)}) collective-permute-start(bf16[2,128,256]{2,1,0:T(8,128)(2,1)S(1)} %get-tuple-element.46), channel_id=1, source_target_pairs={{0,1},{1,2},{2,3},{3,4},{4,5},{5,6},{6,7},{7,8},{8,9},{9,10},{10,1... | collective-permute-start | bytes 393224 | tf_op jit(solution)/shard_map/ppermute | solution.py:15
  162.2 6.1 %collective-permute-start.19 = (bf16[2,128,256]{2,1,0:T(8,128)(2,1)S(1)}, bf16[2,128,256]{2,1,0:T(8,128)(2,1)S(1)}, u32[]{:S(2)}, u32[]{:S(2)}) collective-permute-start(bf16[2,128,256]{2,1,0:T(8,128)(2,1)S(1)} %get-tuple-element.47), channel_id=1, source_target_pairs={{1,0},{2,1},{3,2},{4,3},{5,4},{6,5},{7,6},{8,7},{9,8},{10,9},{11,1... | collective-permute-start | bytes 393224 | tf_op jit(solution)/shard_map/ppermute | solution.py:15
  166.8 13.6 %collective-permute-start.21 = (bf16[2,256,256]{2,1,0:T(8,128)(2,1)S(1)}, bf16[2,256,256]{2,1,0:T(8,128)(2,1)S(1)}, u32[]{:S(2)}, u32[]{:S(2)}) collective-permute-start(bf16[2,256,256]{2,1,0:T(8,128)(2,1)S(1)} %get-tuple-element.25), channel_id=1, source_target_pairs={{32,0},{64,32},{96,64},{33,1},{65,33},{97,65},{34,2},{66,34},{98,6... | collective-permute-start | bytes 786440 | tf_op jit(solution)/shard_map/ppermute | solution.py:15
  169.4 11.0 %collective-permute-start.20 = (bf16[2,256,256]{2,1,0:T(8,128)(2,1)S(1)}, bf16[2,256,256]{2,1,0:T(8,128)(2,1)S(1)}, u32[]{:S(2)}, u32[]{:S(2)}) collective-permute-start(bf16[2,256,256]{2,1,0:T(8,128)(2,1)S(1)} %pad_maximum_fusion.32), channel_id=1, source_target_pairs={{32,0},{64,32},{96,64},{33,1},{65,33},{97,65},{34,2},{66,34},{98,6... | collective-permute-start | bytes 786440 | tf_op jit(solution)/shard_map/ppermute | solution.py:15
  181.9 16.5 %collective-permute-start.23 = (bf16[2,512,256]{2,1,0:T(8,128)(2,1)S(1)}, bf16[2,512,256]{2,1,0:T(8,128)(2,1)S(1)}, u32[]{:S(2)}, u32[]{:S(2)}) collective-permute-start(bf16[2,512,256]{2,1,0:T(8,128)(2,1)S(1)} %get-tuple-element.45), channel_id=1, source_target_pairs={{0,2},{1,3},{2,4},{3,5},{4,6},{5,7},{6,8},{7,9},{8,10},{9,11},{10,... | collective-permute-start | bytes 1572872 | tf_op jit(solution)/shard_map/ppermute | solution.py:15
  186.6 16.3 %collective-permute-start.22 = (bf16[2,512,256]{2,1,0:T(8,128)(2,1)S(1)}, bf16[2,512,256]{2,1,0:T(8,128)(2,1)S(1)}, u32[]{:S(2)}, u32[]{:S(2)}) collective-permute-start(bf16[2,512,256]{2,1,0:T(8,128)(2,1)S(1)} %get-tuple-element.44), channel_id=1, source_target_pairs={{2,0},{3,1},{4,2},{5,3},{6,4},{7,5},{8,6},{9,7},{10,8},{11,9},{12,... | collective-permute-start | bytes 1572872 | tf_op jit(solution)/shard_map/ppermute | solution.py:15
  214.7 2.8 %collective-permute-start.26 = (bf16[16,56,512]{2,1,0:T(8,128)(2,1)}, bf16[16,56,512]{2,1,0:T(8,128)(2,1)}, u32[]{:S(2)}, u32[]{:S(2)}) collective-permute-start(bf16[16,56,512]{2,1,0:T(8,128)(2,1)} %fusion.28), channel_id=1, source_target_pairs={{0,1},{1,0},{2,3},{3,2},{4,5},{5,4},{6,7},{7,6},{8,9},{9,8},{10,11... | collective-permute-start | bytes 2752520 | tf_op jit(solution)/shard_map/ppermute | solution.py:116
  214.7 5.8 %copy-start.12 = (bf16[2,512,256]{1,2,0:T(8,128)(2,1)S(1)}, bf16[2,512,256]{1,2,0:T(8,128)(2,1)}, u32[]{:S(2)}) copy-start(bf16[2,512,256]{1,2,0:T(8,128)(2,1)} %get-tuple-element.60) | copy-start | bytes 1572868
  214.7 5.9 %copy-start.13 = (bf16[2,512,256]{1,2,0:T(8,128)(2,1)S(1)}, bf16[2,512,256]{1,2,0:T(8,128)(2,1)}, u32[]{:S(2)}) copy-start(bf16[2,512,256]{1,2,0:T(8,128)(2,1)} %get-tuple-element.61) | copy-start | bytes 1572868
  220.5 13.5 %collective-permute-start.27 = (bf16[8,56,512]{2,1,0:T(8,128)(2,1)S(1)}, bf16[8,56,512]{2,1,0:T(8,128)(2,1)S(1)}, u32[]{:S(2)}, u32[]{:S(2)}) collective-permute-start(bf16[8,56,512]{2,1,0:T(8,128)(2,1)S(1)} %fusion.69), channel_id=1, source_target_pairs={{0,2},{1,3},{2,0},{3,1},{4,6},{5,7},{6,4},{7,5},{8,10},{9,11},{10,... | collective-permute-start | bytes 1376264 | tf_op jit(solution)/shard_map/ppermute | solution.py:116
  221.6 22.0 %collective-permute-start.24 = (bf16[2,128,256]{2,1,0:T(8,128)(2,1)S(1)}, bf16[2,128,256]{2,1,0:T(8,128)(2,1)S(1)}, u32[]{:S(2)}, u32[]{:S(2)}) collective-permute-start(bf16[2,128,256]{2,1,0:T(8,128)(2,1)S(1)} %get-tuple-element.42), channel_id=1, source_target_pairs={{0,1},{1,2},{2,3},{3,4},{4,5},{5,6},{6,7},{7,8},{8,9},{9,10},{10,1... | collective-permute-start | bytes 393224 | tf_op jit(solution)/shard_map/ppermute | solution.py:15
  223.7 20.0 %collective-permute-start.25 = (bf16[2,128,256]{2,1,0:T(8,128)(2,1)S(1)}, bf16[2,128,256]{2,1,0:T(8,128)(2,1)S(1)}, u32[]{:S(2)}, u32[]{:S(2)}) collective-permute-start(bf16[2,128,256]{2,1,0:T(8,128)(2,1)S(1)} %get-tuple-element.43), channel_id=1, source_target_pairs={{1,0},{2,1},{3,2},{4,3},{5,4},{6,5},{7,6},{8,7},{9,8},{10,9},{11,1... | collective-permute-start | bytes 393224 | tf_op jit(solution)/shard_map/ppermute | solution.py:15
  234.2 7.6 %collective-permute-start.28 = (bf16[4,56,512]{2,1,0:T(8,128)(2,1)S(1)}, bf16[4,56,512]{2,1,0:T(8,128)(2,1)S(1)}, u32[]{:S(2)}, u32[]{:S(2)}) collective-permute-start(bf16[4,56,512]{2,1,0:T(8,128)(2,1)S(1)} %fusion.120), channel_id=1, source_target_pairs={{0,4},{1,5},{2,6},{3,7},{4,0},{5,1},{6,2},{7,3},{8,12},{9,13},{10,... | collective-permute-start | bytes 688136 | tf_op jit(solution)/shard_map/ppermute | solution.py:116
  241.9 7.2 %copy-start.16 = (f32[1,2,256,256]{3,2,1,0:T(8,128)S(1)}, f32[1,2,256,256]{3,2,1,0:T(8,128)}, u32[]{:S(2)}) copy-start(f32[1,2,256,256]{3,2,1,0:T(8,128)} %get-tuple-element.34) | copy-start | bytes 1572868
  241.9 7.1 %copy-start.17 = (f32[1,2,256,256]{3,2,1,0:T(8,128)S(1)}, f32[1,2,256,256]{3,2,1,0:T(8,128)}, u32[]{:S(2)}) copy-start(f32[1,2,256,256]{3,2,1,0:T(8,128)} %get-tuple-element.30) | copy-start | bytes 1572868
  242.0 7.1 %copy-start.18 = (f32[1,2,256,256]{3,2,1,0:T(8,128)S(1)}, f32[1,2,256,256]{3,2,1,0:T(8,128)}, u32[]{:S(2)}) copy-start(f32[1,2,256,256]{3,2,1,0:T(8,128)} %get-tuple-element.26) | copy-start | bytes 1572868
  242.0 7.1 %copy-start.27 = (f32[1,2,128,256]{3,2,1,0:T(8,128)S(1)}, f32[1,2,128,256]{3,2,1,0:T(8,128)}, u32[]{:S(2)}) copy-start(f32[1,2,128,256]{3,2,1,0:T(8,128)} %get-tuple-element.20) | copy-start | bytes 786436
  242.0 7.1 %copy-start.28 = (f32[1,2,128,256]{3,2,1,0:T(8,128)S(1)}, f32[1,2,128,256]{3,2,1,0:T(8,128)}, u32[]{:S(2)}) copy-start(f32[1,2,128,256]{3,2,1,0:T(8,128)} %get-tuple-element.35) | copy-start | bytes 786436
  242.0 7.1 %copy-start.29 = (f32[1,2,128,256]{3,2,1,0:T(8,128)S(1)}, f32[1,2,128,256]{3,2,1,0:T(8,128)}, u32[]{:S(2)}) copy-start(f32[1,2,128,256]{3,2,1,0:T(8,128)} %get-tuple-element.16) | copy-start | bytes 786436
  242.0 7.1 %copy-start.30 = (f32[1,2,128,256]{3,2,1,0:T(8,128)S(1)}, f32[1,2,128,256]{3,2,1,0:T(8,128)}, u32[]{:S(2)}) copy-start(f32[1,2,128,256]{3,2,1,0:T(8,128)} %get-tuple-element.31) | copy-start | bytes 786436
  242.0 7.1 %copy-start.31 = (f32[1,2,128,256]{3,2,1,0:T(8,128)S(1)}, f32[1,2,128,256]{3,2,1,0:T(8,128)}, u32[]{:S(2)}) copy-start(f32[1,2,128,256]{3,2,1,0:T(8,128)} %get-tuple-element.12) | copy-start | bytes 786436
  242.0 7.1 %copy-start.32 = (f32[1,2,128,256]{3,2,1,0:T(8,128)S(1)}, f32[1,2,128,256]{3,2,1,0:T(8,128)}, u32[]{:S(2)}) copy-start(f32[1,2,128,256]{3,2,1,0:T(8,128)} %get-tuple-element.27) | copy-start | bytes 786436
  242.1 5.4 %collective-permute-start.29 = (bf16[2,56,512]{2,1,0:T(8,128)(2,1)S(1)}, bf16[2,56,512]{2,1,0:T(8,128)(2,1)S(1)}, u32[]{:S(2)}, u32[]{:S(2)}) collective-permute-start(bf16[2,56,512]{2,1,0:T(8,128)(2,1)S(1)} %fusion.136), channel_id=1, source_target_pairs={{0,8},{1,9},{2,10},{3,11},{4,12},{5,13},{6,14},{7,15},{8,0},{9,1},... | collective-permute-start | bytes 344072 | tf_op jit(solution)/shard_map/ppermute | solution.py:116
  247.5 5.8 %collective-permute-start.30 = (bf16[1,56,512]{2,1,0:T(8,128)(2,1)S(1)}, bf16[1,56,512]{2,1,0:T(8,128)(2,1)S(1)}, u32[]{:S(2)}, u32[]{:S(2)}) collective-permute-start(bf16[1,56,512]{2,1,0:T(8,128)(2,1)S(1)} %fusion.146), channel_id=1, source_target_pairs={{0,16},{1,17},{2,18},{3,19},{4,20},{5,21},{6,22},{7,23},{8,24},{9,... | collective-permute-start | bytes 172040 | tf_op jit(solution)/shard_map/ppermute | solution.py:116
  (18 other events, 36.2 us)

commit v3 on v2

--- a/solution.py
+++ b/solution.py
@@ -104,19 +104,25 @@
     return third_earlier, first_following
 
 
-def halving_scatter(parts):
+def halving_scatter(parts, order):
     count = parts[0].shape[0]
+    bits = count.bit_length() - 1
     rank = lax.axis_index("seq")
-    bit = 0
-    while (1 << bit) < count:
+    parts = [p.reshape((2,) * bits + p.shape[1:]) for p in parts]
+    left = list(reversed(range(bits)))
+    for bit in order:
+        axis = left.index(bit)
+        left.pop(axis)
         own = ((rank >> bit) & 1) == 1
         pairs = [(j, j ^ (1 << bit)) for j in range(count)]
-        halves = [p.reshape(p.shape[0] // 2, 2, *p.shape[1:]) for p in parts]
-        sends = tuple(jnp.where(own, h[:, 0], h[:, 1]).astype(jnp.bfloat16) for h in halves)
+        lows = [lax.index_in_dim(p, 0, axis, keepdims=False) for p in parts]
+        highs = [lax.index_in_dim(p, 1, axis, keepdims=False) for p in parts]
+        sends = tuple(jnp.where(own, lo, hi).astype(jnp.bfloat16) for lo, hi in zip(lows, highs))
         got = lax.ppermute(sends, "seq", pairs)
-        parts = [jnp.where(own, h[:, 1], h[:, 0]) + g.astype(jnp.float32) for h, g in zip(halves, got)]
-        bit += 1
-    return [p[0] for p in parts]
+        parts = [
+            jnp.where(own, hi, lo) + g.astype(jnp.float32) for lo, hi, g in zip(lows, highs, got)
+        ]
+    return parts
 
 
 def shards(section_inputs, cotangent, conv_weight, out_weight):
@@ -176,7 +182,7 @@
     out_all = jnp.concatenate(
         [acc.reshape(seq_count, out_rows, channels) for acc in out_acc], axis=1
     ).reshape(seq_count, depth * out_rows * channels // (2 * channels), 2 * channels)
-    (mine,) = halving_scatter([jnp.concatenate([conv_all, out_all], axis=1)])
+    (mine,) = halving_scatter([jnp.concatenate([conv_all, out_all], axis=1)], (0, 1, 3, 2, 4))
     conv_grads = mine[: depth * conv_rows].reshape(1, depth, conv_rows, 2 * channels) * grad_scale
     out_grads = mine[depth * conv_rows :].reshape(1, depth, out_rows, channels) * grad_scale
     return (input_grads[None], conv_grads, out_grads)

time: 256 us -> 255 us (level)
  no operation moved by 1% of the time
where the time goes in v3:
time: 255 us; the launch traced here: 254 us
  waiting for transfers between devices  110 us (43%)
  starting transfers between devices  74.2 us (29%)
  matrix products  41.6 us (16%)
  other arithmetic  17.8 us (7%)
  local copies, waits for them, and re-layouts  8.33 us (3%)
    ppermute x26, waiting for transfers between devices, shifted(): lax.ppermute(value, axis, [(source, source + steps) for source in range(l...  88.7 us
    ppermute x26, starting transfers between devices, shifted(): lax.ppermute(value, axis, [(source, source + steps) for source in range(l...  69.5 us
    ppermute x5, waiting for transfers between devices, halving_scatter(): got = lax.ppermute(sends, 'seq', pairs)  21.5 us
    dot_general x8, matrix products, backward_layer(): jnp.einsum('mpc,mpd->cd', taps, grad_pre, preferred_element_type=jnp.floa...  15.8 us
    dot_general x8, matrix products, backward_layer(): jnp.einsum('mpd,cd->mpc', grad_pre, weights, preferred_element_type=jnp.f...  10.4 us
    dot_general x8, matrix products, backward_layer(): jnp.einsum('mpd,cd->mpc', grad_half, out_mat, preferred_element_type=jnp....  7.21 us
    dot_general x7, matrix products, mm(): return jnp.einsum('mpc,cd->mpd', a, b, preferred_element_type=jnp.float32)  5.75 us
  transfers between devices with their start and end apart: 31, of which 23 were waited for; matrix products, arithmetic and copies ran while one was open for 11% of the time, Pallas kernels for 0%

profile of v3, /device:TPU:24, one launch (start us, length us, event | category | flops | bytes accessed | tf_op | source)
XLA Modules:
  0.0 254.1 jit_solution(1642181157744250414)
XLA Ops:
  1.7 1.9 collective-permute-start
  3.6 3.6 %collective-permute-start.1 = (bf16[2,128,256]{2,1,0:T(8,128)(2,1)S(1)}, bf16[2,128,256]{2,1,0:T(8,128)(2,1)S(1)}, u32[]{:S(2)}, u32[]{:S(2)}) collective-permute-start(bf16[2,128,256]{2,1,0:T(8,128)(2,1)S(1)} %get-tuple-element.74), channel_id=1, source_target_pairs={{1,0},{2,1},{3,2},{4,3},{5,4},{6,5},{7,6},{8,7},{9,8},{10,9},{11,1... | collective-permute-start | bytes 393224 | tf_op jit(solution)/shard_map/ppermute | solution.py:15
  7.3 1.6 fusion.101
  9.0 1.8 fusion.58
  12.7 5.6 %collective-permute-start.2 = (bf16[2,512,256]{2,1,0:T(8,128)(2,1)S(1)}, bf16[2,512,256]{2,1,0:T(8,128)(2,1)S(1)}, u32[]{:S(2)}, u32[]{:S(2)}) collective-permute-start(bf16[2,512,256]{2,1,0:T(8,128)(2,1)S(1)} %fusion.2), channel_id=1, source_target_pairs={{0,2},{1,3},{2,4},{3,5},{4,6},{5,7},{6,8},{7,9},{8,10},{9,11},{10,... | collective-permute-start | bytes 1572872 | tf_op jit(solution)/shard_map/ppermute | solution.py:15
  18.5 1.9 collective-permute-start.3
  20.9 8.2 %collective-permute-done.2 = bf16[2,512,256]{2,1,0:T(8,128)(2,1)S(1)} collective-permute-done((bf16[2,512,256]{2,1,0:T(8,128)(2,1)S(1)}, bf16[2,512,256]{2,1,0:T(8,128)(2,1)S(1)}, u32[]{:S(2)}, u32[]{:S(2)}) %collective-permute-start.2) | collective-permute-done | bytes 524320 | tf_op jit(solution)/shard_map/ppermute | solution.py:15
  29.9 5.5 %collective-permute-done.3 = bf16[2,512,256]{2,1,0:T(8,128)(2,1)S(1)} collective-permute-done((bf16[2,512,256]{2,1,0:T(8,128)(2,1)S(1)}, bf16[2,512,256]{2,1,0:T(8,128)(2,1)S(1)}, u32[]{:S(2)}, u32[]{:S(2)}) %collective-permute-start.3) | collective-permute-done | bytes 524320 | tf_op jit(solution)/shard_map/ppermute | solution.py:15
  36.3 2.2 multiply_convert_fusion.15
  39.6 1.9 collective-permute-start.5
  41.6 3.9 %collective-permute-start.4 = (bf16[2,512,256]{2,1,0:T(8,128)(2,1)S(1)}, bf16[2,512,256]{2,1,0:T(8,128)(2,1)S(1)}, u32[]{:S(2)}, u32[]{:S(2)}) collective-permute-start(bf16[2,512,256]{2,1,0:T(8,128)(2,1)S(1)} %get-tuple-element.56), channel_id=1, source_target_pairs={{2,0},{3,1},{4,2},{5,3},{6,4},{7,5},{8,6},{9,7},{10,8},{11,9},{12,... | collective-permute-start | bytes 1572872 | tf_op jit(solution)/shard_map/ppermute | solution.py:15
  45.5 8.2 %collective-permute-done.5 = bf16[2,512,256]{2,1,0:T(8,128)(2,1)S(1)} collective-permute-done((bf16[2,512,256]{2,1,0:T(8,128)(2,1)S(1)}, bf16[2,512,256]{2,1,0:T(8,128)(2,1)S(1)}, u32[]{:S(2)}, u32[]{:S(2)}) %collective-permute-start.5) | collective-permute-done | bytes 524320 | tf_op jit(solution)/shard_map/ppermute | solution.py:15
  53.7 4.0 %collective-permute-done.4 = bf16[2,512,256]{2,1,0:T(8,128)(2,1)S(1)} collective-permute-done((bf16[2,512,256]{2,1,0:T(8,128)(2,1)S(1)}, bf16[2,512,256]{2,1,0:T(8,128)(2,1)S(1)}, u32[]{:S(2)}, u32[]{:S(2)}) %collective-permute-start.4) | collective-permute-done | bytes 524320 | tf_op jit(solution)/shard_map/ppermute | solution.py:15
  58.0 2.0 multiply_convert_fusion.13
  60.0 3.2 %fusion.200 = (bf16[2,512,768]{2,1,0:T(8,128)(2,1)}, f32[2,512,768]{2,1,0:T(8,128)}) fusion(bf16[768,512,1]{1,0,2:T(8,128)(2,1)S(1)} %bitcast.288, bf16[2,512,256]{1,2,0:T(8,128)(2,1)S(1)} %get-tuple-element.37, bf16[2,512,256]{1,2,0:T(8,128)(2,1)S(1)} %get-tuple-element.3), kind=kOutput, calls=%fused_computation.283 | convolution fusion | flops 808189952 | bytes 6553600 | tf_op jit(solution)/shard_map/mpd,cd->mpc/dot_general | solution.py:64
  63.2 1.7 fusion.191
  64.9 1.9 collective-permute-start.6
  66.8 3.6 %collective-permute-start.7 = (bf16[2,128,256]{2,1,0:T(8,128)(2,1)}, bf16[2,128,256]{2,1,0:T(8,128)(2,1)}, u32[]{:S(2)}, u32[]{:S(2)}) collective-permute-start(bf16[2,128,256]{2,1,0:T(8,128)(2,1)} %get-tuple-element.55), channel_id=1, source_target_pairs={{1,0},{2,1},{3,2},{4,3},{5,4},{6,5},{7,6},{8,7},{9,8},{10,9},{11,1... | collective-permute-start | bytes 393224 | tf_op jit(solution)/shard_map/ppermute | solution.py:15
  71.5 1.8 collective-permute-done.7
  73.3 2.3 fusion.167
  75.7 1.3 collective-permute-start.8
  77.0 2.1 fusion.179
  79.1 1.4 collective-permute-start.9
  81.6 2.5 %collective-permute-done.8 = bf16[2,256,256]{2,1,0:T(8,128)(2,1)S(1)} collective-permute-done((bf16[2,256,256]{2,1,0:T(8,128)(2,1)S(1)}, bf16[2,256,256]{2,1,0:T(8,128)(2,1)S(1)}, u32[]{:S(2)}, u32[]{:S(2)}) %collective-permute-start.8) | collective-permute-done | bytes 262176 | tf_op jit(solution)/shard_map/ppermute | solution.py:15
  84.2 6.8 %collective-permute-done.9 = bf16[2,256,256]{2,1,0:T(8,128)(2,1)S(1)} collective-permute-done((bf16[2,256,256]{2,1,0:T(8,128)(2,1)S(1)}, bf16[2,256,256]{2,1,0:T(8,128)(2,1)S(1)}, u32[]{:S(2)}, u32[]{:S(2)}) %collective-permute-start.9) | collective-permute-done | bytes 262176 | tf_op jit(solution)/shard_map/ppermute | solution.py:15
  92.5 5.7 %collective-permute-start.11 = (bf16[2,512,256]{2,1,0:T(8,128)(2,1)S(1)}, bf16[2,512,256]{2,1,0:T(8,128)(2,1)S(1)}, u32[]{:S(2)}, u32[]{:S(2)}) collective-permute-start(bf16[2,512,256]{2,1,0:T(8,128)(2,1)S(1)} %get-tuple-element.53), channel_id=1, source_target_pairs={{0,2},{1,3},{2,4},{3,5},{4,6},{5,7},{6,8},{7,9},{8,10},{9,11},{10,... | collective-permute-start | bytes 1572872 | tf_op jit(solution)/shard_map/ppermute | solution.py:15
  98.2 2.1 collective-permute-start.10
  100.7 2.2 fusion.45
  103.9 5.1 %collective-permute-done.11 = bf16[2,512,256]{2,1,0:T(8,128)(2,1)S(1)} collective-permute-done((bf16[2,512,256]{2,1,0:T(8,128)(2,1)S(1)}, bf16[2,512,256]{2,1,0:T(8,128)(2,1)S(1)}, u32[]{:S(2)}, u32[]{:S(2)}) %collective-permute-start.11) | collective-permute-done | bytes 524320 | tf_op jit(solution)/shard_map/ppermute | solution.py:15
  109.0 5.7 %collective-permute-done.10 = bf16[2,512,256]{2,1,0:T(8,128)(2,1)S(1)} collective-permute-done((bf16[2,512,256]{2,1,0:T(8,128)(2,1)S(1)}, bf16[2,512,256]{2,1,0:T(8,128)(2,1)S(1)}, u32[]{:S(2)}, u32[]{:S(2)}) %collective-permute-start.10) | collective-permute-done | bytes 524320 | tf_op jit(solution)/shard_map/ppermute | solution.py:15
  116.4 1.9 collective-permute-start.12
  118.3 3.6 %collective-permute-start.13 = (bf16[2,128,256]{2,1,0:T(8,128)(2,1)S(1)}, bf16[2,128,256]{2,1,0:T(8,128)(2,1)S(1)}, u32[]{:S(2)}, u32[]{:S(2)}) collective-permute-start(bf16[2,128,256]{2,1,0:T(8,128)(2,1)S(1)} %get-tuple-element.51), channel_id=1, source_target_pairs={{1,0},{2,1},{3,2},{4,3},{5,4},{6,5},{7,6},{8,7},{9,8},{10,9},{11,1... | collective-permute-start | bytes 393224 | tf_op jit(solution)/shard_map/ppermute | solution.py:15
  122.9 1.3 collective-permute-start.15
  125.4 1.3 collective-permute-start.14
  126.7 2.2 fusion.41
  128.9 8.3 %collective-permute-done.14 = bf16[2,256,256]{2,1,0:T(8,128)(2,1)S(1)} collective-permute-done((bf16[2,256,256]{2,1,0:T(8,128)(2,1)S(1)}, bf16[2,256,256]{2,1,0:T(8,128)(2,1)S(1)}, u32[]{:S(2)}, u32[]{:S(2)}) %collective-permute-start.14) | collective-permute-done | bytes 262176 | tf_op jit(solution)/shard_map/ppermute | solution.py:15
  138.7 3.2 %collective-permute-start.17 = (bf16[2,512,256]{2,1,0:T(8,128)(2,1)S(1)}, bf16[2,512,256]{2,1,0:T(8,128)(2,1)S(1)}, u32[]{:S(2)}, u32[]{:S(2)}) collective-permute-start(bf16[2,512,256]{2,1,0:T(8,128)(2,1)S(1)} %get-tuple-element.49), channel_id=1, source_target_pairs={{0,2},{1,3},{2,4},{3,5},{4,6},{5,7},{6,8},{7,9},{8,10},{9,11},{10,... | collective-permute-start | bytes 1572872 | tf_op jit(solution)/shard_map/ppermute | solution.py:15
  141.9 2.7 %collective-permute-start.16 = (bf16[2,512,256]{2,1,0:T(8,128)(2,1)S(1)}, bf16[2,512,256]{2,1,0:T(8,128)(2,1)S(1)}, u32[]{:S(2)}, u32[]{:S(2)}) collective-permute-start(bf16[2,512,256]{2,1,0:T(8,128)(2,1)S(1)} %get-tuple-element.48), channel_id=1, source_target_pairs={{2,0},{3,1},{4,2},{5,3},{6,4},{7,5},{8,6},{9,7},{10,8},{11,9},{12,... | collective-permute-start | bytes 1572872 | tf_op jit(solution)/shard_map/ppermute | solution.py:15
  146.2 8.3 %collective-permute-done.17 = bf16[2,512,256]{2,1,0:T(8,128)(2,1)S(1)} collective-permute-done((bf16[2,512,256]{2,1,0:T(8,128)(2,1)S(1)}, bf16[2,512,256]{2,1,0:T(8,128)(2,1)S(1)}, u32[]{:S(2)}, u32[]{:S(2)}) %collective-permute-start.17) | collective-permute-done | bytes 524320 | tf_op jit(solution)/shard_map/ppermute | solution.py:15
  154.6 4.0 %collective-permute-done.16 = bf16[2,512,256]{2,1,0:T(8,128)(2,1)S(1)} collective-permute-done((bf16[2,512,256]{2,1,0:T(8,128)(2,1)S(1)}, bf16[2,512,256]{2,1,0:T(8,128)(2,1)S(1)}, u32[]{:S(2)}, u32[]{:S(2)}) %collective-permute-start.16) | collective-permute-done | bytes 524320 | tf_op jit(solution)/shard_map/ppermute | solution.py:15
  160.3 1.9 collective-permute-start.18
  162.2 3.6 %collective-permute-start.19 = (bf16[2,128,256]{2,1,0:T(8,128)(2,1)S(1)}, bf16[2,128,256]{2,1,0:T(8,128)(2,1)S(1)}, u32[]{:S(2)}, u32[]{:S(2)}) collective-permute-start(bf16[2,128,256]{2,1,0:T(8,128)(2,1)S(1)} %get-tuple-element.47), channel_id=1, source_target_pairs={{1,0},{2,1},{3,2},{4,3},{5,4},{6,5},{7,6},{8,7},{9,8},{10,9},{11,1... | collective-permute-start | bytes 393224 | tf_op jit(solution)/shard_map/ppermute | solution.py:15
  166.8 1.3 collective-permute-start.21
  169.4 1.5 collective-permute-start.20
  170.9 2.2 fusion.37
  173.4 7.0 %collective-permute-done.20 = bf16[2,256,256]{2,1,0:T(8,128)(2,1)S(1)} collective-permute-done((bf16[2,256,256]{2,1,0:T(8,128)(2,1)S(1)}, bf16[2,256,256]{2,1,0:T(8,128)(2,1)S(1)}, u32[]{:S(2)}, u32[]{:S(2)}) %collective-permute-start.20) | collective-permute-done | bytes 262176 | tf_op jit(solution)/shard_map/ppermute | solution.py:15
  181.9 4.7 %collective-permute-start.23 = (bf16[2,512,256]{2,1,0:T(8,128)(2,1)S(1)}, bf16[2,512,256]{2,1,0:T(8,128)(2,1)S(1)}, u32[]{:S(2)}, u32[]{:S(2)}) collective-permute-start(bf16[2,512,256]{2,1,0:T(8,128)(2,1)S(1)} %get-tuple-element.45), channel_id=1, source_target_pairs={{0,2},{1,3},{2,4},{3,5},{4,6},{5,7},{6,8},{7,9},{8,10},{9,11},{10,... | collective-permute-start | bytes 1572872 | tf_op jit(solution)/shard_map/ppermute | solution.py:15
  186.6 1.9 collective-permute-start.22
  189.2 2.2 bitcast_add_fusion
  191.4 7.0 %collective-permute-done.23 = bf16[2,512,256]{2,1,0:T(8,128)(2,1)S(1)} collective-permute-done((bf16[2,512,256]{2,1,0:T(8,128)(2,1)S(1)}, bf16[2,512,256]{2,1,0:T(8,128)(2,1)S(1)}, u32[]{:S(2)}, u32[]{:S(2)}) %collective-permute-start.23) | collective-permute-done | bytes 524320 | tf_op jit(solution)/shard_map/ppermute | solution.py:15
  198.3 4.6 %collective-permute-done.22 = bf16[2,512,256]{2,1,0:T(8,128)(2,1)S(1)} collective-permute-done((bf16[2,512,256]{2,1,0:T(8,128)(2,1)S(1)}, bf16[2,512,256]{2,1,0:T(8,128)(2,1)S(1)}, u32[]{:S(2)}, u32[]{:S(2)}) %collective-permute-start.22) | collective-permute-done | bytes 524320 | tf_op jit(solution)/shard_map/ppermute | solution.py:15
  203.2 1.3 multiply_convert_fusion.1
  207.3 3.9 %bitcast_add_fusion.3 = f32[768,512]{1,0:T(8,128)S(1)} fusion(f32[768,512,1]{1,0,2:T(8,128)} %fusion.37, f32[768,512,1]{1,0,2:T(8,128)} %fusion.41, f32[768,512,1]{1,0,2:T(8,128)} %fusion.45, bf16[2,512,256]{1,2,0:T(8,128)(2,1)} %get-tuple-element.61, bf16[2,512,256]{1,2,0:T(8,128)(2,1)} %get-tuple-element.60, bf16[2,128,256]{2,1,0:T(8,128)(2,1)S(1)} %copy-done.47, ...), kind=kOutput, calls=%fused_computation.12 | convolution fusion | flops 816447488 | bytes 8912896 | tf_op jit(solution)/shard_map/mpc,mpd->cd/dot_general | solution.py:62
  211.8 1.9 copy-done
  214.7 2.8 %collective-permute-done.26 = bf16[2,2,2,2,56,512]{5,4,3,2,1,0:T(8,128)(2,1)} collective-permute-done((bf16[2,2,2,2,56,512]{5,4,3,2,1,0:T(8,128)(2,1)}, bf16[2,2,2,2,56,512]{5,4,3,2,1,0:T(8,128)(2,1)}, u32[]{:S(2)}, u32[]{:S(2)}) %collective-permute-start.26) | collective-permute-done | bytes 917536 | tf_op jit(solution)/shard_map/ppermute | solution.py:121
  217.5 2.8 %fusion.1 = f32[2,2,2,2,56,512]{5,4,3,2,1,0:T(8,128)S(1)} fusion(bf16[2,2,2,2,56,512]{5,4,3,2,1,0:T(8,128)(2,1)} %collective-permute-done.26, f32[2,2,2,2,2,56,512]{6,5,4,3,2,1,0:T(8,128)} %copy-done, pred[]{:T(512)S(6)} %eq.23), kind=kLoop, calls=%fused_computation.5 | loop fusion | flops 1376256 | bytes 6422529 | tf_op jit(solution)/shard_map/add | solution.py:123
  221.6 2.0 collective-permute-start.24
  223.7 3.5 %collective-permute-start.25 = (bf16[2,128,256]{2,1,0:T(8,128)(2,1)S(1)}, bf16[2,128,256]{2,1,0:T(8,128)(2,1)S(1)}, u32[]{:S(2)}, u32[]{:S(2)}) collective-permute-start(bf16[2,128,256]{2,1,0:T(8,128)(2,1)S(1)} %get-tuple-element.43), channel_id=1, source_target_pairs={{1,0},{2,1},{3,2},{4,3},{5,4},{6,5},{7,6},{8,7},{9,8},{10,9},{11,1... | collective-permute-start | bytes 393224 | tf_op jit(solution)/shard_map/ppermute | solution.py:15
  227.2 6.7 %collective-permute-done.27 = bf16[2,2,2,56,512]{4,3,2,1,0:T(8,128)(2,1)S(1)} collective-permute-done((bf16[2,2,2,56,512]{4,3,2,1,0:T(8,128)(2,1)S(1)}, bf16[2,2,2,56,512]{4,3,2,1,0:T(8,128)(2,1)S(1)}, u32[]{:S(2)}, u32[]{:S(2)}) %collective-permute-start.27) | collective-permute-done | bytes 458784 | tf_op jit(solution)/shard_map/ppermute | solution.py:121
  234.2 1.6 collective-permute-start.28
  236.0 4.3 %collective-permute-done.28 = bf16[2,2,56,512]{3,2,1,0:T(8,128)(2,1)S(1)} collective-permute-done((bf16[2,2,56,512]{3,2,1,0:T(8,128)(2,1)S(1)}, bf16[2,2,56,512]{3,2,1,0:T(8,128)(2,1)S(1)}, u32[]{:S(2)}, u32[]{:S(2)}) %collective-permute-start.28) | collective-permute-done | bytes 229408 | tf_op jit(solution)/shard_map/ppermute | solution.py:121
  241.7 5.3 %collective-permute-done.29 = bf16[2,56,512]{2,1,0:T(8,128)(2,1)S(1)} collective-permute-done((bf16[2,56,512]{2,1,0:T(8,128)(2,1)S(1)}, bf16[2,56,512]{2,1,0:T(8,128)(2,1)S(1)}, u32[]{:S(2)}, u32[]{:S(2)}) %collective-permute-start.29) | collective-permute-done | bytes 114720 | tf_op jit(solution)/shard_map/ppermute | solution.py:121
  247.0 2.1 collective-permute-start.30
  250.4 2.4 collective-permute-done.30
  (186 shorter events, 34.6 us)
Async XLA Ops:
  0.6 8.3 %copy-start.7 = (bf16[1,2,512,256]{3,2,1,0:T(8,128)(2,1)S(1)}, bf16[1,2,512,256]{3,2,1,0:T(8,128)(2,1)}, u32[]{:S(2)}) copy-start(bf16[1,2,512,256]{3,2,1,0:T(8,128)(2,1)} %param.4) | copy-start | bytes 1572868
  1.7 7.3 %collective-permute-start = (bf16[2,128,256]{2,1,0:T(8,128)(2,1)S(1)}, bf16[2,128,256]{2,1,0:T(8,128)(2,1)S(1)}, u32[]{:S(2)}, u32[]{:S(2)}) collective-permute-start(bf16[2,128,256]{2,1,0:T(8,128)(2,1)S(1)} %get-tuple-element.75), channel_id=1, source_target_pairs={{0,1},{1,2},{2,3},{3,4},{4,5},{5,6},{6,7},{7,8},{8,9},{9,10},{10,1... | collective-permute-start | bytes 393224 | tf_op jit(solution)/shard_map/ppermute | solution.py:15
  3.6 7.2 %collective-permute-start.1 = (bf16[2,128,256]{2,1,0:T(8,128)(2,1)S(1)}, bf16[2,128,256]{2,1,0:T(8,128)(2,1)S(1)}, u32[]{:S(2)}, u32[]{:S(2)}) collective-permute-start(bf16[2,128,256]{2,1,0:T(8,128)(2,1)S(1)} %get-tuple-element.74), channel_id=1, source_target_pairs={{1,0},{2,1},{3,2},{4,3},{5,4},{6,5},{7,6},{8,7},{9,8},{10,9},{11,1... | collective-permute-start | bytes 393224 | tf_op jit(solution)/shard_map/ppermute | solution.py:15
  10.9 160.0 %copy-start.46 = (bf16[2,128,256]{2,1,0:T(8,128)(2,1)}, bf16[2,128,256]{2,1,0:T(8,128)(2,1)S(1)}, u32[]{:S(2)}) copy-start(bf16[2,128,256]{2,1,0:T(8,128)(2,1)S(1)} %collective-permute-done.1) | copy-start | bytes 393220
  12.7 8.2 %copy-start.19 = (bf16[2,512,256]{2,1,0:T(8,128)(2,1)}, bf16[2,512,256]{2,1,0:T(8,128)(2,1)S(1)}, u32[]{:S(2)}) copy-start(bf16[2,512,256]{2,1,0:T(8,128)(2,1)S(1)} %fusion.2) | copy-start | bytes 1572868
  12.7 16.4 %collective-permute-start.2 = (bf16[2,512,256]{2,1,0:T(8,128)(2,1)S(1)}, bf16[2,512,256]{2,1,0:T(8,128)(2,1)S(1)}, u32[]{:S(2)}, u32[]{:S(2)}) collective-permute-start(bf16[2,512,256]{2,1,0:T(8,128)(2,1)S(1)} %fusion.2), channel_id=1, source_target_pairs={{0,2},{1,3},{2,4},{3,5},{4,6},{5,7},{6,8},{7,9},{8,10},{9,11},{10,... | collective-permute-start | bytes 1572872 | tf_op jit(solution)/shard_map/ppermute | solution.py:15
  18.5 17.0 %collective-permute-start.3 = (bf16[2,512,256]{2,1,0:T(8,128)(2,1)S(1)}, bf16[2,512,256]{2,1,0:T(8,128)(2,1)S(1)}, u32[]{:S(2)}, u32[]{:S(2)}) collective-permute-start(bf16[2,512,256]{2,1,0:T(8,128)(2,1)S(1)} %fusion.2), channel_id=1, source_target_pairs={{2,0},{3,1},{4,2},{5,3},{6,4},{7,5},{8,6},{9,7},{10,8},{11,9},{12,... | collective-permute-start | bytes 1572872 | tf_op jit(solution)/shard_map/ppermute | solution.py:15
  29.9 6.4 %copy-start.14 = (bf16[2,512,256]{2,1,0:T(8,128)(2,1)S(1)}, bf16[2,512,256]{2,1,0:T(8,128)(2,1)}, u32[]{:S(2)}) copy-start(bf16[2,512,256]{2,1,0:T(8,128)(2,1)} %param.5) | copy-start | bytes 1572868
  39.6 14.0 %collective-permute-start.5 = (bf16[2,512,256]{2,1,0:T(8,128)(2,1)S(1)}, bf16[2,512,256]{2,1,0:T(8,128)(2,1)S(1)}, u32[]{:S(2)}, u32[]{:S(2)}) collective-permute-start(bf16[2,512,256]{2,1,0:T(8,128)(2,1)S(1)} %get-tuple-element.57), channel_id=1, source_target_pairs={{0,2},{1,3},{2,4},{3,5},{4,6},{5,7},{6,8},{7,9},{8,10},{9,11},{10,... | collective-permute-start | bytes 1572872 | tf_op jit(solution)/shard_map/ppermute | solution.py:15
  41.6 16.1 %collective-permute-start.4 = (bf16[2,512,256]{2,1,0:T(8,128)(2,1)S(1)}, bf16[2,512,256]{2,1,0:T(8,128)(2,1)S(1)}, u32[]{:S(2)}, u32[]{:S(2)}) collective-permute-start(bf16[2,512,256]{2,1,0:T(8,128)(2,1)S(1)} %get-tuple-element.56), channel_id=1, source_target_pairs={{2,0},{3,1},{4,2},{5,3},{6,4},{7,5},{8,6},{9,7},{10,8},{11,9},{12,... | collective-permute-start | bytes 1572872 | tf_op jit(solution)/shard_map/ppermute | solution.py:15
  57.9 19.0 %copy-start.1 = (f32[2,512,256]{2,1,0:T(8,128)}, f32[2,512,256]{2,1,0:T(8,128)S(1)}, u32[]{:S(2)}) copy-start(f32[2,512,256]{2,1,0:T(8,128)S(1)} %fusion.18) | copy-start | bytes 3145732
  64.9 6.6 %collective-permute-start.6 = (bf16[2,128,256]{2,1,0:T(8,128)(2,1)}, bf16[2,128,256]{2,1,0:T(8,128)(2,1)}, u32[]{:S(2)}, u32[]{:S(2)}) collective-permute-start(bf16[2,128,256]{2,1,0:T(8,128)(2,1)} %get-tuple-element.54), channel_id=1, source_target_pairs={{0,1},{1,2},{2,3},{3,4},{4,5},{5,6},{6,7},{7,8},{8,9},{9,10},{10,1... | collective-permute-start | bytes 393224 | tf_op jit(solution)/shard_map/ppermute | solution.py:15
  66.8 6.5 %collective-permute-start.7 = (bf16[2,128,256]{2,1,0:T(8,128)(2,1)}, bf16[2,128,256]{2,1,0:T(8,128)(2,1)}, u32[]{:S(2)}, u32[]{:S(2)}) collective-permute-start(bf16[2,128,256]{2,1,0:T(8,128)(2,1)} %get-tuple-element.55), channel_id=1, source_target_pairs={{1,0},{2,1},{3,2},{4,3},{5,4},{6,5},{7,6},{8,7},{9,8},{10,9},{11,1... | collective-permute-start | bytes 393224 | tf_op jit(solution)/shard_map/ppermute | solution.py:15
  73.3 7.3 %copy-start.20 = (bf16[2,512,256]{2,1,0:T(8,128)(2,1)S(1)}, bf16[2,512,256]{2,1,0:T(8,128)(2,1)}, u32[]{:S(2)}) copy-start(bf16[2,512,256]{2,1,0:T(8,128)(2,1)} %copy-done.19) | copy-start | bytes 1572868
  73.3 7.3 %copy-start.34 = (bf16[2,512,256]{2,1,0:T(8,128)(2,1)S(1)}, bf16[2,512,256]{2,1,0:T(8,128)(2,1)}, u32[]{:S(2)}) copy-start(bf16[2,512,256]{2,1,0:T(8,128)(2,1)} %copy-done.33) | copy-start | bytes 1572868
  73.3 7.3 %copy-start.41 = (bf16[2,512,256]{1,2,0:T(8,128)(2,1)S(1)}, bf16[2,512,256]{1,2,0:T(8,128)(2,1)}, u32[]{:S(2)}) copy-start(bf16[2,512,256]{1,2,0:T(8,128)(2,1)} %copy-done.40) | copy-start | bytes 1572868
  73.3 7.3 %copy-start.43 = (bf16[2,512,256]{1,2,0:T(8,128)(2,1)S(1)}, bf16[2,512,256]{1,2,0:T(8,128)(2,1)}, u32[]{:S(2)}) copy-start(bf16[2,512,256]{1,2,0:T(8,128)(2,1)} %copy-done.42) | copy-start | bytes 1572868
  73.3 7.3 %copy-start.45 = (bf16[2,512,256]{2,1,0:T(8,128)(2,1)S(1)}, bf16[2,512,256]{2,1,0:T(8,128)(2,1)}, u32[]{:S(2)}) copy-start(bf16[2,512,256]{2,1,0:T(8,128)(2,1)} %copy-done.44) | copy-start | bytes 1572868
  75.7 8.5 %collective-permute-start.8 = (bf16[2,256,256]{2,1,0:T(8,128)(2,1)S(1)}, bf16[2,256,256]{2,1,0:T(8,128)(2,1)S(1)}, u32[]{:S(2)}, u32[]{:S(2)}) collective-permute-start(bf16[2,256,256]{2,1,0:T(8,128)(2,1)S(1)} %pad_maximum_fusion.30), channel_id=1, source_target_pairs={{32,0},{64,32},{96,64},{33,1},{65,33},{97,65},{34,2},{66,34},{98,6... | collective-permute-start | bytes 786440 | tf_op jit(solution)/shard_map/ppermute | solution.py:15
  79.1 11.8 %copy-start.5 = (f32[2,512,256]{1,2,0:T(8,128)S(1)}, f32[2,512,256]{1,2,0:T(8,128)}, u32[]{:S(2)}) copy-start(f32[2,512,256]{1,2,0:T(8,128)} %get-tuple-element.8) | copy-start | bytes 3145732
  79.1 11.8 %copy-start.6 = (f32[2,512,256]{1,2,0:T(8,128)S(1)}, f32[2,512,256]{1,2,0:T(8,128)}, u32[]{:S(2)}) copy-start(f32[2,512,256]{1,2,0:T(8,128)} %get-tuple-element.40) | copy-start | bytes 3145732
  79.1 11.8 %collective-permute-start.9 = (bf16[2,256,256]{2,1,0:T(8,128)(2,1)S(1)}, bf16[2,256,256]{2,1,0:T(8,128)(2,1)S(1)}, u32[]{:S(2)}, u32[]{:S(2)}) collective-permute-start(bf16[2,256,256]{2,1,0:T(8,128)(2,1)S(1)} %get-tuple-element.33), channel_id=1, source_target_pairs={{32,0},{64,32},{96,64},{33,1},{65,33},{97,65},{34,2},{66,34},{98,6... | collective-permute-start | bytes 786440 | tf_op jit(solution)/shard_map/ppermute | solution.py:15
  91.3 9.0 %copy-start.35 = (bf16[2,512,256]{1,2,0:T(8,128)(2,1)S(1)}, bf16[2,512,256]{1,2,0:T(8,128)(2,1)}, u32[]{:S(2)}) copy-start(bf16[2,512,256]{1,2,0:T(8,128)(2,1)} %get-tuple-element.41) | copy-start | bytes 1572868
  92.3 8.0 %copy-start.15 = (bf16[2,512,256]{2,1,0:T(8,128)(2,1)S(1)}, bf16[2,512,256]{2,1,0:T(8,128)(2,1)}, u32[]{:S(2)}) copy-start(bf16[2,512,256]{2,1,0:T(8,128)(2,1)} %param.5) | copy-start | bytes 1572868
  92.3 8.3 %copy-start.8 = (bf16[1,2,512,256]{3,2,1,0:T(8,128)(2,1)S(1)}, bf16[1,2,512,256]{3,2,1,0:T(8,128)(2,1)}, u32[]{:S(2)}) copy-start(bf16[1,2,512,256]{3,2,1,0:T(8,128)(2,1)} %param.4) | copy-start | bytes 1572868
  92.4 8.3 %copy-start.23 = (bf16[2,384,256]{2,1,0:T(8,128)(2,1)S(1)}, bf16[2,384,256]{2,1,0:T(8,128)(2,1)}, u32[]{:S(2)}) copy-start(bf16[2,384,256]{2,1,0:T(8,128)(2,1)} %copy-done.22) | copy-start | bytes 1179652
  92.4 8.3 %copy-start.26 = (bf16[2,384,256]{2,1,0:T(8,128)(2,1)S(1)}, bf16[2,384,256]{2,1,0:T(8,128)(2,1)}, u32[]{:S(2)}) copy-start(bf16[2,384,256]{2,1,0:T(8,128)(2,1)} %copy-done.25) | copy-start | bytes 1179652
  92.4 8.3 %copy-start.37 = (bf16[2,512,256]{1,2,0:T(8,128)(2,1)S(1)}, bf16[2,512,256]{1,2,0:T(8,128)(2,1)}, u32[]{:S(2)}) copy-start(bf16[2,512,256]{1,2,0:T(8,128)(2,1)} %copy-done.36) | copy-start | bytes 1572868
  92.4 8.3 %copy-start.39 = (bf16[2,512,256]{1,2,0:T(8,128)(2,1)S(1)}, bf16[2,512,256]{1,2,0:T(8,128)(2,1)}, u32[]{:S(2)}) copy-start(bf16[2,512,256]{1,2,0:T(8,128)(2,1)} %copy-done.38) | copy-start | bytes 1572868
  92.4 8.3 %copy-start.49 = (bf16[2,128,256]{2,1,0:T(8,128)(2,1)S(1)}, bf16[2,128,256]{2,1,0:T(8,128)(2,1)}, u32[]{:S(2)}) copy-start(bf16[2,128,256]{2,1,0:T(8,128)(2,1)} %copy-done.48) | copy-start | bytes 393220
  92.5 16.5 %collective-permute-start.11 = (bf16[2,512,256]{2,1,0:T(8,128)(2,1)S(1)}, bf16[2,512,256]{2,1,0:T(8,128)(2,1)S(1)}, u32[]{:S(2)}, u32[]{:S(2)}) collective-permute-start(bf16[2,512,256]{2,1,0:T(8,128)(2,1)S(1)} %get-tuple-element.53), channel_id=1, source_target_pairs={{0,2},{1,3},{2,4},{3,5},{4,6},{5,7},{6,8},{7,9},{8,10},{9,11},{10,... | collective-permute-start | bytes 1572872 | tf_op jit(solution)/shard_map/ppermute | solution.py:15
  98.2 16.6 %collective-permute-start.10 = (bf16[2,512,256]{2,1,0:T(8,128)(2,1)S(1)}, bf16[2,512,256]{2,1,0:T(8,128)(2,1)S(1)}, u32[]{:S(2)}, u32[]{:S(2)}) collective-permute-start(bf16[2,512,256]{2,1,0:T(8,128)(2,1)S(1)} %get-tuple-element.52), channel_id=1, source_target_pairs={{2,0},{3,1},{4,2},{5,3},{6,4},{7,5},{8,6},{9,7},{10,8},{11,9},{12,... | collective-permute-start | bytes 1572872 | tf_op jit(solution)/shard_map/ppermute | solution.py:15
  103.9 11.1 %copy-start.3 = (f32[2,512,256]{1,2,0:T(8,128)S(1)}, f32[2,512,256]{1,2,0:T(8,128)}, u32[]{:S(2)}) copy-start(f32[2,512,256]{1,2,0:T(8,128)} %get-tuple-element.4) | copy-start | bytes 3145732
  103.9 11.1 %copy-start.4 = (f32[2,512,256]{1,2,0:T(8,128)S(1)}, f32[2,512,256]{1,2,0:T(8,128)}, u32[]{:S(2)}) copy-start(f32[2,512,256]{1,2,0:T(8,128)} %get-tuple-element.38) | copy-start | bytes 3145732
  116.4 7.8 %collective-permute-start.12 = (bf16[2,128,256]{2,1,0:T(8,128)(2,1)S(1)}, bf16[2,128,256]{2,1,0:T(8,128)(2,1)S(1)}, u32[]{:S(2)}, u32[]{:S(2)}) collective-permute-start(bf16[2,128,256]{2,1,0:T(8,128)(2,1)S(1)} %get-tuple-element.50), channel_id=1, source_target_pairs={{0,1},{1,2},{2,3},{3,4},{4,5},{5,6},{6,7},{7,8},{8,9},{9,10},{10,1... | collective-permute-start | bytes 393224 | tf_op jit(solution)/shard_map/ppermute | solution.py:15
  118.3 6.1 %collective-permute-start.13 = (bf16[2,128,256]{2,1,0:T(8,128)(2,1)S(1)}, bf16[2,128,256]{2,1,0:T(8,128)(2,1)S(1)}, u32[]{:S(2)}, u32[]{:S(2)}) collective-permute-start(bf16[2,128,256]{2,1,0:T(8,128)(2,1)S(1)} %get-tuple-element.51), channel_id=1, source_target_pairs={{1,0},{2,1},{3,2},{4,3},{5,4},{6,5},{7,6},{8,7},{9,8},{10,9},{11,1... | collective-permute-start | bytes 393224 | tf_op jit(solution)/shard_map/ppermute | solution.py:15
  122.9 14.4 %collective-permute-start.15 = (bf16[2,256,256]{2,1,0:T(8,128)(2,1)S(1)}, bf16[2,256,256]{2,1,0:T(8,128)(2,1)S(1)}, u32[]{:S(2)}, u32[]{:S(2)}) collective-permute-start(bf16[2,256,256]{2,1,0:T(8,128)(2,1)S(1)} %get-tuple-element.29), channel_id=1, source_target_pairs={{32,0},{64,32},{96,64},{33,1},{65,33},{97,65},{34,2},{66,34},{98,6... | collective-permute-start | bytes 786440 | tf_op jit(solution)/shard_map/ppermute | solution.py:15
  125.4 11.8 %collective-permute-start.14 = (bf16[2,256,256]{2,1,0:T(8,128)(2,1)S(1)}, bf16[2,256,256]{2,1,0:T(8,128)(2,1)S(1)}, u32[]{:S(2)}, u32[]{:S(2)}) collective-permute-start(bf16[2,256,256]{2,1,0:T(8,128)(2,1)S(1)} %pad_maximum_fusion.31), channel_id=1, source_target_pairs={{32,0},{64,32},{96,64},{33,1},{65,33},{97,65},{34,2},{66,34},{98,6... | collective-permute-start | bytes 786440 | tf_op jit(solution)/shard_map/ppermute | solution.py:15
  138.7 15.8 %collective-permute-start.17 = (bf16[2,512,256]{2,1,0:T(8,128)(2,1)S(1)}, bf16[2,512,256]{2,1,0:T(8,128)(2,1)S(1)}, u32[]{:S(2)}, u32[]{:S(2)}) collective-permute-start(bf16[2,512,256]{2,1,0:T(8,128)(2,1)S(1)} %get-tuple-element.49), channel_id=1, source_target_pairs={{0,2},{1,3},{2,4},{3,5},{4,6},{5,7},{6,8},{7,9},{8,10},{9,11},{10,... | collective-permute-start | bytes 1572872 | tf_op jit(solution)/shard_map/ppermute | solution.py:15
  141.9 16.7 %collective-permute-start.16 = (bf16[2,512,256]{2,1,0:T(8,128)(2,1)S(1)}, bf16[2,512,256]{2,1,0:T(8,128)(2,1)S(1)}, u32[]{:S(2)}, u32[]{:S(2)}) collective-permute-start(bf16[2,512,256]{2,1,0:T(8,128)(2,1)S(1)} %get-tuple-element.48), channel_id=1, source_target_pairs={{2,0},{3,1},{4,2},{5,3},{6,4},{7,5},{8,6},{9,7},{10,8},{11,9},{12,... | collective-permute-start | bytes 1572872 | tf_op jit(solution)/shard_map/ppermute | solution.py:15
  160.3 7.8 %collective-permute-start.18 = (bf16[2,128,256]{2,1,0:T(8,128)(2,1)S(1)}, bf16[2,128,256]{2,1,0:T(8,128)(2,1)S(1)}, u32[]{:S(2)}, u32[]{:S(2)}) collective-permute-start(bf16[2,128,256]{2,1,0:T(8,128)(2,1)S(1)} %get-tuple-element.46), channel_id=1, source_target_pairs={{0,1},{1,2},{2,3},{3,4},{4,5},{5,6},{6,7},{7,8},{8,9},{9,10},{10,1... | collective-permute-start | bytes 393224 | tf_op jit(solution)/shard_map/ppermute | solution.py:15
  162.2 6.1 %collective-permute-start.19 = (bf16[2,128,256]{2,1,0:T(8,128)(2,1)S(1)}, bf16[2,128,256]{2,1,0:T(8,128)(2,1)S(1)}, u32[]{:S(2)}, u32[]{:S(2)}) collective-permute-start(bf16[2,128,256]{2,1,0:T(8,128)(2,1)S(1)} %get-tuple-element.47), channel_id=1, source_target_pairs={{1,0},{2,1},{3,2},{4,3},{5,4},{6,5},{7,6},{8,7},{9,8},{10,9},{11,1... | collective-permute-start | bytes 393224 | tf_op jit(solution)/shard_map/ppermute | solution.py:15
  166.8 13.6 %collective-permute-start.21 = (bf16[2,256,256]{2,1,0:T(8,128)(2,1)S(1)}, bf16[2,256,256]{2,1,0:T(8,128)(2,1)S(1)}, u32[]{:S(2)}, u32[]{:S(2)}) collective-permute-start(bf16[2,256,256]{2,1,0:T(8,128)(2,1)S(1)} %get-tuple-element.25), channel_id=1, source_target_pairs={{32,0},{64,32},{96,64},{33,1},{65,33},{97,65},{34,2},{66,34},{98,6... | collective-permute-start | bytes 786440 | tf_op jit(solution)/shard_map/ppermute | solution.py:15
  169.4 11.0 %collective-permute-start.20 = (bf16[2,256,256]{2,1,0:T(8,128)(2,1)S(1)}, bf16[2,256,256]{2,1,0:T(8,128)(2,1)S(1)}, u32[]{:S(2)}, u32[]{:S(2)}) collective-permute-start(bf16[2,256,256]{2,1,0:T(8,128)(2,1)S(1)} %pad_maximum_fusion.32), channel_id=1, source_target_pairs={{32,0},{64,32},{96,64},{33,1},{65,33},{97,65},{34,2},{66,34},{98,6... | collective-permute-start | bytes 786440 | tf_op jit(solution)/shard_map/ppermute | solution.py:15
  181.9 16.5 %collective-permute-start.23 = (bf16[2,512,256]{2,1,0:T(8,128)(2,1)S(1)}, bf16[2,512,256]{2,1,0:T(8,128)(2,1)S(1)}, u32[]{:S(2)}, u32[]{:S(2)}) collective-permute-start(bf16[2,512,256]{2,1,0:T(8,128)(2,1)S(1)} %get-tuple-element.45), channel_id=1, source_target_pairs={{0,2},{1,3},{2,4},{3,5},{4,6},{5,7},{6,8},{7,9},{8,10},{9,11},{10,... | collective-permute-start | bytes 1572872 | tf_op jit(solution)/shard_map/ppermute | solution.py:15
  186.6 16.3 %collective-permute-start.22 = (bf16[2,512,256]{2,1,0:T(8,128)(2,1)S(1)}, bf16[2,512,256]{2,1,0:T(8,128)(2,1)S(1)}, u32[]{:S(2)}, u32[]{:S(2)}) collective-permute-start(bf16[2,512,256]{2,1,0:T(8,128)(2,1)S(1)} %get-tuple-element.44), channel_id=1, source_target_pairs={{2,0},{3,1},{4,2},{5,3},{6,4},{7,5},{8,6},{9,7},{10,8},{11,9},{12,... | collective-permute-start | bytes 1572872 | tf_op jit(solution)/shard_map/ppermute | solution.py:15
  214.7 2.8 %collective-permute-start.26 = (bf16[2,2,2,2,56,512]{5,4,3,2,1,0:T(8,128)(2,1)}, bf16[2,2,2,2,56,512]{5,4,3,2,1,0:T(8,128)(2,1)}, u32[]{:S(2)}, u32[]{:S(2)}) collective-permute-start(bf16[2,2,2,2,56,512]{5,4,3,2,1,0:T(8,128)(2,1)} %fusion.30), channel_id=1, source_target_pairs={{0,1},{1,0},{2,3},{3,2},{4,5},{5,4},{6,7},{7,6},{8,9},{9,8},{10,11... | collective-permute-start | bytes 2752520 | tf_op jit(solution)/shard_map/ppermute | solution.py:121
  214.7 5.8 %copy-start.12 = (bf16[2,512,256]{1,2,0:T(8,128)(2,1)S(1)}, bf16[2,512,256]{1,2,0:T(8,128)(2,1)}, u32[]{:S(2)}) copy-start(bf16[2,512,256]{1,2,0:T(8,128)(2,1)} %get-tuple-element.60) | copy-start | bytes 1572868
  214.7 5.9 %copy-start.13 = (bf16[2,512,256]{1,2,0:T(8,128)(2,1)S(1)}, bf16[2,512,256]{1,2,0:T(8,128)(2,1)}, u32[]{:S(2)}) copy-start(bf16[2,512,256]{1,2,0:T(8,128)(2,1)} %get-tuple-element.61) | copy-start | bytes 1572868
  220.5 13.5 %collective-permute-start.27 = (bf16[2,2,2,56,512]{4,3,2,1,0:T(8,128)(2,1)S(1)}, bf16[2,2,2,56,512]{4,3,2,1,0:T(8,128)(2,1)S(1)}, u32[]{:S(2)}, u32[]{:S(2)}) collective-permute-start(bf16[2,2,2,56,512]{4,3,2,1,0:T(8,128)(2,1)S(1)} %fusion.71), channel_id=1, source_target_pairs={{0,2},{1,3},{2,0},{3,1},{4,6},{5,7},{6,4},{7,5},{8,10},{9,11},{10,... | collective-permute-start | bytes 1376264 | tf_op jit(solution)/shard_map/ppermute | solution.py:121
  221.6 19.9 %collective-permute-start.24 = (bf16[2,128,256]{2,1,0:T(8,128)(2,1)S(1)}, bf16[2,128,256]{2,1,0:T(8,128)(2,1)S(1)}, u32[]{:S(2)}, u32[]{:S(2)}) collective-permute-start(bf16[2,128,256]{2,1,0:T(8,128)(2,1)S(1)} %get-tuple-element.42), channel_id=1, source_target_pairs={{0,1},{1,2},{2,3},{3,4},{4,5},{5,6},{6,7},{7,8},{8,9},{9,10},{10,1... | collective-permute-start | bytes 393224 | tf_op jit(solution)/shard_map/ppermute | solution.py:15
  223.7 17.8 %collective-permute-start.25 = (bf16[2,128,256]{2,1,0:T(8,128)(2,1)S(1)}, bf16[2,128,256]{2,1,0:T(8,128)(2,1)S(1)}, u32[]{:S(2)}, u32[]{:S(2)}) collective-permute-start(bf16[2,128,256]{2,1,0:T(8,128)(2,1)S(1)} %get-tuple-element.43), channel_id=1, source_target_pairs={{1,0},{2,1},{3,2},{4,3},{5,4},{6,5},{7,6},{8,7},{9,8},{10,9},{11,1... | collective-permute-start | bytes 393224 | tf_op jit(solution)/shard_map/ppermute | solution.py:15
  234.2 6.1 %collective-permute-start.28 = (bf16[2,2,56,512]{3,2,1,0:T(8,128)(2,1)S(1)}, bf16[2,2,56,512]{3,2,1,0:T(8,128)(2,1)S(1)}, u32[]{:S(2)}, u32[]{:S(2)}) collective-permute-start(bf16[2,2,56,512]{3,2,1,0:T(8,128)(2,1)S(1)} %fusion.122), channel_id=1, source_target_pairs={{0,8},{1,9},{2,10},{3,11},{4,12},{5,13},{6,14},{7,15},{8,0},{9,1},... | collective-permute-start | bytes 688136 | tf_op jit(solution)/shard_map/ppermute | solution.py:121
  240.4 8.7 %copy-start.16 = (f32[1,2,256,256]{3,2,1,0:T(8,128)S(1)}, f32[1,2,256,256]{3,2,1,0:T(8,128)}, u32[]{:S(2)}) copy-start(f32[1,2,256,256]{3,2,1,0:T(8,128)} %get-tuple-element.34) | copy-start | bytes 1572868
  240.4 8.7 %copy-start.17 = (f32[1,2,256,256]{3,2,1,0:T(8,128)S(1)}, f32[1,2,256,256]{3,2,1,0:T(8,128)}, u32[]{:S(2)}) copy-start(f32[1,2,256,256]{3,2,1,0:T(8,128)} %get-tuple-element.30) | copy-start | bytes 1572868
  240.5 8.6 %copy-start.18 = (f32[1,2,256,256]{3,2,1,0:T(8,128)S(1)}, f32[1,2,256,256]{3,2,1,0:T(8,128)}, u32[]{:S(2)}) copy-start(f32[1,2,256,256]{3,2,1,0:T(8,128)} %get-tuple-element.26) | copy-start | bytes 1572868
  240.5 8.6 %copy-start.27 = (f32[1,2,128,256]{3,2,1,0:T(8,128)S(1)}, f32[1,2,128,256]{3,2,1,0:T(8,128)}, u32[]{:S(2)}) copy-start(f32[1,2,128,256]{3,2,1,0:T(8,128)} %get-tuple-element.20) | copy-start | bytes 786436
  240.5 8.6 %copy-start.28 = (f32[1,2,128,256]{3,2,1,0:T(8,128)S(1)}, f32[1,2,128,256]{3,2,1,0:T(8,128)}, u32[]{:S(2)}) copy-start(f32[1,2,128,256]{3,2,1,0:T(8,128)} %get-tuple-element.35) | copy-start | bytes 786436
  240.5 8.6 %copy-start.29 = (f32[1,2,128,256]{3,2,1,0:T(8,128)S(1)}, f32[1,2,128,256]{3,2,1,0:T(8,128)}, u32[]{:S(2)}) copy-start(f32[1,2,128,256]{3,2,1,0:T(8,128)} %get-tuple-element.16) | copy-start | bytes 786436
  240.5 8.6 %copy-start.30 = (f32[1,2,128,256]{3,2,1,0:T(8,128)S(1)}, f32[1,2,128,256]{3,2,1,0:T(8,128)}, u32[]{:S(2)}) copy-start(f32[1,2,128,256]{3,2,1,0:T(8,128)} %get-tuple-element.31) | copy-start | bytes 786436
  240.5 8.6 %copy-start.31 = (f32[1,2,128,256]{3,2,1,0:T(8,128)S(1)}, f32[1,2,128,256]{3,2,1,0:T(8,128)}, u32[]{:S(2)}) copy-start(f32[1,2,128,256]{3,2,1,0:T(8,128)} %get-tuple-element.12) | copy-start | bytes 786436
  240.5 8.6 %copy-start.32 = (f32[1,2,128,256]{3,2,1,0:T(8,128)S(1)}, f32[1,2,128,256]{3,2,1,0:T(8,128)}, u32[]{:S(2)}) copy-start(f32[1,2,128,256]{3,2,1,0:T(8,128)} %get-tuple-element.27) | copy-start | bytes 786436
  240.6 6.4 %collective-permute-start.29 = (bf16[2,56,512]{2,1,0:T(8,128)(2,1)S(1)}, bf16[2,56,512]{2,1,0:T(8,128)(2,1)S(1)}, u32[]{:S(2)}, u32[]{:S(2)}) collective-permute-start(bf16[2,56,512]{2,1,0:T(8,128)(2,1)S(1)} %fusion.137), channel_id=1, source_target_pairs={{0,4},{1,5},{2,6},{3,7},{4,0},{5,1},{6,2},{7,3},{8,12},{9,13},{10,... | collective-permute-start | bytes 344072 | tf_op jit(solution)/shard_map/ppermute | solution.py:121
  247.0 5.8 %collective-permute-start.30 = (bf16[56,512]{1,0:T(8,128)(2,1)S(1)}, bf16[56,512]{1,0:T(8,128)(2,1)S(1)}, u32[]{:S(2)}, u32[]{:S(2)}) collective-permute-start(bf16[56,512]{1,0:T(8,128)(2,1)S(1)} %fusion.147), channel_id=1, source_target_pairs={{0,16},{1,17},{2,18},{3,19},{4,20},{5,21},{6,22},{7,23},{8,24},{9,... | collective-permute-start | bytes 172040 | tf_op jit(solution)/shard_map/ppermute | solution.py:121
  (18 other events, 36.2 us)

commit v4 on v3

--- a/solution.py
+++ b/solution.py
@@ -54,24 +54,22 @@
     taps, gated, factor_a, factor_b = saved
     chans = flowing.shape[2]
     grad_half = flowing.astype(jnp.bfloat16)
-    out_term = jnp.einsum("mpc,mpd->cd", gated, grad_half, preferred_element_type=jnp.float32)
     grad_gated = jnp.einsum("mpd,cd->mpc", grad_half, out_mat, preferred_element_type=jnp.float32)
     grad_pre = jnp.concatenate([grad_gated * factor_a, grad_gated * factor_b], axis=2).astype(
         jnp.bfloat16
     )
-    conv_term = jnp.einsum("mpc,mpd->cd", taps, grad_pre, preferred_element_type=jnp.float32)
     weights = conv.reshape(3 * chans, 2 * chans)
     back = jnp.einsum("mpd,cd->mpc", grad_pre, weights, preferred_element_type=jnp.float32)
     grad_first = back[..., :chans].astype(jnp.bfloat16)
     middle = back[..., chans : 2 * chans]
     grad_third = back[..., 2 * chans :].astype(jnp.bfloat16)
     if layer == 0:
-        return split_near(flowing, middle, grad_first, grad_third, NEAR), conv_term, out_term
+        return split_near(flowing, middle, grad_first, grad_third, NEAR), grad_pre, grad_half
     else:
         third_earlier = shifted(grad_third, "seq", far_hops)
         first_following = shifted(grad_first, "seq", -far_hops)
     grad_conv = middle + first_following.astype(jnp.float32) + third_earlier.astype(jnp.float32)
-    return flowing + grad_conv, conv_term, out_term
+    return flowing + grad_conv, grad_pre, grad_half
 
 
 def split_near(flowing, middle, grad_first, grad_third, width):
@@ -157,11 +155,11 @@
     out_acc = [None] * depth
     for step in range(section_count):
         for layer in reversed(range(depth)):
-            flowing, conv_term, out_term = backward_layer(
+            flowing, grad_pre, grad_half = backward_layer(
                 flowing, stored[layer], conv_mat[layer], out_mat[layer], layer, far_hops
             )
-            conv_acc[layer] = conv_term if step == 0 else conv_acc[layer] + conv_term
-            out_acc[layer] = out_term if step == 0 else out_acc[layer] + out_term
+            conv_acc[layer] = grad_pre if step == 0 else conv_acc[layer] + grad_pre
+            out_acc[layer] = grad_half if step == 0 else out_acc[layer] + grad_half
         low, inner, high = flowing
         flowing = jnp.concatenate([low, inner, high], axis=1)
         input_grads = flowing if step == 0 else input_grads + flowing
@@ -174,6 +172,11 @@
                 [edges[:, :width], inner, edges[:, width:]], axis=1
             ).astype(jnp.float32)
 
+    f32 = jnp.float32
+    for layer in range(depth):
+        taps, gated = stored[layer][0], stored[layer][1]
+        conv_acc[layer] = jnp.einsum("mpc,mpd->cd", taps, conv_acc[layer], preferred_element_type=f32)
+        out_acc[layer] = jnp.einsum("mpc,mpd->cd", gated, out_acc[layer], preferred_element_type=f32)
     conv_rows = 3 * channels // seq_count
     out_rows = channels // seq_count
     conv_all = jnp.concatenate(

time: 255 us -> 260 us (1.020)
  waiting for transfers between devices: 110 us -> 126 us
  matrix products: 41.6 us -> 29.8 us
    ppermute x26, waiting for transfers between devices: 88.7 us -> 105 us  [shifted(): lax.ppermute(value, axis, [(source, source + steps) for source in range(l...]
    dot_general x16 -> x4, matrix products: 18.2 us -> 7.6 us  [the longest x2 5.48 us: shards(): jnp.einsum('mpc,mpd->cd', taps, conv_acc[layer], preferred_element_type=f32)]
  transfers between devices with their start and end apart: 31 -> 31, of which waited for: 23 -> 27; matrix products, arithmetic and copies ran while one was open for 11% -> 6% of each run, Pallas kernels for 0% -> 0%
where the time goes in v4:
time: 260 us; the launch traced here: 259 us
  waiting for transfers between devices  126 us (48%)
  starting transfers between devices  74.5 us (29%)
  matrix products  29.8 us (11%)
  other arithmetic  16.6 us (6%)
  local copies, waits for them, and re-layouts  9.41 us (4%)
    ppermute x26, waiting for transfers between devices, shifted(): lax.ppermute(value, axis, [(source, source + steps) for source in range(l...  105 us
    ppermute x26, starting transfers between devices, shifted(): lax.ppermute(value, axis, [(source, source + steps) for source in range(l...  69.6 us
    ppermute x5, waiting for transfers between devices, halving_scatter(): got = lax.ppermute(sends, 'seq', pairs)  21.3 us
    dot_general x8, matrix products, backward_layer(): jnp.einsum('mpd,cd->mpc', grad_pre, weights, preferred_element_type=jnp.f...  8.23 us
    dot_general x7, matrix products, mm(): return jnp.einsum('mpc,cd->mpd', a, b, preferred_element_type=jnp.float32)  8 us
    dot_general x8, matrix products, backward_layer(): jnp.einsum('mpd,cd->mpc', grad_half, out_mat, preferred_element_type=jnp....  6.01 us
    dot_general x2, matrix products, shards(): jnp.einsum('mpc,mpd->cd', taps, conv_acc[layer], preferred_element_type=f32)  5.48 us
  transfers between devices with their start and end apart: 31, of which 27 were waited for; matrix products, arithmetic and copies ran while one was open for 6% of the time, Pallas kernels for 0%

profile of v4, /device:TPU:24, one launch (start us, length us, event | category | flops | bytes accessed | tf_op | source)
XLA Modules:
  0.0 258.6 jit_solution(3485239785710349373)
XLA Ops:
  1.7 1.9 collective-permute-start
  3.6 3.6 %collective-permute-start.1 = (bf16[2,128,256]{2,1,0:T(8,128)(2,1)S(1)}, bf16[2,128,256]{2,1,0:T(8,128)(2,1)S(1)}, u32[]{:S(2)}, u32[]{:S(2)}) collective-permute-start(bf16[2,128,256]{2,1,0:T(8,128)(2,1)S(1)} %get-tuple-element.73), channel_id=1, source_target_pairs={{1,0},{2,1},{3,2},{4,3},{5,4},{6,5},{7,6},{8,7},{9,8},{10,9},{11,1... | collective-permute-start | bytes 393224 | tf_op jit(solution)/shard_map/ppermute | solution.py:15
  7.3 2.9 %fusion.116 = f32[2,512,512]{1,2,0:T(8,128)} fusion(bf16[1,2,3,256,512]{4,3,2,1,0:T(8,128)(2,1)} %param.6, bf16[1,2,512,256]{3,2,1,0:T(8,128)(2,1)} %param.4), kind=kOutput, calls=%fused_computation.178 | convolution fusion | flops 268435456 | bytes 2883584 | tf_op jit(solution)/shard_map/mpc,cd->mpd/dot_general | solution.py:32
  10.3 1.8 fusion.67
  12.2 1.5 add_add_fusion.1
  15.0 5.6 %collective-permute-start.2 = (bf16[2,512,256]{2,1,0:T(8,128)(2,1)S(1)}, bf16[2,512,256]{2,1,0:T(8,128)(2,1)S(1)}, u32[]{:S(2)}, u32[]{:S(2)}) collective-permute-start(bf16[2,512,256]{2,1,0:T(8,128)(2,1)S(1)} %fusion.18), channel_id=1, source_target_pairs={{0,2},{1,3},{2,4},{3,5},{4,6},{5,7},{6,8},{7,9},{8,10},{9,11},{10,... | collective-permute-start | bytes 1572872 | tf_op jit(solution)/shard_map/ppermute | solution.py:15
  20.8 1.9 collective-permute-start.3
  23.2 8.0 %collective-permute-done.2 = bf16[2,512,256]{2,1,0:T(8,128)(2,1)S(1)} collective-permute-done((bf16[2,512,256]{2,1,0:T(8,128)(2,1)S(1)}, bf16[2,512,256]{2,1,0:T(8,128)(2,1)S(1)}, u32[]{:S(2)}, u32[]{:S(2)}) %collective-permute-start.2) | collective-permute-done | bytes 524320 | tf_op jit(solution)/shard_map/ppermute | solution.py:15
  31.9 4.5 %collective-permute-done.3 = bf16[2,512,256]{2,1,0:T(8,128)(2,1)S(1)} collective-permute-done((bf16[2,512,256]{2,1,0:T(8,128)(2,1)S(1)}, bf16[2,512,256]{2,1,0:T(8,128)(2,1)S(1)}, u32[]{:S(2)}, u32[]{:S(2)}) %collective-permute-start.3) | collective-permute-done | bytes 524320 | tf_op jit(solution)/shard_map/ppermute | solution.py:15
  39.8 1.9 collective-permute-start.5
  41.7 3.9 %collective-permute-start.4 = (bf16[2,512,256]{2,1,0:T(8,128)(2,1)S(1)}, bf16[2,512,256]{2,1,0:T(8,128)(2,1)S(1)}, u32[]{:S(2)}, u32[]{:S(2)}) collective-permute-start(bf16[2,512,256]{2,1,0:T(8,128)(2,1)S(1)} %get-tuple-element.55), channel_id=1, source_target_pairs={{2,0},{3,1},{4,2},{5,3},{6,4},{7,5},{8,6},{9,7},{10,8},{11,9},{12,... | collective-permute-start | bytes 1572872 | tf_op jit(solution)/shard_map/ppermute | solution.py:15
  45.6 6.9 %collective-permute-done.5 = bf16[2,512,256]{2,1,0:T(8,128)(2,1)S(1)} collective-permute-done((bf16[2,512,256]{2,1,0:T(8,128)(2,1)S(1)}, bf16[2,512,256]{2,1,0:T(8,128)(2,1)S(1)}, u32[]{:S(2)}, u32[]{:S(2)}) %collective-permute-start.5) | collective-permute-done | bytes 524320 | tf_op jit(solution)/shard_map/ppermute | solution.py:15
  52.5 4.7 %collective-permute-done.4 = bf16[2,512,256]{2,1,0:T(8,128)(2,1)S(1)} collective-permute-done((bf16[2,512,256]{2,1,0:T(8,128)(2,1)S(1)}, bf16[2,512,256]{2,1,0:T(8,128)(2,1)S(1)}, u32[]{:S(2)}, u32[]{:S(2)}) %collective-permute-start.4) | collective-permute-done | bytes 524320 | tf_op jit(solution)/shard_map/ppermute | solution.py:15
  59.3 1.9 collective-permute-start.6
  61.2 3.6 %collective-permute-start.7 = (bf16[2,128,256]{2,1,0:T(8,128)(2,1)S(1)}, bf16[2,128,256]{2,1,0:T(8,128)(2,1)S(1)}, u32[]{:S(2)}, u32[]{:S(2)}) collective-permute-start(bf16[2,128,256]{2,1,0:T(8,128)(2,1)S(1)} %get-tuple-element.54), channel_id=1, source_target_pairs={{1,0},{2,1},{3,2},{4,3},{5,4},{6,5},{7,6},{8,7},{9,8},{10,9},{11,1... | collective-permute-start | bytes 393224 | tf_op jit(solution)/shard_map/ppermute | solution.py:15
  65.6 1.8 collective-permute-done.7
  68.3 1.3 collective-permute-start.8
  70.6 1.3 collective-permute-start.9
  71.8 4.7 %collective-permute-done.8 = bf16[2,256,256]{2,1,0:T(8,128)(2,1)S(1)} collective-permute-done((bf16[2,256,256]{2,1,0:T(8,128)(2,1)S(1)}, bf16[2,256,256]{2,1,0:T(8,128)(2,1)S(1)}, u32[]{:S(2)}, u32[]{:S(2)}) %collective-permute-start.8) | collective-permute-done | bytes 262176 | tf_op jit(solution)/shard_map/ppermute | solution.py:15
  76.6 5.4 %collective-permute-done.9 = bf16[2,256,256]{2,1,0:T(8,128)(2,1)S(1)} collective-permute-done((bf16[2,256,256]{2,1,0:T(8,128)(2,1)S(1)}, bf16[2,256,256]{2,1,0:T(8,128)(2,1)S(1)}, u32[]{:S(2)}, u32[]{:S(2)}) %collective-permute-start.9) | collective-permute-done | bytes 262176 | tf_op jit(solution)/shard_map/ppermute | solution.py:15
  83.5 6.5 %collective-permute-start.11 = (bf16[2,512,256]{2,1,0:T(8,128)(2,1)S(1)}, bf16[2,512,256]{2,1,0:T(8,128)(2,1)S(1)}, u32[]{:S(2)}, u32[]{:S(2)}) collective-permute-start(bf16[2,512,256]{2,1,0:T(8,128)(2,1)S(1)} %get-tuple-element.52), channel_id=1, source_target_pairs={{0,2},{1,3},{2,4},{3,5},{4,6},{5,7},{6,8},{7,9},{8,10},{9,11},{10,... | collective-permute-start | bytes 1572872 | tf_op jit(solution)/shard_map/ppermute | solution.py:15
  89.9 1.9 collective-permute-start.10
  91.9 8.0 %collective-permute-done.11 = bf16[2,512,256]{2,1,0:T(8,128)(2,1)S(1)} collective-permute-done((bf16[2,512,256]{2,1,0:T(8,128)(2,1)S(1)}, bf16[2,512,256]{2,1,0:T(8,128)(2,1)S(1)}, u32[]{:S(2)}, u32[]{:S(2)}) %collective-permute-start.11) | collective-permute-done | bytes 524320 | tf_op jit(solution)/shard_map/ppermute | solution.py:15
  99.9 6.2 %collective-permute-done.10 = bf16[2,512,256]{2,1,0:T(8,128)(2,1)S(1)} collective-permute-done((bf16[2,512,256]{2,1,0:T(8,128)(2,1)S(1)}, bf16[2,512,256]{2,1,0:T(8,128)(2,1)S(1)}, u32[]{:S(2)}, u32[]{:S(2)}) %collective-permute-start.10) | collective-permute-done | bytes 524320 | tf_op jit(solution)/shard_map/ppermute | solution.py:15
  107.9 2.1 collective-permute-start.12
  110.0 3.6 %collective-permute-start.13 = (bf16[2,128,256]{2,1,0:T(8,128)(2,1)S(1)}, bf16[2,128,256]{2,1,0:T(8,128)(2,1)S(1)}, u32[]{:S(2)}, u32[]{:S(2)}) collective-permute-start(bf16[2,128,256]{2,1,0:T(8,128)(2,1)S(1)} %get-tuple-element.50), channel_id=1, source_target_pairs={{1,0},{2,1},{3,2},{4,3},{5,4},{6,5},{7,6},{8,7},{9,8},{10,9},{11,1... | collective-permute-start | bytes 393224 | tf_op jit(solution)/shard_map/ppermute | solution.py:15
  114.3 1.8 collective-permute-done.13
  117.1 1.3 collective-permute-start.14
  119.3 1.3 collective-permute-start.15
  120.6 6.2 %collective-permute-done.14 = bf16[2,256,256]{2,1,0:T(8,128)(2,1)S(1)} collective-permute-done((bf16[2,256,256]{2,1,0:T(8,128)(2,1)S(1)}, bf16[2,256,256]{2,1,0:T(8,128)(2,1)S(1)}, u32[]{:S(2)}, u32[]{:S(2)}) %collective-permute-start.14) | collective-permute-done | bytes 262176 | tf_op jit(solution)/shard_map/ppermute | solution.py:15
  126.8 5.6 %collective-permute-done.15 = bf16[2,256,256]{2,1,0:T(8,128)(2,1)S(1)} collective-permute-done((bf16[2,256,256]{2,1,0:T(8,128)(2,1)S(1)}, bf16[2,256,256]{2,1,0:T(8,128)(2,1)S(1)}, u32[]{:S(2)}, u32[]{:S(2)}) %collective-permute-start.15) | collective-permute-done | bytes 262176 | tf_op jit(solution)/shard_map/ppermute | solution.py:15
  133.9 3.7 %collective-permute-start.17 = (bf16[2,512,256]{2,1,0:T(8,128)(2,1)S(1)}, bf16[2,512,256]{2,1,0:T(8,128)(2,1)S(1)}, u32[]{:S(2)}, u32[]{:S(2)}) collective-permute-start(bf16[2,512,256]{2,1,0:T(8,128)(2,1)S(1)} %get-tuple-element.48), channel_id=1, source_target_pairs={{0,2},{1,3},{2,4},{3,5},{4,6},{5,7},{6,8},{7,9},{8,10},{9,11},{10,... | collective-permute-start | bytes 1572872 | tf_op jit(solution)/shard_map/ppermute | solution.py:15
  137.5 2.2 collective-permute-start.16
  139.7 10.6 %collective-permute-done.17 = bf16[2,512,256]{2,1,0:T(8,128)(2,1)S(1)} collective-permute-done((bf16[2,512,256]{2,1,0:T(8,128)(2,1)S(1)}, bf16[2,512,256]{2,1,0:T(8,128)(2,1)S(1)}, u32[]{:S(2)}, u32[]{:S(2)}) %collective-permute-start.17) | collective-permute-done | bytes 524320 | tf_op jit(solution)/shard_map/ppermute | solution.py:15
  150.3 4.5 %collective-permute-done.16 = bf16[2,512,256]{2,1,0:T(8,128)(2,1)S(1)} collective-permute-done((bf16[2,512,256]{2,1,0:T(8,128)(2,1)S(1)}, bf16[2,512,256]{2,1,0:T(8,128)(2,1)S(1)}, u32[]{:S(2)}, u32[]{:S(2)}) %collective-permute-start.16) | collective-permute-done | bytes 524320 | tf_op jit(solution)/shard_map/ppermute | solution.py:15
  156.5 1.9 collective-permute-start.18
  158.5 3.6 %collective-permute-start.19 = (bf16[2,128,256]{2,1,0:T(8,128)(2,1)S(1)}, bf16[2,128,256]{2,1,0:T(8,128)(2,1)S(1)}, u32[]{:S(2)}, u32[]{:S(2)}) collective-permute-start(bf16[2,128,256]{2,1,0:T(8,128)(2,1)S(1)} %get-tuple-element.46), channel_id=1, source_target_pairs={{1,0},{2,1},{3,2},{4,3},{5,4},{6,5},{7,6},{8,7},{9,8},{10,9},{11,1... | collective-permute-start | bytes 393224 | tf_op jit(solution)/shard_map/ppermute | solution.py:15
  162.8 1.8 collective-permute-done.19
  166.3 1.3 collective-permute-start.20
  168.6 1.3 collective-permute-start.21
  169.9 6.8 %collective-permute-done.20 = bf16[2,256,256]{2,1,0:T(8,128)(2,1)} collective-permute-done((bf16[2,256,256]{2,1,0:T(8,128)(2,1)}, bf16[2,256,256]{2,1,0:T(8,128)(2,1)}, u32[]{:S(2)}, u32[]{:S(2)}) %collective-permute-start.20) | collective-permute-done | bytes 262176 | tf_op jit(solution)/shard_map/ppermute | solution.py:15
  177.7 4.6 %collective-permute-done.21 = bf16[2,256,256]{2,1,0:T(8,128)(2,1)} collective-permute-done((bf16[2,256,256]{2,1,0:T(8,128)(2,1)}, bf16[2,256,256]{2,1,0:T(8,128)(2,1)}, u32[]{:S(2)}, u32[]{:S(2)}) %collective-permute-start.21) | collective-permute-done | bytes 262176 | tf_op jit(solution)/shard_map/ppermute | solution.py:15
  182.3 2.0 multiply_convert_fusion.3
  185.5 3.1 %collective-permute-start.23 = (bf16[2,512,256]{2,1,0:T(8,128)(2,1)S(1)}, bf16[2,512,256]{2,1,0:T(8,128)(2,1)S(1)}, u32[]{:S(2)}, u32[]{:S(2)}) collective-permute-start(bf16[2,512,256]{2,1,0:T(8,128)(2,1)S(1)} %get-tuple-element.44), channel_id=1, source_target_pairs={{0,2},{1,3},{2,4},{3,5},{4,6},{5,7},{6,8},{7,9},{8,10},{9,11},{10,... | collective-permute-start | bytes 1572872 | tf_op jit(solution)/shard_map/ppermute | solution.py:15
  188.7 3.1 %collective-permute-start.22 = (bf16[2,512,256]{2,1,0:T(8,128)(2,1)S(1)}, bf16[2,512,256]{2,1,0:T(8,128)(2,1)S(1)}, u32[]{:S(2)}, u32[]{:S(2)}) collective-permute-start(bf16[2,512,256]{2,1,0:T(8,128)(2,1)S(1)} %get-tuple-element.43), channel_id=1, source_target_pairs={{2,0},{3,1},{4,2},{5,3},{6,4},{7,5},{8,6},{9,7},{10,8},{11,9},{12,... | collective-permute-start | bytes 1572872 | tf_op jit(solution)/shard_map/ppermute | solution.py:15
  192.0 2.3 fusion.12
  194.3 1.7 convolution_bitcast_fusion
  196.0 6.1 %collective-permute-done.23 = bf16[2,512,256]{2,1,0:T(8,128)(2,1)S(1)} collective-permute-done((bf16[2,512,256]{2,1,0:T(8,128)(2,1)S(1)}, bf16[2,512,256]{2,1,0:T(8,128)(2,1)S(1)}, u32[]{:S(2)}, u32[]{:S(2)}) %collective-permute-start.23) | collective-permute-done | bytes 524320 | tf_op jit(solution)/shard_map/ppermute | solution.py:15
  202.2 4.4 %collective-permute-done.22 = bf16[2,512,256]{2,1,0:T(8,128)(2,1)S(1)} collective-permute-done((bf16[2,512,256]{2,1,0:T(8,128)(2,1)S(1)}, bf16[2,512,256]{2,1,0:T(8,128)(2,1)S(1)}, u32[]{:S(2)}, u32[]{:S(2)}) %collective-permute-start.22) | collective-permute-done | bytes 524320 | tf_op jit(solution)/shard_map/ppermute | solution.py:15
  207.8 1.3 multiply_convert_fusion.1
  211.5 1.2 concatenate.179
  212.8 3.2 %fusion.2 = f32[768,512,1]{1,0,2:T(8,128)S(1)} fusion(bf16[2,128,256]{2,1,0:T(8,128)(2,1)S(1)} %copy-done.75, bf16[2,384,256]{2,1,0:T(8,128)(2,1)} %copy-done.44, bf16[2,512,256]{2,1,0:T(8,128)(2,1)S(1)} %bitcast.243, bf16[2,384,256]{2,1,0:T(8,128)(2,1)} %copy-done.45, bf16[2,128,256]{2,1,0:T(8,128)(2,1)} %copy-done.76, ...), kind=kOutput, calls=%fused_computation.7 | convolution fusion | flops 821559296 | bytes 7340032 | tf_op jit(solution)/shard_map/mpc,mpd->cd/dot_general | solution.py:178
  216.5 1.9 copy-done
  219.5 2.7 %collective-permute-done.26 = bf16[2,2,2,2,56,512]{5,4,3,2,1,0:T(8,128)(2,1)S(1)} collective-permute-done((bf16[2,2,2,2,56,512]{5,4,3,2,1,0:T(8,128)(2,1)}, bf16[2,2,2,2,56,512]{5,4,3,2,1,0:T(8,128)(2,1)S(1)}, u32[]{:S(2)}, u32[]{:S(2)}) %collective-permute-start.26) | collective-permute-done | bytes 917536 | tf_op jit(solution)/shard_map/ppermute | solution.py:119
  222.2 2.6 fusion.1
  226.2 2.2 collective-permute-start.24
  228.4 3.5 %collective-permute-start.25 = (bf16[2,128,256]{2,1,0:T(8,128)(2,1)S(1)}, bf16[2,128,256]{2,1,0:T(8,128)(2,1)S(1)}, u32[]{:S(2)}, u32[]{:S(2)}) collective-permute-start(bf16[2,128,256]{2,1,0:T(8,128)(2,1)S(1)} %get-tuple-element.42), channel_id=1, source_target_pairs={{1,0},{2,1},{3,2},{4,3},{5,4},{6,5},{7,6},{8,7},{9,8},{10,9},{11,1... | collective-permute-start | bytes 393224 | tf_op jit(solution)/shard_map/ppermute | solution.py:15
  231.9 6.6 %collective-permute-done.27 = bf16[2,2,2,56,512]{4,3,2,1,0:T(8,128)(2,1)S(1)} collective-permute-done((bf16[2,2,2,56,512]{4,3,2,1,0:T(8,128)(2,1)S(1)}, bf16[2,2,2,56,512]{4,3,2,1,0:T(8,128)(2,1)S(1)}, u32[]{:S(2)}, u32[]{:S(2)}) %collective-permute-start.27) | collective-permute-done | bytes 458784 | tf_op jit(solution)/shard_map/ppermute | solution.py:119
  238.8 1.4 collective-permute-start.28
  240.4 4.5 %collective-permute-done.28 = bf16[2,2,56,512]{3,2,1,0:T(8,128)(2,1)S(1)} collective-permute-done((bf16[2,2,56,512]{3,2,1,0:T(8,128)(2,1)S(1)}, bf16[2,2,56,512]{3,2,1,0:T(8,128)(2,1)S(1)}, u32[]{:S(2)}, u32[]{:S(2)}) %collective-permute-start.28) | collective-permute-done | bytes 229408 | tf_op jit(solution)/shard_map/ppermute | solution.py:119
  245.4 6.1 %collective-permute-done.29 = bf16[2,56,512]{2,1,0:T(8,128)(2,1)S(1)} collective-permute-done((bf16[2,56,512]{2,1,0:T(8,128)(2,1)S(1)}, bf16[2,56,512]{2,1,0:T(8,128)(2,1)S(1)}, u32[]{:S(2)}, u32[]{:S(2)}) %collective-permute-start.29) | collective-permute-done | bytes 114720 | tf_op jit(solution)/shard_map/ppermute | solution.py:119
  251.6 3.1 %collective-permute-start.30 = (bf16[56,512]{1,0:T(8,128)(2,1)S(1)}, bf16[56,512]{1,0:T(8,128)(2,1)S(1)}, u32[]{:S(2)}, u32[]{:S(2)}) collective-permute-start(bf16[56,512]{1,0:T(8,128)(2,1)S(1)} %fusion.162), channel_id=1, source_target_pairs={{0,16},{1,17},{2,18},{3,19},{4,20},{5,21},{6,22},{7,23},{8,24},{9,... | collective-permute-start | bytes 172040 | tf_op jit(solution)/shard_map/ppermute | solution.py:119
  254.7 1.2 fusion.34
  256.0 1.4 collective-permute-done.30
  (226 shorter events, 34.9 us)
Async XLA Ops:
  0.6 9.6 %copy-start.14 = (bf16[1,2,512,256]{3,2,1,0:T(8,128)(2,1)S(1)}, bf16[1,2,512,256]{3,2,1,0:T(8,128)(2,1)}, u32[]{:S(2)}) copy-start(bf16[1,2,512,256]{3,2,1,0:T(8,128)(2,1)} %param.4) | copy-start | bytes 1572868
  1.7 8.6 %collective-permute-start = (bf16[2,128,256]{2,1,0:T(8,128)(2,1)S(1)}, bf16[2,128,256]{2,1,0:T(8,128)(2,1)S(1)}, u32[]{:S(2)}, u32[]{:S(2)}) collective-permute-start(bf16[2,128,256]{2,1,0:T(8,128)(2,1)S(1)} %get-tuple-element.74), channel_id=1, source_target_pairs={{0,1},{1,2},{2,3},{3,4},{4,5},{5,6},{6,7},{7,8},{8,9},{9,10},{10,1... | collective-permute-start | bytes 393224 | tf_op jit(solution)/shard_map/ppermute | solution.py:15
  3.6 8.5 %collective-permute-start.1 = (bf16[2,128,256]{2,1,0:T(8,128)(2,1)S(1)}, bf16[2,128,256]{2,1,0:T(8,128)(2,1)S(1)}, u32[]{:S(2)}, u32[]{:S(2)}) collective-permute-start(bf16[2,128,256]{2,1,0:T(8,128)(2,1)S(1)} %get-tuple-element.73), channel_id=1, source_target_pairs={{1,0},{2,1},{3,2},{4,3},{5,4},{6,5},{7,6},{8,7},{9,8},{10,9},{11,1... | collective-permute-start | bytes 393224 | tf_op jit(solution)/shard_map/ppermute | solution.py:15
  13.7 6.9 %copy-start.15 = (bf16[1,2,3,256,512]{4,3,2,1,0:T(8,128)(2,1)S(1)}, bf16[1,2,3,256,512]{4,3,2,1,0:T(8,128)(2,1)}, u32[]{:S(2)}) copy-start(bf16[1,2,3,256,512]{4,3,2,1,0:T(8,128)(2,1)} %param.6) | copy-start | bytes 4718596
  15.0 8.2 %copy-start.33 = (bf16[2,512,256]{2,1,0:T(8,128)(2,1)}, bf16[2,512,256]{2,1,0:T(8,128)(2,1)S(1)}, u32[]{:S(2)}) copy-start(bf16[2,512,256]{2,1,0:T(8,128)(2,1)S(1)} %fusion.18) | copy-start | bytes 1572868
  15.0 16.1 %collective-permute-start.2 = (bf16[2,512,256]{2,1,0:T(8,128)(2,1)S(1)}, bf16[2,512,256]{2,1,0:T(8,128)(2,1)S(1)}, u32[]{:S(2)}, u32[]{:S(2)}) collective-permute-start(bf16[2,512,256]{2,1,0:T(8,128)(2,1)S(1)} %fusion.18), channel_id=1, source_target_pairs={{0,2},{1,3},{2,4},{3,5},{4,6},{5,7},{6,8},{7,9},{8,10},{9,11},{10,... | collective-permute-start | bytes 1572872 | tf_op jit(solution)/shard_map/ppermute | solution.py:15
  20.8 15.7 %collective-permute-start.3 = (bf16[2,512,256]{2,1,0:T(8,128)(2,1)S(1)}, bf16[2,512,256]{2,1,0:T(8,128)(2,1)S(1)}, u32[]{:S(2)}, u32[]{:S(2)}) collective-permute-start(bf16[2,512,256]{2,1,0:T(8,128)(2,1)S(1)} %fusion.18), channel_id=1, source_target_pairs={{2,0},{3,1},{4,2},{5,3},{6,4},{7,5},{8,6},{9,7},{10,8},{11,9},{12,... | collective-permute-start | bytes 1572872 | tf_op jit(solution)/shard_map/ppermute | solution.py:15
  38.6 93.7 %copy-start.11 = (f32[2,512,256]{1,2,0:T(8,128)}, f32[2,512,256]{1,2,0:T(8,128)S(1)}, u32[]{:S(2)}) copy-start(f32[2,512,256]{1,2,0:T(8,128)S(1)} %get-tuple-element.8) | copy-start | bytes 3145732
  38.6 93.7 %copy-start.12 = (f32[2,512,256]{1,2,0:T(8,128)}, f32[2,512,256]{1,2,0:T(8,128)S(1)}, u32[]{:S(2)}) copy-start(f32[2,512,256]{1,2,0:T(8,128)S(1)} %get-tuple-element.40) | copy-start | bytes 3145732
  39.8 12.7 %collective-permute-start.5 = (bf16[2,512,256]{2,1,0:T(8,128)(2,1)S(1)}, bf16[2,512,256]{2,1,0:T(8,128)(2,1)S(1)}, u32[]{:S(2)}, u32[]{:S(2)}) collective-permute-start(bf16[2,512,256]{2,1,0:T(8,128)(2,1)S(1)} %get-tuple-element.56), channel_id=1, source_target_pairs={{0,2},{1,3},{2,4},{3,5},{4,6},{5,7},{6,8},{7,9},{8,10},{9,11},{10,... | collective-permute-start | bytes 1572872 | tf_op jit(solution)/shard_map/ppermute | solution.py:15
  41.7 15.5 %collective-permute-start.4 = (bf16[2,512,256]{2,1,0:T(8,128)(2,1)S(1)}, bf16[2,512,256]{2,1,0:T(8,128)(2,1)S(1)}, u32[]{:S(2)}, u32[]{:S(2)}) collective-permute-start(bf16[2,512,256]{2,1,0:T(8,128)(2,1)S(1)} %get-tuple-element.55), channel_id=1, source_target_pairs={{2,0},{3,1},{4,2},{5,3},{6,4},{7,5},{8,6},{9,7},{10,8},{11,9},{12,... | collective-permute-start | bytes 1572872 | tf_op jit(solution)/shard_map/ppermute | solution.py:15
  57.5 12.2 %copy-start.5 = (f32[2,512,256]{2,1,0:T(8,128)}, f32[2,512,256]{2,1,0:T(8,128)S(1)}, u32[]{:S(2)}) copy-start(f32[2,512,256]{2,1,0:T(8,128)S(1)} %fusion.26) | copy-start | bytes 3145732
  58.2 96.9 %copy-start.7 = (f32[2,512,256]{1,2,0:T(8,128)}, f32[2,512,256]{1,2,0:T(8,128)S(1)}, u32[]{:S(2)}) copy-start(f32[2,512,256]{1,2,0:T(8,128)S(1)} %get-tuple-element.4) | copy-start | bytes 3145732
  58.2 96.9 %copy-start.9 = (f32[2,512,256]{1,2,0:T(8,128)}, f32[2,512,256]{1,2,0:T(8,128)S(1)}, u32[]{:S(2)}) copy-start(f32[2,512,256]{1,2,0:T(8,128)S(1)} %get-tuple-element.38) | copy-start | bytes 3145732
  59.3 6.3 %collective-permute-start.6 = (bf16[2,128,256]{2,1,0:T(8,128)(2,1)S(1)}, bf16[2,128,256]{2,1,0:T(8,128)(2,1)S(1)}, u32[]{:S(2)}, u32[]{:S(2)}) collective-permute-start(bf16[2,128,256]{2,1,0:T(8,128)(2,1)S(1)} %get-tuple-element.53), channel_id=1, source_target_pairs={{0,1},{1,2},{2,3},{3,4},{4,5},{5,6},{6,7},{7,8},{8,9},{9,10},{10,1... | collective-permute-start | bytes 393224 | tf_op jit(solution)/shard_map/ppermute | solution.py:15
  61.2 6.1 %collective-permute-start.7 = (bf16[2,128,256]{2,1,0:T(8,128)(2,1)S(1)}, bf16[2,128,256]{2,1,0:T(8,128)(2,1)S(1)}, u32[]{:S(2)}, u32[]{:S(2)}) collective-permute-start(bf16[2,128,256]{2,1,0:T(8,128)(2,1)S(1)} %get-tuple-element.54), channel_id=1, source_target_pairs={{1,0},{2,1},{3,2},{4,3},{5,4},{6,5},{7,6},{8,7},{9,8},{10,9},{11,1... | collective-permute-start | bytes 393224 | tf_op jit(solution)/shard_map/ppermute | solution.py:15
  68.3 8.3 %collective-permute-start.8 = (bf16[2,256,256]{2,1,0:T(8,128)(2,1)S(1)}, bf16[2,256,256]{2,1,0:T(8,128)(2,1)S(1)}, u32[]{:S(2)}, u32[]{:S(2)}) collective-permute-start(bf16[2,256,256]{2,1,0:T(8,128)(2,1)S(1)} %pad_maximum_fusion.29), channel_id=1, source_target_pairs={{32,0},{64,32},{96,64},{33,1},{65,33},{97,65},{34,2},{66,34},{98,6... | collective-permute-start | bytes 786440 | tf_op jit(solution)/shard_map/ppermute | solution.py:15
  70.6 11.4 %collective-permute-start.9 = (bf16[2,256,256]{2,1,0:T(8,128)(2,1)S(1)}, bf16[2,256,256]{2,1,0:T(8,128)(2,1)S(1)}, u32[]{:S(2)}, u32[]{:S(2)}) collective-permute-start(bf16[2,256,256]{2,1,0:T(8,128)(2,1)S(1)} %get-tuple-element.33), channel_id=1, source_target_pairs={{32,0},{64,32},{96,64},{33,1},{65,33},{97,65},{34,2},{66,34},{98,6... | collective-permute-start | bytes 786440 | tf_op jit(solution)/shard_map/ppermute | solution.py:15
  76.6 29.5 %copy-start.46 = (bf16[2,128,256]{2,1,0:T(8,128)(2,1)}, bf16[2,128,256]{2,1,0:T(8,128)(2,1)S(1)}, u32[]{:S(2)}) copy-start(bf16[2,128,256]{2,1,0:T(8,128)(2,1)S(1)} %get-tuple-element.80) | copy-start | bytes 393220
  82.0 24.2 %copy-start.58 = (bf16[2,256,256]{2,1,0:T(8,128)(2,1)}, bf16[2,256,256]{2,1,0:T(8,128)(2,1)S(1)}, u32[]{:S(2)}) copy-start(bf16[2,256,256]{2,1,0:T(8,128)(2,1)S(1)} %collective-permute-done.9) | copy-start | bytes 786436
  83.5 16.4 %collective-permute-start.11 = (bf16[2,512,256]{2,1,0:T(8,128)(2,1)S(1)}, bf16[2,512,256]{2,1,0:T(8,128)(2,1)S(1)}, u32[]{:S(2)}, u32[]{:S(2)}) collective-permute-start(bf16[2,512,256]{2,1,0:T(8,128)(2,1)S(1)} %get-tuple-element.52), channel_id=1, source_target_pairs={{0,2},{1,3},{2,4},{3,5},{4,6},{5,7},{6,8},{7,9},{8,10},{9,11},{10,... | collective-permute-start | bytes 1572872 | tf_op jit(solution)/shard_map/ppermute | solution.py:15
  89.9 16.2 %collective-permute-start.10 = (bf16[2,512,256]{2,1,0:T(8,128)(2,1)S(1)}, bf16[2,512,256]{2,1,0:T(8,128)(2,1)S(1)}, u32[]{:S(2)}, u32[]{:S(2)}) collective-permute-start(bf16[2,512,256]{2,1,0:T(8,128)(2,1)S(1)} %get-tuple-element.51), channel_id=1, source_target_pairs={{2,0},{3,1},{4,2},{5,3},{6,4},{7,5},{8,6},{9,7},{10,8},{11,9},{12,... | collective-permute-start | bytes 1572872 | tf_op jit(solution)/shard_map/ppermute | solution.py:15
  107.9 6.5 %collective-permute-start.12 = (bf16[2,128,256]{2,1,0:T(8,128)(2,1)S(1)}, bf16[2,128,256]{2,1,0:T(8,128)(2,1)S(1)}, u32[]{:S(2)}, u32[]{:S(2)}) collective-permute-start(bf16[2,128,256]{2,1,0:T(8,128)(2,1)S(1)} %get-tuple-element.49), channel_id=1, source_target_pairs={{0,1},{1,2},{2,3},{3,4},{4,5},{5,6},{6,7},{7,8},{8,9},{9,10},{10,1... | collective-permute-start | bytes 393224 | tf_op jit(solution)/shard_map/ppermute | solution.py:15
  110.0 6.1 %collective-permute-start.13 = (bf16[2,128,256]{2,1,0:T(8,128)(2,1)S(1)}, bf16[2,128,256]{2,1,0:T(8,128)(2,1)S(1)}, u32[]{:S(2)}, u32[]{:S(2)}) collective-permute-start(bf16[2,128,256]{2,1,0:T(8,128)(2,1)S(1)} %get-tuple-element.50), channel_id=1, source_target_pairs={{1,0},{2,1},{3,2},{4,3},{5,4},{6,5},{7,6},{8,7},{9,8},{10,9},{11,1... | collective-permute-start | bytes 393224 | tf_op jit(solution)/shard_map/ppermute | solution.py:15
  117.1 9.7 %collective-permute-start.14 = (bf16[2,256,256]{2,1,0:T(8,128)(2,1)S(1)}, bf16[2,256,256]{2,1,0:T(8,128)(2,1)S(1)}, u32[]{:S(2)}, u32[]{:S(2)}) collective-permute-start(bf16[2,256,256]{2,1,0:T(8,128)(2,1)S(1)} %pad_maximum_fusion.30), channel_id=1, source_target_pairs={{32,0},{64,32},{96,64},{33,1},{65,33},{97,65},{34,2},{66,34},{98,6... | collective-permute-start | bytes 786440 | tf_op jit(solution)/shard_map/ppermute | solution.py:15
  119.3 13.1 %collective-permute-start.15 = (bf16[2,256,256]{2,1,0:T(8,128)(2,1)S(1)}, bf16[2,256,256]{2,1,0:T(8,128)(2,1)S(1)}, u32[]{:S(2)}, u32[]{:S(2)}) collective-permute-start(bf16[2,256,256]{2,1,0:T(8,128)(2,1)S(1)} %get-tuple-element.29), channel_id=1, source_target_pairs={{32,0},{64,32},{96,64},{33,1},{65,33},{97,65},{34,2},{66,34},{98,6... | collective-permute-start | bytes 786440 | tf_op jit(solution)/shard_map/ppermute | solution.py:15
  126.8 28.1 %copy-start.48 = (bf16[2,128,256]{2,1,0:T(8,128)(2,1)}, bf16[2,128,256]{2,1,0:T(8,128)(2,1)S(1)}, u32[]{:S(2)}) copy-start(bf16[2,128,256]{2,1,0:T(8,128)(2,1)S(1)} %get-tuple-element.77) | copy-start | bytes 393220
  126.8 28.1 %copy-start.50 = (bf16[2,128,256]{2,1,0:T(8,128)(2,1)}, bf16[2,128,256]{2,1,0:T(8,128)(2,1)S(1)}, u32[]{:S(2)}) copy-start(bf16[2,128,256]{2,1,0:T(8,128)(2,1)S(1)} %get-tuple-element.78) | copy-start | bytes 393220
  132.4 22.5 %copy-start.60 = (bf16[2,256,256]{2,1,0:T(8,128)(2,1)}, bf16[2,256,256]{2,1,0:T(8,128)(2,1)S(1)}, u32[]{:S(2)}) copy-start(bf16[2,256,256]{2,1,0:T(8,128)(2,1)S(1)} %collective-permute-done.15) | copy-start | bytes 786436
  133.9 16.4 %collective-permute-start.17 = (bf16[2,512,256]{2,1,0:T(8,128)(2,1)S(1)}, bf16[2,512,256]{2,1,0:T(8,128)(2,1)S(1)}, u32[]{:S(2)}, u32[]{:S(2)}) collective-permute-start(bf16[2,512,256]{2,1,0:T(8,128)(2,1)S(1)} %get-tuple-element.48), channel_id=1, source_target_pairs={{0,2},{1,3},{2,4},{3,5},{4,6},{5,7},{6,8},{7,9},{8,10},{9,11},{10,... | collective-permute-start | bytes 1572872 | tf_op jit(solution)/shard_map/ppermute | solution.py:15
  137.5 17.3 %collective-permute-start.16 = (bf16[2,512,256]{2,1,0:T(8,128)(2,1)S(1)}, bf16[2,512,256]{2,1,0:T(8,128)(2,1)S(1)}, u32[]{:S(2)}, u32[]{:S(2)}) collective-permute-start(bf16[2,512,256]{2,1,0:T(8,128)(2,1)S(1)} %get-tuple-element.47), channel_id=1, source_target_pairs={{2,0},{3,1},{4,2},{5,3},{6,4},{7,5},{8,6},{9,7},{10,8},{11,9},{12,... | collective-permute-start | bytes 1572872 | tf_op jit(solution)/shard_map/ppermute | solution.py:15
  155.1 12.5 %copy-start.1 = (f32[2,512,256]{2,1,0:T(8,128)}, f32[2,512,256]{2,1,0:T(8,128)S(1)}, u32[]{:S(2)}) copy-start(f32[2,512,256]{2,1,0:T(8,128)S(1)} %fusion.22) | copy-start | bytes 3145732
  156.5 6.3 %collective-permute-start.18 = (bf16[2,128,256]{2,1,0:T(8,128)(2,1)S(1)}, bf16[2,128,256]{2,1,0:T(8,128)(2,1)S(1)}, u32[]{:S(2)}, u32[]{:S(2)}) collective-permute-start(bf16[2,128,256]{2,1,0:T(8,128)(2,1)S(1)} %get-tuple-element.45), channel_id=1, source_target_pairs={{0,1},{1,2},{2,3},{3,4},{4,5},{5,6},{6,7},{7,8},{8,9},{9,10},{10,1... | collective-permute-start | bytes 393224 | tf_op jit(solution)/shard_map/ppermute | solution.py:15
  158.5 6.1 %collective-permute-start.19 = (bf16[2,128,256]{2,1,0:T(8,128)(2,1)S(1)}, bf16[2,128,256]{2,1,0:T(8,128)(2,1)S(1)}, u32[]{:S(2)}, u32[]{:S(2)}) collective-permute-start(bf16[2,128,256]{2,1,0:T(8,128)(2,1)S(1)} %get-tuple-element.46), channel_id=1, source_target_pairs={{1,0},{2,1},{3,2},{4,3},{5,4},{6,5},{7,6},{8,7},{9,8},{10,9},{11,1... | collective-permute-start | bytes 393224 | tf_op jit(solution)/shard_map/ppermute | solution.py:15
  166.3 10.4 %collective-permute-start.20 = (bf16[2,256,256]{2,1,0:T(8,128)(2,1)}, bf16[2,256,256]{2,1,0:T(8,128)(2,1)}, u32[]{:S(2)}, u32[]{:S(2)}) collective-permute-start(bf16[2,256,256]{2,1,0:T(8,128)(2,1)} %pad_maximum_fusion.31), channel_id=1, source_target_pairs={{32,0},{64,32},{96,64},{33,1},{65,33},{97,65},{34,2},{66,34},{98,6... | collective-permute-start | bytes 786440 | tf_op jit(solution)/shard_map/ppermute | solution.py:15
  168.6 13.7 %collective-permute-start.21 = (bf16[2,256,256]{2,1,0:T(8,128)(2,1)}, bf16[2,256,256]{2,1,0:T(8,128)(2,1)}, u32[]{:S(2)}, u32[]{:S(2)}) collective-permute-start(bf16[2,256,256]{2,1,0:T(8,128)(2,1)} %get-tuple-element.25), channel_id=1, source_target_pairs={{32,0},{64,32},{96,64},{33,1},{65,33},{97,65},{34,2},{66,34},{98,6... | collective-permute-start | bytes 786440 | tf_op jit(solution)/shard_map/ppermute | solution.py:15
  184.3 7.5 %copy-start.42 = (bf16[2,512,256]{1,2,0:T(8,128)(2,1)S(1)}, bf16[2,512,256]{1,2,0:T(8,128)(2,1)}, u32[]{:S(2)}) copy-start(bf16[2,512,256]{1,2,0:T(8,128)(2,1)} %copy-done.41) | copy-start | bytes 1572868
  184.3 7.5 %copy-start.65 = (bf16[2,512,256]{2,1,0:T(8,128)(2,1)S(1)}, bf16[2,512,256]{2,1,0:T(8,128)(2,1)}, u32[]{:S(2)}) copy-start(bf16[2,512,256]{2,1,0:T(8,128)(2,1)} %copy-done.64) | copy-start | bytes 1572868
  184.3 7.5 %copy-start.67 = (bf16[2,512,256]{1,2,0:T(8,128)(2,1)S(1)}, bf16[2,512,256]{1,2,0:T(8,128)(2,1)}, u32[]{:S(2)}) copy-start(bf16[2,512,256]{1,2,0:T(8,128)(2,1)} %copy-done.66) | copy-start | bytes 1572868
  184.4 7.5 %copy-start.69 = (bf16[2,512,256]{1,2,0:T(8,128)(2,1)S(1)}, bf16[2,512,256]{1,2,0:T(8,128)(2,1)}, u32[]{:S(2)}) copy-start(bf16[2,512,256]{1,2,0:T(8,128)(2,1)} %copy-done.68) | copy-start | bytes 1572868
  184.4 7.5 %copy-start.73 = (bf16[2,512,256]{2,1,0:T(8,128)(2,1)S(1)}, bf16[2,512,256]{2,1,0:T(8,128)(2,1)}, u32[]{:S(2)}) copy-start(bf16[2,512,256]{2,1,0:T(8,128)(2,1)} %copy-done.72) | copy-start | bytes 1572868
  185.4 6.5 %copy-start.34 = (bf16[2,512,256]{2,1,0:T(8,128)(2,1)S(1)}, bf16[2,512,256]{2,1,0:T(8,128)(2,1)}, u32[]{:S(2)}) copy-start(bf16[2,512,256]{2,1,0:T(8,128)(2,1)} %copy-done.33) | copy-start | bytes 1572868
  185.4 6.5 %copy-start.36 = (bf16[2,512,256]{1,2,0:T(8,128)(2,1)S(1)}, bf16[2,512,256]{1,2,0:T(8,128)(2,1)}, u32[]{:S(2)}) copy-start(bf16[2,512,256]{1,2,0:T(8,128)(2,1)} %copy-done.35) | copy-start | bytes 1572868
  185.5 16.6 %collective-permute-start.23 = (bf16[2,512,256]{2,1,0:T(8,128)(2,1)S(1)}, bf16[2,512,256]{2,1,0:T(8,128)(2,1)S(1)}, u32[]{:S(2)}, u32[]{:S(2)}) collective-permute-start(bf16[2,512,256]{2,1,0:T(8,128)(2,1)S(1)} %get-tuple-element.44), channel_id=1, source_target_pairs={{0,2},{1,3},{2,4},{3,5},{4,6},{5,7},{6,8},{7,9},{8,10},{9,11},{10,... | collective-permute-start | bytes 1572872 | tf_op jit(solution)/shard_map/ppermute | solution.py:15
  188.7 17.8 %collective-permute-start.22 = (bf16[2,512,256]{2,1,0:T(8,128)(2,1)S(1)}, bf16[2,512,256]{2,1,0:T(8,128)(2,1)S(1)}, u32[]{:S(2)}, u32[]{:S(2)}) collective-permute-start(bf16[2,512,256]{2,1,0:T(8,128)(2,1)S(1)} %get-tuple-element.43), channel_id=1, source_target_pairs={{2,0},{3,1},{4,2},{5,3},{6,4},{7,5},{8,6},{9,7},{10,8},{11,9},{12,... | collective-permute-start | bytes 1572872 | tf_op jit(solution)/shard_map/ppermute | solution.py:15
  196.0 11.7 %copy-start.8 = (f32[2,512,256]{1,2,0:T(8,128)S(1)}, f32[2,512,256]{1,2,0:T(8,128)}, u32[]{:S(2)}) copy-start(f32[2,512,256]{1,2,0:T(8,128)} %copy-done.7) | copy-start | bytes 3145732
  196.0 11.7 %copy-start.10 = (f32[2,512,256]{1,2,0:T(8,128)S(1)}, f32[2,512,256]{1,2,0:T(8,128)}, u32[]{:S(2)}) copy-start(f32[2,512,256]{1,2,0:T(8,128)} %copy-done.9) | copy-start | bytes 3145732
  219.5 2.7 %collective-permute-start.26 = (bf16[2,2,2,2,56,512]{5,4,3,2,1,0:T(8,128)(2,1)}, bf16[2,2,2,2,56,512]{5,4,3,2,1,0:T(8,128)(2,1)S(1)}, u32[]{:S(2)}, u32[]{:S(2)}) collective-permute-start(bf16[2,2,2,2,56,512]{5,4,3,2,1,0:T(8,128)(2,1)} %fusion.44), channel_id=1, source_target_pairs={{0,1},{1,0},{2,3},{3,2},{4,5},{5,4},{6,7},{7,6},{8,9},{9,8},{10,11... | collective-permute-start | bytes 2752520 | tf_op jit(solution)/shard_map/ppermute | solution.py:119
  224.8 13.7 %collective-permute-start.27 = (bf16[2,2,2,56,512]{4,3,2,1,0:T(8,128)(2,1)S(1)}, bf16[2,2,2,56,512]{4,3,2,1,0:T(8,128)(2,1)S(1)}, u32[]{:S(2)}, u32[]{:S(2)}) collective-permute-start(bf16[2,2,2,56,512]{4,3,2,1,0:T(8,128)(2,1)S(1)} %fusion.86), channel_id=1, source_target_pairs={{0,2},{1,3},{2,0},{3,1},{4,6},{5,7},{6,4},{7,5},{8,10},{9,11},{10,... | collective-permute-start | bytes 1376264 | tf_op jit(solution)/shard_map/ppermute | solution.py:119
  226.2 14.1 %copy-start.4 = (f32[2,512,256]{2,1,0:T(8,128)S(1)}, f32[2,512,256]{2,1,0:T(8,128)}, u32[]{:S(2)}) copy-start(f32[2,512,256]{2,1,0:T(8,128)} %copy-done.3) | copy-start | bytes 3145732
  226.2 19.0 %collective-permute-start.24 = (bf16[2,128,256]{2,1,0:T(8,128)(2,1)S(1)}, bf16[2,128,256]{2,1,0:T(8,128)(2,1)S(1)}, u32[]{:S(2)}, u32[]{:S(2)}) collective-permute-start(bf16[2,128,256]{2,1,0:T(8,128)(2,1)S(1)} %get-tuple-element.41), channel_id=1, source_target_pairs={{0,1},{1,2},{2,3},{3,4},{4,5},{5,6},{6,7},{7,8},{8,9},{9,10},{10,1... | collective-permute-start | bytes 393224 | tf_op jit(solution)/shard_map/ppermute | solution.py:15
  228.4 16.8 %collective-permute-start.25 = (bf16[2,128,256]{2,1,0:T(8,128)(2,1)S(1)}, bf16[2,128,256]{2,1,0:T(8,128)(2,1)S(1)}, u32[]{:S(2)}, u32[]{:S(2)}) collective-permute-start(bf16[2,128,256]{2,1,0:T(8,128)(2,1)S(1)} %get-tuple-element.42), channel_id=1, source_target_pairs={{1,0},{2,1},{3,2},{4,3},{5,4},{6,5},{7,6},{8,7},{9,8},{10,9},{11,1... | collective-permute-start | bytes 393224 | tf_op jit(solution)/shard_map/ppermute | solution.py:15
  238.8 6.1 %collective-permute-start.28 = (bf16[2,2,56,512]{3,2,1,0:T(8,128)(2,1)S(1)}, bf16[2,2,56,512]{3,2,1,0:T(8,128)(2,1)S(1)}, u32[]{:S(2)}, u32[]{:S(2)}) collective-permute-start(bf16[2,2,56,512]{3,2,1,0:T(8,128)(2,1)S(1)} %fusion.137), channel_id=1, source_target_pairs={{0,8},{1,9},{2,10},{3,11},{4,12},{5,13},{6,14},{7,15},{8,0},{9,1},... | collective-permute-start | bytes 688136 | tf_op jit(solution)/shard_map/ppermute | solution.py:119
  245.0 9.6 %copy-start.30 = (f32[1,2,256,256]{3,2,1,0:T(8,128)S(1)}, f32[1,2,256,256]{3,2,1,0:T(8,128)}, u32[]{:S(2)}) copy-start(f32[1,2,256,256]{3,2,1,0:T(8,128)} %get-tuple-element.34) | copy-start | bytes 1572868
  245.0 9.6 %copy-start.31 = (f32[1,2,256,256]{3,2,1,0:T(8,128)S(1)}, f32[1,2,256,256]{3,2,1,0:T(8,128)}, u32[]{:S(2)}) copy-start(f32[1,2,256,256]{3,2,1,0:T(8,128)} %get-tuple-element.30) | copy-start | bytes 1572868
  245.0 9.6 %copy-start.32 = (f32[1,2,256,256]{3,2,1,0:T(8,128)S(1)}, f32[1,2,256,256]{3,2,1,0:T(8,128)}, u32[]{:S(2)}) copy-start(f32[1,2,256,256]{3,2,1,0:T(8,128)} %get-tuple-element.26) | copy-start | bytes 1572868
  245.0 9.6 %copy-start.52 = (f32[1,2,128,256]{3,2,1,0:T(8,128)S(1)}, f32[1,2,128,256]{3,2,1,0:T(8,128)}, u32[]{:S(2)}) copy-start(f32[1,2,128,256]{3,2,1,0:T(8,128)} %get-tuple-element.20) | copy-start | bytes 786436
  245.1 9.6 %copy-start.53 = (f32[1,2,128,256]{3,2,1,0:T(8,128)S(1)}, f32[1,2,128,256]{3,2,1,0:T(8,128)}, u32[]{:S(2)}) copy-start(f32[1,2,128,256]{3,2,1,0:T(8,128)} %get-tuple-element.35) | copy-start | bytes 786436
  245.1 9.6 %copy-start.54 = (f32[1,2,128,256]{3,2,1,0:T(8,128)S(1)}, f32[1,2,128,256]{3,2,1,0:T(8,128)}, u32[]{:S(2)}) copy-start(f32[1,2,128,256]{3,2,1,0:T(8,128)} %get-tuple-element.16) | copy-start | bytes 786436
  245.1 9.6 %copy-start.55 = (f32[1,2,128,256]{3,2,1,0:T(8,128)S(1)}, f32[1,2,128,256]{3,2,1,0:T(8,128)}, u32[]{:S(2)}) copy-start(f32[1,2,128,256]{3,2,1,0:T(8,128)} %get-tuple-element.31) | copy-start | bytes 786436
  245.1 9.6 %copy-start.56 = (f32[1,2,128,256]{3,2,1,0:T(8,128)S(1)}, f32[1,2,128,256]{3,2,1,0:T(8,128)}, u32[]{:S(2)}) copy-start(f32[1,2,128,256]{3,2,1,0:T(8,128)} %get-tuple-element.12) | copy-start | bytes 786436
  245.1 9.6 %copy-start.57 = (f32[1,2,128,256]{3,2,1,0:T(8,128)S(1)}, f32[1,2,128,256]{3,2,1,0:T(8,128)}, u32[]{:S(2)}) copy-start(f32[1,2,128,256]{3,2,1,0:T(8,128)} %get-tuple-element.27) | copy-start | bytes 786436
  245.1 6.4 %collective-permute-start.29 = (bf16[2,56,512]{2,1,0:T(8,128)(2,1)S(1)}, bf16[2,56,512]{2,1,0:T(8,128)(2,1)S(1)}, u32[]{:S(2)}, u32[]{:S(2)}) collective-permute-start(bf16[2,56,512]{2,1,0:T(8,128)(2,1)S(1)} %fusion.152), channel_id=1, source_target_pairs={{0,4},{1,5},{2,6},{3,7},{4,0},{5,1},{6,2},{7,3},{8,12},{9,13},{10,... | collective-permute-start | bytes 344072 | tf_op jit(solution)/shard_map/ppermute | solution.py:119
  251.6 5.8 %collective-permute-start.30 = (bf16[56,512]{1,0:T(8,128)(2,1)S(1)}, bf16[56,512]{1,0:T(8,128)(2,1)S(1)}, u32[]{:S(2)}, u32[]{:S(2)}) collective-permute-start(bf16[56,512]{1,0:T(8,128)(2,1)S(1)} %fusion.162), channel_id=1, source_target_pairs={{0,16},{1,17},{2,18},{3,19},{4,20},{5,21},{6,22},{7,23},{8,24},{9,... | collective-permute-start | bytes 172040 | tf_op jit(solution)/shard_map/ppermute | solution.py:119
  (44 other events, 126.9 us)

commit v5 on v3

--- a/solution.py
+++ b/solution.py
@@ -72,6 +72,44 @@
         first_following = shifted(grad_first, "seq", -far_hops)
     grad_conv = middle + first_following.astype(jnp.float32) + third_earlier.astype(jnp.float32)
     return flowing + grad_conv, conv_term, out_term
+
+
+def split_rows(value, width):
+    return jnp.concatenate([value[:, :width], value[:, -width:]], axis=1), value[:, width:-width]
+
+
+def join_rows(edges, inner, width):
+    return jnp.concatenate([edges[:, :width], inner, edges[:, width:]], axis=1)
+
+
+def backward_far(pieces, saved, conv, out_mat, far_hops):
+    taps, gated, factor_a, factor_b = saved
+    chans = pieces[0].shape[2]
+    width = NEAR
+    weights = conv.reshape(3 * chans, 2 * chans)
+    f32 = jnp.float32
+    factors = [split_rows(factor_a, width), split_rows(factor_b, width)]
+    outs, pres, halves = [], [], []
+    for index, flowing in enumerate(pieces):
+        grad_half = flowing.astype(jnp.bfloat16)
+        grad_gated = jnp.einsum("mpd,cd->mpc", grad_half, out_mat, preferred_element_type=f32)
+        grad_pre = jnp.concatenate(
+            [grad_gated * factors[0][index], grad_gated * factors[1][index]], axis=2
+        ).astype(jnp.bfloat16)
+        back = jnp.einsum("mpd,cd->mpc", grad_pre, weights, preferred_element_type=f32)
+        grad_first = back[..., :chans].astype(jnp.bfloat16)
+        middle = back[..., chans : 2 * chans]
+        grad_third = back[..., 2 * chans :].astype(jnp.bfloat16)
+        third_earlier = shifted(grad_third, "seq", far_hops)
+        first_following = shifted(grad_first, "seq", -far_hops)
+        outs.append(flowing + (middle + first_following.astype(f32) + third_earlier.astype(f32)))
+        pres.append(grad_pre)
+        halves.append(grad_half)
+    grad_pre = join_rows(pres[0], pres[1], width)
+    grad_half = join_rows(halves[0], halves[1], width)
+    out_term = jnp.einsum("mpc,mpd->cd", gated, grad_half, preferred_element_type=f32)
+    conv_term = jnp.einsum("mpc,mpd->cd", taps, grad_pre, preferred_element_type=f32)
+    return join_rows(outs[0], outs[1], width), conv_term, out_term
 
 
 def split_near(flowing, middle, grad_first, grad_third, width):
@@ -151,15 +189,20 @@
         stored.append(saved)
 
     top = jnp.where(section_rank == section_count - 1, 1.0, 0.0).astype(jnp.float32)
-    flowing = cotangent.astype(jnp.float32) * top
+    flowing = split_rows(cotangent.astype(jnp.float32) * top, NEAR)
     input_grads = None
     conv_acc = [None] * depth
     out_acc = [None] * depth
     for step in range(section_count):
         for layer in reversed(range(depth)):
-            flowing, conv_term, out_term = backward_layer(
-                flowing, stored[layer], conv_mat[layer], out_mat[layer], layer, far_hops
-            )
+            if layer == depth - 1:
+                flowing, conv_term, out_term = backward_far(
+                    flowing, stored[layer], conv_mat[layer], out_mat[layer], far_hops
+                )
+            else:
+                flowing, conv_term, out_term = backward_layer(
+                    flowing, stored[layer], conv_mat[layer], out_mat[layer], layer, far_hops
+                )
             conv_acc[layer] = conv_term if step == 0 else conv_acc[layer] + conv_term
             out_acc[layer] = out_term if step == 0 else out_acc[layer] + out_term
         low, inner, high = flowing
@@ -169,10 +212,7 @@
             bf16 = jnp.bfloat16
             inner = shifted(inner.astype(bf16), "section", -1)
             edges = shifted(jnp.concatenate([low, high], axis=1).astype(bf16), "section", -1)
-            width = low.shape[1]
-            flowing = jnp.concatenate(
-                [edges[:, :width], inner, edges[:, width:]], axis=1
-            ).astype(jnp.float32)
+            flowing = (edges.astype(jnp.float32), inner.astype(jnp.float32))
 
     conv_rows = 3 * channels // seq_count
     out_rows = channels // seq_count

time: 255 us -> 240 us (0.941)
  waiting for transfers between devices: 110 us -> 63.4 us
  starting transfers between devices: 74.2 us -> 102 us
    ppermute x26 -> x34, waiting for transfers between devices: 88.7 us -> 44.1 us  [shifted(): lax.ppermute(value, axis, [(source, source + steps) for source in range(l...]
    ppermute x26 -> x34, starting transfers between devices: 69.5 us -> 96.4 us  [shifted(): lax.ppermute(value, axis, [(source, source + steps) for source in range(l...]
    dot_general x0 -> x24, matrix products: none -> 13.6 us  [the longest x4 5.31 us: backward_far(): jnp.einsum('mpc,mpd->cd', taps, grad_pre, preferred_element_type=f32)]
    dot_general x8 -> x4, matrix products: 10.4 us -> 4.14 us  [backward_layer(): jnp.einsum('mpd,cd->mpc', grad_pre, weights, preferred_element_type=jnp.f...]
    dot_general x8 -> x4, matrix products: 7.21 us -> 2.72 us  [backward_layer(): jnp.einsum('mpd,cd->mpc', grad_half, out_mat, preferred_element_type=jnp....]
    dot_general x8 -> x4, matrix products: 15.8 us -> 13.5 us  [backward_layer(): jnp.einsum('mpc,mpd->cd', taps, grad_pre, preferred_element_type=jnp.floa...]
  transfers between devices with their start and end apart: 31 -> 39, of which waited for: 23 -> 17; matrix products, arithmetic and copies ran while one was open for 11% -> 19% of each run, Pallas kernels for 0% -> 0%
where the time goes in v5:
time: 240 us; the launch traced here: 238 us
  starting transfers between devices  102 us (42%)
  waiting for transfers between devices  63.4 us (26%)
  matrix products  41.9 us (17%)
  other arithmetic  19.2 us (8%)
  local copies, waits for them, and re-layouts  9.32 us (4%)
    ppermute x34, starting transfers between devices, shifted(): lax.ppermute(value, axis, [(source, source + steps) for source in range(l...  96.4 us
    ppermute x34, waiting for transfers between devices, shifted(): lax.ppermute(value, axis, [(source, source + steps) for source in range(l...  44.1 us
    ppermute x5, waiting for transfers between devices, halving_scatter(): got = lax.ppermute(sends, 'seq', pairs)  19.3 us
    dot_general x4, matrix products, backward_layer(): jnp.einsum('mpc,mpd->cd', taps, grad_pre, preferred_element_type=jnp.floa...  13.5 us
    dot_general x7, matrix products, mm(): return jnp.einsum('mpc,cd->mpd', a, b, preferred_element_type=jnp.float32)  6.74 us
    ppermute x5, starting transfers between devices, halving_scatter(): got = lax.ppermute(sends, 'seq', pairs)  5.72 us
    dot_general x4, matrix products, backward_far(): jnp.einsum('mpc,mpd->cd', taps, grad_pre, preferred_element_type=f32)  5.31 us
    dot_general x8, matrix products, backward_far(): jnp.einsum('mpd,cd->mpc', grad_pre, weights, preferred_element_type=f32)  4.96 us
  transfers between devices with their start and end apart: 39, of which 17 were waited for; matrix products, arithmetic and copies ran while one was open for 19% of the time, Pallas kernels for 0%

profile of v5, /device:TPU:24, one launch (start us, length us, event | category | flops | bytes accessed | tf_op | source)
XLA Modules:
  0.0 238.0 jit_solution(10362412509746782471)
XLA Ops:
  0.6 1.8 fusion.308
  2.5 1.9 collective-permute-start
  4.4 3.8 %collective-permute-start.1 = (bf16[2,128,256]{2,1,0:T(8,128)(2,1)}, bf16[2,128,256]{2,1,0:T(8,128)(2,1)S(1)}, u32[]{:S(2)}, u32[]{:S(2)}) collective-permute-start(bf16[2,128,256]{2,1,0:T(8,128)(2,1)} %get-tuple-element.110), channel_id=1, source_target_pairs={{1,0},{2,1},{3,2},{4,3},{5,4},{6,5},{7,6},{8,7},{9,8},{10,9},{11,1... | collective-permute-start | bytes 393224 | tf_op jit(solution)/shard_map/ppermute | solution.py:15
  8.2 2.1 fusion.307
  10.3 1.8 fusion.178
  15.9 1.6 fusion.93
  17.6 1.5 add_add_fusion.1
  20.4 5.6 %collective-permute-start.2 = (bf16[2,512,256]{2,1,0:T(8,128)(2,1)S(1)}, bf16[2,512,256]{2,1,0:T(8,128)(2,1)S(1)}, u32[]{:S(2)}, u32[]{:S(2)}) collective-permute-start(bf16[2,512,256]{2,1,0:T(8,128)(2,1)S(1)} %fusion.2), channel_id=1, source_target_pairs={{0,2},{1,3},{2,4},{3,5},{4,6},{5,7},{6,8},{7,9},{8,10},{9,11},{10,... | collective-permute-start | bytes 1572872 | tf_op jit(solution)/shard_map/ppermute | solution.py:15
  26.0 1.9 collective-permute-start.3
  28.4 7.6 %collective-permute-done.2 = bf16[2,512,256]{2,1,0:T(8,128)(2,1)S(1)} collective-permute-done((bf16[2,512,256]{2,1,0:T(8,128)(2,1)S(1)}, bf16[2,512,256]{2,1,0:T(8,128)(2,1)S(1)}, u32[]{:S(2)}, u32[]{:S(2)}) %collective-permute-start.2) | collective-permute-done | bytes 524320 | tf_op jit(solution)/shard_map/ppermute | solution.py:15
  36.6 4.9 %collective-permute-done.3 = bf16[2,512,256]{2,1,0:T(8,128)(2,1)S(1)} collective-permute-done((bf16[2,512,256]{2,1,0:T(8,128)(2,1)S(1)}, bf16[2,512,256]{2,1,0:T(8,128)(2,1)S(1)}, u32[]{:S(2)}, u32[]{:S(2)}) %collective-permute-start.3) | collective-permute-done | bytes 524320 | tf_op jit(solution)/shard_map/ppermute | solution.py:15
  43.7 1.9 collective-permute-start.5
  45.6 3.9 %collective-permute-start.4 = (bf16[2,256,256]{2,1,0:T(8,128)(2,1)S(1)}, bf16[2,256,256]{2,1,0:T(8,128)(2,1)S(1)}, u32[]{:S(2)}, u32[]{:S(2)}) collective-permute-start(bf16[2,256,256]{2,1,0:T(8,128)(2,1)S(1)} %get-tuple-element.74), channel_id=1, source_target_pairs={{2,0},{3,1},{4,2},{5,3},{6,4},{7,5},{8,6},{9,7},{10,8},{11,9},{12,... | collective-permute-start | bytes 786440 | tf_op jit(solution)/shard_map/ppermute | solution.py:15
  50.3 4.0 %collective-permute-start.7 = (bf16[2,256,256]{2,1,0:T(8,128)(2,1)S(1)}, bf16[2,256,256]{2,1,0:T(8,128)(2,1)S(1)}, u32[]{:S(2)}, u32[]{:S(2)}) collective-permute-start(bf16[2,256,256]{2,1,0:T(8,128)(2,1)S(1)} %get-tuple-element.73), channel_id=1, source_target_pairs={{0,2},{1,3},{2,4},{3,5},{4,6},{5,7},{6,8},{7,9},{8,10},{9,11},{10,... | collective-permute-start | bytes 786440 | tf_op jit(solution)/shard_map/ppermute | solution.py:15
  54.3 1.9 collective-permute-start.6
  58.5 6.1 %collective-permute-done.6 = bf16[2,256,256]{2,1,0:T(8,128)(2,1)S(1)} collective-permute-done((bf16[2,256,256]{2,1,0:T(8,128)(2,1)S(1)}, bf16[2,256,256]{2,1,0:T(8,128)(2,1)S(1)}, u32[]{:S(2)}, u32[]{:S(2)}) %collective-permute-start.6) | collective-permute-done | bytes 262176 | tf_op jit(solution)/shard_map/ppermute | solution.py:15
  66.6 2.1 collective-permute-start.8
  68.7 3.6 %collective-permute-start.9 = (bf16[2,128,256]{2,1,0:T(8,128)(2,1)S(1)}, bf16[2,128,256]{2,1,0:T(8,128)(2,1)S(1)}, u32[]{:S(2)}, u32[]{:S(2)}) collective-permute-start(bf16[2,128,256]{2,1,0:T(8,128)(2,1)S(1)} %get-tuple-element.45), channel_id=1, source_target_pairs={{1,0},{2,1},{3,2},{4,3},{5,4},{6,5},{7,6},{8,7},{9,8},{10,9},{11,1... | collective-permute-start | bytes 393224 | tf_op jit(solution)/shard_map/ppermute | solution.py:15
  73.4 1.3 collective-permute-start.13
  74.7 3.1 %fusion.62 = f32[768,512,1]{1,0,2:T(8,128)} fusion(bf16[2,512,256]{1,2,0:T(8,128)(2,1)S(1)} %get-tuple-element.33, bf16[2,512,256]{1,2,0:T(8,128)(2,1)S(1)} %get-tuple-element.9, bf16[2,128,256]{2,1,0:T(8,128)(2,1)S(1)} %collective-permute-done.1, bf16[2,384,256]{2,1,0:T(8,128)(2,1)S(1)} %copy-done.14, bf16[2,512,256]{2,1,0:T(8,128)(2,1)S(1)} %bitcast.326, ...), kind=kOutput, calls=%fused_computation.108 | convolution fusion | flops 815267840 | bytes 4194304 | tf_op jit(solution)/shard_map/mpc,mpd->cd/dot_general | solution.py:62
  78.8 1.5 collective-permute-start.10
  80.3 2.0 collective-permute-done.13
  83.2 4.0 %collective-permute-start.15 = (bf16[2,256,256]{2,1,0:T(8,128)(2,1)S(1)}, bf16[2,256,256]{2,1,0:T(8,128)(2,1)S(1)}, u32[]{:S(2)}, u32[]{:S(2)}) collective-permute-start(bf16[2,256,256]{2,1,0:T(8,128)(2,1)S(1)} %get-tuple-element.69), channel_id=1, source_target_pairs={{0,2},{1,3},{2,4},{3,5},{4,6},{5,7},{6,8},{7,9},{8,10},{9,11},{10,... | collective-permute-start | bytes 786440 | tf_op jit(solution)/shard_map/ppermute | solution.py:15
  87.2 1.9 collective-permute-start.14
  90.1 6.0 %collective-permute-start.12 = (bf16[2,256,256]{2,1,0:T(8,128)(2,1)S(1)}, bf16[2,256,256]{2,1,0:T(8,128)(2,1)S(1)}, u32[]{:S(2)}, u32[]{:S(2)}) collective-permute-start(bf16[2,256,256]{2,1,0:T(8,128)(2,1)S(1)} %get-tuple-element.71), channel_id=1, source_target_pairs={{0,2},{1,3},{2,4},{3,5},{4,6},{5,7},{6,8},{7,9},{8,10},{9,11},{10,... | collective-permute-start | bytes 786440 | tf_op jit(solution)/shard_map/ppermute | solution.py:15
  96.2 1.9 collective-permute-start.11
  100.0 6.5 %collective-permute-done.11 = bf16[2,256,256]{2,1,0:T(8,128)(2,1)S(1)} collective-permute-done((bf16[2,256,256]{2,1,0:T(8,128)(2,1)S(1)}, bf16[2,256,256]{2,1,0:T(8,128)(2,1)S(1)}, u32[]{:S(2)}, u32[]{:S(2)}) %collective-permute-start.11) | collective-permute-done | bytes 262176 | tf_op jit(solution)/shard_map/ppermute | solution.py:15
  108.1 1.9 collective-permute-start.16
  110.0 3.6 %collective-permute-start.17 = (bf16[2,128,256]{2,1,0:T(8,128)(2,1)S(1)}, bf16[2,128,256]{2,1,0:T(8,128)(2,1)S(1)}, u32[]{:S(2)}, u32[]{:S(2)}) collective-permute-start(bf16[2,128,256]{2,1,0:T(8,128)(2,1)S(1)} %get-tuple-element.43), channel_id=1, source_target_pairs={{1,0},{2,1},{3,2},{4,3},{5,4},{6,5},{7,6},{8,7},{9,8},{10,9},{11,1... | collective-permute-start | bytes 393224 | tf_op jit(solution)/shard_map/ppermute | solution.py:15
  114.8 1.3 collective-permute-start.21
  116.1 3.1 %fusion.60 = f32[768,512,1]{1,0,2:T(8,128)} fusion(bf16[2,512,256]{1,2,0:T(8,128)(2,1)S(1)} %get-tuple-element.53, bf16[2,512,256]{1,2,0:T(8,128)(2,1)S(1)} %get-tuple-element.52, bf16[2,128,256]{2,1,0:T(8,128)(2,1)S(1)} %collective-permute-done.1, bf16[2,384,256]{2,1,0:T(8,128)(2,1)S(1)} %copy-done.14, bf16[2,512,256]{2,1,0:T(8,128)(2,1)S(1)} %bitcast.327, ...), kind=kOutput, calls=%fused_computation.106 | convolution fusion | flops 815267840 | bytes 4194304 | tf_op jit(solution)/shard_map/mpc,mpd->cd/dot_general | solution.py:62
  120.4 1.3 collective-permute-start.18
  121.7 1.9 collective-permute-done.21
  124.6 3.7 %collective-permute-start.23 = (bf16[2,256,256]{2,1,0:T(8,128)(2,1)S(1)}, bf16[2,256,256]{2,1,0:T(8,128)(2,1)S(1)}, u32[]{:S(2)}, u32[]{:S(2)}) collective-permute-start(bf16[2,256,256]{2,1,0:T(8,128)(2,1)S(1)} %get-tuple-element.65), channel_id=1, source_target_pairs={{0,2},{1,3},{2,4},{3,5},{4,6},{5,7},{6,8},{7,9},{8,10},{9,11},{10,... | collective-permute-start | bytes 786440 | tf_op jit(solution)/shard_map/ppermute | solution.py:15
  128.3 2.1 collective-permute-start.22
  131.4 5.9 %collective-permute-start.20 = (bf16[2,256,256]{2,1,0:T(8,128)(2,1)S(1)}, bf16[2,256,256]{2,1,0:T(8,128)(2,1)S(1)}, u32[]{:S(2)}, u32[]{:S(2)}) collective-permute-start(bf16[2,256,256]{2,1,0:T(8,128)(2,1)S(1)} %get-tuple-element.67), channel_id=1, source_target_pairs={{0,2},{1,3},{2,4},{3,5},{4,6},{5,7},{6,8},{7,9},{8,10},{9,11},{10,... | collective-permute-start | bytes 786440 | tf_op jit(solution)/shard_map/ppermute | solution.py:15
  137.3 1.9 collective-permute-start.19
  141.1 6.5 %collective-permute-done.19 = bf16[2,256,256]{2,1,0:T(8,128)(2,1)S(1)} collective-permute-done((bf16[2,256,256]{2,1,0:T(8,128)(2,1)S(1)}, bf16[2,256,256]{2,1,0:T(8,128)(2,1)S(1)}, u32[]{:S(2)}, u32[]{:S(2)}) %collective-permute-start.19) | collective-permute-done | bytes 262176 | tf_op jit(solution)/shard_map/ppermute | solution.py:15
  149.2 1.9 collective-permute-start.24
  151.2 3.6 %collective-permute-start.25 = (bf16[2,128,256]{2,1,0:T(8,128)(2,1)S(1)}, bf16[2,128,256]{2,1,0:T(8,128)(2,1)S(1)}, u32[]{:S(2)}, u32[]{:S(2)}) collective-permute-start(bf16[2,128,256]{2,1,0:T(8,128)(2,1)S(1)} %get-tuple-element.41), channel_id=1, source_target_pairs={{1,0},{2,1},{3,2},{4,3},{5,4},{6,5},{7,6},{8,7},{9,8},{10,9},{11,1... | collective-permute-start | bytes 393224 | tf_op jit(solution)/shard_map/ppermute | solution.py:15
  155.9 1.5 collective-permute-start.29
  157.4 3.2 %fusion.58 = f32[768,512,1]{1,0,2:T(8,128)} fusion(bf16[2,512,256]{1,2,0:T(8,128)(2,1)S(1)} %get-tuple-element.51, bf16[2,512,256]{1,2,0:T(8,128)(2,1)S(1)} %get-tuple-element.50, bf16[2,128,256]{2,1,0:T(8,128)(2,1)S(1)} %collective-permute-done.1, bf16[2,384,256]{2,1,0:T(8,128)(2,1)S(1)} %copy-done.14, bf16[2,512,256]{2,1,0:T(8,128)(2,1)S(1)} %bitcast.328, ...), kind=kOutput, calls=%fused_computation.104 | convolution fusion | flops 815267840 | bytes 4194304 | tf_op jit(solution)/shard_map/mpc,mpd->cd/dot_general | solution.py:62
  161.8 1.3 collective-permute-start.26
  163.1 1.6 collective-permute-done.29
  165.7 3.4 %collective-permute-start.31 = (bf16[2,256,256]{2,1,0:T(8,128)(2,1)S(1)}, bf16[2,256,256]{2,1,0:T(8,128)(2,1)S(1)}, u32[]{:S(2)}, u32[]{:S(2)}) collective-permute-start(bf16[2,256,256]{2,1,0:T(8,128)(2,1)S(1)} %get-tuple-element.61), channel_id=1, source_target_pairs={{0,2},{1,3},{2,4},{3,5},{4,6},{5,7},{6,8},{7,9},{8,10},{9,11},{10,... | collective-permute-start | bytes 786440 | tf_op jit(solution)/shard_map/ppermute | solution.py:15
  169.1 2.4 %collective-permute-start.30 = (bf16[2,256,256]{2,1,0:T(8,128)(2,1)S(1)}, bf16[2,256,256]{2,1,0:T(8,128)(2,1)S(1)}, u32[]{:S(2)}, u32[]{:S(2)}) collective-permute-start(bf16[2,256,256]{2,1,0:T(8,128)(2,1)S(1)} %get-tuple-element.60), channel_id=1, source_target_pairs={{2,0},{3,1},{4,2},{5,3},{6,4},{7,5},{8,6},{9,7},{10,8},{11,9},{12,... | collective-permute-start | bytes 786440 | tf_op jit(solution)/shard_map/ppermute | solution.py:15
  172.6 5.6 %collective-permute-start.28 = (bf16[2,256,256]{2,1,0:T(8,128)(2,1)S(1)}, bf16[2,256,256]{2,1,0:T(8,128)(2,1)S(1)}, u32[]{:S(2)}, u32[]{:S(2)}) collective-permute-start(bf16[2,256,256]{2,1,0:T(8,128)(2,1)S(1)} %get-tuple-element.63), channel_id=1, source_target_pairs={{0,2},{1,3},{2,4},{3,5},{4,6},{5,7},{6,8},{7,9},{8,10},{9,11},{10,... | collective-permute-start | bytes 786440 | tf_op jit(solution)/shard_map/ppermute | solution.py:15
  178.2 1.9 collective-permute-start.27
  180.1 2.2 bitcast_add_fusion
  183.2 5.4 %collective-permute-done.27 = bf16[2,256,256]{2,1,0:T(8,128)(2,1)S(1)} collective-permute-done((bf16[2,256,256]{2,1,0:T(8,128)(2,1)S(1)}, bf16[2,256,256]{2,1,0:T(8,128)(2,1)S(1)}, u32[]{:S(2)}, u32[]{:S(2)}) %collective-permute-start.27) | collective-permute-done | bytes 262176 | tf_op jit(solution)/shard_map/ppermute | solution.py:15
  188.7 1.4 multiply_convert_fusion.1
  190.9 4.1 %bitcast_add_fusion.3 = f32[768,512]{1,0:T(8,128)S(1)} fusion(f32[768,512,1]{1,0,2:T(8,128)} %fusion.58, f32[768,512,1]{1,0,2:T(8,128)} %fusion.60, f32[768,512,1]{1,0,2:T(8,128)} %fusion.62, bf16[2,512,256]{1,2,0:T(8,128)(2,1)} %get-tuple-element.49, bf16[2,512,256]{1,2,0:T(8,128)(2,1)} %get-tuple-element.48, ...), kind=kOutput, calls=%fused_computation.12 | convolution fusion | flops 816447488 | bytes 8912896 | tf_op jit(solution)/shard_map/mpc,mpd->cd/dot_general | solution.py:62
  195.6 1.8 copy-done
  198.5 2.8 %collective-permute-done.34 = bf16[2,2,2,2,56,512]{5,4,3,2,1,0:T(8,128)(2,1)} collective-permute-done((bf16[2,2,2,2,56,512]{5,4,3,2,1,0:T(8,128)(2,1)}, bf16[2,2,2,2,56,512]{5,4,3,2,1,0:T(8,128)(2,1)}, u32[]{:S(2)}, u32[]{:S(2)}) %collective-permute-start.34) | collective-permute-done | bytes 917536 | tf_op jit(solution)/shard_map/ppermute | solution.py:159
  201.3 2.8 %fusion.1 = f32[2,2,2,2,56,512]{5,4,3,2,1,0:T(8,128)S(1)} fusion(bf16[2,2,2,2,56,512]{5,4,3,2,1,0:T(8,128)(2,1)} %collective-permute-done.34, f32[2,2,2,2,2,56,512]{6,5,4,3,2,1,0:T(8,128)} %copy-done, pred[]{:T(512)S(6)} %eq.23), kind=kLoop, calls=%fused_computation.5 | loop fusion | flops 1376256 | bytes 6422529 | tf_op jit(solution)/shard_map/add | solution.py:161
  205.4 2.2 collective-permute-start.32
  207.6 3.5 %collective-permute-start.33 = (bf16[2,128,256]{2,1,0:T(8,128)(2,1)S(1)}, bf16[2,128,256]{2,1,0:T(8,128)(2,1)S(1)}, u32[]{:S(2)}, u32[]{:S(2)}) collective-permute-start(bf16[2,128,256]{2,1,0:T(8,128)(2,1)S(1)} %get-tuple-element.39), channel_id=1, source_target_pairs={{1,0},{2,1},{3,2},{4,3},{5,4},{6,5},{7,6},{8,7},{9,8},{10,9},{11,1... | collective-permute-start | bytes 393224 | tf_op jit(solution)/shard_map/ppermute | solution.py:15
  211.2 6.6 %collective-permute-done.35 = bf16[2,2,2,56,512]{4,3,2,1,0:T(8,128)(2,1)S(1)} collective-permute-done((bf16[2,2,2,56,512]{4,3,2,1,0:T(8,128)(2,1)S(1)}, bf16[2,2,2,56,512]{4,3,2,1,0:T(8,128)(2,1)S(1)}, u32[]{:S(2)}, u32[]{:S(2)}) %collective-permute-start.35) | collective-permute-done | bytes 458784 | tf_op jit(solution)/shard_map/ppermute | solution.py:159
  218.0 2.0 collective-permute-start.36
  220.0 1.3 fusion.70
  221.3 2.9 %collective-permute-done.36 = bf16[2,2,56,512]{3,2,1,0:T(8,128)(2,1)S(1)} collective-permute-done((bf16[2,2,56,512]{3,2,1,0:T(8,128)(2,1)S(1)}, bf16[2,2,56,512]{3,2,1,0:T(8,128)(2,1)S(1)}, u32[]{:S(2)}, u32[]{:S(2)}) %collective-permute-start.36) | collective-permute-done | bytes 229408 | tf_op jit(solution)/shard_map/ppermute | solution.py:159
  224.7 6.1 %collective-permute-done.37 = bf16[2,56,512]{2,1,0:T(8,128)(2,1)S(1)} collective-permute-done((bf16[2,56,512]{2,1,0:T(8,128)(2,1)S(1)}, bf16[2,56,512]{2,1,0:T(8,128)(2,1)S(1)}, u32[]{:S(2)}, u32[]{:S(2)}) %collective-permute-start.37) | collective-permute-done | bytes 114720 | tf_op jit(solution)/shard_map/ppermute | solution.py:159
  230.9 3.6 %collective-permute-start.38 = (bf16[56,512]{1,0:T(8,128)(2,1)S(1)}, bf16[56,512]{1,0:T(8,128)(2,1)S(1)}, u32[]{:S(2)}, u32[]{:S(2)}) collective-permute-start(bf16[56,512]{1,0:T(8,128)(2,1)S(1)} %fusion.221), channel_id=1, source_target_pairs={{0,16},{1,17},{2,18},{3,19},{4,20},{5,21},{6,22},{7,23},{8,24},{9,... | collective-permute-start | bytes 172040 | tf_op jit(solution)/shard_map/ppermute | solution.py:159
  234.5 1.2 fusion.18
  (185 shorter events, 40.0 us)
Async XLA Ops:
  0.6 9.6 %copy-start.4 = (bf16[1,2,3,256,512]{4,3,2,1,0:T(8,128)(2,1)S(1)}, bf16[1,2,3,256,512]{4,3,2,1,0:T(8,128)(2,1)}, u32[]{:S(2)}) copy-start(bf16[1,2,3,256,512]{4,3,2,1,0:T(8,128)(2,1)} %param.6) | copy-start | bytes 4718596
  2.5 13.4 %collective-permute-start = (bf16[2,128,256]{2,1,0:T(8,128)(2,1)}, bf16[2,128,256]{2,1,0:T(8,128)(2,1)}, u32[]{:S(2)}, u32[]{:S(2)}) collective-permute-start(bf16[2,128,256]{2,1,0:T(8,128)(2,1)} %get-tuple-element.111), channel_id=1, source_target_pairs={{0,1},{1,2},{2,3},{3,4},{4,5},{5,6},{6,7},{7,8},{8,9},{9,10},{10,1... | collective-permute-start | bytes 393224 | tf_op jit(solution)/shard_map/ppermute | solution.py:15
  4.4 6.0 %copy-start.3 = (bf16[1,2,512,256]{3,2,1,0:T(8,128)(2,1)S(1)}, bf16[1,2,512,256]{3,2,1,0:T(8,128)(2,1)}, u32[]{:S(2)}) copy-start(bf16[1,2,512,256]{3,2,1,0:T(8,128)(2,1)} %param.4) | copy-start | bytes 1572868
  4.4 13.1 %collective-permute-start.1 = (bf16[2,128,256]{2,1,0:T(8,128)(2,1)}, bf16[2,128,256]{2,1,0:T(8,128)(2,1)S(1)}, u32[]{:S(2)}, u32[]{:S(2)}) collective-permute-start(bf16[2,128,256]{2,1,0:T(8,128)(2,1)} %get-tuple-element.110), channel_id=1, source_target_pairs={{1,0},{2,1},{3,2},{4,3},{5,4},{6,5},{7,6},{8,7},{9,8},{10,9},{11,1... | collective-permute-start | bytes 393224 | tf_op jit(solution)/shard_map/ppermute | solution.py:15
  14.7 2.8 %copy-start.2 = (f32[2,512,512]{1,2,0:T(8,128)S(1)}, f32[2,512,512]{1,2,0:T(8,128)}, u32[]{:S(2)}) copy-start(f32[2,512,512]{1,2,0:T(8,128)} %fusion.178) | copy-start | bytes 6291460
  14.7 2.8 %copy-start.5 = (bf16[1,2,3,256,512]{4,3,2,1,0:T(8,128)(2,1)S(1)}, bf16[1,2,3,256,512]{4,3,2,1,0:T(8,128)(2,1)}, u32[]{:S(2)}) copy-start(bf16[1,2,3,256,512]{4,3,2,1,0:T(8,128)(2,1)} %param.6) | copy-start | bytes 4718596
  20.4 15.7 %collective-permute-start.2 = (bf16[2,512,256]{2,1,0:T(8,128)(2,1)S(1)}, bf16[2,512,256]{2,1,0:T(8,128)(2,1)S(1)}, u32[]{:S(2)}, u32[]{:S(2)}) collective-permute-start(bf16[2,512,256]{2,1,0:T(8,128)(2,1)S(1)} %fusion.2), channel_id=1, source_target_pairs={{0,2},{1,3},{2,4},{3,5},{4,6},{5,7},{6,8},{7,9},{8,10},{9,11},{10,... | collective-permute-start | bytes 1572872 | tf_op jit(solution)/shard_map/ppermute | solution.py:15
  26.0 15.4 %collective-permute-start.3 = (bf16[2,512,256]{2,1,0:T(8,128)(2,1)S(1)}, bf16[2,512,256]{2,1,0:T(8,128)(2,1)S(1)}, u32[]{:S(2)}, u32[]{:S(2)}) collective-permute-start(bf16[2,512,256]{2,1,0:T(8,128)(2,1)S(1)} %fusion.2), channel_id=1, source_target_pairs={{2,0},{3,1},{4,2},{5,3},{6,4},{7,5},{8,6},{9,7},{10,8},{11,9},{12,... | collective-permute-start | bytes 1572872 | tf_op jit(solution)/shard_map/ppermute | solution.py:15
  43.7 14.0 %collective-permute-start.5 = (bf16[2,256,256]{2,1,0:T(8,128)(2,1)S(1)}, bf16[2,256,256]{2,1,0:T(8,128)(2,1)S(1)}, u32[]{:S(2)}, u32[]{:S(2)}) collective-permute-start(bf16[2,256,256]{2,1,0:T(8,128)(2,1)S(1)} %get-tuple-element.75), channel_id=1, source_target_pairs={{0,2},{1,3},{2,4},{3,5},{4,6},{5,7},{6,8},{7,9},{8,10},{9,11},{10,... | collective-permute-start | bytes 786440 | tf_op jit(solution)/shard_map/ppermute | solution.py:15
  45.6 12.0 %collective-permute-start.4 = (bf16[2,256,256]{2,1,0:T(8,128)(2,1)S(1)}, bf16[2,256,256]{2,1,0:T(8,128)(2,1)S(1)}, u32[]{:S(2)}, u32[]{:S(2)}) collective-permute-start(bf16[2,256,256]{2,1,0:T(8,128)(2,1)S(1)} %get-tuple-element.74), channel_id=1, source_target_pairs={{2,0},{3,1},{4,2},{5,3},{6,4},{7,5},{8,6},{9,7},{10,8},{11,9},{12,... | collective-permute-start | bytes 786440 | tf_op jit(solution)/shard_map/ppermute | solution.py:15
  49.6 6.7 %copy-start.26 = (bf16[2,256,256]{2,1,0:T(8,128)(2,1)S(1)}, bf16[2,256,256]{2,1,0:T(8,128)(2,1)}, u32[]{:S(2)}) copy-start(bf16[2,256,256]{2,1,0:T(8,128)(2,1)} %slice.1184) | copy-start | bytes 786436
  50.3 8.3 %collective-permute-start.7 = (bf16[2,256,256]{2,1,0:T(8,128)(2,1)S(1)}, bf16[2,256,256]{2,1,0:T(8,128)(2,1)S(1)}, u32[]{:S(2)}, u32[]{:S(2)}) collective-permute-start(bf16[2,256,256]{2,1,0:T(8,128)(2,1)S(1)} %get-tuple-element.73), channel_id=1, source_target_pairs={{0,2},{1,3},{2,4},{3,5},{4,6},{5,7},{6,8},{7,9},{8,10},{9,11},{10,... | collective-permute-start | bytes 786440 | tf_op jit(solution)/shard_map/ppermute | solution.py:15
  54.3 10.4 %collective-permute-start.6 = (bf16[2,256,256]{2,1,0:T(8,128)(2,1)S(1)}, bf16[2,256,256]{2,1,0:T(8,128)(2,1)S(1)}, u32[]{:S(2)}, u32[]{:S(2)}) collective-permute-start(bf16[2,256,256]{2,1,0:T(8,128)(2,1)S(1)} %get-tuple-element.72), channel_id=1, source_target_pairs={{2,0},{3,1},{4,2},{5,3},{6,4},{7,5},{8,6},{9,7},{10,8},{11,9},{12,... | collective-permute-start | bytes 786440 | tf_op jit(solution)/shard_map/ppermute | solution.py:15
  66.6 8.1 %copy-start.14 = (bf16[2,384,256]{2,1,0:T(8,128)(2,1)S(1)}, bf16[2,384,256]{2,1,0:T(8,128)(2,1)}, u32[]{:S(2)}) copy-start(bf16[2,384,256]{2,1,0:T(8,128)(2,1)} %get-tuple-element.108) | copy-start | bytes 1179652
  66.6 8.1 %copy-start.15 = (bf16[2,384,256]{2,1,0:T(8,128)(2,1)S(1)}, bf16[2,384,256]{2,1,0:T(8,128)(2,1)}, u32[]{:S(2)}) copy-start(bf16[2,384,256]{2,1,0:T(8,128)(2,1)} %get-tuple-element.109) | copy-start | bytes 1179652
  66.6 11.2 %collective-permute-start.8 = (bf16[2,128,256]{2,1,0:T(8,128)(2,1)S(1)}, bf16[2,128,256]{2,1,0:T(8,128)(2,1)S(1)}, u32[]{:S(2)}, u32[]{:S(2)}) collective-permute-start(bf16[2,128,256]{2,1,0:T(8,128)(2,1)S(1)} %get-tuple-element.44), channel_id=1, source_target_pairs={{0,1},{1,2},{2,3},{3,4},{4,5},{5,6},{6,7},{7,8},{8,9},{9,10},{10,1... | collective-permute-start | bytes 393224 | tf_op jit(solution)/shard_map/ppermute | solution.py:15
  68.7 9.1 %collective-permute-start.9 = (bf16[2,128,256]{2,1,0:T(8,128)(2,1)S(1)}, bf16[2,128,256]{2,1,0:T(8,128)(2,1)S(1)}, u32[]{:S(2)}, u32[]{:S(2)}) collective-permute-start(bf16[2,128,256]{2,1,0:T(8,128)(2,1)S(1)} %get-tuple-element.45), channel_id=1, source_target_pairs={{1,0},{2,1},{3,2},{4,3},{5,4},{6,5},{7,6},{8,7},{9,8},{10,9},{11,1... | collective-permute-start | bytes 393224 | tf_op jit(solution)/shard_map/ppermute | solution.py:15
  73.4 8.9 %collective-permute-start.13 = (bf16[2,256,256]{2,1,0:T(8,128)(2,1)S(1)}, bf16[2,256,256]{2,1,0:T(8,128)(2,1)S(1)}, u32[]{:S(2)}, u32[]{:S(2)}) collective-permute-start(bf16[2,256,256]{2,1,0:T(8,128)(2,1)S(1)} %get-tuple-element.7), channel_id=1, source_target_pairs={{32,0},{64,32},{96,64},{33,1},{65,33},{97,65},{34,2},{66,34},{98,6... | collective-permute-start | bytes 786440 | tf_op jit(solution)/shard_map/ppermute | solution.py:15
  78.8 10.3 %collective-permute-start.10 = (bf16[2,256,256]{2,1,0:T(8,128)(2,1)S(1)}, bf16[2,256,256]{2,1,0:T(8,128)(2,1)S(1)}, u32[]{:S(2)}, u32[]{:S(2)}) collective-permute-start(bf16[2,256,256]{2,1,0:T(8,128)(2,1)S(1)} %pad_maximum_fusion.30), channel_id=1, source_target_pairs={{32,0},{64,32},{96,64},{33,1},{65,33},{97,65},{34,2},{66,34},{98,6... | collective-permute-start | bytes 786440 | tf_op jit(solution)/shard_map/ppermute | solution.py:15
  83.2 16.0 %collective-permute-start.15 = (bf16[2,256,256]{2,1,0:T(8,128)(2,1)S(1)}, bf16[2,256,256]{2,1,0:T(8,128)(2,1)S(1)}, u32[]{:S(2)}, u32[]{:S(2)}) collective-permute-start(bf16[2,256,256]{2,1,0:T(8,128)(2,1)S(1)} %get-tuple-element.69), channel_id=1, source_target_pairs={{0,2},{1,3},{2,4},{3,5},{4,6},{5,7},{6,8},{7,9},{8,10},{9,11},{10,... | collective-permute-start | bytes 786440 | tf_op jit(solution)/shard_map/ppermute | solution.py:15
  87.2 12.0 %collective-permute-start.14 = (bf16[2,256,256]{2,1,0:T(8,128)(2,1)S(1)}, bf16[2,256,256]{2,1,0:T(8,128)(2,1)S(1)}, u32[]{:S(2)}, u32[]{:S(2)}) collective-permute-start(bf16[2,256,256]{2,1,0:T(8,128)(2,1)S(1)} %get-tuple-element.68), channel_id=1, source_target_pairs={{2,0},{3,1},{4,2},{5,3},{6,4},{7,5},{8,6},{9,7},{10,8},{11,9},{12,... | collective-permute-start | bytes 786440 | tf_op jit(solution)/shard_map/ppermute | solution.py:15
  90.1 9.9 %collective-permute-start.12 = (bf16[2,256,256]{2,1,0:T(8,128)(2,1)S(1)}, bf16[2,256,256]{2,1,0:T(8,128)(2,1)S(1)}, u32[]{:S(2)}, u32[]{:S(2)}) collective-permute-start(bf16[2,256,256]{2,1,0:T(8,128)(2,1)S(1)} %get-tuple-element.71), channel_id=1, source_target_pairs={{0,2},{1,3},{2,4},{3,5},{4,6},{5,7},{6,8},{7,9},{8,10},{9,11},{10,... | collective-permute-start | bytes 786440 | tf_op jit(solution)/shard_map/ppermute | solution.py:15
  96.2 10.4 %collective-permute-start.11 = (bf16[2,256,256]{2,1,0:T(8,128)(2,1)S(1)}, bf16[2,256,256]{2,1,0:T(8,128)(2,1)S(1)}, u32[]{:S(2)}, u32[]{:S(2)}) collective-permute-start(bf16[2,256,256]{2,1,0:T(8,128)(2,1)S(1)} %get-tuple-element.70), channel_id=1, source_target_pairs={{2,0},{3,1},{4,2},{5,3},{6,4},{7,5},{8,6},{9,7},{10,8},{11,9},{12,... | collective-permute-start | bytes 786440 | tf_op jit(solution)/shard_map/ppermute | solution.py:15
  108.1 11.4 %collective-permute-start.16 = (bf16[2,128,256]{2,1,0:T(8,128)(2,1)S(1)}, bf16[2,128,256]{2,1,0:T(8,128)(2,1)S(1)}, u32[]{:S(2)}, u32[]{:S(2)}) collective-permute-start(bf16[2,128,256]{2,1,0:T(8,128)(2,1)S(1)} %get-tuple-element.42), channel_id=1, source_target_pairs={{0,1},{1,2},{2,3},{3,4},{4,5},{5,6},{6,7},{7,8},{8,9},{9,10},{10,1... | collective-permute-start | bytes 393224 | tf_op jit(solution)/shard_map/ppermute | solution.py:15
  110.0 9.5 %collective-permute-start.17 = (bf16[2,128,256]{2,1,0:T(8,128)(2,1)S(1)}, bf16[2,128,256]{2,1,0:T(8,128)(2,1)S(1)}, u32[]{:S(2)}, u32[]{:S(2)}) collective-permute-start(bf16[2,128,256]{2,1,0:T(8,128)(2,1)S(1)} %get-tuple-element.43), channel_id=1, source_target_pairs={{1,0},{2,1},{3,2},{4,3},{5,4},{6,5},{7,6},{8,7},{9,8},{10,9},{11,1... | collective-permute-start | bytes 393224 | tf_op jit(solution)/shard_map/ppermute | solution.py:15
  114.8 8.9 %collective-permute-start.21 = (bf16[2,256,256]{2,1,0:T(8,128)(2,1)S(1)}, bf16[2,256,256]{2,1,0:T(8,128)(2,1)S(1)}, u32[]{:S(2)}, u32[]{:S(2)}) collective-permute-start(bf16[2,256,256]{2,1,0:T(8,128)(2,1)S(1)} %get-tuple-element.5), channel_id=1, source_target_pairs={{32,0},{64,32},{96,64},{33,1},{65,33},{97,65},{34,2},{66,34},{98,6... | collective-permute-start | bytes 786440 | tf_op jit(solution)/shard_map/ppermute | solution.py:15
  120.4 10.0 %collective-permute-start.18 = (bf16[2,256,256]{2,1,0:T(8,128)(2,1)S(1)}, bf16[2,256,256]{2,1,0:T(8,128)(2,1)S(1)}, u32[]{:S(2)}, u32[]{:S(2)}) collective-permute-start(bf16[2,256,256]{2,1,0:T(8,128)(2,1)S(1)} %pad_maximum_fusion.31), channel_id=1, source_target_pairs={{32,0},{64,32},{96,64},{33,1},{65,33},{97,65},{34,2},{66,34},{98,6... | collective-permute-start | bytes 786440 | tf_op jit(solution)/shard_map/ppermute | solution.py:15
  124.6 16.1 %collective-permute-start.23 = (bf16[2,256,256]{2,1,0:T(8,128)(2,1)S(1)}, bf16[2,256,256]{2,1,0:T(8,128)(2,1)S(1)}, u32[]{:S(2)}, u32[]{:S(2)}) collective-permute-start(bf16[2,256,256]{2,1,0:T(8,128)(2,1)S(1)} %get-tuple-element.65), channel_id=1, source_target_pairs={{0,2},{1,3},{2,4},{3,5},{4,6},{5,7},{6,8},{7,9},{8,10},{9,11},{10,... | collective-permute-start | bytes 786440 | tf_op jit(solution)/shard_map/ppermute | solution.py:15
  128.3 12.3 %collective-permute-start.22 = (bf16[2,256,256]{2,1,0:T(8,128)(2,1)S(1)}, bf16[2,256,256]{2,1,0:T(8,128)(2,1)S(1)}, u32[]{:S(2)}, u32[]{:S(2)}) collective-permute-start(bf16[2,256,256]{2,1,0:T(8,128)(2,1)S(1)} %get-tuple-element.64), channel_id=1, source_target_pairs={{2,0},{3,1},{4,2},{5,3},{6,4},{7,5},{8,6},{9,7},{10,8},{11,9},{12,... | collective-permute-start | bytes 786440 | tf_op jit(solution)/shard_map/ppermute | solution.py:15
  131.4 9.7 %collective-permute-start.20 = (bf16[2,256,256]{2,1,0:T(8,128)(2,1)S(1)}, bf16[2,256,256]{2,1,0:T(8,128)(2,1)S(1)}, u32[]{:S(2)}, u32[]{:S(2)}) collective-permute-start(bf16[2,256,256]{2,1,0:T(8,128)(2,1)S(1)} %get-tuple-element.67), channel_id=1, source_target_pairs={{0,2},{1,3},{2,4},{3,5},{4,6},{5,7},{6,8},{7,9},{8,10},{9,11},{10,... | collective-permute-start | bytes 786440 | tf_op jit(solution)/shard_map/ppermute | solution.py:15
  137.3 10.4 %collective-permute-start.19 = (bf16[2,256,256]{2,1,0:T(8,128)(2,1)S(1)}, bf16[2,256,256]{2,1,0:T(8,128)(2,1)S(1)}, u32[]{:S(2)}, u32[]{:S(2)}) collective-permute-start(bf16[2,256,256]{2,1,0:T(8,128)(2,1)S(1)} %get-tuple-element.66), channel_id=1, source_target_pairs={{2,0},{3,1},{4,2},{5,3},{6,4},{7,5},{8,6},{9,7},{10,8},{11,9},{12,... | collective-permute-start | bytes 786440 | tf_op jit(solution)/shard_map/ppermute | solution.py:15
  149.2 11.6 %collective-permute-start.24 = (bf16[2,128,256]{2,1,0:T(8,128)(2,1)S(1)}, bf16[2,128,256]{2,1,0:T(8,128)(2,1)S(1)}, u32[]{:S(2)}, u32[]{:S(2)}) collective-permute-start(bf16[2,128,256]{2,1,0:T(8,128)(2,1)S(1)} %get-tuple-element.40), channel_id=1, source_target_pairs={{0,1},{1,2},{2,3},{3,4},{4,5},{5,6},{6,7},{7,8},{8,9},{9,10},{10,1... | collective-permute-start | bytes 393224 | tf_op jit(solution)/shard_map/ppermute | solution.py:15
  151.2 9.7 %collective-permute-start.25 = (bf16[2,128,256]{2,1,0:T(8,128)(2,1)S(1)}, bf16[2,128,256]{2,1,0:T(8,128)(2,1)S(1)}, u32[]{:S(2)}, u32[]{:S(2)}) collective-permute-start(bf16[2,128,256]{2,1,0:T(8,128)(2,1)S(1)} %get-tuple-element.41), channel_id=1, source_target_pairs={{1,0},{2,1},{3,2},{4,3},{5,4},{6,5},{7,6},{8,7},{9,8},{10,9},{11,1... | collective-permute-start | bytes 393224 | tf_op jit(solution)/shard_map/ppermute | solution.py:15
  155.9 8.9 %collective-permute-start.29 = (bf16[2,256,256]{2,1,0:T(8,128)(2,1)S(1)}, bf16[2,256,256]{2,1,0:T(8,128)(2,1)S(1)}, u32[]{:S(2)}, u32[]{:S(2)}) collective-permute-start(bf16[2,256,256]{2,1,0:T(8,128)(2,1)S(1)} %get-tuple-element.3), channel_id=1, source_target_pairs={{32,0},{64,32},{96,64},{33,1},{65,33},{97,65},{34,2},{66,34},{98,6... | collective-permute-start | bytes 786440 | tf_op jit(solution)/shard_map/ppermute | solution.py:15
  161.8 9.7 %collective-permute-start.26 = (bf16[2,256,256]{2,1,0:T(8,128)(2,1)S(1)}, bf16[2,256,256]{2,1,0:T(8,128)(2,1)S(1)}, u32[]{:S(2)}, u32[]{:S(2)}) collective-permute-start(bf16[2,256,256]{2,1,0:T(8,128)(2,1)S(1)} %pad_maximum_fusion.32), channel_id=1, source_target_pairs={{32,0},{64,32},{96,64},{33,1},{65,33},{97,65},{34,2},{66,34},{98,6... | collective-permute-start | bytes 786440 | tf_op jit(solution)/shard_map/ppermute | solution.py:15
  165.6 17.4 %copy-start.6 = (f32[2,256,768]{2,1,0:T(8,128)}, f32[2,256,768]{2,1,0:T(8,128)S(1)}, u32[]{:S(2)}) copy-start(f32[2,256,768]{2,1,0:T(8,128)S(1)} %get-tuple-element.141) | copy-start | bytes 4718596
  165.7 17.3 %collective-permute-start.31 = (bf16[2,256,256]{2,1,0:T(8,128)(2,1)S(1)}, bf16[2,256,256]{2,1,0:T(8,128)(2,1)S(1)}, u32[]{:S(2)}, u32[]{:S(2)}) collective-permute-start(bf16[2,256,256]{2,1,0:T(8,128)(2,1)S(1)} %get-tuple-element.61), channel_id=1, source_target_pairs={{0,2},{1,3},{2,4},{3,5},{4,6},{5,7},{6,8},{7,9},{8,10},{9,11},{10,... | collective-permute-start | bytes 786440 | tf_op jit(solution)/shard_map/ppermute | solution.py:15
  169.1 13.9 %collective-permute-start.30 = (bf16[2,256,256]{2,1,0:T(8,128)(2,1)S(1)}, bf16[2,256,256]{2,1,0:T(8,128)(2,1)S(1)}, u32[]{:S(2)}, u32[]{:S(2)}) collective-permute-start(bf16[2,256,256]{2,1,0:T(8,128)(2,1)S(1)} %get-tuple-element.60), channel_id=1, source_target_pairs={{2,0},{3,1},{4,2},{5,3},{6,4},{7,5},{8,6},{9,7},{10,8},{11,9},{12,... | collective-permute-start | bytes 786440 | tf_op jit(solution)/shard_map/ppermute | solution.py:15
  172.6 10.6 %collective-permute-start.28 = (bf16[2,256,256]{2,1,0:T(8,128)(2,1)S(1)}, bf16[2,256,256]{2,1,0:T(8,128)(2,1)S(1)}, u32[]{:S(2)}, u32[]{:S(2)}) collective-permute-start(bf16[2,256,256]{2,1,0:T(8,128)(2,1)S(1)} %get-tuple-element.63), channel_id=1, source_target_pairs={{0,2},{1,3},{2,4},{3,5},{4,6},{5,7},{6,8},{7,9},{8,10},{9,11},{10,... | collective-permute-start | bytes 786440 | tf_op jit(solution)/shard_map/ppermute | solution.py:15
  178.2 10.4 %collective-permute-start.27 = (bf16[2,256,256]{2,1,0:T(8,128)(2,1)S(1)}, bf16[2,256,256]{2,1,0:T(8,128)(2,1)S(1)}, u32[]{:S(2)}, u32[]{:S(2)}) collective-permute-start(bf16[2,256,256]{2,1,0:T(8,128)(2,1)S(1)} %get-tuple-element.62), channel_id=1, source_target_pairs={{2,0},{3,1},{4,2},{5,3},{6,4},{7,5},{8,6},{9,7},{10,8},{11,9},{12,... | collective-permute-start | bytes 786440 | tf_op jit(solution)/shard_map/ppermute | solution.py:15
  183.0 7.1 %copy-start.22 = (bf16[2,256,256]{2,1,0:T(8,128)(2,1)}, bf16[2,256,256]{2,1,0:T(8,128)(2,1)S(1)}, u32[]{:S(2)}) copy-start(bf16[2,256,256]{2,1,0:T(8,128)(2,1)S(1)} %collective-permute-done.31) | copy-start | bytes 786436
  183.0 7.1 %copy-start.24 = (bf16[2,256,256]{2,1,0:T(8,128)(2,1)}, bf16[2,256,256]{2,1,0:T(8,128)(2,1)S(1)}, u32[]{:S(2)}) copy-start(bf16[2,256,256]{2,1,0:T(8,128)(2,1)S(1)} %collective-permute-done.30) | copy-start | bytes 786436
  190.9 4.1 %copy-start.13 = (f32[768,512]{1,0:T(8,128)S(1)}, f32[768,512]{1,0:T(8,128)}, u32[]{:S(2)}) copy-start(f32[768,512]{1,0:T(8,128)} %bitcast_add_fusion) | copy-start | bytes 4718596
  195.6 1.9 copy-start
  198.5 2.8 %collective-permute-start.34 = (bf16[2,2,2,2,56,512]{5,4,3,2,1,0:T(8,128)(2,1)}, bf16[2,2,2,2,56,512]{5,4,3,2,1,0:T(8,128)(2,1)}, u32[]{:S(2)}, u32[]{:S(2)}) collective-permute-start(bf16[2,2,2,2,56,512]{5,4,3,2,1,0:T(8,128)(2,1)} %fusion.52), channel_id=1, source_target_pairs={{0,1},{1,0},{2,3},{3,2},{4,5},{5,4},{6,7},{7,6},{8,9},{9,8},{10,11... | collective-permute-start | bytes 2752520 | tf_op jit(solution)/shard_map/ppermute | solution.py:159
  198.5 5.8 %copy-start.11 = (bf16[2,512,256]{1,2,0:T(8,128)(2,1)S(1)}, bf16[2,512,256]{1,2,0:T(8,128)(2,1)}, u32[]{:S(2)}) copy-start(bf16[2,512,256]{1,2,0:T(8,128)(2,1)} %get-tuple-element.48) | copy-start | bytes 1572868
  198.5 5.9 %copy-start.12 = (bf16[2,512,256]{1,2,0:T(8,128)(2,1)S(1)}, bf16[2,512,256]{1,2,0:T(8,128)(2,1)}, u32[]{:S(2)}) copy-start(bf16[2,512,256]{1,2,0:T(8,128)(2,1)} %get-tuple-element.49) | copy-start | bytes 1572868
  204.2 13.5 %collective-permute-start.35 = (bf16[2,2,2,56,512]{4,3,2,1,0:T(8,128)(2,1)S(1)}, bf16[2,2,2,56,512]{4,3,2,1,0:T(8,128)(2,1)S(1)}, u32[]{:S(2)}, u32[]{:S(2)}) collective-permute-start(bf16[2,2,2,56,512]{4,3,2,1,0:T(8,128)(2,1)S(1)} %fusion.139), channel_id=1, source_target_pairs={{0,2},{1,3},{2,0},{3,1},{4,6},{5,7},{6,4},{7,5},{8,10},{9,11},{10,... | collective-permute-start | bytes 1376264 | tf_op jit(solution)/shard_map/ppermute | solution.py:159
  205.4 14.6 %copy-start.23 = (bf16[2,256,256]{2,1,0:T(8,128)(2,1)S(1)}, bf16[2,256,256]{2,1,0:T(8,128)(2,1)}, u32[]{:S(2)}) copy-start(bf16[2,256,256]{2,1,0:T(8,128)(2,1)} %copy-done.22) | copy-start | bytes 786436
  205.4 14.6 %copy-start.25 = (bf16[2,256,256]{2,1,0:T(8,128)(2,1)S(1)}, bf16[2,256,256]{2,1,0:T(8,128)(2,1)}, u32[]{:S(2)}) copy-start(bf16[2,256,256]{2,1,0:T(8,128)(2,1)} %copy-done.24) | copy-start | bytes 786436
  205.4 19.1 %collective-permute-start.32 = (bf16[2,128,256]{2,1,0:T(8,128)(2,1)S(1)}, bf16[2,128,256]{2,1,0:T(8,128)(2,1)S(1)}, u32[]{:S(2)}, u32[]{:S(2)}) collective-permute-start(bf16[2,128,256]{2,1,0:T(8,128)(2,1)S(1)} %get-tuple-element.38), channel_id=1, source_target_pairs={{0,1},{1,2},{2,3},{3,4},{4,5},{5,6},{6,7},{7,8},{8,9},{9,10},{10,1... | collective-permute-start | bytes 393224 | tf_op jit(solution)/shard_map/ppermute | solution.py:15
  207.6 16.9 %collective-permute-start.33 = (bf16[2,128,256]{2,1,0:T(8,128)(2,1)S(1)}, bf16[2,128,256]{2,1,0:T(8,128)(2,1)S(1)}, u32[]{:S(2)}, u32[]{:S(2)}) collective-permute-start(bf16[2,128,256]{2,1,0:T(8,128)(2,1)S(1)} %get-tuple-element.39), channel_id=1, source_target_pairs={{1,0},{2,1},{3,2},{4,3},{5,4},{6,5},{7,6},{8,7},{9,8},{10,9},{11,1... | collective-permute-start | bytes 393224 | tf_op jit(solution)/shard_map/ppermute | solution.py:15
  218.0 6.2 %collective-permute-start.36 = (bf16[2,2,56,512]{3,2,1,0:T(8,128)(2,1)S(1)}, bf16[2,2,56,512]{3,2,1,0:T(8,128)(2,1)S(1)}, u32[]{:S(2)}, u32[]{:S(2)}) collective-permute-start(bf16[2,2,56,512]{3,2,1,0:T(8,128)(2,1)S(1)} %fusion.187), channel_id=1, source_target_pairs={{0,8},{1,9},{2,10},{3,11},{4,12},{5,13},{6,14},{7,15},{8,0},{9,1},... | collective-permute-start | bytes 688136 | tf_op jit(solution)/shard_map/ppermute | solution.py:159
  224.3 10.1 %copy-start.8 = (f32[2,256,256]{2,1,0:T(8,128)S(1)}, f32[2,256,256]{2,1,0:T(8,128)}, u32[]{:S(2)}) copy-start(f32[2,256,256]{2,1,0:T(8,128)} %get-tuple-element.8) | copy-start | bytes 1572868
  224.3 10.1 %copy-start.9 = (f32[2,256,256]{2,1,0:T(8,128)S(1)}, f32[2,256,256]{2,1,0:T(8,128)}, u32[]{:S(2)}) copy-start(f32[2,256,256]{2,1,0:T(8,128)} %get-tuple-element.6) | copy-start | bytes 1572868
  224.4 10.1 %copy-start.10 = (f32[2,256,256]{2,1,0:T(8,128)S(1)}, f32[2,256,256]{2,1,0:T(8,128)}, u32[]{:S(2)}) copy-start(f32[2,256,256]{2,1,0:T(8,128)} %get-tuple-element.4) | copy-start | bytes 1572868
  224.4 10.1 %copy-start.16 = (f32[1,2,128,256]{3,2,1,0:T(8,128)S(1)}, f32[1,2,128,256]{3,2,1,0:T(8,128)}, u32[]{:S(2)}) copy-start(f32[1,2,128,256]{3,2,1,0:T(8,128)} %get-tuple-element.22) | copy-start | bytes 786436
  224.4 10.1 %copy-start.17 = (f32[1,2,128,256]{3,2,1,0:T(8,128)S(1)}, f32[1,2,128,256]{3,2,1,0:T(8,128)}, u32[]{:S(2)}) copy-start(f32[1,2,128,256]{3,2,1,0:T(8,128)} %get-tuple-element.31) | copy-start | bytes 786436
  224.4 10.1 %copy-start.18 = (f32[1,2,128,256]{3,2,1,0:T(8,128)S(1)}, f32[1,2,128,256]{3,2,1,0:T(8,128)}, u32[]{:S(2)}) copy-start(f32[1,2,128,256]{3,2,1,0:T(8,128)} %get-tuple-element.18) | copy-start | bytes 786436
  224.4 10.1 %copy-start.19 = (f32[1,2,128,256]{3,2,1,0:T(8,128)S(1)}, f32[1,2,128,256]{3,2,1,0:T(8,128)}, u32[]{:S(2)}) copy-start(f32[1,2,128,256]{3,2,1,0:T(8,128)} %get-tuple-element.29) | copy-start | bytes 786436
  224.4 10.1 %copy-start.20 = (f32[1,2,128,256]{3,2,1,0:T(8,128)S(1)}, f32[1,2,128,256]{3,2,1,0:T(8,128)}, u32[]{:S(2)}) copy-start(f32[1,2,128,256]{3,2,1,0:T(8,128)} %get-tuple-element.14) | copy-start | bytes 786436
  224.4 10.1 %copy-start.21 = (f32[1,2,128,256]{3,2,1,0:T(8,128)S(1)}, f32[1,2,128,256]{3,2,1,0:T(8,128)}, u32[]{:S(2)}) copy-start(f32[1,2,128,256]{3,2,1,0:T(8,128)} %get-tuple-element.27) | copy-start | bytes 786436
  224.5 6.4 %collective-permute-start.37 = (bf16[2,56,512]{2,1,0:T(8,128)(2,1)S(1)}, bf16[2,56,512]{2,1,0:T(8,128)(2,1)S(1)}, u32[]{:S(2)}, u32[]{:S(2)}) collective-permute-start(bf16[2,56,512]{2,1,0:T(8,128)(2,1)S(1)} %fusion.215), channel_id=1, source_target_pairs={{0,4},{1,5},{2,6},{3,7},{4,0},{5,1},{6,2},{7,3},{8,12},{9,13},{10,... | collective-permute-start | bytes 344072 | tf_op jit(solution)/shard_map/ppermute | solution.py:159
  230.9 5.8 %collective-permute-start.38 = (bf16[56,512]{1,0:T(8,128)(2,1)S(1)}, bf16[56,512]{1,0:T(8,128)(2,1)S(1)}, u32[]{:S(2)}, u32[]{:S(2)}) collective-permute-start(bf16[56,512]{1,0:T(8,128)(2,1)S(1)} %fusion.221), channel_id=1, source_target_pairs={{0,16},{1,17},{2,18},{3,19},{4,20},{5,21},{6,22},{7,23},{8,24},{9,... | collective-permute-start | bytes 172040 | tf_op jit(solution)/shard_map/ppermute | solution.py:159
  (2 other events, 2.0 us)

commit v6 on v5

--- a/solution.py
+++ b/solution.py
@@ -177,11 +177,33 @@
     grad_scale = 1.0 / math.sqrt(batch_count * positions * seq_count)
 
     hidden = section_inputs[0]
-    stored = []
-    for layer in range(depth):
-        if layer == 0:
-            earlier, following = halo_sides(hidden, NEAR)
-        else:
+    width = NEAR
+    rows = hidden.shape[1]
+    from_low = shifted(hidden[:, rows - width :], "seq", 1)
+    from_high = shifted(hidden[:, :width], "seq", -1)
+    edge_parts = (
+        jnp.concatenate([from_low, hidden[:, rows - 2 * width : rows - width]], axis=1),
+        jnp.concatenate([hidden[:, :width], hidden[:, rows - width :]], axis=1),
+        jnp.concatenate([hidden[:, width : 2 * width], from_high], axis=1),
+    )
+    inner_parts = (
+        hidden[:, : rows - 2 * width],
+        hidden[:, width : rows - width],
+        hidden[:, 2 * width :],
+    )
+    pieces = []
+    for earlier, middle_rows, following in (edge_parts, inner_parts):
+        pieces.append(
+            forward_layer(middle_rows, earlier, following, conv_mat[0], out_mat[0], False)
+        )
+    saved0 = tuple(join_rows(e, i, width) for e, i in zip(pieces[0][1], pieces[1][1]))
+    stored = [saved0]
+    nxt = [p[0] for p in pieces]
+    earlier = join_rows(*[shifted(v, "seq", far_hops) for v in nxt], width)
+    following = join_rows(*[shifted(v, "seq", -far_hops) for v in nxt], width)
+    hidden = join_rows(nxt[0], nxt[1], width)
+    for layer in range(1, depth):
+        if layer > 1:
             earlier, following = far_sides(hidden, far_hops)
         hidden, saved = forward_layer(
             hidden, earlier, following, conv_mat[layer], out_mat[layer], layer + 1 == depth

time: 240 us -> 258 us (1.075)
  starting transfers between devices: 102 us -> 109 us
  waiting for transfers between devices: 63.4 us -> 67.3 us
  other arithmetic: 19.2 us -> 23 us
  matrix products: 41.9 us -> 45.2 us
    ppermute x34 -> x36, starting transfers between devices: 96.4 us -> 104 us  [shifted(): lax.ppermute(value, axis, [(source, source + steps) for source in range(l...]
    dot_general x7 -> x11, matrix products: 6.74 us -> 14.4 us  [mm(): return jnp.einsum('mpc,cd->mpd', a, b, preferred_element_type=jnp.float32)]
    ppermute x34 -> x36, waiting for transfers between devices: 44.1 us -> 48.2 us  [shifted(): lax.ppermute(value, axis, [(source, source + steps) for source in range(l...]
    dot_general x4, matrix products: 13.5 us -> 10.7 us  [backward_layer(): jnp.einsum('mpc,mpd->cd', taps, grad_pre, preferred_element_type=jnp.floa...]
  transfers between devices with their start and end apart: 39 -> 41, of which waited for: 17 -> 17; matrix products, arithmetic and copies ran while one was open for 19% -> 17% of each run, Pallas kernels for 0% -> 0%
where the time goes in v6:
time: 258 us; the launch traced here: 257 us
  starting transfers between devices  109 us (42%)
  waiting for transfers between devices  67.3 us (26%)
  matrix products  45.2 us (18%)
  other arithmetic  23 us (9%)
  local copies, waits for them, and re-layouts  10 us (4%)
    ppermute x36, starting transfers between devices, shifted(): lax.ppermute(value, axis, [(source, source + steps) for source in range(l...  104 us
    ppermute x36, waiting for transfers between devices, shifted(): lax.ppermute(value, axis, [(source, source + steps) for source in range(l...  48.2 us
    ppermute x5, waiting for transfers between devices, halving_scatter(): got = lax.ppermute(sends, 'seq', pairs)  19.1 us
    dot_general x11, matrix products, mm(): return jnp.einsum('mpc,cd->mpd', a, b, preferred_element_type=jnp.float32)  14.4 us
    dot_general x4, matrix products, backward_layer(): jnp.einsum('mpc,mpd->cd', taps, grad_pre, preferred_element_type=jnp.floa...  10.7 us
  transfers between devices with their start and end apart: 41, of which 17 were waited for; matrix products, arithmetic and copies ran while one was open for 17% of the time, Pallas kernels for 0%

profile of v6, /device:TPU:24, one launch (start us, length us, event | category | flops | bytes accessed | tf_op | source)
XLA Modules:
  0.0 257.0 jit_solution(3017268666755693744)
XLA Ops:
  0.6 1.4 fusion.201
  2.0 1.4 convolution_add_fusion.1
  6.0 3.5 %collective-permute-start.3 = (bf16[2,256,256]{2,1,0:T(8,128)(2,1)}, bf16[2,256,256]{2,1,0:T(8,128)(2,1)}, u32[]{:S(2)}, u32[]{:S(2)}) collective-permute-start(bf16[2,256,256]{2,1,0:T(8,128)(2,1)} %fusion.4), channel_id=1, source_target_pairs={{0,2},{1,3},{2,4},{3,5},{4,6},{5,7},{6,8},{7,9},{8,10},{9,11},{10,... | collective-permute-start | bytes 786440 | tf_op jit(solution)/shard_map/ppermute | solution.py:15
  9.5 2.4 collective-permute-start.5
  12.6 1.9 collective-permute-start.1
  14.6 2.4 collective-permute-start
  17.1 2.2 fusion.199
  24.2 1.4 fusion.189
  28.3 5.6 %collective-permute-start.2 = (bf16[2,256,256]{2,1,0:T(8,128)(2,1)S(1)}, bf16[2,256,256]{2,1,0:T(8,128)(2,1)S(1)}, u32[]{:S(2)}, u32[]{:S(2)}) collective-permute-start(bf16[2,256,256]{2,1,0:T(8,128)(2,1)S(1)} %fusion.3), channel_id=1, source_target_pairs={{0,2},{1,3},{2,4},{3,5},{4,6},{5,7},{6,8},{7,9},{8,10},{9,11},{10,... | collective-permute-start | bytes 786440 | tf_op jit(solution)/shard_map/ppermute | solution.py:15
  33.9 1.9 collective-permute-start.4
  36.0 1.5 fusion.102
  38.8 1.4 collective-permute-done.2
  40.1 6.2 %collective-permute-done.4 = bf16[2,256,256]{2,1,0:T(8,128)(2,1)S(1)} collective-permute-done((bf16[2,256,256]{2,1,0:T(8,128)(2,1)S(1)}, bf16[2,256,256]{2,1,0:T(8,128)(2,1)S(1)}, u32[]{:S(2)}, u32[]{:S(2)}) %collective-permute-start.4) | collective-permute-done | bytes 262176 | tf_op jit(solution)/shard_map/ppermute | solution.py:15
  46.4 1.4 fusion.96
  47.9 1.5 add_add_fusion
  51.2 1.9 collective-permute-start.7
  53.1 3.9 %collective-permute-start.6 = (bf16[2,256,256]{2,1,0:T(8,128)(2,1)S(1)}, bf16[2,256,256]{2,1,0:T(8,128)(2,1)S(1)}, u32[]{:S(2)}, u32[]{:S(2)}) collective-permute-start(bf16[2,256,256]{2,1,0:T(8,128)(2,1)S(1)} %get-tuple-element.78), channel_id=1, source_target_pairs={{2,0},{3,1},{4,2},{5,3},{6,4},{7,5},{8,6},{9,7},{10,8},{11,9},{12,... | collective-permute-start | bytes 786440 | tf_op jit(solution)/shard_map/ppermute | solution.py:15
  57.8 4.0 %collective-permute-start.9 = (bf16[2,256,256]{2,1,0:T(8,128)(2,1)S(1)}, bf16[2,256,256]{2,1,0:T(8,128)(2,1)S(1)}, u32[]{:S(2)}, u32[]{:S(2)}) collective-permute-start(bf16[2,256,256]{2,1,0:T(8,128)(2,1)S(1)} %get-tuple-element.77), channel_id=1, source_target_pairs={{0,2},{1,3},{2,4},{3,5},{4,6},{5,7},{6,8},{7,9},{8,10},{9,11},{10,... | collective-permute-start | bytes 786440 | tf_op jit(solution)/shard_map/ppermute | solution.py:15
  61.8 1.9 collective-permute-start.8
  64.0 1.3 maximum_maximum_fusion
  66.7 6.1 %collective-permute-done.8 = bf16[2,256,256]{2,1,0:T(8,128)(2,1)S(1)} collective-permute-done((bf16[2,256,256]{2,1,0:T(8,128)(2,1)S(1)}, bf16[2,256,256]{2,1,0:T(8,128)(2,1)S(1)}, u32[]{:S(2)}, u32[]{:S(2)}) %collective-permute-start.8) | collective-permute-done | bytes 262176 | tf_op jit(solution)/shard_map/ppermute | solution.py:15
  74.4 1.9 collective-permute-start.10
  76.3 3.6 %collective-permute-start.11 = (bf16[2,128,256]{2,1,0:T(8,128)(2,1)S(1)}, bf16[2,128,256]{2,1,0:T(8,128)(2,1)S(1)}, u32[]{:S(2)}, u32[]{:S(2)}) collective-permute-start(bf16[2,128,256]{2,1,0:T(8,128)(2,1)S(1)} %get-tuple-element.39), channel_id=1, source_target_pairs={{1,0},{2,1},{3,2},{4,3},{5,4},{6,5},{7,6},{8,7},{9,8},{10,9},{11,1... | collective-permute-start | bytes 393224 | tf_op jit(solution)/shard_map/ppermute | solution.py:15
  82.4 2.2 fusion.59
  85.4 1.3 collective-permute-start.12
  86.7 3.5 %collective-permute-done.15 = bf16[2,256,256]{2,1,0:T(8,128)(2,1)S(1)} collective-permute-done((bf16[2,256,256]{2,1,0:T(8,128)(2,1)S(1)}, bf16[2,256,256]{2,1,0:T(8,128)(2,1)S(1)}, u32[]{:S(2)}, u32[]{:S(2)}) %collective-permute-start.15) | collective-permute-done | bytes 262176 | tf_op jit(solution)/shard_map/ppermute | solution.py:15
  91.1 5.0 %collective-permute-start.17 = (bf16[2,256,256]{2,1,0:T(8,128)(2,1)S(1)}, bf16[2,256,256]{2,1,0:T(8,128)(2,1)S(1)}, u32[]{:S(2)}, u32[]{:S(2)}) collective-permute-start(bf16[2,256,256]{2,1,0:T(8,128)(2,1)S(1)} %get-tuple-element.73), channel_id=1, source_target_pairs={{0,2},{1,3},{2,4},{3,5},{4,6},{5,7},{6,8},{7,9},{8,10},{9,11},{10,... | collective-permute-start | bytes 786440 | tf_op jit(solution)/shard_map/ppermute | solution.py:15
  96.1 1.9 collective-permute-start.16
  99.1 6.0 %collective-permute-start.14 = (bf16[2,256,256]{2,1,0:T(8,128)(2,1)S(1)}, bf16[2,256,256]{2,1,0:T(8,128)(2,1)S(1)}, u32[]{:S(2)}, u32[]{:S(2)}) collective-permute-start(bf16[2,256,256]{2,1,0:T(8,128)(2,1)S(1)} %get-tuple-element.75), channel_id=1, source_target_pairs={{0,2},{1,3},{2,4},{3,5},{4,6},{5,7},{6,8},{7,9},{8,10},{9,11},{10,... | collective-permute-start | bytes 786440 | tf_op jit(solution)/shard_map/ppermute | solution.py:15
  105.2 1.9 collective-permute-start.13
  109.0 6.5 %collective-permute-done.13 = bf16[2,256,256]{2,1,0:T(8,128)(2,1)S(1)} collective-permute-done((bf16[2,256,256]{2,1,0:T(8,128)(2,1)S(1)}, bf16[2,256,256]{2,1,0:T(8,128)(2,1)S(1)}, u32[]{:S(2)}, u32[]{:S(2)}) %collective-permute-start.13) | collective-permute-done | bytes 262176 | tf_op jit(solution)/shard_map/ppermute | solution.py:15
  117.1 2.2 fusion.57
  119.3 1.9 collective-permute-start.18
  121.2 3.6 %collective-permute-start.19 = (bf16[2,128,256]{2,1,0:T(8,128)(2,1)S(1)}, bf16[2,128,256]{2,1,0:T(8,128)(2,1)S(1)}, u32[]{:S(2)}, u32[]{:S(2)}) collective-permute-start(bf16[2,128,256]{2,1,0:T(8,128)(2,1)S(1)} %get-tuple-element.37), channel_id=1, source_target_pairs={{1,0},{2,1},{3,2},{4,3},{5,4},{6,5},{7,6},{8,7},{9,8},{10,9},{11,1... | collective-permute-start | bytes 393224 | tf_op jit(solution)/shard_map/ppermute | solution.py:15
  128.5 1.3 collective-permute-start.20
  129.8 5.1 %collective-permute-done.23 = bf16[2,256,256]{2,1,0:T(8,128)(2,1)S(1)} collective-permute-done((bf16[2,256,256]{2,1,0:T(8,128)(2,1)S(1)}, bf16[2,256,256]{2,1,0:T(8,128)(2,1)S(1)}, u32[]{:S(2)}, u32[]{:S(2)}) %collective-permute-start.23) | collective-permute-done | bytes 262176 | tf_op jit(solution)/shard_map/ppermute | solution.py:15
  135.8 4.7 %collective-permute-start.25 = (bf16[2,256,256]{2,1,0:T(8,128)(2,1)S(1)}, bf16[2,256,256]{2,1,0:T(8,128)(2,1)S(1)}, u32[]{:S(2)}, u32[]{:S(2)}) collective-permute-start(bf16[2,256,256]{2,1,0:T(8,128)(2,1)S(1)} %get-tuple-element.69), channel_id=1, source_target_pairs={{0,2},{1,3},{2,4},{3,5},{4,6},{5,7},{6,8},{7,9},{8,10},{9,11},{10,... | collective-permute-start | bytes 786440 | tf_op jit(solution)/shard_map/ppermute | solution.py:15
  140.5 1.9 collective-permute-start.24
  143.5 6.0 %collective-permute-start.22 = (bf16[2,256,256]{2,1,0:T(8,128)(2,1)S(1)}, bf16[2,256,256]{2,1,0:T(8,128)(2,1)S(1)}, u32[]{:S(2)}, u32[]{:S(2)}) collective-permute-start(bf16[2,256,256]{2,1,0:T(8,128)(2,1)S(1)} %get-tuple-element.71), channel_id=1, source_target_pairs={{0,2},{1,3},{2,4},{3,5},{4,6},{5,7},{6,8},{7,9},{8,10},{9,11},{10,... | collective-permute-start | bytes 786440 | tf_op jit(solution)/shard_map/ppermute | solution.py:15
  149.5 1.9 collective-permute-start.21
  153.4 6.5 %collective-permute-done.21 = bf16[2,256,256]{2,1,0:T(8,128)(2,1)S(1)} collective-permute-done((bf16[2,256,256]{2,1,0:T(8,128)(2,1)S(1)}, bf16[2,256,256]{2,1,0:T(8,128)(2,1)S(1)}, u32[]{:S(2)}, u32[]{:S(2)}) %collective-permute-start.21) | collective-permute-done | bytes 262176 | tf_op jit(solution)/shard_map/ppermute | solution.py:15
  161.5 2.2 fusion.55
  163.7 1.9 collective-permute-start.26
  165.7 3.6 %collective-permute-start.27 = (bf16[2,128,256]{2,1,0:T(8,128)(2,1)S(1)}, bf16[2,128,256]{2,1,0:T(8,128)(2,1)S(1)}, u32[]{:S(2)}, u32[]{:S(2)}) collective-permute-start(bf16[2,128,256]{2,1,0:T(8,128)(2,1)S(1)} %get-tuple-element.35), channel_id=1, source_target_pairs={{1,0},{2,1},{3,2},{4,3},{5,4},{6,5},{7,6},{8,7},{9,8},{10,9},{11,1... | collective-permute-start | bytes 393224 | tf_op jit(solution)/shard_map/ppermute | solution.py:15
  174.2 5.1 %collective-permute-done.31 = bf16[2,256,256]{2,1,0:T(8,128)(2,1)S(1)} collective-permute-done((bf16[2,256,256]{2,1,0:T(8,128)(2,1)S(1)}, bf16[2,256,256]{2,1,0:T(8,128)(2,1)S(1)}, u32[]{:S(2)}, u32[]{:S(2)}) %collective-permute-start.31) | collective-permute-done | bytes 262176 | tf_op jit(solution)/shard_map/ppermute | solution.py:15
  180.3 5.3 %collective-permute-start.33 = (bf16[2,256,256]{2,1,0:T(8,128)(2,1)S(1)}, bf16[2,256,256]{2,1,0:T(8,128)(2,1)S(1)}, u32[]{:S(2)}, u32[]{:S(2)}) collective-permute-start(bf16[2,256,256]{2,1,0:T(8,128)(2,1)S(1)} %get-tuple-element.65), channel_id=1, source_target_pairs={{0,2},{1,3},{2,4},{3,5},{4,6},{5,7},{6,8},{7,9},{8,10},{9,11},{10,... | collective-permute-start | bytes 786440 | tf_op jit(solution)/shard_map/ppermute | solution.py:15
  185.7 2.1 collective-permute-start.32
  188.9 6.0 %collective-permute-start.30 = (bf16[2,256,256]{2,1,0:T(8,128)(2,1)S(1)}, bf16[2,256,256]{2,1,0:T(8,128)(2,1)S(1)}, u32[]{:S(2)}, u32[]{:S(2)}) collective-permute-start(bf16[2,256,256]{2,1,0:T(8,128)(2,1)S(1)} %get-tuple-element.67), channel_id=1, source_target_pairs={{0,2},{1,3},{2,4},{3,5},{4,6},{5,7},{6,8},{7,9},{8,10},{9,11},{10,... | collective-permute-start | bytes 786440 | tf_op jit(solution)/shard_map/ppermute | solution.py:15
  194.9 1.9 collective-permute-start.29
  198.8 6.5 %collective-permute-done.29 = bf16[2,256,256]{2,1,0:T(8,128)(2,1)S(1)} collective-permute-done((bf16[2,256,256]{2,1,0:T(8,128)(2,1)S(1)}, bf16[2,256,256]{2,1,0:T(8,128)(2,1)S(1)}, u32[]{:S(2)}, u32[]{:S(2)}) %collective-permute-start.29) | collective-permute-done | bytes 262176 | tf_op jit(solution)/shard_map/ppermute | solution.py:15
  205.4 1.3 multiply_convert_fusion.1
  208.3 2.0 concatenate.293
  210.3 4.1 %bitcast_add_fusion.3 = f32[768,512]{1,0:T(8,128)S(1)} fusion(f32[768,512,1]{1,0,2:T(8,128)} %fusion.55, f32[768,512,1]{1,0,2:T(8,128)} %fusion.57, f32[768,512,1]{1,0,2:T(8,128)} %fusion.59, bf16[2,512,256]{2,1,0:T(8,128)(2,1)} %get-tuple-element.43, bf16[2,512,256]{2,1,0:T(8,128)(2,1)} %get-tuple-element.42, bf16[2,128,768]{2,1,0:T(8,128)(2,1)} %copy-done.32, ...), kind=kOutput, calls=%fused_computation.11 | convolution fusion | flops 816447488 | bytes 8912896 | tf_op jit(solution)/shard_map/mpc,mpd->cd/dot_general | solution.py:62
  215.1 1.9 copy-done
  218.1 2.7 %collective-permute-done.36 = bf16[2,2,2,2,56,512]{5,4,3,2,1,0:T(8,128)(2,1)S(1)} collective-permute-done((bf16[2,2,2,2,56,512]{5,4,3,2,1,0:T(8,128)(2,1)}, bf16[2,2,2,2,56,512]{5,4,3,2,1,0:T(8,128)(2,1)S(1)}, u32[]{:S(2)}, u32[]{:S(2)}) %collective-permute-start.36) | collective-permute-done | bytes 917536 | tf_op jit(solution)/shard_map/ppermute | solution.py:159
  220.7 2.6 fusion.1
  225.5 2.0 collective-permute-start.34
  227.6 3.6 %collective-permute-start.35 = (bf16[2,128,256]{2,1,0:T(8,128)(2,1)S(1)}, bf16[2,128,256]{2,1,0:T(8,128)(2,1)S(1)}, u32[]{:S(2)}, u32[]{:S(2)}) collective-permute-start(bf16[2,128,256]{2,1,0:T(8,128)(2,1)S(1)} %get-tuple-element.33), channel_id=1, source_target_pairs={{1,0},{2,1},{3,2},{4,3},{5,4},{6,5},{7,6},{8,7},{9,8},{10,9},{11,1... | collective-permute-start | bytes 393224 | tf_op jit(solution)/shard_map/ppermute | solution.py:15
  231.3 5.6 %collective-permute-done.37 = bf16[2,2,2,56,512]{4,3,2,1,0:T(8,128)(2,1)S(1)} collective-permute-done((bf16[2,2,2,56,512]{4,3,2,1,0:T(8,128)(2,1)S(1)}, bf16[2,2,2,56,512]{4,3,2,1,0:T(8,128)(2,1)S(1)}, u32[]{:S(2)}, u32[]{:S(2)}) %collective-permute-start.37) | collective-permute-done | bytes 458784 | tf_op jit(solution)/shard_map/ppermute | solution.py:159
  237.2 1.9 collective-permute-start.38
  240.3 2.9 %collective-permute-done.38 = bf16[2,2,56,512]{3,2,1,0:T(8,128)(2,1)S(1)} collective-permute-done((bf16[2,2,56,512]{3,2,1,0:T(8,128)(2,1)S(1)}, bf16[2,2,56,512]{3,2,1,0:T(8,128)(2,1)S(1)}, u32[]{:S(2)}, u32[]{:S(2)}) %collective-permute-start.38) | collective-permute-done | bytes 229408 | tf_op jit(solution)/shard_map/ppermute | solution.py:159
  243.8 6.1 %collective-permute-done.39 = bf16[2,56,512]{2,1,0:T(8,128)(2,1)S(1)} collective-permute-done((bf16[2,56,512]{2,1,0:T(8,128)(2,1)S(1)}, bf16[2,56,512]{2,1,0:T(8,128)(2,1)S(1)}, u32[]{:S(2)}, u32[]{:S(2)}) %collective-permute-start.39) | collective-permute-done | bytes 114720 | tf_op jit(solution)/shard_map/ppermute | solution.py:159
  249.9 2.7 %collective-permute-start.40 = (bf16[56,512]{1,0:T(8,128)(2,1)S(1)}, bf16[56,512]{1,0:T(8,128)(2,1)S(1)}, u32[]{:S(2)}, u32[]{:S(2)}) collective-permute-start(bf16[56,512]{1,0:T(8,128)(2,1)S(1)} %fusion.243), channel_id=1, source_target_pairs={{0,16},{1,17},{2,18},{3,19},{4,20},{5,21},{6,22},{7,23},{8,24},{9,... | collective-permute-start | bytes 172040 | tf_op jit(solution)/shard_map/ppermute | solution.py:159
  254.0 1.8 collective-permute-done.40
  (224 shorter events, 54.3 us)
Async XLA Ops:
  5.0 9.5 %copy-start.16 = (bf16[2,256,256]{2,1,0:T(8,128)(2,1)}, bf16[2,256,256]{2,1,0:T(8,128)(2,1)S(1)}, u32[]{:S(2)}) copy-start(bf16[2,256,256]{2,1,0:T(8,128)(2,1)S(1)} %get-tuple-element.52) | copy-start | bytes 786436
  6.0 40.4 %collective-permute-start.3 = (bf16[2,256,256]{2,1,0:T(8,128)(2,1)}, bf16[2,256,256]{2,1,0:T(8,128)(2,1)}, u32[]{:S(2)}, u32[]{:S(2)}) collective-permute-start(bf16[2,256,256]{2,1,0:T(8,128)(2,1)} %fusion.4), channel_id=1, source_target_pairs={{0,2},{1,3},{2,4},{3,5},{4,6},{5,7},{6,8},{7,9},{8,10},{9,11},{10,... | collective-permute-start | bytes 786440 | tf_op jit(solution)/shard_map/ppermute | solution.py:15
  9.5 38.4 %collective-permute-start.5 = (bf16[2,256,256]{2,1,0:T(8,128)(2,1)}, bf16[2,256,256]{2,1,0:T(8,128)(2,1)}, u32[]{:S(2)}, u32[]{:S(2)}) collective-permute-start(bf16[2,256,256]{2,1,0:T(8,128)(2,1)} %fusion.4), channel_id=1, source_target_pairs={{2,0},{3,1},{4,2},{5,3},{6,4},{7,5},{8,6},{9,7},{10,8},{11,9},{12,... | collective-permute-start | bytes 786440 | tf_op jit(solution)/shard_map/ppermute | solution.py:15
  12.6 11.6 %collective-permute-start.1 = (bf16[2,128,256]{2,1,0:T(8,128)(2,1)}, bf16[2,128,256]{2,1,0:T(8,128)(2,1)}, u32[]{:S(2)}, u32[]{:S(2)}) collective-permute-start(bf16[2,128,256]{2,1,0:T(8,128)(2,1)} %get-tuple-element.122), channel_id=1, source_target_pairs={{1,0},{2,1},{3,2},{4,3},{5,4},{6,5},{7,6},{8,7},{9,8},{10,9},{11,1... | collective-permute-start | bytes 393224 | tf_op jit(solution)/shard_map/ppermute | solution.py:15
  14.6 11.1 %collective-permute-start = (bf16[2,128,256]{2,1,0:T(8,128)(2,1)}, bf16[2,128,256]{2,1,0:T(8,128)(2,1)}, u32[]{:S(2)}, u32[]{:S(2)}) collective-permute-start(bf16[2,128,256]{2,1,0:T(8,128)(2,1)} %get-tuple-element.121), channel_id=1, source_target_pairs={{0,1},{1,2},{2,3},{3,4},{4,5},{5,6},{6,7},{7,8},{8,9},{9,10},{10,1... | collective-permute-start | bytes 393224 | tf_op jit(solution)/shard_map/ppermute | solution.py:15
  28.3 11.8 %collective-permute-start.2 = (bf16[2,256,256]{2,1,0:T(8,128)(2,1)S(1)}, bf16[2,256,256]{2,1,0:T(8,128)(2,1)S(1)}, u32[]{:S(2)}, u32[]{:S(2)}) collective-permute-start(bf16[2,256,256]{2,1,0:T(8,128)(2,1)S(1)} %fusion.3), channel_id=1, source_target_pairs={{0,2},{1,3},{2,4},{3,5},{4,6},{5,7},{6,8},{7,9},{8,10},{9,11},{10,... | collective-permute-start | bytes 786440 | tf_op jit(solution)/shard_map/ppermute | solution.py:15
  33.9 12.4 %collective-permute-start.4 = (bf16[2,256,256]{2,1,0:T(8,128)(2,1)S(1)}, bf16[2,256,256]{2,1,0:T(8,128)(2,1)S(1)}, u32[]{:S(2)}, u32[]{:S(2)}) collective-permute-start(bf16[2,256,256]{2,1,0:T(8,128)(2,1)S(1)} %fusion.3), channel_id=1, source_target_pairs={{2,0},{3,1},{4,2},{5,3},{6,4},{7,5},{8,6},{9,7},{10,8},{11,9},{12,... | collective-permute-start | bytes 786440 | tf_op jit(solution)/shard_map/ppermute | solution.py:15
  38.7 122.7 %copy-start.31 = (bf16[2,128,768]{2,1,0:T(8,128)(2,1)}, bf16[2,128,768]{2,1,0:T(8,128)(2,1)S(1)}, u32[]{:S(2)}) copy-start(bf16[2,128,768]{2,1,0:T(8,128)(2,1)S(1)} %get-tuple-element.62) | copy-start | bytes 1179652
  38.7 122.7 %copy-start.32 = (bf16[2,128,768]{2,1,0:T(8,128)(2,1)}, bf16[2,128,768]{2,1,0:T(8,128)(2,1)S(1)}, u32[]{:S(2)}) copy-start(bf16[2,128,768]{2,1,0:T(8,128)(2,1)S(1)} %get-tuple-element.63) | copy-start | bytes 1179652
  51.2 15.2 %collective-permute-start.7 = (bf16[2,256,256]{2,1,0:T(8,128)(2,1)S(1)}, bf16[2,256,256]{2,1,0:T(8,128)(2,1)S(1)}, u32[]{:S(2)}, u32[]{:S(2)}) collective-permute-start(bf16[2,256,256]{2,1,0:T(8,128)(2,1)S(1)} %get-tuple-element.79), channel_id=1, source_target_pairs={{0,2},{1,3},{2,4},{3,5},{4,6},{5,7},{6,8},{7,9},{8,10},{9,11},{10,... | collective-permute-start | bytes 786440 | tf_op jit(solution)/shard_map/ppermute | solution.py:15
  53.1 13.3 %collective-permute-start.6 = (bf16[2,256,256]{2,1,0:T(8,128)(2,1)S(1)}, bf16[2,256,256]{2,1,0:T(8,128)(2,1)S(1)}, u32[]{:S(2)}, u32[]{:S(2)}) collective-permute-start(bf16[2,256,256]{2,1,0:T(8,128)(2,1)S(1)} %get-tuple-element.78), channel_id=1, source_target_pairs={{2,0},{3,1},{4,2},{5,3},{6,4},{7,5},{8,6},{9,7},{10,8},{11,9},{12,... | collective-permute-start | bytes 786440 | tf_op jit(solution)/shard_map/ppermute | solution.py:15
  57.1 6.7 %copy-start.33 = (bf16[2,256,256]{2,1,0:T(8,128)(2,1)S(1)}, bf16[2,256,256]{2,1,0:T(8,128)(2,1)}, u32[]{:S(2)}) copy-start(bf16[2,256,256]{2,1,0:T(8,128)(2,1)} %slice.1331) | copy-start | bytes 786436
  57.8 8.9 %collective-permute-start.9 = (bf16[2,256,256]{2,1,0:T(8,128)(2,1)S(1)}, bf16[2,256,256]{2,1,0:T(8,128)(2,1)S(1)}, u32[]{:S(2)}, u32[]{:S(2)}) collective-permute-start(bf16[2,256,256]{2,1,0:T(8,128)(2,1)S(1)} %get-tuple-element.77), channel_id=1, source_target_pairs={{0,2},{1,3},{2,4},{3,5},{4,6},{5,7},{6,8},{7,9},{8,10},{9,11},{10,... | collective-permute-start | bytes 786440 | tf_op jit(solution)/shard_map/ppermute | solution.py:15
  61.8 11.0 %collective-permute-start.8 = (bf16[2,256,256]{2,1,0:T(8,128)(2,1)S(1)}, bf16[2,256,256]{2,1,0:T(8,128)(2,1)S(1)}, u32[]{:S(2)}, u32[]{:S(2)}) collective-permute-start(bf16[2,256,256]{2,1,0:T(8,128)(2,1)S(1)} %get-tuple-element.76), channel_id=1, source_target_pairs={{2,0},{3,1},{4,2},{5,3},{6,4},{7,5},{8,6},{9,7},{10,8},{11,9},{12,... | collective-permute-start | bytes 786440 | tf_op jit(solution)/shard_map/ppermute | solution.py:15
  66.6 6.4 %copy-start.29 = (f32[2,256,256]{2,1,0:T(8,128)S(1)}, f32[2,256,256]{2,1,0:T(8,128)}, u32[]{:S(2)}) copy-start(f32[2,256,256]{2,1,0:T(8,128)} %get-tuple-element.50) | copy-start | bytes 1572868
  66.6 6.4 %copy-start.30 = (f32[2,256,256]{2,1,0:T(8,128)S(1)}, f32[2,256,256]{2,1,0:T(8,128)}, u32[]{:S(2)}) copy-start(f32[2,256,256]{2,1,0:T(8,128)} %get-tuple-element.51) | copy-start | bytes 1572868
  74.4 10.2 %collective-permute-start.10 = (bf16[2,128,256]{2,1,0:T(8,128)(2,1)S(1)}, bf16[2,128,256]{2,1,0:T(8,128)(2,1)S(1)}, u32[]{:S(2)}, u32[]{:S(2)}) collective-permute-start(bf16[2,128,256]{2,1,0:T(8,128)(2,1)S(1)} %get-tuple-element.38), channel_id=1, source_target_pairs={{0,1},{1,2},{2,3},{3,4},{4,5},{5,6},{6,7},{7,8},{8,9},{9,10},{10,1... | collective-permute-start | bytes 393224 | tf_op jit(solution)/shard_map/ppermute | solution.py:15
  76.3 8.2 %collective-permute-start.11 = (bf16[2,128,256]{2,1,0:T(8,128)(2,1)S(1)}, bf16[2,128,256]{2,1,0:T(8,128)(2,1)S(1)}, u32[]{:S(2)}, u32[]{:S(2)}) collective-permute-start(bf16[2,128,256]{2,1,0:T(8,128)(2,1)S(1)} %get-tuple-element.39), channel_id=1, source_target_pairs={{1,0},{2,1},{3,2},{4,3},{5,4},{6,5},{7,6},{8,7},{9,8},{10,9},{11,1... | collective-permute-start | bytes 393224 | tf_op jit(solution)/shard_map/ppermute | solution.py:15
  81.0 9.1 %collective-permute-start.15 = (bf16[2,256,256]{2,1,0:T(8,128)(2,1)S(1)}, bf16[2,256,256]{2,1,0:T(8,128)(2,1)S(1)}, u32[]{:S(2)}, u32[]{:S(2)}) collective-permute-start(bf16[2,256,256]{2,1,0:T(8,128)(2,1)S(1)} %get-tuple-element.7), channel_id=1, source_target_pairs={{32,0},{64,32},{96,64},{33,1},{65,33},{97,65},{34,2},{66,34},{98,6... | collective-permute-start | bytes 786440 | tf_op jit(solution)/shard_map/ppermute | solution.py:15
  85.4 12.7 %collective-permute-start.12 = (bf16[2,256,256]{2,1,0:T(8,128)(2,1)S(1)}, bf16[2,256,256]{2,1,0:T(8,128)(2,1)S(1)}, u32[]{:S(2)}, u32[]{:S(2)}) collective-permute-start(bf16[2,256,256]{2,1,0:T(8,128)(2,1)S(1)} %pad_maximum_fusion.34), channel_id=1, source_target_pairs={{32,0},{64,32},{96,64},{33,1},{65,33},{97,65},{34,2},{66,34},{98,6... | collective-permute-start | bytes 786440 | tf_op jit(solution)/shard_map/ppermute | solution.py:15
  91.1 17.1 %collective-permute-start.17 = (bf16[2,256,256]{2,1,0:T(8,128)(2,1)S(1)}, bf16[2,256,256]{2,1,0:T(8,128)(2,1)S(1)}, u32[]{:S(2)}, u32[]{:S(2)}) collective-permute-start(bf16[2,256,256]{2,1,0:T(8,128)(2,1)S(1)} %get-tuple-element.73), channel_id=1, source_target_pairs={{0,2},{1,3},{2,4},{3,5},{4,6},{5,7},{6,8},{7,9},{8,10},{9,11},{10,... | collective-permute-start | bytes 786440 | tf_op jit(solution)/shard_map/ppermute | solution.py:15
  96.1 12.0 %collective-permute-start.16 = (bf16[2,256,256]{2,1,0:T(8,128)(2,1)S(1)}, bf16[2,256,256]{2,1,0:T(8,128)(2,1)S(1)}, u32[]{:S(2)}, u32[]{:S(2)}) collective-permute-start(bf16[2,256,256]{2,1,0:T(8,128)(2,1)S(1)} %get-tuple-element.72), channel_id=1, source_target_pairs={{2,0},{3,1},{4,2},{5,3},{6,4},{7,5},{8,6},{9,7},{10,8},{11,9},{12,... | collective-permute-start | bytes 786440 | tf_op jit(solution)/shard_map/ppermute | solution.py:15
  99.1 9.9 %collective-permute-start.14 = (bf16[2,256,256]{2,1,0:T(8,128)(2,1)S(1)}, bf16[2,256,256]{2,1,0:T(8,128)(2,1)S(1)}, u32[]{:S(2)}, u32[]{:S(2)}) collective-permute-start(bf16[2,256,256]{2,1,0:T(8,128)(2,1)S(1)} %get-tuple-element.75), channel_id=1, source_target_pairs={{0,2},{1,3},{2,4},{3,5},{4,6},{5,7},{6,8},{7,9},{8,10},{9,11},{10,... | collective-permute-start | bytes 786440 | tf_op jit(solution)/shard_map/ppermute | solution.py:15
  105.2 10.4 %collective-permute-start.13 = (bf16[2,256,256]{2,1,0:T(8,128)(2,1)S(1)}, bf16[2,256,256]{2,1,0:T(8,128)(2,1)S(1)}, u32[]{:S(2)}, u32[]{:S(2)}) collective-permute-start(bf16[2,256,256]{2,1,0:T(8,128)(2,1)S(1)} %get-tuple-element.74), channel_id=1, source_target_pairs={{2,0},{3,1},{4,2},{5,3},{6,4},{7,5},{8,6},{9,7},{10,8},{11,9},{12,... | collective-permute-start | bytes 786440 | tf_op jit(solution)/shard_map/ppermute | solution.py:15
  119.3 8.3 %collective-permute-start.18 = (bf16[2,128,256]{2,1,0:T(8,128)(2,1)S(1)}, bf16[2,128,256]{2,1,0:T(8,128)(2,1)S(1)}, u32[]{:S(2)}, u32[]{:S(2)}) collective-permute-start(bf16[2,128,256]{2,1,0:T(8,128)(2,1)S(1)} %get-tuple-element.36), channel_id=1, source_target_pairs={{0,1},{1,2},{2,3},{3,4},{4,5},{5,6},{6,7},{7,8},{8,9},{9,10},{10,1... | collective-permute-start | bytes 393224 | tf_op jit(solution)/shard_map/ppermute | solution.py:15
  121.2 6.3 %collective-permute-start.19 = (bf16[2,128,256]{2,1,0:T(8,128)(2,1)S(1)}, bf16[2,128,256]{2,1,0:T(8,128)(2,1)S(1)}, u32[]{:S(2)}, u32[]{:S(2)}) collective-permute-start(bf16[2,128,256]{2,1,0:T(8,128)(2,1)S(1)} %get-tuple-element.37), channel_id=1, source_target_pairs={{1,0},{2,1},{3,2},{4,3},{5,4},{6,5},{7,6},{8,7},{9,8},{10,9},{11,1... | collective-permute-start | bytes 393224 | tf_op jit(solution)/shard_map/ppermute | solution.py:15
  125.9 9.0 %collective-permute-start.23 = (bf16[2,256,256]{2,1,0:T(8,128)(2,1)S(1)}, bf16[2,256,256]{2,1,0:T(8,128)(2,1)S(1)}, u32[]{:S(2)}, u32[]{:S(2)}) collective-permute-start(bf16[2,256,256]{2,1,0:T(8,128)(2,1)S(1)} %get-tuple-element.5), channel_id=1, source_target_pairs={{32,0},{64,32},{96,64},{33,1},{65,33},{97,65},{34,2},{66,34},{98,6... | collective-permute-start | bytes 786440 | tf_op jit(solution)/shard_map/ppermute | solution.py:15
  128.5 14.0 %collective-permute-start.20 = (bf16[2,256,256]{2,1,0:T(8,128)(2,1)S(1)}, bf16[2,256,256]{2,1,0:T(8,128)(2,1)S(1)}, u32[]{:S(2)}, u32[]{:S(2)}) collective-permute-start(bf16[2,256,256]{2,1,0:T(8,128)(2,1)S(1)} %pad_maximum_fusion.35), channel_id=1, source_target_pairs={{32,0},{64,32},{96,64},{33,1},{65,33},{97,65},{34,2},{66,34},{98,6... | collective-permute-start | bytes 786440 | tf_op jit(solution)/shard_map/ppermute | solution.py:15
  135.8 17.0 %collective-permute-start.25 = (bf16[2,256,256]{2,1,0:T(8,128)(2,1)S(1)}, bf16[2,256,256]{2,1,0:T(8,128)(2,1)S(1)}, u32[]{:S(2)}, u32[]{:S(2)}) collective-permute-start(bf16[2,256,256]{2,1,0:T(8,128)(2,1)S(1)} %get-tuple-element.69), channel_id=1, source_target_pairs={{0,2},{1,3},{2,4},{3,5},{4,6},{5,7},{6,8},{7,9},{8,10},{9,11},{10,... | collective-permute-start | bytes 786440 | tf_op jit(solution)/shard_map/ppermute | solution.py:15
  140.5 12.3 %collective-permute-start.24 = (bf16[2,256,256]{2,1,0:T(8,128)(2,1)S(1)}, bf16[2,256,256]{2,1,0:T(8,128)(2,1)S(1)}, u32[]{:S(2)}, u32[]{:S(2)}) collective-permute-start(bf16[2,256,256]{2,1,0:T(8,128)(2,1)S(1)} %get-tuple-element.68), channel_id=1, source_target_pairs={{2,0},{3,1},{4,2},{5,3},{6,4},{7,5},{8,6},{9,7},{10,8},{11,9},{12,... | collective-permute-start | bytes 786440 | tf_op jit(solution)/shard_map/ppermute | solution.py:15
  143.5 9.9 %collective-permute-start.22 = (bf16[2,256,256]{2,1,0:T(8,128)(2,1)S(1)}, bf16[2,256,256]{2,1,0:T(8,128)(2,1)S(1)}, u32[]{:S(2)}, u32[]{:S(2)}) collective-permute-start(bf16[2,256,256]{2,1,0:T(8,128)(2,1)S(1)} %get-tuple-element.71), channel_id=1, source_target_pairs={{0,2},{1,3},{2,4},{3,5},{4,6},{5,7},{6,8},{7,9},{8,10},{9,11},{10,... | collective-permute-start | bytes 786440 | tf_op jit(solution)/shard_map/ppermute | solution.py:15
  149.5 10.4 %collective-permute-start.21 = (bf16[2,256,256]{2,1,0:T(8,128)(2,1)S(1)}, bf16[2,256,256]{2,1,0:T(8,128)(2,1)S(1)}, u32[]{:S(2)}, u32[]{:S(2)}) collective-permute-start(bf16[2,256,256]{2,1,0:T(8,128)(2,1)S(1)} %get-tuple-element.70), channel_id=1, source_target_pairs={{2,0},{3,1},{4,2},{5,3},{6,4},{7,5},{8,6},{9,7},{10,8},{11,9},{12,... | collective-permute-start | bytes 786440 | tf_op jit(solution)/shard_map/ppermute | solution.py:15
  163.7 8.3 %collective-permute-start.26 = (bf16[2,128,256]{2,1,0:T(8,128)(2,1)S(1)}, bf16[2,128,256]{2,1,0:T(8,128)(2,1)S(1)}, u32[]{:S(2)}, u32[]{:S(2)}) collective-permute-start(bf16[2,128,256]{2,1,0:T(8,128)(2,1)S(1)} %get-tuple-element.34), channel_id=1, source_target_pairs={{0,1},{1,2},{2,3},{3,4},{4,5},{5,6},{6,7},{7,8},{8,9},{9,10},{10,1... | collective-permute-start | bytes 393224 | tf_op jit(solution)/shard_map/ppermute | solution.py:15
  165.7 6.3 %collective-permute-start.27 = (bf16[2,128,256]{2,1,0:T(8,128)(2,1)S(1)}, bf16[2,128,256]{2,1,0:T(8,128)(2,1)S(1)}, u32[]{:S(2)}, u32[]{:S(2)}) collective-permute-start(bf16[2,128,256]{2,1,0:T(8,128)(2,1)S(1)} %get-tuple-element.35), channel_id=1, source_target_pairs={{1,0},{2,1},{3,2},{4,3},{5,4},{6,5},{7,6},{8,7},{9,8},{10,9},{11,1... | collective-permute-start | bytes 393224 | tf_op jit(solution)/shard_map/ppermute | solution.py:15
  170.4 9.0 %collective-permute-start.31 = (bf16[2,256,256]{2,1,0:T(8,128)(2,1)S(1)}, bf16[2,256,256]{2,1,0:T(8,128)(2,1)S(1)}, u32[]{:S(2)}, u32[]{:S(2)}) collective-permute-start(bf16[2,256,256]{2,1,0:T(8,128)(2,1)S(1)} %get-tuple-element.3), channel_id=1, source_target_pairs={{32,0},{64,32},{96,64},{33,1},{65,33},{97,65},{34,2},{66,34},{98,6... | collective-permute-start | bytes 786440 | tf_op jit(solution)/shard_map/ppermute | solution.py:15
  172.9 14.9 %collective-permute-start.28 = (bf16[2,256,256]{2,1,0:T(8,128)(2,1)S(1)}, bf16[2,256,256]{2,1,0:T(8,128)(2,1)S(1)}, u32[]{:S(2)}, u32[]{:S(2)}) collective-permute-start(bf16[2,256,256]{2,1,0:T(8,128)(2,1)S(1)} %pad_maximum_fusion.36), channel_id=1, source_target_pairs={{32,0},{64,32},{96,64},{33,1},{65,33},{97,65},{34,2},{66,34},{98,6... | collective-permute-start | bytes 786440 | tf_op jit(solution)/shard_map/ppermute | solution.py:15
  179.4 19.2 %copy-start.7 = (bf16[2,256,256]{2,1,0:T(8,128)(2,1)}, bf16[2,256,256]{2,1,0:T(8,128)(2,1)S(1)}, u32[]{:S(2)}) copy-start(bf16[2,256,256]{2,1,0:T(8,128)(2,1)S(1)} %collective-permute-done.31) | copy-start | bytes 786436
  180.3 18.3 %copy-start.5 = (f32[2,256,768]{2,1,0:T(8,128)}, f32[2,256,768]{2,1,0:T(8,128)S(1)}, u32[]{:S(2)}) copy-start(f32[2,256,768]{2,1,0:T(8,128)S(1)} %get-tuple-element.160) | copy-start | bytes 4718596
  180.3 18.2 %collective-permute-start.33 = (bf16[2,256,256]{2,1,0:T(8,128)(2,1)S(1)}, bf16[2,256,256]{2,1,0:T(8,128)(2,1)S(1)}, u32[]{:S(2)}, u32[]{:S(2)}) collective-permute-start(bf16[2,256,256]{2,1,0:T(8,128)(2,1)S(1)} %get-tuple-element.65), channel_id=1, source_target_pairs={{0,2},{1,3},{2,4},{3,5},{4,6},{5,7},{6,8},{7,9},{8,10},{9,11},{10,... | collective-permute-start | bytes 786440 | tf_op jit(solution)/shard_map/ppermute | solution.py:15
  185.7 12.9 %collective-permute-start.32 = (bf16[2,256,256]{2,1,0:T(8,128)(2,1)S(1)}, bf16[2,256,256]{2,1,0:T(8,128)(2,1)S(1)}, u32[]{:S(2)}, u32[]{:S(2)}) collective-permute-start(bf16[2,256,256]{2,1,0:T(8,128)(2,1)S(1)} %get-tuple-element.64), channel_id=1, source_target_pairs={{2,0},{3,1},{4,2},{5,3},{6,4},{7,5},{8,6},{9,7},{10,8},{11,9},{12,... | collective-permute-start | bytes 786440 | tf_op jit(solution)/shard_map/ppermute | solution.py:15
  188.9 9.9 %collective-permute-start.30 = (bf16[2,256,256]{2,1,0:T(8,128)(2,1)S(1)}, bf16[2,256,256]{2,1,0:T(8,128)(2,1)S(1)}, u32[]{:S(2)}, u32[]{:S(2)}) collective-permute-start(bf16[2,256,256]{2,1,0:T(8,128)(2,1)S(1)} %get-tuple-element.67), channel_id=1, source_target_pairs={{0,2},{1,3},{2,4},{3,5},{4,6},{5,7},{6,8},{7,9},{8,10},{9,11},{10,... | collective-permute-start | bytes 786440 | tf_op jit(solution)/shard_map/ppermute | solution.py:15
  194.9 10.4 %collective-permute-start.29 = (bf16[2,256,256]{2,1,0:T(8,128)(2,1)S(1)}, bf16[2,256,256]{2,1,0:T(8,128)(2,1)S(1)}, u32[]{:S(2)}, u32[]{:S(2)}) collective-permute-start(bf16[2,256,256]{2,1,0:T(8,128)(2,1)S(1)} %get-tuple-element.66), channel_id=1, source_target_pairs={{2,0},{3,1},{4,2},{5,3},{6,4},{7,5},{8,6},{9,7},{10,8},{11,9},{12,... | collective-permute-start | bytes 786440 | tf_op jit(solution)/shard_map/ppermute | solution.py:15
  198.5 6.9 %copy-start.23 = (bf16[2,256,256]{2,1,0:T(8,128)(2,1)}, bf16[2,256,256]{2,1,0:T(8,128)(2,1)S(1)}, u32[]{:S(2)}) copy-start(bf16[2,256,256]{2,1,0:T(8,128)(2,1)S(1)} %collective-permute-done.33) | copy-start | bytes 786436
  198.5 6.8 %copy-start.25 = (bf16[2,256,256]{2,1,0:T(8,128)(2,1)}, bf16[2,256,256]{2,1,0:T(8,128)(2,1)S(1)}, u32[]{:S(2)}) copy-start(bf16[2,256,256]{2,1,0:T(8,128)(2,1)S(1)} %collective-permute-done.32) | copy-start | bytes 786436
  207.4 2.9 %copy-start.35 = (bf16[2,256,256]{2,1,0:T(8,128)(2,1)S(1)}, bf16[2,256,256]{2,1,0:T(8,128)(2,1)}, u32[]{:S(2)}) copy-start(bf16[2,256,256]{2,1,0:T(8,128)(2,1)} %get-tuple-element.80) | copy-start | bytes 786436
  210.3 4.1 %copy-start.11 = (f32[2,2,2,2,2,8,512]{6,5,4,3,2,1,0:T(8,128)S(1)}, f32[2,2,2,2,2,8,512]{6,5,4,3,2,1,0:T(8,128)}, u32[]{:S(2)}) copy-start(f32[2,2,2,2,2,8,512]{6,5,4,3,2,1,0:T(8,128)} %concatenate.293) | copy-start | bytes 1572868
  218.1 2.7 %collective-permute-start.36 = (bf16[2,2,2,2,56,512]{5,4,3,2,1,0:T(8,128)(2,1)}, bf16[2,2,2,2,56,512]{5,4,3,2,1,0:T(8,128)(2,1)S(1)}, u32[]{:S(2)}, u32[]{:S(2)}) collective-permute-start(bf16[2,2,2,2,56,512]{5,4,3,2,1,0:T(8,128)(2,1)} %fusion.50), channel_id=1, source_target_pairs={{0,1},{1,0},{2,3},{3,2},{4,5},{5,4},{6,7},{7,6},{8,9},{9,8},{10,11... | collective-permute-start | bytes 2752520 | tf_op jit(solution)/shard_map/ppermute | solution.py:159
  223.4 13.5 %collective-permute-start.37 = (bf16[2,2,2,56,512]{4,3,2,1,0:T(8,128)(2,1)S(1)}, bf16[2,2,2,56,512]{4,3,2,1,0:T(8,128)(2,1)S(1)}, u32[]{:S(2)}, u32[]{:S(2)}) collective-permute-start(bf16[2,2,2,56,512]{4,3,2,1,0:T(8,128)(2,1)S(1)} %fusion.154), channel_id=1, source_target_pairs={{0,2},{1,3},{2,0},{3,1},{4,6},{5,7},{6,4},{7,5},{8,10},{9,11},{10,... | collective-permute-start | bytes 1376264 | tf_op jit(solution)/shard_map/ppermute | solution.py:159
  225.5 18.0 %collective-permute-start.34 = (bf16[2,128,256]{2,1,0:T(8,128)(2,1)S(1)}, bf16[2,128,256]{2,1,0:T(8,128)(2,1)S(1)}, u32[]{:S(2)}, u32[]{:S(2)}) collective-permute-start(bf16[2,128,256]{2,1,0:T(8,128)(2,1)S(1)} %get-tuple-element.32), channel_id=1, source_target_pairs={{0,1},{1,2},{2,3},{3,4},{4,5},{5,6},{6,7},{7,8},{8,9},{9,10},{10,1... | collective-permute-start | bytes 393224 | tf_op jit(solution)/shard_map/ppermute | solution.py:15
  227.6 11.4 %copy-start.8 = (bf16[2,256,256]{2,1,0:T(8,128)(2,1)S(1)}, bf16[2,256,256]{2,1,0:T(8,128)(2,1)}, u32[]{:S(2)}) copy-start(bf16[2,256,256]{2,1,0:T(8,128)(2,1)} %copy-done.7) | copy-start | bytes 786436
  227.6 11.4 %copy-start.24 = (bf16[2,256,256]{2,1,0:T(8,128)(2,1)S(1)}, bf16[2,256,256]{2,1,0:T(8,128)(2,1)}, u32[]{:S(2)}) copy-start(bf16[2,256,256]{2,1,0:T(8,128)(2,1)} %copy-done.23) | copy-start | bytes 786436
  227.6 11.4 %copy-start.26 = (bf16[2,256,256]{2,1,0:T(8,128)(2,1)S(1)}, bf16[2,256,256]{2,1,0:T(8,128)(2,1)}, u32[]{:S(2)}) copy-start(bf16[2,256,256]{2,1,0:T(8,128)(2,1)} %copy-done.25) | copy-start | bytes 786436
  227.6 16.0 %collective-permute-start.35 = (bf16[2,128,256]{2,1,0:T(8,128)(2,1)S(1)}, bf16[2,128,256]{2,1,0:T(8,128)(2,1)S(1)}, u32[]{:S(2)}, u32[]{:S(2)}) collective-permute-start(bf16[2,128,256]{2,1,0:T(8,128)(2,1)S(1)} %get-tuple-element.33), channel_id=1, source_target_pairs={{1,0},{2,1},{3,2},{4,3},{5,4},{6,5},{7,6},{8,7},{9,8},{10,9},{11,1... | collective-permute-start | bytes 393224 | tf_op jit(solution)/shard_map/ppermute | solution.py:15
  237.2 6.1 %collective-permute-start.38 = (bf16[2,2,56,512]{3,2,1,0:T(8,128)(2,1)S(1)}, bf16[2,2,56,512]{3,2,1,0:T(8,128)(2,1)S(1)}, u32[]{:S(2)}, u32[]{:S(2)}) collective-permute-start(bf16[2,2,56,512]{3,2,1,0:T(8,128)(2,1)S(1)} %fusion.213), channel_id=1, source_target_pairs={{0,8},{1,9},{2,10},{3,11},{4,12},{5,13},{6,14},{7,15},{8,0},{9,1},... | collective-permute-start | bytes 688136 | tf_op jit(solution)/shard_map/ppermute | solution.py:159
  243.4 9.2 %copy-start.12 = (f32[2,256,256]{2,1,0:T(8,128)S(1)}, f32[2,256,256]{2,1,0:T(8,128)}, u32[]{:S(2)}) copy-start(f32[2,256,256]{2,1,0:T(8,128)} %get-tuple-element.8) | copy-start | bytes 1572868
  243.4 9.2 %copy-start.13 = (f32[2,256,256]{2,1,0:T(8,128)S(1)}, f32[2,256,256]{2,1,0:T(8,128)}, u32[]{:S(2)}) copy-start(f32[2,256,256]{2,1,0:T(8,128)} %get-tuple-element.6) | copy-start | bytes 1572868
  243.4 9.2 %copy-start.14 = (f32[2,256,256]{2,1,0:T(8,128)S(1)}, f32[2,256,256]{2,1,0:T(8,128)}, u32[]{:S(2)}) copy-start(f32[2,256,256]{2,1,0:T(8,128)} %get-tuple-element.4) | copy-start | bytes 1572868
  243.4 9.2 %copy-start.18 = (f32[1,2,128,256]{3,2,1,0:T(8,128)S(1)}, f32[1,2,128,256]{3,2,1,0:T(8,128)}, u32[]{:S(2)}) copy-start(f32[1,2,128,256]{3,2,1,0:T(8,128)} %get-tuple-element.27) | copy-start | bytes 786436
  243.5 9.2 %copy-start.19 = (f32[1,2,128,256]{3,2,1,0:T(8,128)S(1)}, f32[1,2,128,256]{3,2,1,0:T(8,128)}, u32[]{:S(2)}) copy-start(f32[1,2,128,256]{3,2,1,0:T(8,128)} %get-tuple-element.14) | copy-start | bytes 786436
  243.5 9.2 %copy-start.20 = (f32[1,2,128,256]{3,2,1,0:T(8,128)S(1)}, f32[1,2,128,256]{3,2,1,0:T(8,128)}, u32[]{:S(2)}) copy-start(f32[1,2,128,256]{3,2,1,0:T(8,128)} %get-tuple-element.25) | copy-start | bytes 786436
  243.5 9.2 %copy-start.21 = (f32[1,2,128,256]{3,2,1,0:T(8,128)S(1)}, f32[1,2,128,256]{3,2,1,0:T(8,128)}, u32[]{:S(2)}) copy-start(f32[1,2,128,256]{3,2,1,0:T(8,128)} %get-tuple-element.10) | copy-start | bytes 786436
  243.5 9.2 %copy-start.22 = (f32[1,2,128,256]{3,2,1,0:T(8,128)S(1)}, f32[1,2,128,256]{3,2,1,0:T(8,128)}, u32[]{:S(2)}) copy-start(f32[1,2,128,256]{3,2,1,0:T(8,128)} %get-tuple-element.23) | copy-start | bytes 786436
  243.5 6.4 %collective-permute-start.39 = (bf16[2,56,512]{2,1,0:T(8,128)(2,1)S(1)}, bf16[2,56,512]{2,1,0:T(8,128)(2,1)S(1)}, u32[]{:S(2)}, u32[]{:S(2)}) collective-permute-start(bf16[2,56,512]{2,1,0:T(8,128)(2,1)S(1)} %fusion.242), channel_id=1, source_target_pairs={{0,4},{1,5},{2,6},{3,7},{4,0},{5,1},{6,2},{7,3},{8,12},{9,13},{10,... | collective-permute-start | bytes 344072 | tf_op jit(solution)/shard_map/ppermute | solution.py:159
  249.9 5.8 %collective-permute-start.40 = (bf16[56,512]{1,0:T(8,128)(2,1)S(1)}, bf16[56,512]{1,0:T(8,128)(2,1)S(1)}, u32[]{:S(2)}, u32[]{:S(2)}) collective-permute-start(bf16[56,512]{1,0:T(8,128)(2,1)S(1)} %fusion.243), channel_id=1, source_target_pairs={{0,16},{1,17},{2,18},{3,19},{4,20},{5,21},{6,22},{7,23},{8,24},{9,... | collective-permute-start | bytes 172040 | tf_op jit(solution)/shard_map/ppermute | solution.py:159
  (15 other events, 26.7 us)

commit v7 on v5

--- a/solution.py
+++ b/solution.py
@@ -189,13 +189,13 @@
         stored.append(saved)
 
     top = jnp.where(section_rank == section_count - 1, 1.0, 0.0).astype(jnp.float32)
-    flowing = split_rows(cotangent.astype(jnp.float32) * top, NEAR)
+    flowing = cotangent.astype(jnp.float32) * top
     input_grads = None
     conv_acc = [None] * depth
     out_acc = [None] * depth
     for step in range(section_count):
         for layer in reversed(range(depth)):
-            if layer == depth - 1:
+            if layer == depth - 1 and step > 0:
                 flowing, conv_term, out_term = backward_far(
                     flowing, stored[layer], conv_mat[layer], out_mat[layer], far_hops
                 )

time: 240 us -> 234 us (0.975)
  waiting for transfers between devices: 63.4 us -> 73.2 us
  starting transfers between devices: 102 us -> 97.9 us
  matrix products: 41.9 us -> 38.1 us
  local copies, waits for them, and re-layouts: 9.32 us -> 5.73 us
  other arithmetic: 19.2 us -> 16.2 us
    ppermute x34 -> x32, waiting for transfers between devices: 44.1 us -> 53.6 us  [shifted(): lax.ppermute(value, axis, [(source, source + steps) for source in range(l...]
    ppermute x34 -> x32, starting transfers between devices: 96.4 us -> 92.7 us  [shifted(): lax.ppermute(value, axis, [(source, source + steps) for source in range(l...]
    dot_general x4 -> x5, matrix products: 13.5 us -> 11.7 us  [backward_layer(): jnp.einsum('mpc,mpd->cd', taps, grad_pre, preferred_element_type=jnp.floa...]
    dot_general x8 -> x6, matrix products: 4.96 us -> 3.72 us  [backward_far(): jnp.einsum('mpd,cd->mpc', grad_pre, weights, preferred_element_type=f32)]
    dot_general x4 -> x5, matrix products: 4.14 us -> 5.17 us  [backward_layer(): jnp.einsum('mpd,cd->mpc', grad_pre, weights, preferred_element_type=jnp.f...]
    dot_general x4 -> x3, matrix products: 5.31 us -> 4.29 us  [backward_far(): jnp.einsum('mpc,mpd->cd', taps, grad_pre, preferred_element_type=f32)]
  transfers between devices with their start and end apart: 39 -> 37, of which waited for: 17 -> 17; matrix products, arithmetic and copies ran while one was open for 19% -> 15% of each run, Pallas kernels for 0% -> 0%
where the time goes in v7:
time: 234 us; the launch traced here: 233 us
  starting transfers between devices  97.9 us (42%)
  waiting for transfers between devices  73.2 us (31%)
  matrix products  38.1 us (16%)
  other arithmetic  16.2 us (7%)
  local copies, waits for them, and re-layouts  5.73 us (2%)
    ppermute x32, starting transfers between devices, shifted(): lax.ppermute(value, axis, [(source, source + steps) for source in range(l...  92.7 us
    ppermute x32, waiting for transfers between devices, shifted(): lax.ppermute(value, axis, [(source, source + steps) for source in range(l...  53.6 us
    ppermute x5, waiting for transfers between devices, halving_scatter(): got = lax.ppermute(sends, 'seq', pairs)  19.7 us
    dot_general x5, matrix products, backward_layer(): jnp.einsum('mpc,mpd->cd', taps, grad_pre, preferred_element_type=jnp.floa...  11.7 us
    dot_general x7, matrix products, mm(): return jnp.einsum('mpc,cd->mpd', a, b, preferred_element_type=jnp.float32)  5.77 us
    ppermute x5, starting transfers between devices, halving_scatter(): got = lax.ppermute(sends, 'seq', pairs)  5.21 us
    dot_general x5, matrix products, backward_layer(): jnp.einsum('mpd,cd->mpc', grad_pre, weights, preferred_element_type=jnp.f...  5.17 us
  transfers between devices with their start and end apart: 37, of which 17 were waited for; matrix products, arithmetic and copies ran while one was open for 15% of the time, Pallas kernels for 0%

profile of v7, /device:TPU:24, one launch (start us, length us, event | category | flops | bytes accessed | tf_op | source)
XLA Modules:
  0.0 233.1 jit_solution(7621913881144404979)
XLA Ops:
  1.7 1.9 collective-permute-start
  3.6 3.6 %collective-permute-start.1 = (bf16[2,128,256]{2,1,0:T(8,128)(2,1)S(1)}, bf16[2,128,256]{2,1,0:T(8,128)(2,1)S(1)}, u32[]{:S(2)}, u32[]{:S(2)}) collective-permute-start(bf16[2,128,256]{2,1,0:T(8,128)(2,1)S(1)} %get-tuple-element.102), channel_id=1, source_target_pairs={{1,0},{2,1},{3,2},{4,3},{5,4},{6,5},{7,6},{8,7},{9,8},{10,9},{11,1... | collective-permute-start | bytes 393224 | tf_op jit(solution)/shard_map/ppermute | solution.py:15
  7.3 1.6 fusion.161
  9.0 1.8 fusion.85
  12.7 5.6 %collective-permute-start.2 = (bf16[2,512,256]{2,1,0:T(8,128)(2,1)S(1)}, bf16[2,512,256]{2,1,0:T(8,128)(2,1)S(1)}, u32[]{:S(2)}, u32[]{:S(2)}) collective-permute-start(bf16[2,512,256]{2,1,0:T(8,128)(2,1)S(1)} %fusion.2), channel_id=1, source_target_pairs={{0,2},{1,3},{2,4},{3,5},{4,6},{5,7},{6,8},{7,9},{8,10},{9,11},{10,... | collective-permute-start | bytes 1572872 | tf_op jit(solution)/shard_map/ppermute | solution.py:15
  18.4 1.9 collective-permute-start.3
  20.9 8.2 %collective-permute-done.2 = bf16[2,512,256]{2,1,0:T(8,128)(2,1)S(1)} collective-permute-done((bf16[2,512,256]{2,1,0:T(8,128)(2,1)S(1)}, bf16[2,512,256]{2,1,0:T(8,128)(2,1)S(1)}, u32[]{:S(2)}, u32[]{:S(2)}) %collective-permute-start.2) | collective-permute-done | bytes 524320 | tf_op jit(solution)/shard_map/ppermute | solution.py:15
  29.6 5.8 %collective-permute-done.3 = bf16[2,512,256]{2,1,0:T(8,128)(2,1)S(1)} collective-permute-done((bf16[2,512,256]{2,1,0:T(8,128)(2,1)S(1)}, bf16[2,512,256]{2,1,0:T(8,128)(2,1)S(1)}, u32[]{:S(2)}, u32[]{:S(2)}) %collective-permute-start.3) | collective-permute-done | bytes 524320 | tf_op jit(solution)/shard_map/ppermute | solution.py:15
  37.8 1.9 collective-permute-start.5
  39.7 3.9 %collective-permute-start.4 = (bf16[2,512,256]{2,1,0:T(8,128)(2,1)S(1)}, bf16[2,512,256]{2,1,0:T(8,128)(2,1)S(1)}, u32[]{:S(2)}, u32[]{:S(2)}) collective-permute-start(bf16[2,512,256]{2,1,0:T(8,128)(2,1)S(1)} %get-tuple-element.50), channel_id=1, source_target_pairs={{2,0},{3,1},{4,2},{5,3},{6,4},{7,5},{8,6},{9,7},{10,8},{11,9},{12,... | collective-permute-start | bytes 1572872 | tf_op jit(solution)/shard_map/ppermute | solution.py:15
  45.1 6.7 %collective-permute-done.5 = bf16[2,512,256]{2,1,0:T(8,128)(2,1)S(1)} collective-permute-done((bf16[2,512,256]{2,1,0:T(8,128)(2,1)S(1)}, bf16[2,512,256]{2,1,0:T(8,128)(2,1)S(1)}, u32[]{:S(2)}, u32[]{:S(2)}) %collective-permute-start.5) | collective-permute-done | bytes 524320 | tf_op jit(solution)/shard_map/ppermute | solution.py:15
  51.8 4.0 %collective-permute-done.4 = bf16[2,512,256]{2,1,0:T(8,128)(2,1)S(1)} collective-permute-done((bf16[2,512,256]{2,1,0:T(8,128)(2,1)S(1)}, bf16[2,512,256]{2,1,0:T(8,128)(2,1)S(1)}, u32[]{:S(2)}, u32[]{:S(2)}) %collective-permute-start.4) | collective-permute-done | bytes 524320 | tf_op jit(solution)/shard_map/ppermute | solution.py:15
  57.9 2.1 collective-permute-start.6
  59.9 3.6 %collective-permute-start.7 = (bf16[2,128,256]{2,1,0:T(8,128)(2,1)S(1)}, bf16[2,128,256]{2,1,0:T(8,128)(2,1)S(1)}, u32[]{:S(2)}, u32[]{:S(2)}) collective-permute-start(bf16[2,128,256]{2,1,0:T(8,128)(2,1)S(1)} %get-tuple-element.49), channel_id=1, source_target_pairs={{1,0},{2,1},{3,2},{4,3},{5,4},{6,5},{7,6},{8,7},{9,8},{10,9},{11,1... | collective-permute-start | bytes 393224 | tf_op jit(solution)/shard_map/ppermute | solution.py:15
  64.5 1.3 collective-permute-start.11
  65.8 2.2 fusion.57
  69.0 1.3 collective-permute-start.8
  70.3 3.9 %collective-permute-done.11 = bf16[2,256,256]{2,1,0:T(8,128)(2,1)S(1)} collective-permute-done((bf16[2,256,256]{2,1,0:T(8,128)(2,1)S(1)}, bf16[2,256,256]{2,1,0:T(8,128)(2,1)S(1)}, u32[]{:S(2)}, u32[]{:S(2)}) %collective-permute-start.11) | collective-permute-done | bytes 262176 | tf_op jit(solution)/shard_map/ppermute | solution.py:15
  75.2 4.5 %collective-permute-start.13 = (bf16[2,256,256]{2,1,0:T(8,128)(2,1)S(1)}, bf16[2,256,256]{2,1,0:T(8,128)(2,1)S(1)}, u32[]{:S(2)}, u32[]{:S(2)}) collective-permute-start(bf16[2,256,256]{2,1,0:T(8,128)(2,1)S(1)} %get-tuple-element.73), channel_id=1, source_target_pairs={{0,2},{1,3},{2,4},{3,5},{4,6},{5,7},{6,8},{7,9},{8,10},{9,11},{10,... | collective-permute-start | bytes 786440 | tf_op jit(solution)/shard_map/ppermute | solution.py:15
  79.6 2.1 collective-permute-start.12
  82.7 6.0 %collective-permute-start.10 = (bf16[2,256,256]{2,1,0:T(8,128)(2,1)S(1)}, bf16[2,256,256]{2,1,0:T(8,128)(2,1)S(1)}, u32[]{:S(2)}, u32[]{:S(2)}) collective-permute-start(bf16[2,256,256]{2,1,0:T(8,128)(2,1)S(1)} %get-tuple-element.75), channel_id=1, source_target_pairs={{0,2},{1,3},{2,4},{3,5},{4,6},{5,7},{6,8},{7,9},{8,10},{9,11},{10,... | collective-permute-start | bytes 786440 | tf_op jit(solution)/shard_map/ppermute | solution.py:15
  88.7 1.9 collective-permute-start.9
  92.6 6.5 %collective-permute-done.9 = bf16[2,256,256]{2,1,0:T(8,128)(2,1)S(1)} collective-permute-done((bf16[2,256,256]{2,1,0:T(8,128)(2,1)S(1)}, bf16[2,256,256]{2,1,0:T(8,128)(2,1)S(1)}, u32[]{:S(2)}, u32[]{:S(2)}) %collective-permute-start.9) | collective-permute-done | bytes 262176 | tf_op jit(solution)/shard_map/ppermute | solution.py:15
  100.7 1.9 collective-permute-start.14
  102.6 3.6 %collective-permute-start.15 = (bf16[2,128,256]{2,1,0:T(8,128)(2,1)S(1)}, bf16[2,128,256]{2,1,0:T(8,128)(2,1)S(1)}, u32[]{:S(2)}, u32[]{:S(2)}) collective-permute-start(bf16[2,128,256]{2,1,0:T(8,128)(2,1)S(1)} %get-tuple-element.47), channel_id=1, source_target_pairs={{1,0},{2,1},{3,2},{4,3},{5,4},{6,5},{7,6},{8,7},{9,8},{10,9},{11,1... | collective-permute-start | bytes 393224 | tf_op jit(solution)/shard_map/ppermute | solution.py:15
  106.3 1.1 fusion.261
  107.3 1.3 collective-permute-start.19
  108.6 2.2 fusion.55
  112.1 1.3 collective-permute-start.16
  113.4 2.9 %collective-permute-done.19 = bf16[2,256,256]{2,1,0:T(8,128)(2,1)S(1)} collective-permute-done((bf16[2,256,256]{2,1,0:T(8,128)(2,1)S(1)}, bf16[2,256,256]{2,1,0:T(8,128)(2,1)S(1)}, u32[]{:S(2)}, u32[]{:S(2)}) %collective-permute-start.19) | collective-permute-done | bytes 262176 | tf_op jit(solution)/shard_map/ppermute | solution.py:15
  117.2 4.6 %collective-permute-start.21 = (bf16[2,256,256]{2,1,0:T(8,128)(2,1)S(1)}, bf16[2,256,256]{2,1,0:T(8,128)(2,1)S(1)}, u32[]{:S(2)}, u32[]{:S(2)}) collective-permute-start(bf16[2,256,256]{2,1,0:T(8,128)(2,1)S(1)} %get-tuple-element.69), channel_id=1, source_target_pairs={{0,2},{1,3},{2,4},{3,5},{4,6},{5,7},{6,8},{7,9},{8,10},{9,11},{10,... | collective-permute-start | bytes 786440 | tf_op jit(solution)/shard_map/ppermute | solution.py:15
  121.8 1.9 collective-permute-start.20
  124.7 6.0 %collective-permute-start.18 = (bf16[2,256,256]{2,1,0:T(8,128)(2,1)S(1)}, bf16[2,256,256]{2,1,0:T(8,128)(2,1)S(1)}, u32[]{:S(2)}, u32[]{:S(2)}) collective-permute-start(bf16[2,256,256]{2,1,0:T(8,128)(2,1)S(1)} %get-tuple-element.71), channel_id=1, source_target_pairs={{0,2},{1,3},{2,4},{3,5},{4,6},{5,7},{6,8},{7,9},{8,10},{9,11},{10,... | collective-permute-start | bytes 786440 | tf_op jit(solution)/shard_map/ppermute | solution.py:15
  130.7 1.9 collective-permute-start.17
  134.6 6.5 %collective-permute-done.17 = bf16[2,256,256]{2,1,0:T(8,128)(2,1)S(1)} collective-permute-done((bf16[2,256,256]{2,1,0:T(8,128)(2,1)S(1)}, bf16[2,256,256]{2,1,0:T(8,128)(2,1)S(1)}, u32[]{:S(2)}, u32[]{:S(2)}) %collective-permute-start.17) | collective-permute-done | bytes 262176 | tf_op jit(solution)/shard_map/ppermute | solution.py:15
  142.7 1.9 collective-permute-start.22
  144.6 3.6 %collective-permute-start.23 = (bf16[2,128,256]{2,1,0:T(8,128)(2,1)S(1)}, bf16[2,128,256]{2,1,0:T(8,128)(2,1)S(1)}, u32[]{:S(2)}, u32[]{:S(2)}) collective-permute-start(bf16[2,128,256]{2,1,0:T(8,128)(2,1)S(1)} %get-tuple-element.45), channel_id=1, source_target_pairs={{1,0},{2,1},{3,2},{4,3},{5,4},{6,5},{7,6},{8,7},{9,8},{10,9},{11,1... | collective-permute-start | bytes 393224 | tf_op jit(solution)/shard_map/ppermute | solution.py:15
  148.3 1.1 fusion.259
  149.3 1.3 collective-permute-start.27
  150.6 2.2 fusion.53
  154.1 1.5 collective-permute-start.24
  155.7 2.6 %collective-permute-done.27 = bf16[2,256,256]{2,1,0:T(8,128)(2,1)S(1)} collective-permute-done((bf16[2,256,256]{2,1,0:T(8,128)(2,1)S(1)}, bf16[2,256,256]{2,1,0:T(8,128)(2,1)S(1)}, u32[]{:S(2)}, u32[]{:S(2)}) %collective-permute-start.27) | collective-permute-done | bytes 262176 | tf_op jit(solution)/shard_map/ppermute | solution.py:15
  159.2 4.5 %collective-permute-start.29 = (bf16[2,256,256]{2,1,0:T(8,128)(2,1)S(1)}, bf16[2,256,256]{2,1,0:T(8,128)(2,1)S(1)}, u32[]{:S(2)}, u32[]{:S(2)}) collective-permute-start(bf16[2,256,256]{2,1,0:T(8,128)(2,1)S(1)} %get-tuple-element.65), channel_id=1, source_target_pairs={{0,2},{1,3},{2,4},{3,5},{4,6},{5,7},{6,8},{7,9},{8,10},{9,11},{10,... | collective-permute-start | bytes 786440 | tf_op jit(solution)/shard_map/ppermute | solution.py:15
  163.7 1.9 collective-permute-start.28
  166.7 6.0 %collective-permute-start.26 = (bf16[2,256,256]{2,1,0:T(8,128)(2,1)S(1)}, bf16[2,256,256]{2,1,0:T(8,128)(2,1)S(1)}, u32[]{:S(2)}, u32[]{:S(2)}) collective-permute-start(bf16[2,256,256]{2,1,0:T(8,128)(2,1)S(1)} %get-tuple-element.67), channel_id=1, source_target_pairs={{0,2},{1,3},{2,4},{3,5},{4,6},{5,7},{6,8},{7,9},{8,10},{9,11},{10,... | collective-permute-start | bytes 786440 | tf_op jit(solution)/shard_map/ppermute | solution.py:15
  172.8 1.9 collective-permute-start.25
  174.7 2.2 bitcast_add_fusion
  177.8 5.4 %collective-permute-done.25 = bf16[2,256,256]{2,1,0:T(8,128)(2,1)S(1)} collective-permute-done((bf16[2,256,256]{2,1,0:T(8,128)(2,1)S(1)}, bf16[2,256,256]{2,1,0:T(8,128)(2,1)S(1)}, u32[]{:S(2)}, u32[]{:S(2)}) %collective-permute-start.25) | collective-permute-done | bytes 262176 | tf_op jit(solution)/shard_map/ppermute | solution.py:15
  183.3 1.3 multiply_convert_fusion.1
  186.2 4.0 %bitcast_add_fusion.3 = f32[768,512]{1,0:T(8,128)S(1)} fusion(f32[768,512,1]{1,0,2:T(8,128)} %fusion.53, f32[768,512,1]{1,0,2:T(8,128)} %fusion.55, f32[768,512,1]{1,0,2:T(8,128)} %fusion.57, bf16[2,512,256]{1,2,0:T(8,128)(2,1)} %get-tuple-element.55, bf16[2,512,256]{1,2,0:T(8,128)(2,1)} %get-tuple-element.54, ...), kind=kOutput, calls=%fused_computation.12 | convolution fusion | flops 816447488 | bytes 8912896 | tf_op jit(solution)/shard_map/mpc,mpd->cd/dot_general | solution.py:62
  190.8 1.9 copy-done
  192.7 1.1 fusion.47
  193.8 2.8 %collective-permute-done.32 = bf16[2,2,2,2,56,512]{5,4,3,2,1,0:T(8,128)(2,1)} collective-permute-done((bf16[2,2,2,2,56,512]{5,4,3,2,1,0:T(8,128)(2,1)}, bf16[2,2,2,2,56,512]{5,4,3,2,1,0:T(8,128)(2,1)}, u32[]{:S(2)}, u32[]{:S(2)}) %collective-permute-start.32) | collective-permute-done | bytes 917536 | tf_op jit(solution)/shard_map/ppermute | solution.py:159
  196.6 2.8 %fusion.1 = f32[2,2,2,2,56,512]{5,4,3,2,1,0:T(8,128)S(1)} fusion(bf16[2,2,2,2,56,512]{5,4,3,2,1,0:T(8,128)(2,1)} %collective-permute-done.32, f32[2,2,2,2,2,56,512]{6,5,4,3,2,1,0:T(8,128)} %copy-done, pred[]{:T(512)S(6)} %eq.23), kind=kLoop, calls=%fused_computation.5 | loop fusion | flops 1376256 | bytes 6422529 | tf_op jit(solution)/shard_map/add | solution.py:161
  200.7 2.2 collective-permute-start.30
  202.9 3.5 %collective-permute-start.31 = (bf16[2,128,256]{2,1,0:T(8,128)(2,1)S(1)}, bf16[2,128,256]{2,1,0:T(8,128)(2,1)S(1)}, u32[]{:S(2)}, u32[]{:S(2)}) collective-permute-start(bf16[2,128,256]{2,1,0:T(8,128)(2,1)S(1)} %get-tuple-element.43), channel_id=1, source_target_pairs={{1,0},{2,1},{3,2},{4,3},{5,4},{6,5},{7,6},{8,7},{9,8},{10,9},{11,1... | collective-permute-start | bytes 393224 | tf_op jit(solution)/shard_map/ppermute | solution.py:15
  206.4 6.6 %collective-permute-done.33 = bf16[2,2,2,56,512]{4,3,2,1,0:T(8,128)(2,1)S(1)} collective-permute-done((bf16[2,2,2,56,512]{4,3,2,1,0:T(8,128)(2,1)S(1)}, bf16[2,2,2,56,512]{4,3,2,1,0:T(8,128)(2,1)S(1)}, u32[]{:S(2)}, u32[]{:S(2)}) %collective-permute-start.33) | collective-permute-done | bytes 458784 | tf_op jit(solution)/shard_map/ppermute | solution.py:159
  213.3 1.7 collective-permute-start.34
  215.0 1.3 fusion.66
  216.3 3.1 %collective-permute-done.34 = bf16[2,2,56,512]{3,2,1,0:T(8,128)(2,1)S(1)} collective-permute-done((bf16[2,2,56,512]{3,2,1,0:T(8,128)(2,1)S(1)}, bf16[2,2,56,512]{3,2,1,0:T(8,128)(2,1)S(1)}, u32[]{:S(2)}, u32[]{:S(2)}) %collective-permute-start.34) | collective-permute-done | bytes 229408 | tf_op jit(solution)/shard_map/ppermute | solution.py:159
  219.9 6.1 %collective-permute-done.35 = bf16[2,56,512]{2,1,0:T(8,128)(2,1)S(1)} collective-permute-done((bf16[2,56,512]{2,1,0:T(8,128)(2,1)S(1)}, bf16[2,56,512]{2,1,0:T(8,128)(2,1)S(1)}, u32[]{:S(2)}, u32[]{:S(2)}) %collective-permute-start.35) | collective-permute-done | bytes 114720 | tf_op jit(solution)/shard_map/ppermute | solution.py:159
  226.1 3.3 %collective-permute-start.36 = (bf16[56,512]{1,0:T(8,128)(2,1)S(1)}, bf16[56,512]{1,0:T(8,128)(2,1)S(1)}, u32[]{:S(2)}, u32[]{:S(2)}) collective-permute-start(bf16[56,512]{1,0:T(8,128)(2,1)S(1)} %fusion.203), channel_id=1, source_target_pairs={{0,16},{1,17},{2,18},{3,19},{4,20},{5,21},{6,22},{7,23},{8,24},{9,... | collective-permute-start | bytes 172040 | tf_op jit(solution)/shard_map/ppermute | solution.py:159
  229.5 1.2 fusion.20
  230.7 1.1 collective-permute-done.36
  (173 shorter events, 33.1 us)
Async XLA Ops:
  0.6 8.3 %copy-start.1 = (bf16[1,2,512,256]{3,2,1,0:T(8,128)(2,1)S(1)}, bf16[1,2,512,256]{3,2,1,0:T(8,128)(2,1)}, u32[]{:S(2)}) copy-start(bf16[1,2,512,256]{3,2,1,0:T(8,128)(2,1)} %param.4) | copy-start | bytes 1572868
  1.7 7.3 %collective-permute-start = (bf16[2,128,256]{2,1,0:T(8,128)(2,1)S(1)}, bf16[2,128,256]{2,1,0:T(8,128)(2,1)S(1)}, u32[]{:S(2)}, u32[]{:S(2)}) collective-permute-start(bf16[2,128,256]{2,1,0:T(8,128)(2,1)S(1)} %get-tuple-element.103), channel_id=1, source_target_pairs={{0,1},{1,2},{2,3},{3,4},{4,5},{5,6},{6,7},{7,8},{8,9},{9,10},{10,1... | collective-permute-start | bytes 393224 | tf_op jit(solution)/shard_map/ppermute | solution.py:15
  3.6 7.2 %collective-permute-start.1 = (bf16[2,128,256]{2,1,0:T(8,128)(2,1)S(1)}, bf16[2,128,256]{2,1,0:T(8,128)(2,1)S(1)}, u32[]{:S(2)}, u32[]{:S(2)}) collective-permute-start(bf16[2,128,256]{2,1,0:T(8,128)(2,1)S(1)} %get-tuple-element.102), channel_id=1, source_target_pairs={{1,0},{2,1},{3,2},{4,3},{5,4},{6,5},{7,6},{8,7},{9,8},{10,9},{11,1... | collective-permute-start | bytes 393224 | tf_op jit(solution)/shard_map/ppermute | solution.py:15
  8.9 2.0 copy-start.3
  9.0 141.6 %copy-start.14 = (bf16[2,384,256]{2,1,0:T(8,128)(2,1)}, bf16[2,384,256]{2,1,0:T(8,128)(2,1)S(1)}, u32[]{:S(2)}) copy-start(bf16[2,384,256]{2,1,0:T(8,128)(2,1)S(1)} %get-tuple-element.100) | copy-start | bytes 1179652
  9.0 141.6 %copy-start.15 = (bf16[2,384,256]{2,1,0:T(8,128)(2,1)}, bf16[2,384,256]{2,1,0:T(8,128)(2,1)S(1)}, u32[]{:S(2)}) copy-start(bf16[2,384,256]{2,1,0:T(8,128)(2,1)S(1)} %get-tuple-element.101) | copy-start | bytes 1179652
  9.0 2.4 %copy-start.26 = (bf16[2,128,256]{2,1,0:T(8,128)(2,1)}, bf16[2,128,256]{2,1,0:T(8,128)(2,1)S(1)}, u32[]{:S(2)}) copy-start(bf16[2,128,256]{2,1,0:T(8,128)(2,1)S(1)} %collective-permute-done) | copy-start | bytes 393220
  12.7 16.4 %collective-permute-start.2 = (bf16[2,512,256]{2,1,0:T(8,128)(2,1)S(1)}, bf16[2,512,256]{2,1,0:T(8,128)(2,1)S(1)}, u32[]{:S(2)}, u32[]{:S(2)}) collective-permute-start(bf16[2,512,256]{2,1,0:T(8,128)(2,1)S(1)} %fusion.2), channel_id=1, source_target_pairs={{0,2},{1,3},{2,4},{3,5},{4,6},{5,7},{6,8},{7,9},{8,10},{9,11},{10,... | collective-permute-start | bytes 1572872 | tf_op jit(solution)/shard_map/ppermute | solution.py:15
  18.4 17.0 %collective-permute-start.3 = (bf16[2,512,256]{2,1,0:T(8,128)(2,1)S(1)}, bf16[2,512,256]{2,1,0:T(8,128)(2,1)S(1)}, u32[]{:S(2)}, u32[]{:S(2)}) collective-permute-start(bf16[2,512,256]{2,1,0:T(8,128)(2,1)S(1)} %fusion.2), channel_id=1, source_target_pairs={{2,0},{3,1},{4,2},{5,3},{6,4},{7,5},{8,6},{9,7},{10,8},{11,9},{12,... | collective-permute-start | bytes 1572872 | tf_op jit(solution)/shard_map/ppermute | solution.py:15
  29.6 6.4 %copy-start.7 = (bf16[2,512,256]{2,1,0:T(8,128)(2,1)S(1)}, bf16[2,512,256]{2,1,0:T(8,128)(2,1)}, u32[]{:S(2)}) copy-start(bf16[2,512,256]{2,1,0:T(8,128)(2,1)} %param.5) | copy-start | bytes 1572868
  37.8 14.0 %collective-permute-start.5 = (bf16[2,512,256]{2,1,0:T(8,128)(2,1)S(1)}, bf16[2,512,256]{2,1,0:T(8,128)(2,1)S(1)}, u32[]{:S(2)}, u32[]{:S(2)}) collective-permute-start(bf16[2,512,256]{2,1,0:T(8,128)(2,1)S(1)} %get-tuple-element.51), channel_id=1, source_target_pairs={{0,2},{1,3},{2,4},{3,5},{4,6},{5,7},{6,8},{7,9},{8,10},{9,11},{10,... | collective-permute-start | bytes 1572872 | tf_op jit(solution)/shard_map/ppermute | solution.py:15
  39.7 16.1 %collective-permute-start.4 = (bf16[2,512,256]{2,1,0:T(8,128)(2,1)S(1)}, bf16[2,512,256]{2,1,0:T(8,128)(2,1)S(1)}, u32[]{:S(2)}, u32[]{:S(2)}) collective-permute-start(bf16[2,512,256]{2,1,0:T(8,128)(2,1)S(1)} %get-tuple-element.50), channel_id=1, source_target_pairs={{2,0},{3,1},{4,2},{5,3},{6,4},{7,5},{8,6},{9,7},{10,8},{11,9},{12,... | collective-permute-start | bytes 1572872 | tf_op jit(solution)/shard_map/ppermute | solution.py:15
  57.8 8.0 %copy-start.27 = (bf16[2,128,256]{2,1,0:T(8,128)(2,1)S(1)}, bf16[2,128,256]{2,1,0:T(8,128)(2,1)}, u32[]{:S(2)}) copy-start(bf16[2,128,256]{2,1,0:T(8,128)(2,1)} %copy-done.26) | copy-start | bytes 393220
  57.9 10.1 %collective-permute-start.6 = (bf16[2,128,256]{2,1,0:T(8,128)(2,1)S(1)}, bf16[2,128,256]{2,1,0:T(8,128)(2,1)S(1)}, u32[]{:S(2)}, u32[]{:S(2)}) collective-permute-start(bf16[2,128,256]{2,1,0:T(8,128)(2,1)S(1)} %get-tuple-element.48), channel_id=1, source_target_pairs={{0,1},{1,2},{2,3},{3,4},{4,5},{5,6},{6,7},{7,8},{8,9},{9,10},{10,1... | collective-permute-start | bytes 393224 | tf_op jit(solution)/shard_map/ppermute | solution.py:15
  59.9 8.1 %collective-permute-start.7 = (bf16[2,128,256]{2,1,0:T(8,128)(2,1)S(1)}, bf16[2,128,256]{2,1,0:T(8,128)(2,1)S(1)}, u32[]{:S(2)}, u32[]{:S(2)}) collective-permute-start(bf16[2,128,256]{2,1,0:T(8,128)(2,1)S(1)} %get-tuple-element.49), channel_id=1, source_target_pairs={{1,0},{2,1},{3,2},{4,3},{5,4},{6,5},{7,6},{8,7},{9,8},{10,9},{11,1... | collective-permute-start | bytes 393224 | tf_op jit(solution)/shard_map/ppermute | solution.py:15
  64.5 9.7 %collective-permute-start.11 = (bf16[2,256,256]{2,1,0:T(8,128)(2,1)S(1)}, bf16[2,256,256]{2,1,0:T(8,128)(2,1)S(1)}, u32[]{:S(2)}, u32[]{:S(2)}) collective-permute-start(bf16[2,256,256]{2,1,0:T(8,128)(2,1)S(1)} %get-tuple-element.19), channel_id=1, source_target_pairs={{32,0},{64,32},{96,64},{33,1},{65,33},{97,65},{34,2},{66,34},{98,6... | collective-permute-start | bytes 786440 | tf_op jit(solution)/shard_map/ppermute | solution.py:15
  69.0 12.7 %collective-permute-start.8 = (bf16[2,256,256]{2,1,0:T(8,128)(2,1)S(1)}, bf16[2,256,256]{2,1,0:T(8,128)(2,1)S(1)}, u32[]{:S(2)}, u32[]{:S(2)}) collective-permute-start(bf16[2,256,256]{2,1,0:T(8,128)(2,1)S(1)} %pad_maximum_fusion.29), channel_id=1, source_target_pairs={{32,0},{64,32},{96,64},{33,1},{65,33},{97,65},{34,2},{66,34},{98,6... | collective-permute-start | bytes 786440 | tf_op jit(solution)/shard_map/ppermute | solution.py:15
  75.2 16.7 %collective-permute-start.13 = (bf16[2,256,256]{2,1,0:T(8,128)(2,1)S(1)}, bf16[2,256,256]{2,1,0:T(8,128)(2,1)S(1)}, u32[]{:S(2)}, u32[]{:S(2)}) collective-permute-start(bf16[2,256,256]{2,1,0:T(8,128)(2,1)S(1)} %get-tuple-element.73), channel_id=1, source_target_pairs={{0,2},{1,3},{2,4},{3,5},{4,6},{5,7},{6,8},{7,9},{8,10},{9,11},{10,... | collective-permute-start | bytes 786440 | tf_op jit(solution)/shard_map/ppermute | solution.py:15
  79.6 12.2 %collective-permute-start.12 = (bf16[2,256,256]{2,1,0:T(8,128)(2,1)S(1)}, bf16[2,256,256]{2,1,0:T(8,128)(2,1)S(1)}, u32[]{:S(2)}, u32[]{:S(2)}) collective-permute-start(bf16[2,256,256]{2,1,0:T(8,128)(2,1)S(1)} %get-tuple-element.72), channel_id=1, source_target_pairs={{2,0},{3,1},{4,2},{5,3},{6,4},{7,5},{8,6},{9,7},{10,8},{11,9},{12,... | collective-permute-start | bytes 786440 | tf_op jit(solution)/shard_map/ppermute | solution.py:15
  82.7 9.9 %collective-permute-start.10 = (bf16[2,256,256]{2,1,0:T(8,128)(2,1)S(1)}, bf16[2,256,256]{2,1,0:T(8,128)(2,1)S(1)}, u32[]{:S(2)}, u32[]{:S(2)}) collective-permute-start(bf16[2,256,256]{2,1,0:T(8,128)(2,1)S(1)} %get-tuple-element.75), channel_id=1, source_target_pairs={{0,2},{1,3},{2,4},{3,5},{4,6},{5,7},{6,8},{7,9},{8,10},{9,11},{10,... | collective-permute-start | bytes 786440 | tf_op jit(solution)/shard_map/ppermute | solution.py:15
  88.7 10.4 %collective-permute-start.9 = (bf16[2,256,256]{2,1,0:T(8,128)(2,1)S(1)}, bf16[2,256,256]{2,1,0:T(8,128)(2,1)S(1)}, u32[]{:S(2)}, u32[]{:S(2)}) collective-permute-start(bf16[2,256,256]{2,1,0:T(8,128)(2,1)S(1)} %get-tuple-element.74), channel_id=1, source_target_pairs={{2,0},{3,1},{4,2},{5,3},{6,4},{7,5},{8,6},{9,7},{10,8},{11,9},{12,... | collective-permute-start | bytes 786440 | tf_op jit(solution)/shard_map/ppermute | solution.py:15
  100.7 10.4 %collective-permute-start.14 = (bf16[2,128,256]{2,1,0:T(8,128)(2,1)S(1)}, bf16[2,128,256]{2,1,0:T(8,128)(2,1)S(1)}, u32[]{:S(2)}, u32[]{:S(2)}) collective-permute-start(bf16[2,128,256]{2,1,0:T(8,128)(2,1)S(1)} %get-tuple-element.46), channel_id=1, source_target_pairs={{0,1},{1,2},{2,3},{3,4},{4,5},{5,6},{6,7},{7,8},{8,9},{9,10},{10,1... | collective-permute-start | bytes 393224 | tf_op jit(solution)/shard_map/ppermute | solution.py:15
  102.6 8.5 %collective-permute-start.15 = (bf16[2,128,256]{2,1,0:T(8,128)(2,1)S(1)}, bf16[2,128,256]{2,1,0:T(8,128)(2,1)S(1)}, u32[]{:S(2)}, u32[]{:S(2)}) collective-permute-start(bf16[2,128,256]{2,1,0:T(8,128)(2,1)S(1)} %get-tuple-element.47), channel_id=1, source_target_pairs={{1,0},{2,1},{3,2},{4,3},{5,4},{6,5},{7,6},{8,7},{9,8},{10,9},{11,1... | collective-permute-start | bytes 393224 | tf_op jit(solution)/shard_map/ppermute | solution.py:15
  107.3 9.0 %collective-permute-start.19 = (bf16[2,256,256]{2,1,0:T(8,128)(2,1)S(1)}, bf16[2,256,256]{2,1,0:T(8,128)(2,1)S(1)}, u32[]{:S(2)}, u32[]{:S(2)}) collective-permute-start(bf16[2,256,256]{2,1,0:T(8,128)(2,1)S(1)} %get-tuple-element.5), channel_id=1, source_target_pairs={{32,0},{64,32},{96,64},{33,1},{65,33},{97,65},{34,2},{66,34},{98,6... | collective-permute-start | bytes 786440 | tf_op jit(solution)/shard_map/ppermute | solution.py:15
  112.1 11.6 %collective-permute-start.16 = (bf16[2,256,256]{2,1,0:T(8,128)(2,1)S(1)}, bf16[2,256,256]{2,1,0:T(8,128)(2,1)S(1)}, u32[]{:S(2)}, u32[]{:S(2)}) collective-permute-start(bf16[2,256,256]{2,1,0:T(8,128)(2,1)S(1)} %pad_maximum_fusion.30), channel_id=1, source_target_pairs={{32,0},{64,32},{96,64},{33,1},{65,33},{97,65},{34,2},{66,34},{98,6... | collective-permute-start | bytes 786440 | tf_op jit(solution)/shard_map/ppermute | solution.py:15
  117.2 16.9 %collective-permute-start.21 = (bf16[2,256,256]{2,1,0:T(8,128)(2,1)S(1)}, bf16[2,256,256]{2,1,0:T(8,128)(2,1)S(1)}, u32[]{:S(2)}, u32[]{:S(2)}) collective-permute-start(bf16[2,256,256]{2,1,0:T(8,128)(2,1)S(1)} %get-tuple-element.69), channel_id=1, source_target_pairs={{0,2},{1,3},{2,4},{3,5},{4,6},{5,7},{6,8},{7,9},{8,10},{9,11},{10,... | collective-permute-start | bytes 786440 | tf_op jit(solution)/shard_map/ppermute | solution.py:15
  121.8 12.3 %collective-permute-start.20 = (bf16[2,256,256]{2,1,0:T(8,128)(2,1)S(1)}, bf16[2,256,256]{2,1,0:T(8,128)(2,1)S(1)}, u32[]{:S(2)}, u32[]{:S(2)}) collective-permute-start(bf16[2,256,256]{2,1,0:T(8,128)(2,1)S(1)} %get-tuple-element.68), channel_id=1, source_target_pairs={{2,0},{3,1},{4,2},{5,3},{6,4},{7,5},{8,6},{9,7},{10,8},{11,9},{12,... | collective-permute-start | bytes 786440 | tf_op jit(solution)/shard_map/ppermute | solution.py:15
  124.7 9.9 %collective-permute-start.18 = (bf16[2,256,256]{2,1,0:T(8,128)(2,1)S(1)}, bf16[2,256,256]{2,1,0:T(8,128)(2,1)S(1)}, u32[]{:S(2)}, u32[]{:S(2)}) collective-permute-start(bf16[2,256,256]{2,1,0:T(8,128)(2,1)S(1)} %get-tuple-element.71), channel_id=1, source_target_pairs={{0,2},{1,3},{2,4},{3,5},{4,6},{5,7},{6,8},{7,9},{8,10},{9,11},{10,... | collective-permute-start | bytes 786440 | tf_op jit(solution)/shard_map/ppermute | solution.py:15
  130.7 10.4 %collective-permute-start.17 = (bf16[2,256,256]{2,1,0:T(8,128)(2,1)S(1)}, bf16[2,256,256]{2,1,0:T(8,128)(2,1)S(1)}, u32[]{:S(2)}, u32[]{:S(2)}) collective-permute-start(bf16[2,256,256]{2,1,0:T(8,128)(2,1)S(1)} %get-tuple-element.70), channel_id=1, source_target_pairs={{2,0},{3,1},{4,2},{5,3},{6,4},{7,5},{8,6},{9,7},{10,8},{11,9},{12,... | collective-permute-start | bytes 786440 | tf_op jit(solution)/shard_map/ppermute | solution.py:15
  142.7 10.5 %collective-permute-start.22 = (bf16[2,128,256]{2,1,0:T(8,128)(2,1)S(1)}, bf16[2,128,256]{2,1,0:T(8,128)(2,1)S(1)}, u32[]{:S(2)}, u32[]{:S(2)}) collective-permute-start(bf16[2,128,256]{2,1,0:T(8,128)(2,1)S(1)} %get-tuple-element.44), channel_id=1, source_target_pairs={{0,1},{1,2},{2,3},{3,4},{4,5},{5,6},{6,7},{7,8},{8,9},{9,10},{10,1... | collective-permute-start | bytes 393224 | tf_op jit(solution)/shard_map/ppermute | solution.py:15
  144.6 8.6 %collective-permute-start.23 = (bf16[2,128,256]{2,1,0:T(8,128)(2,1)S(1)}, bf16[2,128,256]{2,1,0:T(8,128)(2,1)S(1)}, u32[]{:S(2)}, u32[]{:S(2)}) collective-permute-start(bf16[2,128,256]{2,1,0:T(8,128)(2,1)S(1)} %get-tuple-element.45), channel_id=1, source_target_pairs={{1,0},{2,1},{3,2},{4,3},{5,4},{6,5},{7,6},{8,7},{9,8},{10,9},{11,1... | collective-permute-start | bytes 393224 | tf_op jit(solution)/shard_map/ppermute | solution.py:15
  149.3 9.0 %collective-permute-start.27 = (bf16[2,256,256]{2,1,0:T(8,128)(2,1)S(1)}, bf16[2,256,256]{2,1,0:T(8,128)(2,1)S(1)}, u32[]{:S(2)}, u32[]{:S(2)}) collective-permute-start(bf16[2,256,256]{2,1,0:T(8,128)(2,1)S(1)} %get-tuple-element.3), channel_id=1, source_target_pairs={{32,0},{64,32},{96,64},{33,1},{65,33},{97,65},{34,2},{66,34},{98,6... | collective-permute-start | bytes 786440 | tf_op jit(solution)/shard_map/ppermute | solution.py:15
  154.1 11.5 %collective-permute-start.24 = (bf16[2,256,256]{2,1,0:T(8,128)(2,1)S(1)}, bf16[2,256,256]{2,1,0:T(8,128)(2,1)S(1)}, u32[]{:S(2)}, u32[]{:S(2)}) collective-permute-start(bf16[2,256,256]{2,1,0:T(8,128)(2,1)S(1)} %pad_maximum_fusion.31), channel_id=1, source_target_pairs={{32,0},{64,32},{96,64},{33,1},{65,33},{97,65},{34,2},{66,34},{98,6... | collective-permute-start | bytes 786440 | tf_op jit(solution)/shard_map/ppermute | solution.py:15
  158.3 19.4 %copy-start.5 = (bf16[2,256,256]{2,1,0:T(8,128)(2,1)}, bf16[2,256,256]{2,1,0:T(8,128)(2,1)S(1)}, u32[]{:S(2)}) copy-start(bf16[2,256,256]{2,1,0:T(8,128)(2,1)S(1)} %collective-permute-done.27) | copy-start | bytes 786436
  159.2 18.5 %copy-start.4 = (f32[2,256,768]{2,1,0:T(8,128)}, f32[2,256,768]{2,1,0:T(8,128)S(1)}, u32[]{:S(2)}) copy-start(f32[2,256,768]{2,1,0:T(8,128)S(1)} %get-tuple-element.129) | copy-start | bytes 4718596
  159.2 18.4 %collective-permute-start.29 = (bf16[2,256,256]{2,1,0:T(8,128)(2,1)S(1)}, bf16[2,256,256]{2,1,0:T(8,128)(2,1)S(1)}, u32[]{:S(2)}, u32[]{:S(2)}) collective-permute-start(bf16[2,256,256]{2,1,0:T(8,128)(2,1)S(1)} %get-tuple-element.65), channel_id=1, source_target_pairs={{0,2},{1,3},{2,4},{3,5},{4,6},{5,7},{6,8},{7,9},{8,10},{9,11},{10,... | collective-permute-start | bytes 786440 | tf_op jit(solution)/shard_map/ppermute | solution.py:15
  163.7 13.9 %collective-permute-start.28 = (bf16[2,256,256]{2,1,0:T(8,128)(2,1)S(1)}, bf16[2,256,256]{2,1,0:T(8,128)(2,1)S(1)}, u32[]{:S(2)}, u32[]{:S(2)}) collective-permute-start(bf16[2,256,256]{2,1,0:T(8,128)(2,1)S(1)} %get-tuple-element.64), channel_id=1, source_target_pairs={{2,0},{3,1},{4,2},{5,3},{6,4},{7,5},{8,6},{9,7},{10,8},{11,9},{12,... | collective-permute-start | bytes 786440 | tf_op jit(solution)/shard_map/ppermute | solution.py:15
  166.7 11.0 %collective-permute-start.26 = (bf16[2,256,256]{2,1,0:T(8,128)(2,1)S(1)}, bf16[2,256,256]{2,1,0:T(8,128)(2,1)S(1)}, u32[]{:S(2)}, u32[]{:S(2)}) collective-permute-start(bf16[2,256,256]{2,1,0:T(8,128)(2,1)S(1)} %get-tuple-element.67), channel_id=1, source_target_pairs={{0,2},{1,3},{2,4},{3,5},{4,6},{5,7},{6,8},{7,9},{8,10},{9,11},{10,... | collective-permute-start | bytes 786440 | tf_op jit(solution)/shard_map/ppermute | solution.py:15
  172.8 10.4 %collective-permute-start.25 = (bf16[2,256,256]{2,1,0:T(8,128)(2,1)S(1)}, bf16[2,256,256]{2,1,0:T(8,128)(2,1)S(1)}, u32[]{:S(2)}, u32[]{:S(2)}) collective-permute-start(bf16[2,256,256]{2,1,0:T(8,128)(2,1)S(1)} %get-tuple-element.66), channel_id=1, source_target_pairs={{2,0},{3,1},{4,2},{5,3},{6,4},{7,5},{8,6},{9,7},{10,8},{11,9},{12,... | collective-permute-start | bytes 786440 | tf_op jit(solution)/shard_map/ppermute | solution.py:15
  177.6 7.0 %copy-start.22 = (bf16[2,256,256]{2,1,0:T(8,128)(2,1)}, bf16[2,256,256]{2,1,0:T(8,128)(2,1)S(1)}, u32[]{:S(2)}) copy-start(bf16[2,256,256]{2,1,0:T(8,128)(2,1)S(1)} %collective-permute-done.29) | copy-start | bytes 786436
  177.6 7.0 %copy-start.24 = (bf16[2,256,256]{2,1,0:T(8,128)(2,1)}, bf16[2,256,256]{2,1,0:T(8,128)(2,1)S(1)}, u32[]{:S(2)}) copy-start(bf16[2,256,256]{2,1,0:T(8,128)(2,1)S(1)} %collective-permute-done.28) | copy-start | bytes 786436
  186.2 4.1 %copy-start.13 = (f32[768,512]{1,0:T(8,128)S(1)}, f32[768,512]{1,0:T(8,128)}, u32[]{:S(2)}) copy-start(f32[768,512]{1,0:T(8,128)} %bitcast_add_fusion) | copy-start | bytes 4718596
  190.8 1.9 copy-start
  193.8 2.8 %collective-permute-start.32 = (bf16[2,2,2,2,56,512]{5,4,3,2,1,0:T(8,128)(2,1)}, bf16[2,2,2,2,56,512]{5,4,3,2,1,0:T(8,128)(2,1)}, u32[]{:S(2)}, u32[]{:S(2)}) collective-permute-start(bf16[2,2,2,2,56,512]{5,4,3,2,1,0:T(8,128)(2,1)} %fusion.47), channel_id=1, source_target_pairs={{0,1},{1,0},{2,3},{3,2},{4,5},{5,4},{6,7},{7,6},{8,9},{9,8},{10,11... | collective-permute-start | bytes 2752520 | tf_op jit(solution)/shard_map/ppermute | solution.py:159
  193.8 5.8 %copy-start.11 = (bf16[2,512,256]{1,2,0:T(8,128)(2,1)S(1)}, bf16[2,512,256]{1,2,0:T(8,128)(2,1)}, u32[]{:S(2)}) copy-start(bf16[2,512,256]{1,2,0:T(8,128)(2,1)} %get-tuple-element.54) | copy-start | bytes 1572868
  193.8 5.9 %copy-start.12 = (bf16[2,512,256]{1,2,0:T(8,128)(2,1)S(1)}, bf16[2,512,256]{1,2,0:T(8,128)(2,1)}, u32[]{:S(2)}) copy-start(bf16[2,512,256]{1,2,0:T(8,128)(2,1)} %get-tuple-element.55) | copy-start | bytes 1572868
  199.5 13.5 %collective-permute-start.33 = (bf16[2,2,2,56,512]{4,3,2,1,0:T(8,128)(2,1)S(1)}, bf16[2,2,2,56,512]{4,3,2,1,0:T(8,128)(2,1)S(1)}, u32[]{:S(2)}, u32[]{:S(2)}) collective-permute-start(bf16[2,2,2,56,512]{4,3,2,1,0:T(8,128)(2,1)S(1)} %fusion.125), channel_id=1, source_target_pairs={{0,2},{1,3},{2,0},{3,1},{4,6},{5,7},{6,4},{7,5},{8,10},{9,11},{10,... | collective-permute-start | bytes 1376264 | tf_op jit(solution)/shard_map/ppermute | solution.py:159
  200.7 14.3 %copy-start.6 = (bf16[2,256,256]{2,1,0:T(8,128)(2,1)S(1)}, bf16[2,256,256]{2,1,0:T(8,128)(2,1)}, u32[]{:S(2)}) copy-start(bf16[2,256,256]{2,1,0:T(8,128)(2,1)} %copy-done.5) | copy-start | bytes 786436
  200.7 14.3 %copy-start.23 = (bf16[2,256,256]{2,1,0:T(8,128)(2,1)S(1)}, bf16[2,256,256]{2,1,0:T(8,128)(2,1)}, u32[]{:S(2)}) copy-start(bf16[2,256,256]{2,1,0:T(8,128)(2,1)} %copy-done.22) | copy-start | bytes 786436
  200.7 14.3 %copy-start.25 = (bf16[2,256,256]{2,1,0:T(8,128)(2,1)S(1)}, bf16[2,256,256]{2,1,0:T(8,128)(2,1)}, u32[]{:S(2)}) copy-start(bf16[2,256,256]{2,1,0:T(8,128)(2,1)} %copy-done.24) | copy-start | bytes 786436
  200.7 19.0 %collective-permute-start.30 = (bf16[2,128,256]{2,1,0:T(8,128)(2,1)S(1)}, bf16[2,128,256]{2,1,0:T(8,128)(2,1)S(1)}, u32[]{:S(2)}, u32[]{:S(2)}) collective-permute-start(bf16[2,128,256]{2,1,0:T(8,128)(2,1)S(1)} %get-tuple-element.42), channel_id=1, source_target_pairs={{0,1},{1,2},{2,3},{3,4},{4,5},{5,6},{6,7},{7,8},{8,9},{9,10},{10,1... | collective-permute-start | bytes 393224 | tf_op jit(solution)/shard_map/ppermute | solution.py:15
  202.9 16.8 %collective-permute-start.31 = (bf16[2,128,256]{2,1,0:T(8,128)(2,1)S(1)}, bf16[2,128,256]{2,1,0:T(8,128)(2,1)S(1)}, u32[]{:S(2)}, u32[]{:S(2)}) collective-permute-start(bf16[2,128,256]{2,1,0:T(8,128)(2,1)S(1)} %get-tuple-element.43), channel_id=1, source_target_pairs={{1,0},{2,1},{3,2},{4,3},{5,4},{6,5},{7,6},{8,7},{9,8},{10,9},{11,1... | collective-permute-start | bytes 393224 | tf_op jit(solution)/shard_map/ppermute | solution.py:15
  213.3 6.1 %collective-permute-start.34 = (bf16[2,2,56,512]{3,2,1,0:T(8,128)(2,1)S(1)}, bf16[2,2,56,512]{3,2,1,0:T(8,128)(2,1)S(1)}, u32[]{:S(2)}, u32[]{:S(2)}) collective-permute-start(bf16[2,2,56,512]{3,2,1,0:T(8,128)(2,1)S(1)} %fusion.173), channel_id=1, source_target_pairs={{0,8},{1,9},{2,10},{3,11},{4,12},{5,13},{6,14},{7,15},{8,0},{9,1},... | collective-permute-start | bytes 688136 | tf_op jit(solution)/shard_map/ppermute | solution.py:159
  219.5 9.9 %copy-start.8 = (f32[1,2,256,256]{3,2,1,0:T(8,128)S(1)}, f32[1,2,256,256]{3,2,1,0:T(8,128)}, u32[]{:S(2)}) copy-start(f32[1,2,256,256]{3,2,1,0:T(8,128)} %get-tuple-element.20) | copy-start | bytes 1572868
  219.5 9.9 %copy-start.9 = (f32[2,256,256]{2,1,0:T(8,128)S(1)}, f32[2,256,256]{2,1,0:T(8,128)}, u32[]{:S(2)}) copy-start(f32[2,256,256]{2,1,0:T(8,128)} %get-tuple-element.6) | copy-start | bytes 1572868
  219.5 9.9 %copy-start.10 = (f32[2,256,256]{2,1,0:T(8,128)S(1)}, f32[2,256,256]{2,1,0:T(8,128)}, u32[]{:S(2)}) copy-start(f32[2,256,256]{2,1,0:T(8,128)} %get-tuple-element.4) | copy-start | bytes 1572868
  219.5 9.9 %copy-start.16 = (f32[1,2,128,256]{3,2,1,0:T(8,128)S(1)}, f32[1,2,128,256]{3,2,1,0:T(8,128)}, u32[]{:S(2)}) copy-start(f32[1,2,128,256]{3,2,1,0:T(8,128)} %get-tuple-element.16) | copy-start | bytes 786436
  219.5 9.9 %copy-start.17 = (f32[1,2,128,256]{3,2,1,0:T(8,128)S(1)}, f32[1,2,128,256]{3,2,1,0:T(8,128)}, u32[]{:S(2)}) copy-start(f32[1,2,128,256]{3,2,1,0:T(8,128)} %get-tuple-element.21) | copy-start | bytes 786436
  219.6 9.9 %copy-start.18 = (f32[1,2,128,256]{3,2,1,0:T(8,128)S(1)}, f32[1,2,128,256]{3,2,1,0:T(8,128)}, u32[]{:S(2)}) copy-start(f32[1,2,128,256]{3,2,1,0:T(8,128)} %get-tuple-element.28) | copy-start | bytes 786436
  219.6 9.9 %copy-start.19 = (f32[1,2,128,256]{3,2,1,0:T(8,128)S(1)}, f32[1,2,128,256]{3,2,1,0:T(8,128)}, u32[]{:S(2)}) copy-start(f32[1,2,128,256]{3,2,1,0:T(8,128)} %get-tuple-element.35) | copy-start | bytes 786436
  219.6 9.9 %copy-start.20 = (f32[1,2,128,256]{3,2,1,0:T(8,128)S(1)}, f32[1,2,128,256]{3,2,1,0:T(8,128)}, u32[]{:S(2)}) copy-start(f32[1,2,128,256]{3,2,1,0:T(8,128)} %get-tuple-element.24) | copy-start | bytes 786436
  219.6 9.9 %copy-start.21 = (f32[1,2,128,256]{3,2,1,0:T(8,128)S(1)}, f32[1,2,128,256]{3,2,1,0:T(8,128)}, u32[]{:S(2)}) copy-start(f32[1,2,128,256]{3,2,1,0:T(8,128)} %get-tuple-element.33) | copy-start | bytes 786436
  219.6 6.4 %collective-permute-start.35 = (bf16[2,56,512]{2,1,0:T(8,128)(2,1)S(1)}, bf16[2,56,512]{2,1,0:T(8,128)(2,1)S(1)}, u32[]{:S(2)}, u32[]{:S(2)}) collective-permute-start(bf16[2,56,512]{2,1,0:T(8,128)(2,1)S(1)} %fusion.197), channel_id=1, source_target_pairs={{0,4},{1,5},{2,6},{3,7},{4,0},{5,1},{6,2},{7,3},{8,12},{9,13},{10,... | collective-permute-start | bytes 344072 | tf_op jit(solution)/shard_map/ppermute | solution.py:159
  226.1 5.8 %collective-permute-start.36 = (bf16[56,512]{1,0:T(8,128)(2,1)S(1)}, bf16[56,512]{1,0:T(8,128)(2,1)S(1)}, u32[]{:S(2)}, u32[]{:S(2)}) collective-permute-start(bf16[56,512]{1,0:T(8,128)(2,1)S(1)} %fusion.203), channel_id=1, source_target_pairs={{0,16},{1,17},{2,18},{3,19},{4,20},{5,21},{6,22},{7,23},{8,24},{9,... | collective-permute-start | bytes 172040 | tf_op jit(solution)/shard_map/ppermute | solution.py:159
  (2 other events, 1.9 us)

commit v8 on v7

--- a/solution.py
+++ b/solution.py
@@ -109,7 +109,47 @@
     grad_half = join_rows(halves[0], halves[1], width)
     out_term = jnp.einsum("mpc,mpd->cd", gated, grad_half, preferred_element_type=f32)
     conv_term = jnp.einsum("mpc,mpd->cd", taps, grad_pre, preferred_element_type=f32)
-    return join_rows(outs[0], outs[1], width), conv_term, out_term
+    return tuple(outs), conv_term, out_term
+
+
+def backward_near_pieces(pieces, saved, conv, out_mat):
+    taps, gated, factor_a, factor_b = saved
+    chans = pieces[0].shape[2]
+    width = NEAR
+    weights = conv.reshape(3 * chans, 2 * chans)
+    f32 = jnp.float32
+    factors = [split_rows(factor_a, width), split_rows(factor_b, width)]
+    firsts, middles, thirds, pres, halves = [], [], [], [], []
+    for index, flowing in enumerate(pieces):
+        grad_half = flowing.astype(jnp.bfloat16)
+        grad_gated = jnp.einsum("mpd,cd->mpc", grad_half, out_mat, preferred_element_type=f32)
+        grad_pre = jnp.concatenate(
+            [grad_gated * factors[0][index], grad_gated * factors[1][index]], axis=2
+        ).astype(jnp.bfloat16)
+        back = jnp.einsum("mpd,cd->mpc", grad_pre, weights, preferred_element_type=f32)
+        firsts.append(back[..., :chans].astype(jnp.bfloat16))
+        middles.append(back[..., chans : 2 * chans])
+        thirds.append(back[..., 2 * chans :].astype(jnp.bfloat16))
+        pres.append(grad_pre)
+        halves.append(grad_half)
+    (first_e, first_i), (third_e, third_i) = firsts, thirds
+    (middle_e, middle_i), (flow_e, flow_i) = middles, pieces
+    low_in = shifted(third_e[:, width:], "seq", 1)
+    high_in = shifted(first_e[:, :width], "seq", -1)
+    first_up = jnp.concatenate([first_i[:, width:], first_e[:, width:]], axis=1)
+    third_up = jnp.concatenate([third_e[:, :width], third_i[:, :width]], axis=1)
+    inner = flow_i + (middle_i + first_up.astype(f32) + third_up.astype(f32))
+    low = flow_e[:, :width] + (
+        middle_e[:, :width] + first_i[:, :width].astype(f32) + low_in.astype(f32)
+    )
+    high = flow_e[:, width:] + (
+        middle_e[:, width:] + high_in.astype(f32) + third_i[:, width:].astype(f32)
+    )
+    grad_pre = join_rows(pres[0], pres[1], width)
+    grad_half = join_rows(halves[0], halves[1], width)
+    out_term = jnp.einsum("mpc,mpd->cd", gated, grad_half, preferred_element_type=f32)
+    conv_term = jnp.einsum("mpc,mpd->cd", taps, grad_pre, preferred_element_type=f32)
+    return (low, inner, high), conv_term, out_term
 
 
 def split_near(flowing, middle, grad_first, grad_third, width):
@@ -199,6 +239,10 @@
                 flowing, conv_term, out_term = backward_far(
                     flowing, stored[layer], conv_mat[layer], out_mat[layer], far_hops
                 )
+            elif layer == 0 and depth == 2 and step > 0:
+                flowing, conv_term, out_term = backward_near_pieces(
+                    flowing, stored[layer], conv_mat[layer], out_mat[layer]
+                )
             else:
                 flowing, conv_term, out_term = backward_layer(
                     flowing, stored[layer], conv_mat[layer], out_mat[layer], layer, far_hops

time: 234 us -> 231 us (0.987)
  waiting for transfers between devices: 73.2 us -> 69.6 us
    dot_general x0 -> x18, matrix products: none -> 15.3 us  [the longest x3 8.24 us: backward_near_pieces(): jnp.einsum('mpc,mpd->cd', taps, grad_pre, preferred_element_type=f32)]
    dot_general x5 -> x2, matrix products: 11.7 us -> 3.21 us  [backward_layer(): jnp.einsum('mpc,mpd->cd', taps, grad_pre, preferred_element_type=jnp.floa...]
    dot_general x5 -> x2, matrix products: 5.17 us -> 2.05 us  [backward_layer(): jnp.einsum('mpd,cd->mpc', grad_pre, weights, preferred_element_type=jnp.f...]
    ppermute x32, waiting for transfers between devices: 53.6 us -> 50.5 us  [shifted(): lax.ppermute(value, axis, [(source, source + steps) for source in range(l...]
  transfers between devices with their start and end apart: 37 -> 37, of which waited for: 17 -> 15; matrix products, arithmetic and copies ran while one was open for 15% -> 17% of each run, Pallas kernels for 0% -> 0%
where the time goes in v8:
time: 231 us; the launch traced here: 229 us
  starting transfers between devices  97.7 us (42%)
  waiting for transfers between devices  69.6 us (30%)
  matrix products  38.9 us (17%)
  other arithmetic  15.1 us (7%)
  local copies, waits for them, and re-layouts  5.88 us (3%)
    ppermute x32, starting transfers between devices, shifted(): lax.ppermute(value, axis, [(source, source + steps) for source in range(l...  92.4 us
    ppermute x32, waiting for transfers between devices, shifted(): lax.ppermute(value, axis, [(source, source + steps) for source in range(l...  50.5 us
    ppermute x5, waiting for transfers between devices, halving_scatter(): got = lax.ppermute(sends, 'seq', pairs)  19.1 us
    dot_general x3, matrix products, backward_near_pieces(): jnp.einsum('mpc,mpd->cd', taps, grad_pre, preferred_element_type=f32)  8.24 us
    dot_general x7, matrix products, mm(): return jnp.einsum('mpc,cd->mpd', a, b, preferred_element_type=jnp.float32)  5.75 us
    ppermute x5, starting transfers between devices, halving_scatter(): got = lax.ppermute(sends, 'seq', pairs)  5.34 us
  transfers between devices with their start and end apart: 37, of which 15 were waited for; matrix products, arithmetic and copies ran while one was open for 17% of the time, Pallas kernels for 0%

profile of v8, /device:TPU:24, one launch (start us, length us, event | category | flops | bytes accessed | tf_op | source)
XLA Modules:
  0.0 229.4 jit_solution(4998269111907263408)
XLA Ops:
  0.6 1.0 fusion.352
  1.7 1.9 collective-permute-start
  3.6 3.6 %collective-permute-start.1 = (bf16[2,128,256]{2,1,0:T(8,128)(2,1)S(1)}, bf16[2,128,256]{2,1,0:T(8,128)(2,1)S(1)}, u32[]{:S(2)}, u32[]{:S(2)}) collective-permute-start(bf16[2,128,256]{2,1,0:T(8,128)(2,1)S(1)} %get-tuple-element.130), channel_id=1, source_target_pairs={{1,0},{2,1},{3,2},{4,3},{5,4},{6,5},{7,6},{8,7},{9,8},{10,9},{11,1... | collective-permute-start | bytes 393224 | tf_op jit(solution)/shard_map/ppermute | solution.py:15
  7.3 1.6 fusion.215
  9.0 1.8 fusion.106
  12.7 5.6 %collective-permute-start.2 = (bf16[2,512,256]{2,1,0:T(8,128)(2,1)S(1)}, bf16[2,512,256]{2,1,0:T(8,128)(2,1)S(1)}, u32[]{:S(2)}, u32[]{:S(2)}) collective-permute-start(bf16[2,512,256]{2,1,0:T(8,128)(2,1)S(1)} %fusion.2), channel_id=1, source_target_pairs={{0,2},{1,3},{2,4},{3,5},{4,6},{5,7},{6,8},{7,9},{8,10},{9,11},{10,... | collective-permute-start | bytes 1572872 | tf_op jit(solution)/shard_map/ppermute | solution.py:15
  18.4 1.9 collective-permute-start.3
  20.8 8.2 %collective-permute-done.2 = bf16[2,512,256]{2,1,0:T(8,128)(2,1)S(1)} collective-permute-done((bf16[2,512,256]{2,1,0:T(8,128)(2,1)S(1)}, bf16[2,512,256]{2,1,0:T(8,128)(2,1)S(1)}, u32[]{:S(2)}, u32[]{:S(2)}) %collective-permute-start.2) | collective-permute-done | bytes 524320 | tf_op jit(solution)/shard_map/ppermute | solution.py:15
  29.6 5.8 %collective-permute-done.3 = bf16[2,512,256]{2,1,0:T(8,128)(2,1)S(1)} collective-permute-done((bf16[2,512,256]{2,1,0:T(8,128)(2,1)S(1)}, bf16[2,512,256]{2,1,0:T(8,128)(2,1)S(1)}, u32[]{:S(2)}, u32[]{:S(2)}) %collective-permute-start.3) | collective-permute-done | bytes 524320 | tf_op jit(solution)/shard_map/ppermute | solution.py:15
  37.8 1.9 collective-permute-start.5
  39.7 3.9 %collective-permute-start.4 = (bf16[2,512,256]{2,1,0:T(8,128)(2,1)S(1)}, bf16[2,512,256]{2,1,0:T(8,128)(2,1)S(1)}, u32[]{:S(2)}, u32[]{:S(2)}) collective-permute-start(bf16[2,512,256]{2,1,0:T(8,128)(2,1)S(1)} %get-tuple-element.50), channel_id=1, source_target_pairs={{2,0},{3,1},{4,2},{5,3},{6,4},{7,5},{8,6},{9,7},{10,8},{11,9},{12,... | collective-permute-start | bytes 1572872 | tf_op jit(solution)/shard_map/ppermute | solution.py:15
  45.1 6.7 %collective-permute-done.5 = bf16[2,512,256]{2,1,0:T(8,128)(2,1)S(1)} collective-permute-done((bf16[2,512,256]{2,1,0:T(8,128)(2,1)S(1)}, bf16[2,512,256]{2,1,0:T(8,128)(2,1)S(1)}, u32[]{:S(2)}, u32[]{:S(2)}) %collective-permute-start.5) | collective-permute-done | bytes 524320 | tf_op jit(solution)/shard_map/ppermute | solution.py:15
  51.8 4.0 %collective-permute-done.4 = bf16[2,512,256]{2,1,0:T(8,128)(2,1)S(1)} collective-permute-done((bf16[2,512,256]{2,1,0:T(8,128)(2,1)S(1)}, bf16[2,512,256]{2,1,0:T(8,128)(2,1)S(1)}, u32[]{:S(2)}, u32[]{:S(2)}) %collective-permute-start.4) | collective-permute-done | bytes 524320 | tf_op jit(solution)/shard_map/ppermute | solution.py:15
  57.8 2.1 collective-permute-start.6
  59.9 3.6 %collective-permute-start.7 = (bf16[2,128,256]{2,1,0:T(8,128)(2,1)S(1)}, bf16[2,128,256]{2,1,0:T(8,128)(2,1)S(1)}, u32[]{:S(2)}, u32[]{:S(2)}) collective-permute-start(bf16[2,128,256]{2,1,0:T(8,128)(2,1)S(1)} %get-tuple-element.49), channel_id=1, source_target_pairs={{1,0},{2,1},{3,2},{4,3},{5,4},{6,5},{7,6},{8,7},{9,8},{10,9},{11,1... | collective-permute-start | bytes 393224 | tf_op jit(solution)/shard_map/ppermute | solution.py:15
  64.5 1.3 collective-permute-start.11
  65.8 2.2 fusion.75
  69.1 1.3 collective-permute-start.8
  70.4 3.8 %collective-permute-done.11 = bf16[2,256,256]{2,1,0:T(8,128)(2,1)S(1)} collective-permute-done((bf16[2,256,256]{2,1,0:T(8,128)(2,1)S(1)}, bf16[2,256,256]{2,1,0:T(8,128)(2,1)S(1)}, u32[]{:S(2)}, u32[]{:S(2)}) %collective-permute-start.11) | collective-permute-done | bytes 262176 | tf_op jit(solution)/shard_map/ppermute | solution.py:15
  75.1 4.3 %collective-permute-start.13 = (bf16[2,256,256]{2,1,0:T(8,128)(2,1)S(1)}, bf16[2,256,256]{2,1,0:T(8,128)(2,1)S(1)}, u32[]{:S(2)}, u32[]{:S(2)}) collective-permute-start(bf16[2,256,256]{2,1,0:T(8,128)(2,1)S(1)} %get-tuple-element.91), channel_id=1, source_target_pairs={{0,2},{1,3},{2,4},{3,5},{4,6},{5,7},{6,8},{7,9},{8,10},{9,11},{10,... | collective-permute-start | bytes 786440 | tf_op jit(solution)/shard_map/ppermute | solution.py:15
  79.4 2.1 collective-permute-start.12
  82.5 6.0 %collective-permute-start.10 = (bf16[2,256,256]{2,1,0:T(8,128)(2,1)S(1)}, bf16[2,256,256]{2,1,0:T(8,128)(2,1)S(1)}, u32[]{:S(2)}, u32[]{:S(2)}) collective-permute-start(bf16[2,256,256]{2,1,0:T(8,128)(2,1)S(1)} %get-tuple-element.89), channel_id=1, source_target_pairs={{0,2},{1,3},{2,4},{3,5},{4,6},{5,7},{6,8},{7,9},{8,10},{9,11},{10,... | collective-permute-start | bytes 786440 | tf_op jit(solution)/shard_map/ppermute | solution.py:15
  88.5 1.9 collective-permute-start.9
  92.7 6.2 %collective-permute-done.9 = bf16[2,256,256]{2,1,0:T(8,128)(2,1)S(1)} collective-permute-done((bf16[2,256,256]{2,1,0:T(8,128)(2,1)S(1)}, bf16[2,256,256]{2,1,0:T(8,128)(2,1)S(1)}, u32[]{:S(2)}, u32[]{:S(2)}) %collective-permute-start.9) | collective-permute-done | bytes 262176 | tf_op jit(solution)/shard_map/ppermute | solution.py:15
  100.1 1.9 collective-permute-start.14
  102.0 3.6 %collective-permute-start.15 = (bf16[2,128,256]{2,1,0:T(8,128)(2,1)S(1)}, bf16[2,128,256]{2,1,0:T(8,128)(2,1)S(1)}, u32[]{:S(2)}, u32[]{:S(2)}) collective-permute-start(bf16[2,128,256]{2,1,0:T(8,128)(2,1)S(1)} %get-tuple-element.83), channel_id=1, source_target_pairs={{1,0},{2,1},{3,2},{4,3},{5,4},{6,5},{7,6},{8,7},{9,8},{10,9},{11,1... | collective-permute-start | bytes 393224 | tf_op jit(solution)/shard_map/ppermute | solution.py:15
  105.7 1.1 fusion.328
  106.8 1.3 collective-permute-start.19
  108.0 2.2 fusion.21
  111.5 1.3 collective-permute-start.16
  112.8 2.9 %collective-permute-done.19 = bf16[2,256,256]{2,1,0:T(8,128)(2,1)S(1)} collective-permute-done((bf16[2,256,256]{2,1,0:T(8,128)(2,1)S(1)}, bf16[2,256,256]{2,1,0:T(8,128)(2,1)S(1)}, u32[]{:S(2)}, u32[]{:S(2)}) %collective-permute-start.19) | collective-permute-done | bytes 262176 | tf_op jit(solution)/shard_map/ppermute | solution.py:15
  116.7 4.6 %collective-permute-start.21 = (bf16[2,256,256]{2,1,0:T(8,128)(2,1)S(1)}, bf16[2,256,256]{2,1,0:T(8,128)(2,1)S(1)}, u32[]{:S(2)}, u32[]{:S(2)}) collective-permute-start(bf16[2,256,256]{2,1,0:T(8,128)(2,1)S(1)} %get-tuple-element.81), channel_id=1, source_target_pairs={{0,2},{1,3},{2,4},{3,5},{4,6},{5,7},{6,8},{7,9},{8,10},{9,11},{10,... | collective-permute-start | bytes 786440 | tf_op jit(solution)/shard_map/ppermute | solution.py:15
  121.2 1.9 collective-permute-start.20
  124.1 6.0 %collective-permute-start.18 = (bf16[2,256,256]{2,1,0:T(8,128)(2,1)S(1)}, bf16[2,256,256]{2,1,0:T(8,128)(2,1)S(1)}, u32[]{:S(2)}, u32[]{:S(2)}) collective-permute-start(bf16[2,256,256]{2,1,0:T(8,128)(2,1)S(1)} %get-tuple-element.79), channel_id=1, source_target_pairs={{0,2},{1,3},{2,4},{3,5},{4,6},{5,7},{6,8},{7,9},{8,10},{9,11},{10,... | collective-permute-start | bytes 786440 | tf_op jit(solution)/shard_map/ppermute | solution.py:15
  130.2 1.9 collective-permute-start.17
  134.7 5.9 %collective-permute-done.17 = bf16[2,256,256]{2,1,0:T(8,128)(2,1)S(1)} collective-permute-done((bf16[2,256,256]{2,1,0:T(8,128)(2,1)S(1)}, bf16[2,256,256]{2,1,0:T(8,128)(2,1)S(1)}, u32[]{:S(2)}, u32[]{:S(2)}) %collective-permute-start.17) | collective-permute-done | bytes 262176 | tf_op jit(solution)/shard_map/ppermute | solution.py:15
  141.7 1.9 collective-permute-start.22
  143.7 3.6 %collective-permute-start.23 = (bf16[2,128,256]{2,1,0:T(8,128)(2,1)S(1)}, bf16[2,128,256]{2,1,0:T(8,128)(2,1)S(1)}, u32[]{:S(2)}, u32[]{:S(2)}) collective-permute-start(bf16[2,128,256]{2,1,0:T(8,128)(2,1)S(1)} %get-tuple-element.73), channel_id=1, source_target_pairs={{1,0},{2,1},{3,2},{4,3},{5,4},{6,5},{7,6},{8,7},{9,8},{10,9},{11,1... | collective-permute-start | bytes 393224 | tf_op jit(solution)/shard_map/ppermute | solution.py:15
  147.3 1.0 fusion.322
  148.4 1.5 collective-permute-start.27
  149.9 2.3 fusion.29
  153.4 1.3 collective-permute-start.24
  154.7 2.5 %collective-permute-done.27 = bf16[2,256,256]{2,1,0:T(8,128)(2,1)S(1)} collective-permute-done((bf16[2,256,256]{2,1,0:T(8,128)(2,1)S(1)}, bf16[2,256,256]{2,1,0:T(8,128)(2,1)S(1)}, u32[]{:S(2)}, u32[]{:S(2)}) %collective-permute-start.27) | collective-permute-done | bytes 262176 | tf_op jit(solution)/shard_map/ppermute | solution.py:15
  158.2 4.3 %collective-permute-start.29 = (bf16[2,256,256]{2,1,0:T(8,128)(2,1)S(1)}, bf16[2,256,256]{2,1,0:T(8,128)(2,1)S(1)}, u32[]{:S(2)}, u32[]{:S(2)}) collective-permute-start(bf16[2,256,256]{2,1,0:T(8,128)(2,1)S(1)} %get-tuple-element.69), channel_id=1, source_target_pairs={{0,2},{1,3},{2,4},{3,5},{4,6},{5,7},{6,8},{7,9},{8,10},{9,11},{10,... | collective-permute-start | bytes 786440 | tf_op jit(solution)/shard_map/ppermute | solution.py:15
  162.5 1.9 collective-permute-start.28
  165.5 6.0 %collective-permute-start.26 = (bf16[2,256,256]{2,1,0:T(8,128)(2,1)S(1)}, bf16[2,256,256]{2,1,0:T(8,128)(2,1)S(1)}, u32[]{:S(2)}, u32[]{:S(2)}) collective-permute-start(bf16[2,256,256]{2,1,0:T(8,128)(2,1)S(1)} %get-tuple-element.71), channel_id=1, source_target_pairs={{0,2},{1,3},{2,4},{3,5},{4,6},{5,7},{6,8},{7,9},{8,10},{9,11},{10,... | collective-permute-start | bytes 786440 | tf_op jit(solution)/shard_map/ppermute | solution.py:15
  171.6 1.9 collective-permute-start.25
  173.5 2.2 bitcast_add_fusion
  176.5 1.1 multiply_convert_fusion.5
  177.6 4.3 %collective-permute-done.25 = bf16[2,256,256]{2,1,0:T(8,128)(2,1)S(1)} collective-permute-done((bf16[2,256,256]{2,1,0:T(8,128)(2,1)S(1)}, bf16[2,256,256]{2,1,0:T(8,128)(2,1)S(1)}, u32[]{:S(2)}, u32[]{:S(2)}) %collective-permute-start.25) | collective-permute-done | bytes 262176 | tf_op jit(solution)/shard_map/ppermute | solution.py:15
  184.8 3.8 %bitcast_add_fusion.3 = f32[768,512]{1,0:T(8,128)S(1)} fusion(f32[768,512,1]{1,0,2:T(8,128)} %fusion.29, f32[768,512,1]{1,0,2:T(8,128)} %fusion.21, f32[768,512,1]{1,0,2:T(8,128)} %fusion.75, bf16[2,128,512]{1,2,0:T(8,128)(2,1)S(1)} %get-tuple-element.93, bf16[2,256,256]{1,2,0:T(8,128)(2,1)S(1)} %copy-done.19, bf16[2,256,256]{1,2,0:T(8,128)(2,1)S(1)} %copy-done.18, ...), kind=kOutput, calls=%fused_computation.12 | convolution fusion | flops 818544640 | bytes 8912896 | tf_op jit(solution)/shard_map/mpc,mpd->cd/dot_general | solution.py:151
  189.2 1.8 copy-done
  192.0 1.9 collective-permute-done.32
  193.9 1.7 fusion.1
  196.5 2.2 collective-permute-start.30
  198.7 3.5 %collective-permute-start.31 = (bf16[2,128,256]{2,1,0:T(8,128)(2,1)S(1)}, bf16[2,128,256]{2,1,0:T(8,128)(2,1)S(1)}, u32[]{:S(2)}, u32[]{:S(2)}) collective-permute-start(bf16[2,128,256]{2,1,0:T(8,128)(2,1)S(1)} %get-tuple-element.63), channel_id=1, source_target_pairs={{1,0},{2,1},{3,2},{4,3},{5,4},{6,5},{7,6},{8,7},{9,8},{10,9},{11,1... | collective-permute-start | bytes 393224 | tf_op jit(solution)/shard_map/ppermute | solution.py:15
  202.3 7.0 %collective-permute-done.33 = bf16[2,2,2,56,512]{4,3,2,1,0:T(8,128)(2,1)S(1)} collective-permute-done((bf16[2,2,2,56,512]{4,3,2,1,0:T(8,128)(2,1)S(1)}, bf16[2,2,2,56,512]{4,3,2,1,0:T(8,128)(2,1)S(1)}, u32[]{:S(2)}, u32[]{:S(2)}) %collective-permute-start.33) | collective-permute-done | bytes 458784 | tf_op jit(solution)/shard_map/ppermute | solution.py:199
  209.5 1.7 collective-permute-start.34
  211.2 1.3 fusion.87
  212.6 3.0 %collective-permute-done.34 = bf16[2,2,56,512]{3,2,1,0:T(8,128)(2,1)S(1)} collective-permute-done((bf16[2,2,56,512]{3,2,1,0:T(8,128)(2,1)S(1)}, bf16[2,2,56,512]{3,2,1,0:T(8,128)(2,1)S(1)}, u32[]{:S(2)}, u32[]{:S(2)}) %collective-permute-start.34) | collective-permute-done | bytes 229408 | tf_op jit(solution)/shard_map/ppermute | solution.py:199
  216.1 6.1 %collective-permute-done.35 = bf16[2,56,512]{2,1,0:T(8,128)(2,1)S(1)} collective-permute-done((bf16[2,56,512]{2,1,0:T(8,128)(2,1)S(1)}, bf16[2,56,512]{2,1,0:T(8,128)(2,1)S(1)}, u32[]{:S(2)}, u32[]{:S(2)}) %collective-permute-start.35) | collective-permute-done | bytes 114720 | tf_op jit(solution)/shard_map/ppermute | solution.py:199
  222.3 3.4 %collective-permute-start.36 = (bf16[56,512]{1,0:T(8,128)(2,1)S(1)}, bf16[56,512]{1,0:T(8,128)(2,1)S(1)}, u32[]{:S(2)}, u32[]{:S(2)}) collective-permute-start(bf16[56,512]{1,0:T(8,128)(2,1)S(1)} %fusion.258), channel_id=1, source_target_pairs={{0,16},{1,17},{2,18},{3,19},{4,20},{5,21},{6,22},{7,23},{8,24},{9,... | collective-permute-start | bytes 172040 | tf_op jit(solution)/shard_map/ppermute | solution.py:199
  225.8 1.2 fusion.20
  227.0 1.1 collective-permute-done.36
  (192 shorter events, 33.7 us)
Async XLA Ops:
  0.6 8.3 %copy-start.3 = (bf16[1,2,512,256]{3,2,1,0:T(8,128)(2,1)S(1)}, bf16[1,2,512,256]{3,2,1,0:T(8,128)(2,1)}, u32[]{:S(2)}) copy-start(bf16[1,2,512,256]{3,2,1,0:T(8,128)(2,1)} %param.4) | copy-start | bytes 1572868
  1.7 7.3 %collective-permute-start = (bf16[2,128,256]{2,1,0:T(8,128)(2,1)S(1)}, bf16[2,128,256]{2,1,0:T(8,128)(2,1)S(1)}, u32[]{:S(2)}, u32[]{:S(2)}) collective-permute-start(bf16[2,128,256]{2,1,0:T(8,128)(2,1)S(1)} %get-tuple-element.131), channel_id=1, source_target_pairs={{0,1},{1,2},{2,3},{3,4},{4,5},{5,6},{6,7},{7,8},{8,9},{9,10},{10,1... | collective-permute-start | bytes 393224 | tf_op jit(solution)/shard_map/ppermute | solution.py:15
  3.6 7.2 %collective-permute-start.1 = (bf16[2,128,256]{2,1,0:T(8,128)(2,1)S(1)}, bf16[2,128,256]{2,1,0:T(8,128)(2,1)S(1)}, u32[]{:S(2)}, u32[]{:S(2)}) collective-permute-start(bf16[2,128,256]{2,1,0:T(8,128)(2,1)S(1)} %get-tuple-element.130), channel_id=1, source_target_pairs={{1,0},{2,1},{3,2},{4,3},{5,4},{6,5},{7,6},{8,7},{9,8},{10,9},{11,1... | collective-permute-start | bytes 393224 | tf_op jit(solution)/shard_map/ppermute | solution.py:15
  8.9 2.0 copy-start.4
  9.0 140.9 %copy-start.16 = (bf16[2,384,256]{2,1,0:T(8,128)(2,1)}, bf16[2,384,256]{2,1,0:T(8,128)(2,1)S(1)}, u32[]{:S(2)}) copy-start(bf16[2,384,256]{2,1,0:T(8,128)(2,1)S(1)} %get-tuple-element.128) | copy-start | bytes 1179652
  9.0 140.9 %copy-start.17 = (bf16[2,384,256]{2,1,0:T(8,128)(2,1)}, bf16[2,384,256]{2,1,0:T(8,128)(2,1)S(1)}, u32[]{:S(2)}) copy-start(bf16[2,384,256]{2,1,0:T(8,128)(2,1)S(1)} %get-tuple-element.129) | copy-start | bytes 1179652
  9.0 2.8 %copy-start.30 = (bf16[2,128,256]{2,1,0:T(8,128)(2,1)}, bf16[2,128,256]{2,1,0:T(8,128)(2,1)S(1)}, u32[]{:S(2)}) copy-start(bf16[2,128,256]{2,1,0:T(8,128)(2,1)S(1)} %collective-permute-done) | copy-start | bytes 393220
  12.7 16.4 %collective-permute-start.2 = (bf16[2,512,256]{2,1,0:T(8,128)(2,1)S(1)}, bf16[2,512,256]{2,1,0:T(8,128)(2,1)S(1)}, u32[]{:S(2)}, u32[]{:S(2)}) collective-permute-start(bf16[2,512,256]{2,1,0:T(8,128)(2,1)S(1)} %fusion.2), channel_id=1, source_target_pairs={{0,2},{1,3},{2,4},{3,5},{4,6},{5,7},{6,8},{7,9},{8,10},{9,11},{10,... | collective-permute-start | bytes 1572872 | tf_op jit(solution)/shard_map/ppermute | solution.py:15
  18.4 17.0 %collective-permute-start.3 = (bf16[2,512,256]{2,1,0:T(8,128)(2,1)S(1)}, bf16[2,512,256]{2,1,0:T(8,128)(2,1)S(1)}, u32[]{:S(2)}, u32[]{:S(2)}) collective-permute-start(bf16[2,512,256]{2,1,0:T(8,128)(2,1)S(1)} %fusion.2), channel_id=1, source_target_pairs={{2,0},{3,1},{4,2},{5,3},{6,4},{7,5},{8,6},{9,7},{10,8},{11,9},{12,... | collective-permute-start | bytes 1572872 | tf_op jit(solution)/shard_map/ppermute | solution.py:15
  29.6 6.4 %copy-start.10 = (bf16[2,512,256]{2,1,0:T(8,128)(2,1)S(1)}, bf16[2,512,256]{2,1,0:T(8,128)(2,1)}, u32[]{:S(2)}) copy-start(bf16[2,512,256]{2,1,0:T(8,128)(2,1)} %param.5) | copy-start | bytes 1572868
  37.8 14.0 %collective-permute-start.5 = (bf16[2,512,256]{2,1,0:T(8,128)(2,1)S(1)}, bf16[2,512,256]{2,1,0:T(8,128)(2,1)S(1)}, u32[]{:S(2)}, u32[]{:S(2)}) collective-permute-start(bf16[2,512,256]{2,1,0:T(8,128)(2,1)S(1)} %get-tuple-element.51), channel_id=1, source_target_pairs={{0,2},{1,3},{2,4},{3,5},{4,6},{5,7},{6,8},{7,9},{8,10},{9,11},{10,... | collective-permute-start | bytes 1572872 | tf_op jit(solution)/shard_map/ppermute | solution.py:15
  39.7 16.1 %collective-permute-start.4 = (bf16[2,512,256]{2,1,0:T(8,128)(2,1)S(1)}, bf16[2,512,256]{2,1,0:T(8,128)(2,1)S(1)}, u32[]{:S(2)}, u32[]{:S(2)}) collective-permute-start(bf16[2,512,256]{2,1,0:T(8,128)(2,1)S(1)} %get-tuple-element.50), channel_id=1, source_target_pairs={{2,0},{3,1},{4,2},{5,3},{6,4},{7,5},{8,6},{9,7},{10,8},{11,9},{12,... | collective-permute-start | bytes 1572872 | tf_op jit(solution)/shard_map/ppermute | solution.py:15
  57.8 8.0 %copy-start.31 = (bf16[2,128,256]{2,1,0:T(8,128)(2,1)S(1)}, bf16[2,128,256]{2,1,0:T(8,128)(2,1)}, u32[]{:S(2)}) copy-start(bf16[2,128,256]{2,1,0:T(8,128)(2,1)} %copy-done.30) | copy-start | bytes 393220
  57.8 10.2 %collective-permute-start.6 = (bf16[2,128,256]{2,1,0:T(8,128)(2,1)S(1)}, bf16[2,128,256]{2,1,0:T(8,128)(2,1)S(1)}, u32[]{:S(2)}, u32[]{:S(2)}) collective-permute-start(bf16[2,128,256]{2,1,0:T(8,128)(2,1)S(1)} %get-tuple-element.48), channel_id=1, source_target_pairs={{0,1},{1,2},{2,3},{3,4},{4,5},{5,6},{6,7},{7,8},{8,9},{9,10},{10,1... | collective-permute-start | bytes 393224 | tf_op jit(solution)/shard_map/ppermute | solution.py:15
  59.9 8.2 %collective-permute-start.7 = (bf16[2,128,256]{2,1,0:T(8,128)(2,1)S(1)}, bf16[2,128,256]{2,1,0:T(8,128)(2,1)S(1)}, u32[]{:S(2)}, u32[]{:S(2)}) collective-permute-start(bf16[2,128,256]{2,1,0:T(8,128)(2,1)S(1)} %get-tuple-element.49), channel_id=1, source_target_pairs={{1,0},{2,1},{3,2},{4,3},{5,4},{6,5},{7,6},{8,7},{9,8},{10,9},{11,1... | collective-permute-start | bytes 393224 | tf_op jit(solution)/shard_map/ppermute | solution.py:15
  64.5 9.7 %collective-permute-start.11 = (bf16[2,256,256]{2,1,0:T(8,128)(2,1)S(1)}, bf16[2,256,256]{2,1,0:T(8,128)(2,1)S(1)}, u32[]{:S(2)}, u32[]{:S(2)}) collective-permute-start(bf16[2,256,256]{2,1,0:T(8,128)(2,1)S(1)} %get-tuple-element.27), channel_id=1, source_target_pairs={{32,0},{64,32},{96,64},{33,1},{65,33},{97,65},{34,2},{66,34},{98,6... | collective-permute-start | bytes 786440 | tf_op jit(solution)/shard_map/ppermute | solution.py:15
  69.1 12.5 %collective-permute-start.8 = (bf16[2,256,256]{2,1,0:T(8,128)(2,1)S(1)}, bf16[2,256,256]{2,1,0:T(8,128)(2,1)S(1)}, u32[]{:S(2)}, u32[]{:S(2)}) collective-permute-start(bf16[2,256,256]{2,1,0:T(8,128)(2,1)S(1)} %pad_maximum_fusion.25), channel_id=1, source_target_pairs={{32,0},{64,32},{96,64},{33,1},{65,33},{97,65},{34,2},{66,34},{98,6... | collective-permute-start | bytes 786440 | tf_op jit(solution)/shard_map/ppermute | solution.py:15
  75.1 16.6 %collective-permute-start.13 = (bf16[2,256,256]{2,1,0:T(8,128)(2,1)S(1)}, bf16[2,256,256]{2,1,0:T(8,128)(2,1)S(1)}, u32[]{:S(2)}, u32[]{:S(2)}) collective-permute-start(bf16[2,256,256]{2,1,0:T(8,128)(2,1)S(1)} %get-tuple-element.91), channel_id=1, source_target_pairs={{0,2},{1,3},{2,4},{3,5},{4,6},{5,7},{6,8},{7,9},{8,10},{9,11},{10,... | collective-permute-start | bytes 786440 | tf_op jit(solution)/shard_map/ppermute | solution.py:15
  79.4 12.2 %collective-permute-start.12 = (bf16[2,256,256]{2,1,0:T(8,128)(2,1)S(1)}, bf16[2,256,256]{2,1,0:T(8,128)(2,1)S(1)}, u32[]{:S(2)}, u32[]{:S(2)}) collective-permute-start(bf16[2,256,256]{2,1,0:T(8,128)(2,1)S(1)} %get-tuple-element.90), channel_id=1, source_target_pairs={{2,0},{3,1},{4,2},{5,3},{6,4},{7,5},{8,6},{9,7},{10,8},{11,9},{12,... | collective-permute-start | bytes 786440 | tf_op jit(solution)/shard_map/ppermute | solution.py:15
  82.5 10.2 %collective-permute-start.10 = (bf16[2,256,256]{2,1,0:T(8,128)(2,1)S(1)}, bf16[2,256,256]{2,1,0:T(8,128)(2,1)S(1)}, u32[]{:S(2)}, u32[]{:S(2)}) collective-permute-start(bf16[2,256,256]{2,1,0:T(8,128)(2,1)S(1)} %get-tuple-element.89), channel_id=1, source_target_pairs={{0,2},{1,3},{2,4},{3,5},{4,6},{5,7},{6,8},{7,9},{8,10},{9,11},{10,... | collective-permute-start | bytes 786440 | tf_op jit(solution)/shard_map/ppermute | solution.py:15
  88.5 10.4 %collective-permute-start.9 = (bf16[2,256,256]{2,1,0:T(8,128)(2,1)S(1)}, bf16[2,256,256]{2,1,0:T(8,128)(2,1)S(1)}, u32[]{:S(2)}, u32[]{:S(2)}) collective-permute-start(bf16[2,256,256]{2,1,0:T(8,128)(2,1)S(1)} %get-tuple-element.88), channel_id=1, source_target_pairs={{2,0},{3,1},{4,2},{5,3},{6,4},{7,5},{8,6},{9,7},{10,8},{11,9},{12,... | collective-permute-start | bytes 786440 | tf_op jit(solution)/shard_map/ppermute | solution.py:15
  100.1 10.4 %collective-permute-start.14 = (bf16[2,128,256]{2,1,0:T(8,128)(2,1)S(1)}, bf16[2,128,256]{2,1,0:T(8,128)(2,1)S(1)}, u32[]{:S(2)}, u32[]{:S(2)}) collective-permute-start(bf16[2,128,256]{2,1,0:T(8,128)(2,1)S(1)} %get-tuple-element.82), channel_id=1, source_target_pairs={{0,1},{1,2},{2,3},{3,4},{4,5},{5,6},{6,7},{7,8},{8,9},{9,10},{10,1... | collective-permute-start | bytes 393224 | tf_op jit(solution)/shard_map/ppermute | solution.py:15
  102.0 8.5 %collective-permute-start.15 = (bf16[2,128,256]{2,1,0:T(8,128)(2,1)S(1)}, bf16[2,128,256]{2,1,0:T(8,128)(2,1)S(1)}, u32[]{:S(2)}, u32[]{:S(2)}) collective-permute-start(bf16[2,128,256]{2,1,0:T(8,128)(2,1)S(1)} %get-tuple-element.83), channel_id=1, source_target_pairs={{1,0},{2,1},{3,2},{4,3},{5,4},{6,5},{7,6},{8,7},{9,8},{10,9},{11,1... | collective-permute-start | bytes 393224 | tf_op jit(solution)/shard_map/ppermute | solution.py:15
  106.8 9.0 %collective-permute-start.19 = (bf16[2,256,256]{2,1,0:T(8,128)(2,1)S(1)}, bf16[2,256,256]{2,1,0:T(8,128)(2,1)S(1)}, u32[]{:S(2)}, u32[]{:S(2)}) collective-permute-start(bf16[2,256,256]{2,1,0:T(8,128)(2,1)S(1)} %get-tuple-element.9), channel_id=1, source_target_pairs={{32,0},{64,32},{96,64},{33,1},{65,33},{97,65},{34,2},{66,34},{98,6... | collective-permute-start | bytes 786440 | tf_op jit(solution)/shard_map/ppermute | solution.py:15
  111.5 11.6 %collective-permute-start.16 = (bf16[2,256,256]{2,1,0:T(8,128)(2,1)S(1)}, bf16[2,256,256]{2,1,0:T(8,128)(2,1)S(1)}, u32[]{:S(2)}, u32[]{:S(2)}) collective-permute-start(bf16[2,256,256]{2,1,0:T(8,128)(2,1)S(1)} %pad_maximum_fusion.26), channel_id=1, source_target_pairs={{32,0},{64,32},{96,64},{33,1},{65,33},{97,65},{34,2},{66,34},{98,6... | collective-permute-start | bytes 786440 | tf_op jit(solution)/shard_map/ppermute | solution.py:15
  116.7 16.9 %collective-permute-start.21 = (bf16[2,256,256]{2,1,0:T(8,128)(2,1)S(1)}, bf16[2,256,256]{2,1,0:T(8,128)(2,1)S(1)}, u32[]{:S(2)}, u32[]{:S(2)}) collective-permute-start(bf16[2,256,256]{2,1,0:T(8,128)(2,1)S(1)} %get-tuple-element.81), channel_id=1, source_target_pairs={{0,2},{1,3},{2,4},{3,5},{4,6},{5,7},{6,8},{7,9},{8,10},{9,11},{10,... | collective-permute-start | bytes 786440 | tf_op jit(solution)/shard_map/ppermute | solution.py:15
  121.2 12.4 %collective-permute-start.20 = (bf16[2,256,256]{2,1,0:T(8,128)(2,1)S(1)}, bf16[2,256,256]{2,1,0:T(8,128)(2,1)S(1)}, u32[]{:S(2)}, u32[]{:S(2)}) collective-permute-start(bf16[2,256,256]{2,1,0:T(8,128)(2,1)S(1)} %get-tuple-element.80), channel_id=1, source_target_pairs={{2,0},{3,1},{4,2},{5,3},{6,4},{7,5},{8,6},{9,7},{10,8},{11,9},{12,... | collective-permute-start | bytes 786440 | tf_op jit(solution)/shard_map/ppermute | solution.py:15
  124.1 10.5 %collective-permute-start.18 = (bf16[2,256,256]{2,1,0:T(8,128)(2,1)S(1)}, bf16[2,256,256]{2,1,0:T(8,128)(2,1)S(1)}, u32[]{:S(2)}, u32[]{:S(2)}) collective-permute-start(bf16[2,256,256]{2,1,0:T(8,128)(2,1)S(1)} %get-tuple-element.79), channel_id=1, source_target_pairs={{0,2},{1,3},{2,4},{3,5},{4,6},{5,7},{6,8},{7,9},{8,10},{9,11},{10,... | collective-permute-start | bytes 786440 | tf_op jit(solution)/shard_map/ppermute | solution.py:15
  130.2 10.4 %collective-permute-start.17 = (bf16[2,256,256]{2,1,0:T(8,128)(2,1)S(1)}, bf16[2,256,256]{2,1,0:T(8,128)(2,1)S(1)}, u32[]{:S(2)}, u32[]{:S(2)}) collective-permute-start(bf16[2,256,256]{2,1,0:T(8,128)(2,1)S(1)} %get-tuple-element.78), channel_id=1, source_target_pairs={{2,0},{3,1},{4,2},{5,3},{6,4},{7,5},{8,6},{9,7},{10,8},{11,9},{12,... | collective-permute-start | bytes 786440 | tf_op jit(solution)/shard_map/ppermute | solution.py:15
  141.7 10.7 %collective-permute-start.22 = (bf16[2,128,256]{2,1,0:T(8,128)(2,1)S(1)}, bf16[2,128,256]{2,1,0:T(8,128)(2,1)S(1)}, u32[]{:S(2)}, u32[]{:S(2)}) collective-permute-start(bf16[2,128,256]{2,1,0:T(8,128)(2,1)S(1)} %get-tuple-element.72), channel_id=1, source_target_pairs={{0,1},{1,2},{2,3},{3,4},{4,5},{5,6},{6,7},{7,8},{8,9},{9,10},{10,1... | collective-permute-start | bytes 393224 | tf_op jit(solution)/shard_map/ppermute | solution.py:15
  143.7 8.8 %collective-permute-start.23 = (bf16[2,128,256]{2,1,0:T(8,128)(2,1)S(1)}, bf16[2,128,256]{2,1,0:T(8,128)(2,1)S(1)}, u32[]{:S(2)}, u32[]{:S(2)}) collective-permute-start(bf16[2,128,256]{2,1,0:T(8,128)(2,1)S(1)} %get-tuple-element.73), channel_id=1, source_target_pairs={{1,0},{2,1},{3,2},{4,3},{5,4},{6,5},{7,6},{8,7},{9,8},{10,9},{11,1... | collective-permute-start | bytes 393224 | tf_op jit(solution)/shard_map/ppermute | solution.py:15
  148.4 8.9 %collective-permute-start.27 = (bf16[2,256,256]{2,1,0:T(8,128)(2,1)S(1)}, bf16[2,256,256]{2,1,0:T(8,128)(2,1)S(1)}, u32[]{:S(2)}, u32[]{:S(2)}) collective-permute-start(bf16[2,256,256]{2,1,0:T(8,128)(2,1)S(1)} %get-tuple-element.3), channel_id=1, source_target_pairs={{32,0},{64,32},{96,64},{33,1},{65,33},{97,65},{34,2},{66,34},{98,6... | collective-permute-start | bytes 786440 | tf_op jit(solution)/shard_map/ppermute | solution.py:15
  153.4 11.0 %collective-permute-start.24 = (bf16[2,256,256]{2,1,0:T(8,128)(2,1)S(1)}, bf16[2,256,256]{2,1,0:T(8,128)(2,1)S(1)}, u32[]{:S(2)}, u32[]{:S(2)}) collective-permute-start(bf16[2,256,256]{2,1,0:T(8,128)(2,1)S(1)} %pad_maximum_fusion.27), channel_id=1, source_target_pairs={{32,0},{64,32},{96,64},{33,1},{65,33},{97,65},{34,2},{66,34},{98,6... | collective-permute-start | bytes 786440 | tf_op jit(solution)/shard_map/ppermute | solution.py:15
  157.2 19.2 %copy-start.8 = (bf16[2,256,256]{2,1,0:T(8,128)(2,1)}, bf16[2,256,256]{2,1,0:T(8,128)(2,1)S(1)}, u32[]{:S(2)}) copy-start(bf16[2,256,256]{2,1,0:T(8,128)(2,1)S(1)} %collective-permute-done.27) | copy-start | bytes 786436
  158.1 18.3 %copy-start.5 = (f32[2,256,768]{2,1,0:T(8,128)}, f32[2,256,768]{2,1,0:T(8,128)S(1)}, u32[]{:S(2)}) copy-start(f32[2,256,768]{2,1,0:T(8,128)S(1)} %get-tuple-element.169) | copy-start | bytes 4718596
  158.2 18.2 %collective-permute-start.29 = (bf16[2,256,256]{2,1,0:T(8,128)(2,1)S(1)}, bf16[2,256,256]{2,1,0:T(8,128)(2,1)S(1)}, u32[]{:S(2)}, u32[]{:S(2)}) collective-permute-start(bf16[2,256,256]{2,1,0:T(8,128)(2,1)S(1)} %get-tuple-element.69), channel_id=1, source_target_pairs={{0,2},{1,3},{2,4},{3,5},{4,6},{5,7},{6,8},{7,9},{8,10},{9,11},{10,... | collective-permute-start | bytes 786440 | tf_op jit(solution)/shard_map/ppermute | solution.py:15
  162.5 13.8 %collective-permute-start.28 = (bf16[2,256,256]{2,1,0:T(8,128)(2,1)S(1)}, bf16[2,256,256]{2,1,0:T(8,128)(2,1)S(1)}, u32[]{:S(2)}, u32[]{:S(2)}) collective-permute-start(bf16[2,256,256]{2,1,0:T(8,128)(2,1)S(1)} %get-tuple-element.68), channel_id=1, source_target_pairs={{2,0},{3,1},{4,2},{5,3},{6,4},{7,5},{8,6},{9,7},{10,8},{11,9},{12,... | collective-permute-start | bytes 786440 | tf_op jit(solution)/shard_map/ppermute | solution.py:15
  165.5 12.1 %collective-permute-start.26 = (bf16[2,256,256]{2,1,0:T(8,128)(2,1)S(1)}, bf16[2,256,256]{2,1,0:T(8,128)(2,1)S(1)}, u32[]{:S(2)}, u32[]{:S(2)}) collective-permute-start(bf16[2,256,256]{2,1,0:T(8,128)(2,1)S(1)} %get-tuple-element.71), channel_id=1, source_target_pairs={{0,2},{1,3},{2,4},{3,5},{4,6},{5,7},{6,8},{7,9},{8,10},{9,11},{10,... | collective-permute-start | bytes 786440 | tf_op jit(solution)/shard_map/ppermute | solution.py:15
  171.6 10.4 %collective-permute-start.25 = (bf16[2,256,256]{2,1,0:T(8,128)(2,1)S(1)}, bf16[2,256,256]{2,1,0:T(8,128)(2,1)S(1)}, u32[]{:S(2)}, u32[]{:S(2)}) collective-permute-start(bf16[2,256,256]{2,1,0:T(8,128)(2,1)S(1)} %get-tuple-element.70), channel_id=1, source_target_pairs={{2,0},{3,1},{4,2},{5,3},{6,4},{7,5},{8,6},{9,7},{10,8},{11,9},{12,... | collective-permute-start | bytes 786440 | tf_op jit(solution)/shard_map/ppermute | solution.py:15
  176.4 6.5 %copy-start.26 = (bf16[2,256,256]{2,1,0:T(8,128)(2,1)}, bf16[2,256,256]{2,1,0:T(8,128)(2,1)S(1)}, u32[]{:S(2)}) copy-start(bf16[2,256,256]{2,1,0:T(8,128)(2,1)S(1)} %collective-permute-done.29) | copy-start | bytes 786436
  176.4 6.5 %copy-start.28 = (bf16[2,256,256]{2,1,0:T(8,128)(2,1)}, bf16[2,256,256]{2,1,0:T(8,128)(2,1)S(1)}, u32[]{:S(2)}) copy-start(bf16[2,256,256]{2,1,0:T(8,128)(2,1)S(1)} %collective-permute-done.28) | copy-start | bytes 786436
  184.8 3.8 %copy-start.15 = (f32[768,512]{1,0:T(8,128)S(1)}, f32[768,512]{1,0:T(8,128)}, u32[]{:S(2)}) copy-start(f32[768,512]{1,0:T(8,128)} %bitcast_add_fusion) | copy-start | bytes 4718596
  191.2 2.7 %collective-permute-start.32 = (bf16[2,2,2,2,56,512]{5,4,3,2,1,0:T(8,128)(2,1)S(1)}, bf16[2,2,2,2,56,512]{5,4,3,2,1,0:T(8,128)(2,1)}, u32[]{:S(2)}, u32[]{:S(2)}) collective-permute-start(bf16[2,2,2,2,56,512]{5,4,3,2,1,0:T(8,128)(2,1)S(1)} %fusion.70), channel_id=1, source_target_pairs={{0,1},{1,0},{2,3},{3,2},{4,5},{5,4},{6,7},{7,6},{8,9},{9,8},{10,11... | collective-permute-start | bytes 2752520 | tf_op jit(solution)/shard_map/ppermute | solution.py:199
  191.3 2.6 %copy-start.1 = (f32[2,2,2,2,2,56,512]{6,5,4,3,2,1,0:T(8,128)S(1)}, f32[2,2,2,2,2,56,512]{6,5,4,3,2,1,0:T(8,128)}, u32[]{:S(2)}) copy-start(f32[2,2,2,2,2,56,512]{6,5,4,3,2,1,0:T(8,128)} %copy-done) | copy-start | bytes 11010052
  192.0 3.8 %copy-start.7 = (bf16[2,256,256]{1,2,0:T(8,128)(2,1)S(1)}, bf16[2,256,256]{1,2,0:T(8,128)(2,1)}, u32[]{:S(2)}) copy-start(bf16[2,256,256]{1,2,0:T(8,128)(2,1)} %copy-done.6) | copy-start | bytes 786436
  195.7 13.5 %collective-permute-start.33 = (bf16[2,2,2,56,512]{4,3,2,1,0:T(8,128)(2,1)S(1)}, bf16[2,2,2,56,512]{4,3,2,1,0:T(8,128)(2,1)S(1)}, u32[]{:S(2)}, u32[]{:S(2)}) collective-permute-start(bf16[2,2,2,56,512]{4,3,2,1,0:T(8,128)(2,1)S(1)} %fusion.173), channel_id=1, source_target_pairs={{0,2},{1,3},{2,0},{3,1},{4,6},{5,7},{6,4},{7,5},{8,10},{9,11},{10,... | collective-permute-start | bytes 1376264 | tf_op jit(solution)/shard_map/ppermute | solution.py:199
  196.5 14.7 %copy-start.9 = (bf16[2,256,256]{2,1,0:T(8,128)(2,1)S(1)}, bf16[2,256,256]{2,1,0:T(8,128)(2,1)}, u32[]{:S(2)}) copy-start(bf16[2,256,256]{2,1,0:T(8,128)(2,1)} %copy-done.8) | copy-start | bytes 786436
  196.5 14.7 %copy-start.27 = (bf16[2,256,256]{2,1,0:T(8,128)(2,1)S(1)}, bf16[2,256,256]{2,1,0:T(8,128)(2,1)}, u32[]{:S(2)}) copy-start(bf16[2,256,256]{2,1,0:T(8,128)(2,1)} %copy-done.26) | copy-start | bytes 786436
  196.5 14.7 %copy-start.29 = (bf16[2,256,256]{2,1,0:T(8,128)(2,1)S(1)}, bf16[2,256,256]{2,1,0:T(8,128)(2,1)}, u32[]{:S(2)}) copy-start(bf16[2,256,256]{2,1,0:T(8,128)(2,1)} %copy-done.28) | copy-start | bytes 786436
  196.5 19.4 %collective-permute-start.30 = (bf16[2,128,256]{2,1,0:T(8,128)(2,1)S(1)}, bf16[2,128,256]{2,1,0:T(8,128)(2,1)S(1)}, u32[]{:S(2)}, u32[]{:S(2)}) collective-permute-start(bf16[2,128,256]{2,1,0:T(8,128)(2,1)S(1)} %get-tuple-element.62), channel_id=1, source_target_pairs={{0,1},{1,2},{2,3},{3,4},{4,5},{5,6},{6,7},{7,8},{8,9},{9,10},{10,1... | collective-permute-start | bytes 393224 | tf_op jit(solution)/shard_map/ppermute | solution.py:15
  198.7 17.2 %collective-permute-start.31 = (bf16[2,128,256]{2,1,0:T(8,128)(2,1)S(1)}, bf16[2,128,256]{2,1,0:T(8,128)(2,1)S(1)}, u32[]{:S(2)}, u32[]{:S(2)}) collective-permute-start(bf16[2,128,256]{2,1,0:T(8,128)(2,1)S(1)} %get-tuple-element.63), channel_id=1, source_target_pairs={{1,0},{2,1},{3,2},{4,3},{5,4},{6,5},{7,6},{8,7},{9,8},{10,9},{11,1... | collective-permute-start | bytes 393224 | tf_op jit(solution)/shard_map/ppermute | solution.py:15
  209.5 6.1 %collective-permute-start.34 = (bf16[2,2,56,512]{3,2,1,0:T(8,128)(2,1)S(1)}, bf16[2,2,56,512]{3,2,1,0:T(8,128)(2,1)S(1)}, u32[]{:S(2)}, u32[]{:S(2)}) collective-permute-start(bf16[2,2,56,512]{3,2,1,0:T(8,128)(2,1)S(1)} %fusion.227), channel_id=1, source_target_pairs={{0,8},{1,9},{2,10},{3,11},{4,12},{5,13},{6,14},{7,15},{8,0},{9,1},... | collective-permute-start | bytes 688136 | tf_op jit(solution)/shard_map/ppermute | solution.py:199
  211.2 4.7 %copy-start.14 = (f32[2,256,256]{2,1,0:T(8,128)S(1)}, f32[2,256,256]{2,1,0:T(8,128)}, u32[]{:S(2)}) copy-start(f32[2,256,256]{2,1,0:T(8,128)} %get-tuple-element.6) | copy-start | bytes 1572868
  215.7 10.0 %copy-start.11 = (f32[1,2,256,256]{3,2,1,0:T(8,128)S(1)}, f32[1,2,256,256]{3,2,1,0:T(8,128)}, u32[]{:S(2)}) copy-start(f32[1,2,256,256]{3,2,1,0:T(8,128)} %get-tuple-element.28) | copy-start | bytes 1572868
  215.8 9.9 %copy-start.12 = (f32[2,256,256]{2,1,0:T(8,128)S(1)}, f32[2,256,256]{2,1,0:T(8,128)}, u32[]{:S(2)}) copy-start(f32[2,256,256]{2,1,0:T(8,128)} %get-tuple-element.10) | copy-start | bytes 1572868
  215.8 9.9 %copy-start.13 = (f32[2,256,256]{2,1,0:T(8,128)S(1)}, f32[2,256,256]{2,1,0:T(8,128)}, u32[]{:S(2)}) copy-start(f32[2,256,256]{2,1,0:T(8,128)} %get-tuple-element.4) | copy-start | bytes 1572868
  215.8 9.9 %copy-start.20 = (f32[1,2,128,256]{3,2,1,0:T(8,128)S(1)}, f32[1,2,128,256]{3,2,1,0:T(8,128)}, u32[]{:S(2)}) copy-start(f32[1,2,128,256]{3,2,1,0:T(8,128)} %get-tuple-element.22) | copy-start | bytes 786436
  215.8 9.9 %copy-start.21 = (f32[1,2,128,256]{3,2,1,0:T(8,128)S(1)}, f32[1,2,128,256]{3,2,1,0:T(8,128)}, u32[]{:S(2)}) copy-start(f32[1,2,128,256]{3,2,1,0:T(8,128)} %get-tuple-element.25) | copy-start | bytes 786436
  215.8 9.9 %copy-start.22 = (f32[1,2,128,256]{3,2,1,0:T(8,128)S(1)}, f32[1,2,128,256]{3,2,1,0:T(8,128)}, u32[]{:S(2)}) copy-start(f32[1,2,128,256]{3,2,1,0:T(8,128)} %get-tuple-element.38) | copy-start | bytes 786436
  215.8 9.9 %copy-start.23 = (f32[1,2,128,256]{3,2,1,0:T(8,128)S(1)}, f32[1,2,128,256]{3,2,1,0:T(8,128)}, u32[]{:S(2)}) copy-start(f32[1,2,128,256]{3,2,1,0:T(8,128)} %get-tuple-element.45) | copy-start | bytes 786436
  215.8 9.9 %copy-start.24 = (f32[1,2,128,256]{3,2,1,0:T(8,128)S(1)}, f32[1,2,128,256]{3,2,1,0:T(8,128)}, u32[]{:S(2)}) copy-start(f32[1,2,128,256]{3,2,1,0:T(8,128)} %get-tuple-element.34) | copy-start | bytes 786436
  215.8 9.9 %copy-start.25 = (f32[1,2,128,256]{3,2,1,0:T(8,128)S(1)}, f32[1,2,128,256]{3,2,1,0:T(8,128)}, u32[]{:S(2)}) copy-start(f32[1,2,128,256]{3,2,1,0:T(8,128)} %get-tuple-element.43) | copy-start | bytes 786436
  215.9 6.4 %collective-permute-start.35 = (bf16[2,56,512]{2,1,0:T(8,128)(2,1)S(1)}, bf16[2,56,512]{2,1,0:T(8,128)(2,1)S(1)}, u32[]{:S(2)}, u32[]{:S(2)}) collective-permute-start(bf16[2,56,512]{2,1,0:T(8,128)(2,1)S(1)} %fusion.257), channel_id=1, source_target_pairs={{0,4},{1,5},{2,6},{3,7},{4,0},{5,1},{6,2},{7,3},{8,12},{9,13},{10,... | collective-permute-start | bytes 344072 | tf_op jit(solution)/shard_map/ppermute | solution.py:199
  222.3 5.8 %collective-permute-start.36 = (bf16[56,512]{1,0:T(8,128)(2,1)S(1)}, bf16[56,512]{1,0:T(8,128)(2,1)S(1)}, u32[]{:S(2)}, u32[]{:S(2)}) collective-permute-start(bf16[56,512]{1,0:T(8,128)(2,1)S(1)} %fusion.258), channel_id=1, source_target_pairs={{0,16},{1,17},{2,18},{3,19},{4,20},{5,21},{6,22},{7,23},{8,24},{9,... | collective-permute-start | bytes 172040 | tf_op jit(solution)/shard_map/ppermute | solution.py:199
  (5 other events, 5.7 us)

commit v9 on v8

--- a/solution.py
+++ b/solution.py
@@ -239,7 +239,9 @@
                 flowing, conv_term, out_term = backward_far(
                     flowing, stored[layer], conv_mat[layer], out_mat[layer], far_hops
                 )
-            elif layer == 0 and depth == 2 and step > 0:
+            elif layer == 0 and depth == 2:
+                if step == 0:
+                    flowing = split_rows(flowing, NEAR)
                 flowing, conv_term, out_term = backward_near_pieces(
                     flowing, stored[layer], conv_mat[layer], out_mat[layer]
                 )

time: 231 us -> 233 us (level)
  waiting for transfers between devices: 69.6 us -> 66.1 us
    ppermute x32, waiting for transfers between devices: 50.5 us -> 47.2 us  [shifted(): lax.ppermute(value, axis, [(source, source + steps) for source in range(l...]
    dot_general x3 -> x4, matrix products: 8.24 us -> 10.5 us  [backward_near_pieces(): jnp.einsum('mpc,mpd->cd', taps, grad_pre, preferred_element_type=f32)]
    dot_general x6 -> x8, matrix products: 3.72 us -> 4.96 us  [backward_near_pieces(): jnp.einsum('mpd,cd->mpc', grad_pre, weights, preferred_element_type=f32)]
where the time goes in v9:
time: 233 us; the launch traced here: 231 us
  starting transfers between devices  98.6 us (42%)
  waiting for transfers between devices  66.1 us (28%)
  matrix products  40.1 us (17%)
  other arithmetic  16.3 us (7%)
  local copies, waits for them, and re-layouts  8.14 us (3%)
    ppermute x32, starting transfers between devices, shifted(): lax.ppermute(value, axis, [(source, source + steps) for source in range(l...  91.1 us
    ppermute x32, waiting for transfers between devices, shifted(): lax.ppermute(value, axis, [(source, source + steps) for source in range(l...  47.2 us
    ppermute x5, waiting for transfers between devices, halving_scatter(): got = lax.ppermute(sends, 'seq', pairs)  19 us
    dot_general x4, matrix products, backward_near_pieces(): jnp.einsum('mpc,mpd->cd', taps, grad_pre, preferred_element_type=f32)  10.5 us
    ppermute x5, starting transfers between devices, halving_scatter(): got = lax.ppermute(sends, 'seq', pairs)  7.48 us
    dot_general x7, matrix products, mm(): return jnp.einsum('mpc,cd->mpd', a, b, preferred_element_type=jnp.float32)  6.9 us
    dot_general x8, matrix products, backward_near_pieces(): jnp.einsum('mpd,cd->mpc', grad_pre, weights, preferred_element_type=f32)  4.96 us
  transfers between devices with their start and end apart: 37, of which 15 were waited for; matrix products, arithmetic and copies ran while one was open for 17% of the time, Pallas kernels for 0%

profile of v9, /device:TPU:24, one launch (start us, length us, event | category | flops | bytes accessed | tf_op | source)
XLA Modules:
  0.0 231.3 jit_solution(15155234655435963790)
XLA Ops:
  1.7 1.9 collective-permute-start
  3.6 3.6 %collective-permute-start.1 = (bf16[2,128,256]{2,1,0:T(8,128)(2,1)S(1)}, bf16[2,128,256]{2,1,0:T(8,128)(2,1)S(1)}, u32[]{:S(2)}, u32[]{:S(2)}) collective-permute-start(bf16[2,128,256]{2,1,0:T(8,128)(2,1)S(1)} %get-tuple-element.139), channel_id=1, source_target_pairs={{1,0},{2,1},{3,2},{4,3},{5,4},{6,5},{7,6},{8,7},{9,8},{10,9},{11,1... | collective-permute-start | bytes 393224 | tf_op jit(solution)/shard_map/ppermute | solution.py:15
  7.3 1.5 fusion.358
  8.8 2.8 %fusion.237 = f32[2,512,512]{1,2,0:T(8,128)} fusion(bf16[1,2,3,256,512]{4,3,2,1,0:T(8,128)(2,1)} %param.6, bf16[1,2,512,256]{3,2,1,0:T(8,128)(2,1)S(1)} %copy-done.4), kind=kOutput, calls=%fused_computation.361 | convolution fusion | flops 268435456 | bytes 2883584 | tf_op jit(solution)/shard_map/mpc,cd->mpd/dot_general | solution.py:32
  11.6 1.8 fusion.113
  15.8 5.6 %collective-permute-start.2 = (bf16[2,512,256]{2,1,0:T(8,128)(2,1)S(1)}, bf16[2,512,256]{2,1,0:T(8,128)(2,1)S(1)}, u32[]{:S(2)}, u32[]{:S(2)}) collective-permute-start(bf16[2,512,256]{2,1,0:T(8,128)(2,1)S(1)} %fusion.2), channel_id=1, source_target_pairs={{0,2},{1,3},{2,4},{3,5},{4,6},{5,7},{6,8},{7,9},{8,10},{9,11},{10,... | collective-permute-start | bytes 1572872 | tf_op jit(solution)/shard_map/ppermute | solution.py:15
  21.4 1.9 collective-permute-start.3
  23.9 7.6 %collective-permute-done.2 = bf16[2,512,256]{2,1,0:T(8,128)(2,1)S(1)} collective-permute-done((bf16[2,512,256]{2,1,0:T(8,128)(2,1)S(1)}, bf16[2,512,256]{2,1,0:T(8,128)(2,1)S(1)}, u32[]{:S(2)}, u32[]{:S(2)}) %collective-permute-start.2) | collective-permute-done | bytes 524320 | tf_op jit(solution)/shard_map/ppermute | solution.py:15
  32.0 4.8 %collective-permute-done.3 = bf16[2,512,256]{2,1,0:T(8,128)(2,1)S(1)} collective-permute-done((bf16[2,512,256]{2,1,0:T(8,128)(2,1)S(1)}, bf16[2,512,256]{2,1,0:T(8,128)(2,1)S(1)}, u32[]{:S(2)}, u32[]{:S(2)}) %collective-permute-start.3) | collective-permute-done | bytes 524320 | tf_op jit(solution)/shard_map/ppermute | solution.py:15
  39.2 1.9 collective-permute-start.5
  41.1 3.9 %collective-permute-start.4 = (bf16[2,512,256]{2,1,0:T(8,128)(2,1)S(1)}, bf16[2,512,256]{2,1,0:T(8,128)(2,1)S(1)}, u32[]{:S(2)}, u32[]{:S(2)}) collective-permute-start(bf16[2,512,256]{2,1,0:T(8,128)(2,1)S(1)} %get-tuple-element.45), channel_id=1, source_target_pairs={{2,0},{3,1},{4,2},{5,3},{6,4},{7,5},{8,6},{9,7},{10,8},{11,9},{12,... | collective-permute-start | bytes 1572872 | tf_op jit(solution)/shard_map/ppermute | solution.py:15
  46.5 5.1 %collective-permute-done.5 = bf16[2,512,256]{2,1,0:T(8,128)(2,1)S(1)} collective-permute-done((bf16[2,512,256]{2,1,0:T(8,128)(2,1)S(1)}, bf16[2,512,256]{2,1,0:T(8,128)(2,1)S(1)}, u32[]{:S(2)}, u32[]{:S(2)}) %collective-permute-start.5) | collective-permute-done | bytes 524320 | tf_op jit(solution)/shard_map/ppermute | solution.py:15
  51.6 4.8 %collective-permute-done.4 = bf16[2,512,256]{2,1,0:T(8,128)(2,1)S(1)} collective-permute-done((bf16[2,512,256]{2,1,0:T(8,128)(2,1)S(1)}, bf16[2,512,256]{2,1,0:T(8,128)(2,1)S(1)}, u32[]{:S(2)}, u32[]{:S(2)}) %collective-permute-start.4) | collective-permute-done | bytes 524320 | tf_op jit(solution)/shard_map/ppermute | solution.py:15
  58.1 1.9 collective-permute-start.6
  60.0 3.6 %collective-permute-start.7 = (bf16[2,128,256]{2,1,0:T(8,128)(2,1)S(1)}, bf16[2,128,256]{2,1,0:T(8,128)(2,1)S(1)}, u32[]{:S(2)}, u32[]{:S(2)}) collective-permute-start(bf16[2,128,256]{2,1,0:T(8,128)(2,1)S(1)} %get-tuple-element.90), channel_id=1, source_target_pairs={{1,0},{2,1},{3,2},{4,3},{5,4},{6,5},{7,6},{8,7},{9,8},{10,9},{11,1... | collective-permute-start | bytes 393224 | tf_op jit(solution)/shard_map/ppermute | solution.py:15
  64.5 1.3 collective-permute-start.11
  65.8 2.2 fusion.21
  69.0 1.3 collective-permute-start.8
  70.2 3.1 %collective-permute-done.11 = bf16[2,256,256]{2,1,0:T(8,128)(2,1)S(1)} collective-permute-done((bf16[2,256,256]{2,1,0:T(8,128)(2,1)S(1)}, bf16[2,256,256]{2,1,0:T(8,128)(2,1)S(1)}, u32[]{:S(2)}, u32[]{:S(2)}) %collective-permute-start.11) | collective-permute-done | bytes 262176 | tf_op jit(solution)/shard_map/ppermute | solution.py:15
  74.3 3.8 %collective-permute-start.13 = (bf16[2,256,256]{2,1,0:T(8,128)(2,1)S(1)}, bf16[2,256,256]{2,1,0:T(8,128)(2,1)S(1)}, u32[]{:S(2)}, u32[]{:S(2)}) collective-permute-start(bf16[2,256,256]{2,1,0:T(8,128)(2,1)S(1)} %get-tuple-element.88), channel_id=1, source_target_pairs={{0,2},{1,3},{2,4},{3,5},{4,6},{5,7},{6,8},{7,9},{8,10},{9,11},{10,... | collective-permute-start | bytes 786440 | tf_op jit(solution)/shard_map/ppermute | solution.py:15
  78.1 2.3 collective-permute-start.12
  81.3 5.9 %collective-permute-start.10 = (bf16[2,256,256]{2,1,0:T(8,128)(2,1)S(1)}, bf16[2,256,256]{2,1,0:T(8,128)(2,1)S(1)}, u32[]{:S(2)}, u32[]{:S(2)}) collective-permute-start(bf16[2,256,256]{2,1,0:T(8,128)(2,1)S(1)} %get-tuple-element.86), channel_id=1, source_target_pairs={{0,2},{1,3},{2,4},{3,5},{4,6},{5,7},{6,8},{7,9},{8,10},{9,11},{10,... | collective-permute-start | bytes 786440 | tf_op jit(solution)/shard_map/ppermute | solution.py:15
  87.2 1.9 collective-permute-start.9
  91.4 6.2 %collective-permute-done.9 = bf16[2,256,256]{2,1,0:T(8,128)(2,1)S(1)} collective-permute-done((bf16[2,256,256]{2,1,0:T(8,128)(2,1)S(1)}, bf16[2,256,256]{2,1,0:T(8,128)(2,1)S(1)}, u32[]{:S(2)}, u32[]{:S(2)}) %collective-permute-start.9) | collective-permute-done | bytes 262176 | tf_op jit(solution)/shard_map/ppermute | solution.py:15
  98.7 1.9 collective-permute-start.14
  100.7 3.6 %collective-permute-start.15 = (bf16[2,128,256]{2,1,0:T(8,128)(2,1)S(1)}, bf16[2,128,256]{2,1,0:T(8,128)(2,1)S(1)}, u32[]{:S(2)}, u32[]{:S(2)}) collective-permute-start(bf16[2,128,256]{2,1,0:T(8,128)(2,1)S(1)} %get-tuple-element.80), channel_id=1, source_target_pairs={{1,0},{2,1},{3,2},{4,3},{5,4},{6,5},{7,6},{8,7},{9,8},{10,9},{11,1... | collective-permute-start | bytes 393224 | tf_op jit(solution)/shard_map/ppermute | solution.py:15
  104.3 1.1 fusion.353
  105.4 1.3 collective-permute-start.19
  106.7 2.2 fusion.29
  110.2 1.3 collective-permute-start.16
  111.5 2.8 %collective-permute-done.19 = bf16[2,256,256]{2,1,0:T(8,128)(2,1)S(1)} collective-permute-done((bf16[2,256,256]{2,1,0:T(8,128)(2,1)S(1)}, bf16[2,256,256]{2,1,0:T(8,128)(2,1)S(1)}, u32[]{:S(2)}, u32[]{:S(2)}) %collective-permute-start.19) | collective-permute-done | bytes 262176 | tf_op jit(solution)/shard_map/ppermute | solution.py:15
  115.2 3.9 %collective-permute-start.21 = (bf16[2,256,256]{2,1,0:T(8,128)(2,1)S(1)}, bf16[2,256,256]{2,1,0:T(8,128)(2,1)S(1)}, u32[]{:S(2)}, u32[]{:S(2)}) collective-permute-start(bf16[2,256,256]{2,1,0:T(8,128)(2,1)S(1)} %get-tuple-element.78), channel_id=1, source_target_pairs={{0,2},{1,3},{2,4},{3,5},{4,6},{5,7},{6,8},{7,9},{8,10},{9,11},{10,... | collective-permute-start | bytes 786440 | tf_op jit(solution)/shard_map/ppermute | solution.py:15
  119.2 1.9 collective-permute-start.20
  122.1 6.0 %collective-permute-start.18 = (bf16[2,256,256]{2,1,0:T(8,128)(2,1)S(1)}, bf16[2,256,256]{2,1,0:T(8,128)(2,1)S(1)}, u32[]{:S(2)}, u32[]{:S(2)}) collective-permute-start(bf16[2,256,256]{2,1,0:T(8,128)(2,1)S(1)} %get-tuple-element.76), channel_id=1, source_target_pairs={{0,2},{1,3},{2,4},{3,5},{4,6},{5,7},{6,8},{7,9},{8,10},{9,11},{10,... | collective-permute-start | bytes 786440 | tf_op jit(solution)/shard_map/ppermute | solution.py:15
  128.1 1.9 collective-permute-start.17
  132.6 5.9 %collective-permute-done.17 = bf16[2,256,256]{2,1,0:T(8,128)(2,1)S(1)} collective-permute-done((bf16[2,256,256]{2,1,0:T(8,128)(2,1)S(1)}, bf16[2,256,256]{2,1,0:T(8,128)(2,1)S(1)}, u32[]{:S(2)}, u32[]{:S(2)}) %collective-permute-start.17) | collective-permute-done | bytes 262176 | tf_op jit(solution)/shard_map/ppermute | solution.py:15
  139.7 1.9 collective-permute-start.22
  141.6 3.6 %collective-permute-start.23 = (bf16[2,128,256]{2,1,0:T(8,128)(2,1)S(1)}, bf16[2,128,256]{2,1,0:T(8,128)(2,1)S(1)}, u32[]{:S(2)}, u32[]{:S(2)}) collective-permute-start(bf16[2,128,256]{2,1,0:T(8,128)(2,1)S(1)} %get-tuple-element.70), channel_id=1, source_target_pairs={{1,0},{2,1},{3,2},{4,3},{5,4},{6,5},{7,6},{8,7},{9,8},{10,9},{11,1... | collective-permute-start | bytes 393224 | tf_op jit(solution)/shard_map/ppermute | solution.py:15
  146.3 1.5 collective-permute-start.27
  147.9 2.3 fusion.37
  151.4 1.3 collective-permute-start.24
  152.7 2.5 %collective-permute-done.27 = bf16[2,256,256]{2,1,0:T(8,128)(2,1)S(1)} collective-permute-done((bf16[2,256,256]{2,1,0:T(8,128)(2,1)S(1)}, bf16[2,256,256]{2,1,0:T(8,128)(2,1)S(1)}, u32[]{:S(2)}, u32[]{:S(2)}) %collective-permute-start.27) | collective-permute-done | bytes 262176 | tf_op jit(solution)/shard_map/ppermute | solution.py:15
  156.2 4.3 %collective-permute-start.29 = (bf16[2,256,256]{2,1,0:T(8,128)(2,1)S(1)}, bf16[2,256,256]{2,1,0:T(8,128)(2,1)S(1)}, u32[]{:S(2)}, u32[]{:S(2)}) collective-permute-start(bf16[2,256,256]{2,1,0:T(8,128)(2,1)S(1)} %get-tuple-element.66), channel_id=1, source_target_pairs={{0,2},{1,3},{2,4},{3,5},{4,6},{5,7},{6,8},{7,9},{8,10},{9,11},{10,... | collective-permute-start | bytes 786440 | tf_op jit(solution)/shard_map/ppermute | solution.py:15
  160.5 1.9 collective-permute-start.28
  163.5 6.0 %collective-permute-start.26 = (bf16[2,256,256]{2,1,0:T(8,128)(2,1)S(1)}, bf16[2,256,256]{2,1,0:T(8,128)(2,1)S(1)}, u32[]{:S(2)}, u32[]{:S(2)}) collective-permute-start(bf16[2,256,256]{2,1,0:T(8,128)(2,1)S(1)} %get-tuple-element.68), channel_id=1, source_target_pairs={{0,2},{1,3},{2,4},{3,5},{4,6},{5,7},{6,8},{7,9},{8,10},{9,11},{10,... | collective-permute-start | bytes 786440 | tf_op jit(solution)/shard_map/ppermute | solution.py:15
  169.5 1.9 collective-permute-start.25
  171.5 2.2 bitcast_add_fusion
  174.5 1.1 multiply_convert_fusion.3
  175.6 4.3 %collective-permute-done.25 = bf16[2,256,256]{2,1,0:T(8,128)(2,1)S(1)} collective-permute-done((bf16[2,256,256]{2,1,0:T(8,128)(2,1)S(1)}, bf16[2,256,256]{2,1,0:T(8,128)(2,1)S(1)}, u32[]{:S(2)}, u32[]{:S(2)}) %collective-permute-start.25) | collective-permute-done | bytes 262176 | tf_op jit(solution)/shard_map/ppermute | solution.py:15
  182.6 1.2 concatenate.321
  183.9 3.9 %bitcast_add_fusion.3 = f32[768,512]{1,0:T(8,128)S(1)} fusion(f32[768,512,1]{1,0,2:T(8,128)} %fusion.37, f32[768,512,1]{1,0,2:T(8,128)} %fusion.29, f32[768,512,1]{1,0,2:T(8,128)} %fusion.21, bf16[2,128,512]{1,2,0:T(8,128)(2,1)S(1)} %get-tuple-element.96, bf16[2,256,256]{1,2,0:T(8,128)(2,1)} %get-tuple-element.110, bf16[2,256,256]{1,2,0:T(8,128)(2,1)S(1)} %copy-done.14, ...), kind=kOutput, calls=%fused_computation.12 | convolution fusion | flops 818544640 | bytes 8912896 | tf_op jit(solution)/shard_map/mpc,mpd->cd/dot_general | solution.py:151
  188.4 1.8 copy-done
  190.2 1.1 fusion.78
  191.9 2.2 collective-permute-done.32
  194.1 1.7 fusion.1
  196.7 2.0 collective-permute-start.30
  198.8 3.7 %collective-permute-start.31 = (bf16[2,128,256]{2,1,0:T(8,128)(2,1)S(1)}, bf16[2,128,256]{2,1,0:T(8,128)(2,1)S(1)}, u32[]{:S(2)}, u32[]{:S(2)}) collective-permute-start(bf16[2,128,256]{2,1,0:T(8,128)(2,1)S(1)} %get-tuple-element.60), channel_id=1, source_target_pairs={{1,0},{2,1},{3,2},{4,3},{5,4},{6,5},{7,6},{8,7},{9,8},{10,9},{11,1... | collective-permute-start | bytes 393224 | tf_op jit(solution)/shard_map/ppermute | solution.py:15
  202.4 7.0 %collective-permute-done.33 = bf16[2,2,2,56,512]{4,3,2,1,0:T(8,128)(2,1)S(1)} collective-permute-done((bf16[2,2,2,56,512]{4,3,2,1,0:T(8,128)(2,1)S(1)}, bf16[2,2,2,56,512]{4,3,2,1,0:T(8,128)(2,1)S(1)}, u32[]{:S(2)}, u32[]{:S(2)}) %collective-permute-start.33) | collective-permute-done | bytes 458784 | tf_op jit(solution)/shard_map/ppermute | solution.py:199
  209.7 2.8 %collective-permute-start.34 = (bf16[2,2,56,512]{3,2,1,0:T(8,128)(2,1)S(1)}, bf16[2,2,56,512]{3,2,1,0:T(8,128)(2,1)S(1)}, u32[]{:S(2)}, u32[]{:S(2)}) collective-permute-start(bf16[2,2,56,512]{3,2,1,0:T(8,128)(2,1)S(1)} %fusion.246), channel_id=1, source_target_pairs={{0,8},{1,9},{2,10},{3,11},{4,12},{5,13},{6,14},{7,15},{8,0},{9,1},... | collective-permute-start | bytes 688136 | tf_op jit(solution)/shard_map/ppermute | solution.py:199
  212.5 1.4 fusion.94
  213.8 2.9 %collective-permute-done.34 = bf16[2,2,56,512]{3,2,1,0:T(8,128)(2,1)S(1)} collective-permute-done((bf16[2,2,56,512]{3,2,1,0:T(8,128)(2,1)S(1)}, bf16[2,2,56,512]{3,2,1,0:T(8,128)(2,1)S(1)}, u32[]{:S(2)}, u32[]{:S(2)}) %collective-permute-start.34) | collective-permute-done | bytes 229408 | tf_op jit(solution)/shard_map/ppermute | solution.py:199
  217.2 6.1 %collective-permute-done.35 = bf16[2,56,512]{2,1,0:T(8,128)(2,1)S(1)} collective-permute-done((bf16[2,56,512]{2,1,0:T(8,128)(2,1)S(1)}, bf16[2,56,512]{2,1,0:T(8,128)(2,1)S(1)}, u32[]{:S(2)}, u32[]{:S(2)}) %collective-permute-start.35) | collective-permute-done | bytes 114720 | tf_op jit(solution)/shard_map/ppermute | solution.py:199
  223.4 4.5 %collective-permute-start.36 = (bf16[56,512]{1,0:T(8,128)(2,1)S(1)}, bf16[56,512]{1,0:T(8,128)(2,1)S(1)}, u32[]{:S(2)}, u32[]{:S(2)}) collective-permute-start(bf16[56,512]{1,0:T(8,128)(2,1)S(1)} %fusion.279), channel_id=1, source_target_pairs={{0,16},{1,17},{2,18},{3,19},{4,20},{5,21},{6,22},{7,23},{8,24},{9,... | collective-permute-start | bytes 172040 | tf_op jit(solution)/shard_map/ppermute | solution.py:199
  227.9 1.2 fusion.20
  (190 shorter events, 36.3 us)
Async XLA Ops:
  0.6 8.1 %copy-start.4 = (bf16[1,2,512,256]{3,2,1,0:T(8,128)(2,1)S(1)}, bf16[1,2,512,256]{3,2,1,0:T(8,128)(2,1)}, u32[]{:S(2)}) copy-start(bf16[1,2,512,256]{3,2,1,0:T(8,128)(2,1)} %param.4) | copy-start | bytes 1572868
  1.7 9.9 %collective-permute-start = (bf16[2,128,256]{2,1,0:T(8,128)(2,1)S(1)}, bf16[2,128,256]{2,1,0:T(8,128)(2,1)S(1)}, u32[]{:S(2)}, u32[]{:S(2)}) collective-permute-start(bf16[2,128,256]{2,1,0:T(8,128)(2,1)S(1)} %get-tuple-element.140), channel_id=1, source_target_pairs={{0,1},{1,2},{2,3},{3,4},{4,5},{5,6},{6,7},{7,8},{8,9},{9,10},{10,1... | collective-permute-start | bytes 393224 | tf_op jit(solution)/shard_map/ppermute | solution.py:15
  3.6 9.8 %collective-permute-start.1 = (bf16[2,128,256]{2,1,0:T(8,128)(2,1)S(1)}, bf16[2,128,256]{2,1,0:T(8,128)(2,1)S(1)}, u32[]{:S(2)}, u32[]{:S(2)}) collective-permute-start(bf16[2,128,256]{2,1,0:T(8,128)(2,1)S(1)} %get-tuple-element.139), channel_id=1, source_target_pairs={{1,0},{2,1},{3,2},{4,3},{5,4},{6,5},{7,6},{8,7},{9,8},{10,9},{11,1... | collective-permute-start | bytes 393224 | tf_op jit(solution)/shard_map/ppermute | solution.py:15
  11.5 1.9 copy-start.5
  11.6 136.3 %copy-start.12 = (bf16[2,384,256]{2,1,0:T(8,128)(2,1)}, bf16[2,384,256]{2,1,0:T(8,128)(2,1)S(1)}, u32[]{:S(2)}) copy-start(bf16[2,384,256]{2,1,0:T(8,128)(2,1)S(1)} %get-tuple-element.137) | copy-start | bytes 1179652
  11.6 136.3 %copy-start.13 = (bf16[2,384,256]{2,1,0:T(8,128)(2,1)}, bf16[2,384,256]{2,1,0:T(8,128)(2,1)S(1)}, u32[]{:S(2)}) copy-start(bf16[2,384,256]{2,1,0:T(8,128)(2,1)S(1)} %get-tuple-element.138) | copy-start | bytes 1179652
  11.6 2.4 %copy-start.3 = (f32[2,512,512]{1,2,0:T(8,128)S(1)}, f32[2,512,512]{1,2,0:T(8,128)}, u32[]{:S(2)}) copy-start(f32[2,512,512]{1,2,0:T(8,128)} %fusion.237) | copy-start | bytes 6291460
  11.6 2.9 %copy-start.26 = (bf16[2,128,256]{2,1,0:T(8,128)(2,1)}, bf16[2,128,256]{2,1,0:T(8,128)(2,1)S(1)}, u32[]{:S(2)}) copy-start(bf16[2,128,256]{2,1,0:T(8,128)(2,1)S(1)} %collective-permute-done) | copy-start | bytes 393220
  15.8 15.7 %collective-permute-start.2 = (bf16[2,512,256]{2,1,0:T(8,128)(2,1)S(1)}, bf16[2,512,256]{2,1,0:T(8,128)(2,1)S(1)}, u32[]{:S(2)}, u32[]{:S(2)}) collective-permute-start(bf16[2,512,256]{2,1,0:T(8,128)(2,1)S(1)} %fusion.2), channel_id=1, source_target_pairs={{0,2},{1,3},{2,4},{3,5},{4,6},{5,7},{6,8},{7,9},{8,10},{9,11},{10,... | collective-permute-start | bytes 1572872 | tf_op jit(solution)/shard_map/ppermute | solution.py:15
  21.4 15.4 %collective-permute-start.3 = (bf16[2,512,256]{2,1,0:T(8,128)(2,1)S(1)}, bf16[2,512,256]{2,1,0:T(8,128)(2,1)S(1)}, u32[]{:S(2)}, u32[]{:S(2)}) collective-permute-start(bf16[2,512,256]{2,1,0:T(8,128)(2,1)S(1)} %fusion.2), channel_id=1, source_target_pairs={{2,0},{3,1},{4,2},{5,3},{6,4},{7,5},{8,6},{9,7},{10,8},{11,9},{12,... | collective-permute-start | bytes 1572872 | tf_op jit(solution)/shard_map/ppermute | solution.py:15
  32.0 5.4 %copy-start.7 = (bf16[2,512,256]{2,1,0:T(8,128)(2,1)S(1)}, bf16[2,512,256]{2,1,0:T(8,128)(2,1)}, u32[]{:S(2)}) copy-start(bf16[2,512,256]{2,1,0:T(8,128)(2,1)} %param.5) | copy-start | bytes 1572868
  39.2 12.4 %collective-permute-start.5 = (bf16[2,512,256]{2,1,0:T(8,128)(2,1)S(1)}, bf16[2,512,256]{2,1,0:T(8,128)(2,1)S(1)}, u32[]{:S(2)}, u32[]{:S(2)}) collective-permute-start(bf16[2,512,256]{2,1,0:T(8,128)(2,1)S(1)} %get-tuple-element.46), channel_id=1, source_target_pairs={{0,2},{1,3},{2,4},{3,5},{4,6},{5,7},{6,8},{7,9},{8,10},{9,11},{10,... | collective-permute-start | bytes 1572872 | tf_op jit(solution)/shard_map/ppermute | solution.py:15
  41.1 15.3 %collective-permute-start.4 = (bf16[2,512,256]{2,1,0:T(8,128)(2,1)S(1)}, bf16[2,512,256]{2,1,0:T(8,128)(2,1)S(1)}, u32[]{:S(2)}, u32[]{:S(2)}) collective-permute-start(bf16[2,512,256]{2,1,0:T(8,128)(2,1)S(1)} %get-tuple-element.45), channel_id=1, source_target_pairs={{2,0},{3,1},{4,2},{5,3},{6,4},{7,5},{8,6},{9,7},{10,8},{11,9},{12,... | collective-permute-start | bytes 1572872 | tf_op jit(solution)/shard_map/ppermute | solution.py:15
  58.1 9.9 %collective-permute-start.6 = (bf16[2,128,256]{2,1,0:T(8,128)(2,1)S(1)}, bf16[2,128,256]{2,1,0:T(8,128)(2,1)S(1)}, u32[]{:S(2)}, u32[]{:S(2)}) collective-permute-start(bf16[2,128,256]{2,1,0:T(8,128)(2,1)S(1)} %get-tuple-element.89), channel_id=1, source_target_pairs={{0,1},{1,2},{2,3},{3,4},{4,5},{5,6},{6,7},{7,8},{8,9},{9,10},{10,1... | collective-permute-start | bytes 393224 | tf_op jit(solution)/shard_map/ppermute | solution.py:15
  60.0 8.0 %collective-permute-start.7 = (bf16[2,128,256]{2,1,0:T(8,128)(2,1)S(1)}, bf16[2,128,256]{2,1,0:T(8,128)(2,1)S(1)}, u32[]{:S(2)}, u32[]{:S(2)}) collective-permute-start(bf16[2,128,256]{2,1,0:T(8,128)(2,1)S(1)} %get-tuple-element.90), channel_id=1, source_target_pairs={{1,0},{2,1},{3,2},{4,3},{5,4},{6,5},{7,6},{8,7},{9,8},{10,9},{11,1... | collective-permute-start | bytes 393224 | tf_op jit(solution)/shard_map/ppermute | solution.py:15
  64.3 1.5 copy-start.27
  64.5 8.9 %collective-permute-start.11 = (bf16[2,256,256]{2,1,0:T(8,128)(2,1)S(1)}, bf16[2,256,256]{2,1,0:T(8,128)(2,1)S(1)}, u32[]{:S(2)}, u32[]{:S(2)}) collective-permute-start(bf16[2,256,256]{2,1,0:T(8,128)(2,1)S(1)} %get-tuple-element.23), channel_id=1, source_target_pairs={{32,0},{64,32},{96,64},{33,1},{65,33},{97,65},{34,2},{66,34},{98,6... | collective-permute-start | bytes 786440 | tf_op jit(solution)/shard_map/ppermute | solution.py:15
  69.0 11.4 %collective-permute-start.8 = (bf16[2,256,256]{2,1,0:T(8,128)(2,1)S(1)}, bf16[2,256,256]{2,1,0:T(8,128)(2,1)S(1)}, u32[]{:S(2)}, u32[]{:S(2)}) collective-permute-start(bf16[2,256,256]{2,1,0:T(8,128)(2,1)S(1)} %pad_maximum_fusion.24), channel_id=1, source_target_pairs={{32,0},{64,32},{96,64},{33,1},{65,33},{97,65},{34,2},{66,34},{98,6... | collective-permute-start | bytes 786440 | tf_op jit(solution)/shard_map/ppermute | solution.py:15
  74.3 16.0 %collective-permute-start.13 = (bf16[2,256,256]{2,1,0:T(8,128)(2,1)S(1)}, bf16[2,256,256]{2,1,0:T(8,128)(2,1)S(1)}, u32[]{:S(2)}, u32[]{:S(2)}) collective-permute-start(bf16[2,256,256]{2,1,0:T(8,128)(2,1)S(1)} %get-tuple-element.88), channel_id=1, source_target_pairs={{0,2},{1,3},{2,4},{3,5},{4,6},{5,7},{6,8},{7,9},{8,10},{9,11},{10,... | collective-permute-start | bytes 786440 | tf_op jit(solution)/shard_map/ppermute | solution.py:15
  78.1 12.2 %collective-permute-start.12 = (bf16[2,256,256]{2,1,0:T(8,128)(2,1)S(1)}, bf16[2,256,256]{2,1,0:T(8,128)(2,1)S(1)}, u32[]{:S(2)}, u32[]{:S(2)}) collective-permute-start(bf16[2,256,256]{2,1,0:T(8,128)(2,1)S(1)} %get-tuple-element.87), channel_id=1, source_target_pairs={{2,0},{3,1},{4,2},{5,3},{6,4},{7,5},{8,6},{9,7},{10,8},{11,9},{12,... | collective-permute-start | bytes 786440 | tf_op jit(solution)/shard_map/ppermute | solution.py:15
  81.3 10.1 %collective-permute-start.10 = (bf16[2,256,256]{2,1,0:T(8,128)(2,1)S(1)}, bf16[2,256,256]{2,1,0:T(8,128)(2,1)S(1)}, u32[]{:S(2)}, u32[]{:S(2)}) collective-permute-start(bf16[2,256,256]{2,1,0:T(8,128)(2,1)S(1)} %get-tuple-element.86), channel_id=1, source_target_pairs={{0,2},{1,3},{2,4},{3,5},{4,6},{5,7},{6,8},{7,9},{8,10},{9,11},{10,... | collective-permute-start | bytes 786440 | tf_op jit(solution)/shard_map/ppermute | solution.py:15
  87.2 10.4 %collective-permute-start.9 = (bf16[2,256,256]{2,1,0:T(8,128)(2,1)S(1)}, bf16[2,256,256]{2,1,0:T(8,128)(2,1)S(1)}, u32[]{:S(2)}, u32[]{:S(2)}) collective-permute-start(bf16[2,256,256]{2,1,0:T(8,128)(2,1)S(1)} %get-tuple-element.85), channel_id=1, source_target_pairs={{2,0},{3,1},{4,2},{5,3},{6,4},{7,5},{8,6},{9,7},{10,8},{11,9},{12,... | collective-permute-start | bytes 786440 | tf_op jit(solution)/shard_map/ppermute | solution.py:15
  98.7 10.4 %collective-permute-start.14 = (bf16[2,128,256]{2,1,0:T(8,128)(2,1)S(1)}, bf16[2,128,256]{2,1,0:T(8,128)(2,1)S(1)}, u32[]{:S(2)}, u32[]{:S(2)}) collective-permute-start(bf16[2,128,256]{2,1,0:T(8,128)(2,1)S(1)} %get-tuple-element.79), channel_id=1, source_target_pairs={{0,1},{1,2},{2,3},{3,4},{4,5},{5,6},{6,7},{7,8},{8,9},{9,10},{10,1... | collective-permute-start | bytes 393224 | tf_op jit(solution)/shard_map/ppermute | solution.py:15
  100.7 8.5 %collective-permute-start.15 = (bf16[2,128,256]{2,1,0:T(8,128)(2,1)S(1)}, bf16[2,128,256]{2,1,0:T(8,128)(2,1)S(1)}, u32[]{:S(2)}, u32[]{:S(2)}) collective-permute-start(bf16[2,128,256]{2,1,0:T(8,128)(2,1)S(1)} %get-tuple-element.80), channel_id=1, source_target_pairs={{1,0},{2,1},{3,2},{4,3},{5,4},{6,5},{7,6},{8,7},{9,8},{10,9},{11,1... | collective-permute-start | bytes 393224 | tf_op jit(solution)/shard_map/ppermute | solution.py:15
  105.4 8.9 %collective-permute-start.19 = (bf16[2,256,256]{2,1,0:T(8,128)(2,1)S(1)}, bf16[2,256,256]{2,1,0:T(8,128)(2,1)S(1)}, u32[]{:S(2)}, u32[]{:S(2)}) collective-permute-start(bf16[2,256,256]{2,1,0:T(8,128)(2,1)S(1)} %get-tuple-element.9), channel_id=1, source_target_pairs={{32,0},{64,32},{96,64},{33,1},{65,33},{97,65},{34,2},{66,34},{98,6... | collective-permute-start | bytes 786440 | tf_op jit(solution)/shard_map/ppermute | solution.py:15
  110.2 11.0 %collective-permute-start.16 = (bf16[2,256,256]{2,1,0:T(8,128)(2,1)S(1)}, bf16[2,256,256]{2,1,0:T(8,128)(2,1)S(1)}, u32[]{:S(2)}, u32[]{:S(2)}) collective-permute-start(bf16[2,256,256]{2,1,0:T(8,128)(2,1)S(1)} %pad_maximum_fusion.25), channel_id=1, source_target_pairs={{32,0},{64,32},{96,64},{33,1},{65,33},{97,65},{34,2},{66,34},{98,6... | collective-permute-start | bytes 786440 | tf_op jit(solution)/shard_map/ppermute | solution.py:15
  115.2 16.3 %collective-permute-start.21 = (bf16[2,256,256]{2,1,0:T(8,128)(2,1)S(1)}, bf16[2,256,256]{2,1,0:T(8,128)(2,1)S(1)}, u32[]{:S(2)}, u32[]{:S(2)}) collective-permute-start(bf16[2,256,256]{2,1,0:T(8,128)(2,1)S(1)} %get-tuple-element.78), channel_id=1, source_target_pairs={{0,2},{1,3},{2,4},{3,5},{4,6},{5,7},{6,8},{7,9},{8,10},{9,11},{10,... | collective-permute-start | bytes 786440 | tf_op jit(solution)/shard_map/ppermute | solution.py:15
  119.2 12.3 %collective-permute-start.20 = (bf16[2,256,256]{2,1,0:T(8,128)(2,1)S(1)}, bf16[2,256,256]{2,1,0:T(8,128)(2,1)S(1)}, u32[]{:S(2)}, u32[]{:S(2)}) collective-permute-start(bf16[2,256,256]{2,1,0:T(8,128)(2,1)S(1)} %get-tuple-element.77), channel_id=1, source_target_pairs={{2,0},{3,1},{4,2},{5,3},{6,4},{7,5},{8,6},{9,7},{10,8},{11,9},{12,... | collective-permute-start | bytes 786440 | tf_op jit(solution)/shard_map/ppermute | solution.py:15
  122.1 10.5 %collective-permute-start.18 = (bf16[2,256,256]{2,1,0:T(8,128)(2,1)S(1)}, bf16[2,256,256]{2,1,0:T(8,128)(2,1)S(1)}, u32[]{:S(2)}, u32[]{:S(2)}) collective-permute-start(bf16[2,256,256]{2,1,0:T(8,128)(2,1)S(1)} %get-tuple-element.76), channel_id=1, source_target_pairs={{0,2},{1,3},{2,4},{3,5},{4,6},{5,7},{6,8},{7,9},{8,10},{9,11},{10,... | collective-permute-start | bytes 786440 | tf_op jit(solution)/shard_map/ppermute | solution.py:15
  128.1 10.4 %collective-permute-start.17 = (bf16[2,256,256]{2,1,0:T(8,128)(2,1)S(1)}, bf16[2,256,256]{2,1,0:T(8,128)(2,1)S(1)}, u32[]{:S(2)}, u32[]{:S(2)}) collective-permute-start(bf16[2,256,256]{2,1,0:T(8,128)(2,1)S(1)} %get-tuple-element.75), channel_id=1, source_target_pairs={{2,0},{3,1},{4,2},{5,3},{6,4},{7,5},{8,6},{9,7},{10,8},{11,9},{12,... | collective-permute-start | bytes 786440 | tf_op jit(solution)/shard_map/ppermute | solution.py:15
  139.7 10.7 %collective-permute-start.22 = (bf16[2,128,256]{2,1,0:T(8,128)(2,1)S(1)}, bf16[2,128,256]{2,1,0:T(8,128)(2,1)S(1)}, u32[]{:S(2)}, u32[]{:S(2)}) collective-permute-start(bf16[2,128,256]{2,1,0:T(8,128)(2,1)S(1)} %get-tuple-element.69), channel_id=1, source_target_pairs={{0,1},{1,2},{2,3},{3,4},{4,5},{5,6},{6,7},{7,8},{8,9},{9,10},{10,1... | collective-permute-start | bytes 393224 | tf_op jit(solution)/shard_map/ppermute | solution.py:15
  141.6 8.8 %collective-permute-start.23 = (bf16[2,128,256]{2,1,0:T(8,128)(2,1)S(1)}, bf16[2,128,256]{2,1,0:T(8,128)(2,1)S(1)}, u32[]{:S(2)}, u32[]{:S(2)}) collective-permute-start(bf16[2,128,256]{2,1,0:T(8,128)(2,1)S(1)} %get-tuple-element.70), channel_id=1, source_target_pairs={{1,0},{2,1},{3,2},{4,3},{5,4},{6,5},{7,6},{8,7},{9,8},{10,9},{11,1... | collective-permute-start | bytes 393224 | tf_op jit(solution)/shard_map/ppermute | solution.py:15
  146.3 8.9 %collective-permute-start.27 = (bf16[2,256,256]{2,1,0:T(8,128)(2,1)S(1)}, bf16[2,256,256]{2,1,0:T(8,128)(2,1)S(1)}, u32[]{:S(2)}, u32[]{:S(2)}) collective-permute-start(bf16[2,256,256]{2,1,0:T(8,128)(2,1)S(1)} %get-tuple-element.3), channel_id=1, source_target_pairs={{32,0},{64,32},{96,64},{33,1},{65,33},{97,65},{34,2},{66,34},{98,6... | collective-permute-start | bytes 786440 | tf_op jit(solution)/shard_map/ppermute | solution.py:15
  151.4 11.0 %collective-permute-start.24 = (bf16[2,256,256]{2,1,0:T(8,128)(2,1)S(1)}, bf16[2,256,256]{2,1,0:T(8,128)(2,1)S(1)}, u32[]{:S(2)}, u32[]{:S(2)}) collective-permute-start(bf16[2,256,256]{2,1,0:T(8,128)(2,1)S(1)} %pad_maximum_fusion.26), channel_id=1, source_target_pairs={{32,0},{64,32},{96,64},{33,1},{65,33},{97,65},{34,2},{66,34},{98,6... | collective-permute-start | bytes 786440 | tf_op jit(solution)/shard_map/ppermute | solution.py:15
  156.1 18.2 %copy-start.6 = (f32[2,256,768]{2,1,0:T(8,128)}, f32[2,256,768]{2,1,0:T(8,128)S(1)}, u32[]{:S(2)}) copy-start(f32[2,256,768]{2,1,0:T(8,128)S(1)} %get-tuple-element.180) | copy-start | bytes 4718596
  156.2 18.1 %collective-permute-start.29 = (bf16[2,256,256]{2,1,0:T(8,128)(2,1)S(1)}, bf16[2,256,256]{2,1,0:T(8,128)(2,1)S(1)}, u32[]{:S(2)}, u32[]{:S(2)}) collective-permute-start(bf16[2,256,256]{2,1,0:T(8,128)(2,1)S(1)} %get-tuple-element.66), channel_id=1, source_target_pairs={{0,2},{1,3},{2,4},{3,5},{4,6},{5,7},{6,8},{7,9},{8,10},{9,11},{10,... | collective-permute-start | bytes 786440 | tf_op jit(solution)/shard_map/ppermute | solution.py:15
  160.5 13.8 %collective-permute-start.28 = (bf16[2,256,256]{2,1,0:T(8,128)(2,1)S(1)}, bf16[2,256,256]{2,1,0:T(8,128)(2,1)S(1)}, u32[]{:S(2)}, u32[]{:S(2)}) collective-permute-start(bf16[2,256,256]{2,1,0:T(8,128)(2,1)S(1)} %get-tuple-element.65), channel_id=1, source_target_pairs={{2,0},{3,1},{4,2},{5,3},{6,4},{7,5},{8,6},{9,7},{10,8},{11,9},{12,... | collective-permute-start | bytes 786440 | tf_op jit(solution)/shard_map/ppermute | solution.py:15
  163.5 12.1 %collective-permute-start.26 = (bf16[2,256,256]{2,1,0:T(8,128)(2,1)S(1)}, bf16[2,256,256]{2,1,0:T(8,128)(2,1)S(1)}, u32[]{:S(2)}, u32[]{:S(2)}) collective-permute-start(bf16[2,256,256]{2,1,0:T(8,128)(2,1)S(1)} %get-tuple-element.68), channel_id=1, source_target_pairs={{0,2},{1,3},{2,4},{3,5},{4,6},{5,7},{6,8},{7,9},{8,10},{9,11},{10,... | collective-permute-start | bytes 786440 | tf_op jit(solution)/shard_map/ppermute | solution.py:15
  169.5 10.4 %collective-permute-start.25 = (bf16[2,256,256]{2,1,0:T(8,128)(2,1)S(1)}, bf16[2,256,256]{2,1,0:T(8,128)(2,1)S(1)}, u32[]{:S(2)}, u32[]{:S(2)}) collective-permute-start(bf16[2,256,256]{2,1,0:T(8,128)(2,1)S(1)} %get-tuple-element.67), channel_id=1, source_target_pairs={{2,0},{3,1},{4,2},{5,3},{6,4},{7,5},{8,6},{9,7},{10,8},{11,9},{12,... | collective-permute-start | bytes 786440 | tf_op jit(solution)/shard_map/ppermute | solution.py:15
  174.3 6.5 %copy-start.22 = (bf16[2,256,256]{2,1,0:T(8,128)(2,1)}, bf16[2,256,256]{2,1,0:T(8,128)(2,1)S(1)}, u32[]{:S(2)}) copy-start(bf16[2,256,256]{2,1,0:T(8,128)(2,1)S(1)} %collective-permute-done.29) | copy-start | bytes 786436
  174.3 6.5 %copy-start.24 = (bf16[2,256,256]{2,1,0:T(8,128)(2,1)}, bf16[2,256,256]{2,1,0:T(8,128)(2,1)S(1)}, u32[]{:S(2)}) copy-start(bf16[2,256,256]{2,1,0:T(8,128)(2,1)S(1)} %collective-permute-done.28) | copy-start | bytes 786436
  181.8 2.1 copy-start.14
  183.9 3.9 %copy-start.11 = (f32[768,512]{1,0:T(8,128)S(1)}, f32[768,512]{1,0:T(8,128)}, u32[]{:S(2)}) copy-start(f32[768,512]{1,0:T(8,128)} %bitcast_add_fusion) | copy-start | bytes 4718596
  188.3 1.9 copy-start
  190.2 1.1 copy-start.15
  191.3 2.8 %collective-permute-start.32 = (bf16[2,2,2,2,56,512]{5,4,3,2,1,0:T(8,128)(2,1)}, bf16[2,2,2,2,56,512]{5,4,3,2,1,0:T(8,128)(2,1)}, u32[]{:S(2)}, u32[]{:S(2)}) collective-permute-start(bf16[2,2,2,2,56,512]{5,4,3,2,1,0:T(8,128)(2,1)} %fusion.78), channel_id=1, source_target_pairs={{0,1},{1,0},{2,3},{3,2},{4,5},{5,4},{6,7},{7,6},{8,9},{9,8},{10,11... | collective-permute-start | bytes 2752520 | tf_op jit(solution)/shard_map/ppermute | solution.py:199
  191.3 2.8 %copy-start.1 = (f32[2,2,2,2,2,56,512]{6,5,4,3,2,1,0:T(8,128)S(1)}, f32[2,2,2,2,2,56,512]{6,5,4,3,2,1,0:T(8,128)}, u32[]{:S(2)}) copy-start(f32[2,2,2,2,2,56,512]{6,5,4,3,2,1,0:T(8,128)} %copy-done) | copy-start | bytes 11010052
  195.9 13.5 %collective-permute-start.33 = (bf16[2,2,2,56,512]{4,3,2,1,0:T(8,128)(2,1)S(1)}, bf16[2,2,2,56,512]{4,3,2,1,0:T(8,128)(2,1)S(1)}, u32[]{:S(2)}, u32[]{:S(2)}) collective-permute-start(bf16[2,2,2,56,512]{4,3,2,1,0:T(8,128)(2,1)S(1)} %fusion.189), channel_id=1, source_target_pairs={{0,2},{1,3},{2,0},{3,1},{4,6},{5,7},{6,4},{7,5},{8,10},{9,11},{10,... | collective-permute-start | bytes 1376264 | tf_op jit(solution)/shard_map/ppermute | solution.py:199
  196.7 20.3 %collective-permute-start.30 = (bf16[2,128,256]{2,1,0:T(8,128)(2,1)S(1)}, bf16[2,128,256]{2,1,0:T(8,128)(2,1)S(1)}, u32[]{:S(2)}, u32[]{:S(2)}) collective-permute-start(bf16[2,128,256]{2,1,0:T(8,128)(2,1)S(1)} %get-tuple-element.59), channel_id=1, source_target_pairs={{0,1},{1,2},{2,3},{3,4},{4,5},{5,6},{6,7},{7,8},{8,9},{9,10},{10,1... | collective-permute-start | bytes 393224 | tf_op jit(solution)/shard_map/ppermute | solution.py:15
  198.7 13.7 %copy-start.23 = (bf16[2,256,256]{2,1,0:T(8,128)(2,1)S(1)}, bf16[2,256,256]{2,1,0:T(8,128)(2,1)}, u32[]{:S(2)}) copy-start(bf16[2,256,256]{2,1,0:T(8,128)(2,1)} %copy-done.22) | copy-start | bytes 786436
  198.8 13.7 %copy-start.25 = (bf16[2,256,256]{2,1,0:T(8,128)(2,1)S(1)}, bf16[2,256,256]{2,1,0:T(8,128)(2,1)}, u32[]{:S(2)}) copy-start(bf16[2,256,256]{2,1,0:T(8,128)(2,1)} %copy-done.24) | copy-start | bytes 786436
  198.8 18.3 %collective-permute-start.31 = (bf16[2,128,256]{2,1,0:T(8,128)(2,1)S(1)}, bf16[2,128,256]{2,1,0:T(8,128)(2,1)S(1)}, u32[]{:S(2)}, u32[]{:S(2)}) collective-permute-start(bf16[2,128,256]{2,1,0:T(8,128)(2,1)S(1)} %get-tuple-element.60), channel_id=1, source_target_pairs={{1,0},{2,1},{3,2},{4,3},{5,4},{6,5},{7,6},{8,7},{9,8},{10,9},{11,1... | collective-permute-start | bytes 393224 | tf_op jit(solution)/shard_map/ppermute | solution.py:15
  209.7 7.0 %collective-permute-start.34 = (bf16[2,2,56,512]{3,2,1,0:T(8,128)(2,1)S(1)}, bf16[2,2,56,512]{3,2,1,0:T(8,128)(2,1)S(1)}, u32[]{:S(2)}, u32[]{:S(2)}) collective-permute-start(bf16[2,2,56,512]{3,2,1,0:T(8,128)(2,1)S(1)} %fusion.246), channel_id=1, source_target_pairs={{0,8},{1,9},{2,10},{3,11},{4,12},{5,13},{6,14},{7,15},{8,0},{9,1},... | collective-permute-start | bytes 688136 | tf_op jit(solution)/shard_map/ppermute | solution.py:199
  212.5 4.6 %copy-start.10 = (f32[2,256,256]{2,1,0:T(8,128)S(1)}, f32[2,256,256]{2,1,0:T(8,128)}, u32[]{:S(2)}) copy-start(f32[2,256,256]{2,1,0:T(8,128)} %get-tuple-element.6) | copy-start | bytes 1572868
  216.8 11.1 %copy-start.8 = (f32[2,256,256]{2,1,0:T(8,128)S(1)}, f32[2,256,256]{2,1,0:T(8,128)}, u32[]{:S(2)}) copy-start(f32[2,256,256]{2,1,0:T(8,128)} %get-tuple-element.10) | copy-start | bytes 1572868
  216.8 11.1 %copy-start.9 = (f32[2,256,256]{2,1,0:T(8,128)S(1)}, f32[2,256,256]{2,1,0:T(8,128)}, u32[]{:S(2)}) copy-start(f32[2,256,256]{2,1,0:T(8,128)} %get-tuple-element.4) | copy-start | bytes 1572868
  216.8 11.1 %copy-start.16 = (f32[1,2,128,256]{3,2,1,0:T(8,128)S(1)}, f32[1,2,128,256]{3,2,1,0:T(8,128)}, u32[]{:S(2)}) copy-start(f32[1,2,128,256]{3,2,1,0:T(8,128)} %get-tuple-element.18) | copy-start | bytes 786436
  216.9 11.1 %copy-start.17 = (f32[1,2,128,256]{3,2,1,0:T(8,128)S(1)}, f32[1,2,128,256]{3,2,1,0:T(8,128)}, u32[]{:S(2)}) copy-start(f32[1,2,128,256]{3,2,1,0:T(8,128)} %get-tuple-element.21) | copy-start | bytes 786436
  216.9 11.0 %copy-start.18 = (f32[1,2,128,256]{3,2,1,0:T(8,128)S(1)}, f32[1,2,128,256]{3,2,1,0:T(8,128)}, u32[]{:S(2)}) copy-start(f32[1,2,128,256]{3,2,1,0:T(8,128)} %get-tuple-element.32) | copy-start | bytes 786436
  216.9 11.0 %copy-start.19 = (f32[1,2,128,256]{3,2,1,0:T(8,128)S(1)}, f32[1,2,128,256]{3,2,1,0:T(8,128)}, u32[]{:S(2)}) copy-start(f32[1,2,128,256]{3,2,1,0:T(8,128)} %get-tuple-element.39) | copy-start | bytes 786436
  216.9 11.0 %copy-start.20 = (f32[1,2,128,256]{3,2,1,0:T(8,128)S(1)}, f32[1,2,128,256]{3,2,1,0:T(8,128)}, u32[]{:S(2)}) copy-start(f32[1,2,128,256]{3,2,1,0:T(8,128)} %get-tuple-element.28) | copy-start | bytes 786436
  216.9 11.0 %copy-start.21 = (f32[1,2,128,256]{3,2,1,0:T(8,128)S(1)}, f32[1,2,128,256]{3,2,1,0:T(8,128)}, u32[]{:S(2)}) copy-start(f32[1,2,128,256]{3,2,1,0:T(8,128)} %get-tuple-element.37) | copy-start | bytes 786436
  216.9 6.4 %collective-permute-start.35 = (bf16[2,56,512]{2,1,0:T(8,128)(2,1)S(1)}, bf16[2,56,512]{2,1,0:T(8,128)(2,1)S(1)}, u32[]{:S(2)}, u32[]{:S(2)}) collective-permute-start(bf16[2,56,512]{2,1,0:T(8,128)(2,1)S(1)} %fusion.278), channel_id=1, source_target_pairs={{0,4},{1,5},{2,6},{3,7},{4,0},{5,1},{6,2},{7,3},{8,12},{9,13},{10,... | collective-permute-start | bytes 344072 | tf_op jit(solution)/shard_map/ppermute | solution.py:199
  223.4 6.7 %collective-permute-start.36 = (bf16[56,512]{1,0:T(8,128)(2,1)S(1)}, bf16[56,512]{1,0:T(8,128)(2,1)S(1)}, u32[]{:S(2)}, u32[]{:S(2)}) collective-permute-start(bf16[56,512]{1,0:T(8,128)(2,1)S(1)} %fusion.279), channel_id=1, source_target_pairs={{0,16},{1,17},{2,18},{3,19},{4,20},{5,21},{6,22},{7,23},{8,24},{9,... | collective-permute-start | bytes 172040 | tf_op jit(solution)/shard_map/ppermute | solution.py:199
  (1 other events, 1.0 us)

commit v10 on v8

--- a/solution.py
+++ b/solution.py
@@ -266,7 +266,7 @@
     out_all = jnp.concatenate(
         [acc.reshape(seq_count, out_rows, channels) for acc in out_acc], axis=1
     ).reshape(seq_count, depth * out_rows * channels // (2 * channels), 2 * channels)
-    (mine,) = halving_scatter([jnp.concatenate([conv_all, out_all], axis=1)], (0, 1, 3, 2, 4))
+    (mine,) = halving_scatter([jnp.concatenate([conv_all, out_all], axis=1)], (0, 3, 1, 2, 4))
     conv_grads = mine[: depth * conv_rows].reshape(1, depth, conv_rows, 2 * channels) * grad_scale
     out_grads = mine[depth * conv_rows :].reshape(1, depth, out_rows, channels) * grad_scale
     return (input_grads[None], conv_grads, out_grads)

time: 231 us -> 232 us (level)
  transfers between devices with their start and end apart: 37 -> 37, of which waited for: 15 -> 15; matrix products, arithmetic and copies ran while one was open for 17% -> 16% of each run, Pallas kernels for 0% -> 0%
where the time goes in v10:
time: 232 us; the launch traced here: 231 us
  starting transfers between devices  97.7 us (42%)
  waiting for transfers between devices  70.9 us (31%)
  matrix products  38.9 us (17%)
  other arithmetic  15.1 us (7%)
  local copies, waits for them, and re-layouts  5.88 us (3%)
    ppermute x32, starting transfers between devices, shifted(): lax.ppermute(value, axis, [(source, source + steps) for source in range(l...  92.4 us
    ppermute x32, waiting for transfers between devices, shifted(): lax.ppermute(value, axis, [(source, source + steps) for source in range(l...  50.5 us
    ppermute x5, waiting for transfers between devices, halving_scatter(): got = lax.ppermute(sends, 'seq', pairs)  20.4 us
    dot_general x3, matrix products, backward_near_pieces(): jnp.einsum('mpc,mpd->cd', taps, grad_pre, preferred_element_type=f32)  8.24 us
    dot_general x7, matrix products, mm(): return jnp.einsum('mpc,cd->mpd', a, b, preferred_element_type=jnp.float32)  5.75 us
    ppermute x5, starting transfers between devices, halving_scatter(): got = lax.ppermute(sends, 'seq', pairs)  5.34 us
  transfers between devices with their start and end apart: 37, of which 15 were waited for; matrix products, arithmetic and copies ran while one was open for 16% of the time, Pallas kernels for 0%

profile of v10, /device:TPU:24, one launch (start us, length us, event | category | flops | bytes accessed | tf_op | source)
XLA Modules:
  0.0 230.7 jit_solution(13257912027727330829)
XLA Ops:
  0.6 1.0 fusion.352
  1.7 1.9 collective-permute-start
  3.6 3.6 %collective-permute-start.1 = (bf16[2,128,256]{2,1,0:T(8,128)(2,1)S(1)}, bf16[2,128,256]{2,1,0:T(8,128)(2,1)S(1)}, u32[]{:S(2)}, u32[]{:S(2)}) collective-permute-start(bf16[2,128,256]{2,1,0:T(8,128)(2,1)S(1)} %get-tuple-element.130), channel_id=1, source_target_pairs={{1,0},{2,1},{3,2},{4,3},{5,4},{6,5},{7,6},{8,7},{9,8},{10,9},{11,1... | collective-permute-start | bytes 393224 | tf_op jit(solution)/shard_map/ppermute | solution.py:15
  7.3 1.6 fusion.215
  9.0 1.8 fusion.106
  12.7 5.6 %collective-permute-start.2 = (bf16[2,512,256]{2,1,0:T(8,128)(2,1)S(1)}, bf16[2,512,256]{2,1,0:T(8,128)(2,1)S(1)}, u32[]{:S(2)}, u32[]{:S(2)}) collective-permute-start(bf16[2,512,256]{2,1,0:T(8,128)(2,1)S(1)} %fusion.2), channel_id=1, source_target_pairs={{0,2},{1,3},{2,4},{3,5},{4,6},{5,7},{6,8},{7,9},{8,10},{9,11},{10,... | collective-permute-start | bytes 1572872 | tf_op jit(solution)/shard_map/ppermute | solution.py:15
  18.4 1.9 collective-permute-start.3
  20.8 8.2 %collective-permute-done.2 = bf16[2,512,256]{2,1,0:T(8,128)(2,1)S(1)} collective-permute-done((bf16[2,512,256]{2,1,0:T(8,128)(2,1)S(1)}, bf16[2,512,256]{2,1,0:T(8,128)(2,1)S(1)}, u32[]{:S(2)}, u32[]{:S(2)}) %collective-permute-start.2) | collective-permute-done | bytes 524320 | tf_op jit(solution)/shard_map/ppermute | solution.py:15
  29.6 5.8 %collective-permute-done.3 = bf16[2,512,256]{2,1,0:T(8,128)(2,1)S(1)} collective-permute-done((bf16[2,512,256]{2,1,0:T(8,128)(2,1)S(1)}, bf16[2,512,256]{2,1,0:T(8,128)(2,1)S(1)}, u32[]{:S(2)}, u32[]{:S(2)}) %collective-permute-start.3) | collective-permute-done | bytes 524320 | tf_op jit(solution)/shard_map/ppermute | solution.py:15
  37.8 1.9 collective-permute-start.5
  39.7 3.9 %collective-permute-start.4 = (bf16[2,512,256]{2,1,0:T(8,128)(2,1)S(1)}, bf16[2,512,256]{2,1,0:T(8,128)(2,1)S(1)}, u32[]{:S(2)}, u32[]{:S(2)}) collective-permute-start(bf16[2,512,256]{2,1,0:T(8,128)(2,1)S(1)} %get-tuple-element.50), channel_id=1, source_target_pairs={{2,0},{3,1},{4,2},{5,3},{6,4},{7,5},{8,6},{9,7},{10,8},{11,9},{12,... | collective-permute-start | bytes 1572872 | tf_op jit(solution)/shard_map/ppermute | solution.py:15
  45.1 6.7 %collective-permute-done.5 = bf16[2,512,256]{2,1,0:T(8,128)(2,1)S(1)} collective-permute-done((bf16[2,512,256]{2,1,0:T(8,128)(2,1)S(1)}, bf16[2,512,256]{2,1,0:T(8,128)(2,1)S(1)}, u32[]{:S(2)}, u32[]{:S(2)}) %collective-permute-start.5) | collective-permute-done | bytes 524320 | tf_op jit(solution)/shard_map/ppermute | solution.py:15
  51.8 4.0 %collective-permute-done.4 = bf16[2,512,256]{2,1,0:T(8,128)(2,1)S(1)} collective-permute-done((bf16[2,512,256]{2,1,0:T(8,128)(2,1)S(1)}, bf16[2,512,256]{2,1,0:T(8,128)(2,1)S(1)}, u32[]{:S(2)}, u32[]{:S(2)}) %collective-permute-start.4) | collective-permute-done | bytes 524320 | tf_op jit(solution)/shard_map/ppermute | solution.py:15
  57.8 2.1 collective-permute-start.6
  59.9 3.6 %collective-permute-start.7 = (bf16[2,128,256]{2,1,0:T(8,128)(2,1)S(1)}, bf16[2,128,256]{2,1,0:T(8,128)(2,1)S(1)}, u32[]{:S(2)}, u32[]{:S(2)}) collective-permute-start(bf16[2,128,256]{2,1,0:T(8,128)(2,1)S(1)} %get-tuple-element.49), channel_id=1, source_target_pairs={{1,0},{2,1},{3,2},{4,3},{5,4},{6,5},{7,6},{8,7},{9,8},{10,9},{11,1... | collective-permute-start | bytes 393224 | tf_op jit(solution)/shard_map/ppermute | solution.py:15
  64.5 1.3 collective-permute-start.11
  65.8 2.2 fusion.75
  69.1 1.3 collective-permute-start.8
  70.4 3.8 %collective-permute-done.11 = bf16[2,256,256]{2,1,0:T(8,128)(2,1)S(1)} collective-permute-done((bf16[2,256,256]{2,1,0:T(8,128)(2,1)S(1)}, bf16[2,256,256]{2,1,0:T(8,128)(2,1)S(1)}, u32[]{:S(2)}, u32[]{:S(2)}) %collective-permute-start.11) | collective-permute-done | bytes 262176 | tf_op jit(solution)/shard_map/ppermute | solution.py:15
  75.1 4.3 %collective-permute-start.13 = (bf16[2,256,256]{2,1,0:T(8,128)(2,1)S(1)}, bf16[2,256,256]{2,1,0:T(8,128)(2,1)S(1)}, u32[]{:S(2)}, u32[]{:S(2)}) collective-permute-start(bf16[2,256,256]{2,1,0:T(8,128)(2,1)S(1)} %get-tuple-element.91), channel_id=1, source_target_pairs={{0,2},{1,3},{2,4},{3,5},{4,6},{5,7},{6,8},{7,9},{8,10},{9,11},{10,... | collective-permute-start | bytes 786440 | tf_op jit(solution)/shard_map/ppermute | solution.py:15
  79.4 2.1 collective-permute-start.12
  82.5 6.0 %collective-permute-start.10 = (bf16[2,256,256]{2,1,0:T(8,128)(2,1)S(1)}, bf16[2,256,256]{2,1,0:T(8,128)(2,1)S(1)}, u32[]{:S(2)}, u32[]{:S(2)}) collective-permute-start(bf16[2,256,256]{2,1,0:T(8,128)(2,1)S(1)} %get-tuple-element.89), channel_id=1, source_target_pairs={{0,2},{1,3},{2,4},{3,5},{4,6},{5,7},{6,8},{7,9},{8,10},{9,11},{10,... | collective-permute-start | bytes 786440 | tf_op jit(solution)/shard_map/ppermute | solution.py:15
  88.5 1.9 collective-permute-start.9
  92.7 6.2 %collective-permute-done.9 = bf16[2,256,256]{2,1,0:T(8,128)(2,1)S(1)} collective-permute-done((bf16[2,256,256]{2,1,0:T(8,128)(2,1)S(1)}, bf16[2,256,256]{2,1,0:T(8,128)(2,1)S(1)}, u32[]{:S(2)}, u32[]{:S(2)}) %collective-permute-start.9) | collective-permute-done | bytes 262176 | tf_op jit(solution)/shard_map/ppermute | solution.py:15
  100.1 1.9 collective-permute-start.14
  102.0 3.6 %collective-permute-start.15 = (bf16[2,128,256]{2,1,0:T(8,128)(2,1)S(1)}, bf16[2,128,256]{2,1,0:T(8,128)(2,1)S(1)}, u32[]{:S(2)}, u32[]{:S(2)}) collective-permute-start(bf16[2,128,256]{2,1,0:T(8,128)(2,1)S(1)} %get-tuple-element.83), channel_id=1, source_target_pairs={{1,0},{2,1},{3,2},{4,3},{5,4},{6,5},{7,6},{8,7},{9,8},{10,9},{11,1... | collective-permute-start | bytes 393224 | tf_op jit(solution)/shard_map/ppermute | solution.py:15
  105.7 1.1 fusion.328
  106.8 1.3 collective-permute-start.19
  108.0 2.2 fusion.21
  111.5 1.3 collective-permute-start.16
  112.8 2.9 %collective-permute-done.19 = bf16[2,256,256]{2,1,0:T(8,128)(2,1)S(1)} collective-permute-done((bf16[2,256,256]{2,1,0:T(8,128)(2,1)S(1)}, bf16[2,256,256]{2,1,0:T(8,128)(2,1)S(1)}, u32[]{:S(2)}, u32[]{:S(2)}) %collective-permute-start.19) | collective-permute-done | bytes 262176 | tf_op jit(solution)/shard_map/ppermute | solution.py:15
  116.7 4.6 %collective-permute-start.21 = (bf16[2,256,256]{2,1,0:T(8,128)(2,1)S(1)}, bf16[2,256,256]{2,1,0:T(8,128)(2,1)S(1)}, u32[]{:S(2)}, u32[]{:S(2)}) collective-permute-start(bf16[2,256,256]{2,1,0:T(8,128)(2,1)S(1)} %get-tuple-element.81), channel_id=1, source_target_pairs={{0,2},{1,3},{2,4},{3,5},{4,6},{5,7},{6,8},{7,9},{8,10},{9,11},{10,... | collective-permute-start | bytes 786440 | tf_op jit(solution)/shard_map/ppermute | solution.py:15
  121.2 1.9 collective-permute-start.20
  124.1 6.0 %collective-permute-start.18 = (bf16[2,256,256]{2,1,0:T(8,128)(2,1)S(1)}, bf16[2,256,256]{2,1,0:T(8,128)(2,1)S(1)}, u32[]{:S(2)}, u32[]{:S(2)}) collective-permute-start(bf16[2,256,256]{2,1,0:T(8,128)(2,1)S(1)} %get-tuple-element.79), channel_id=1, source_target_pairs={{0,2},{1,3},{2,4},{3,5},{4,6},{5,7},{6,8},{7,9},{8,10},{9,11},{10,... | collective-permute-start | bytes 786440 | tf_op jit(solution)/shard_map/ppermute | solution.py:15
  130.2 1.9 collective-permute-start.17
  134.7 5.9 %collective-permute-done.17 = bf16[2,256,256]{2,1,0:T(8,128)(2,1)S(1)} collective-permute-done((bf16[2,256,256]{2,1,0:T(8,128)(2,1)S(1)}, bf16[2,256,256]{2,1,0:T(8,128)(2,1)S(1)}, u32[]{:S(2)}, u32[]{:S(2)}) %collective-permute-start.17) | collective-permute-done | bytes 262176 | tf_op jit(solution)/shard_map/ppermute | solution.py:15
  141.7 1.9 collective-permute-start.22
  143.7 3.6 %collective-permute-start.23 = (bf16[2,128,256]{2,1,0:T(8,128)(2,1)S(1)}, bf16[2,128,256]{2,1,0:T(8,128)(2,1)S(1)}, u32[]{:S(2)}, u32[]{:S(2)}) collective-permute-start(bf16[2,128,256]{2,1,0:T(8,128)(2,1)S(1)} %get-tuple-element.73), channel_id=1, source_target_pairs={{1,0},{2,1},{3,2},{4,3},{5,4},{6,5},{7,6},{8,7},{9,8},{10,9},{11,1... | collective-permute-start | bytes 393224 | tf_op jit(solution)/shard_map/ppermute | solution.py:15
  147.3 1.0 fusion.322
  148.4 1.5 collective-permute-start.27
  149.9 2.3 fusion.29
  153.4 1.3 collective-permute-start.24
  154.7 2.5 %collective-permute-done.27 = bf16[2,256,256]{2,1,0:T(8,128)(2,1)S(1)} collective-permute-done((bf16[2,256,256]{2,1,0:T(8,128)(2,1)S(1)}, bf16[2,256,256]{2,1,0:T(8,128)(2,1)S(1)}, u32[]{:S(2)}, u32[]{:S(2)}) %collective-permute-start.27) | collective-permute-done | bytes 262176 | tf_op jit(solution)/shard_map/ppermute | solution.py:15
  158.2 4.3 %collective-permute-start.29 = (bf16[2,256,256]{2,1,0:T(8,128)(2,1)S(1)}, bf16[2,256,256]{2,1,0:T(8,128)(2,1)S(1)}, u32[]{:S(2)}, u32[]{:S(2)}) collective-permute-start(bf16[2,256,256]{2,1,0:T(8,128)(2,1)S(1)} %get-tuple-element.69), channel_id=1, source_target_pairs={{0,2},{1,3},{2,4},{3,5},{4,6},{5,7},{6,8},{7,9},{8,10},{9,11},{10,... | collective-permute-start | bytes 786440 | tf_op jit(solution)/shard_map/ppermute | solution.py:15
  162.5 1.9 collective-permute-start.28
  165.5 6.0 %collective-permute-start.26 = (bf16[2,256,256]{2,1,0:T(8,128)(2,1)S(1)}, bf16[2,256,256]{2,1,0:T(8,128)(2,1)S(1)}, u32[]{:S(2)}, u32[]{:S(2)}) collective-permute-start(bf16[2,256,256]{2,1,0:T(8,128)(2,1)S(1)} %get-tuple-element.71), channel_id=1, source_target_pairs={{0,2},{1,3},{2,4},{3,5},{4,6},{5,7},{6,8},{7,9},{8,10},{9,11},{10,... | collective-permute-start | bytes 786440 | tf_op jit(solution)/shard_map/ppermute | solution.py:15
  171.6 1.9 collective-permute-start.25
  173.5 2.2 bitcast_add_fusion
  176.5 1.1 multiply_convert_fusion.5
  177.6 4.3 %collective-permute-done.25 = bf16[2,256,256]{2,1,0:T(8,128)(2,1)S(1)} collective-permute-done((bf16[2,256,256]{2,1,0:T(8,128)(2,1)S(1)}, bf16[2,256,256]{2,1,0:T(8,128)(2,1)S(1)}, u32[]{:S(2)}, u32[]{:S(2)}) %collective-permute-start.25) | collective-permute-done | bytes 262176 | tf_op jit(solution)/shard_map/ppermute | solution.py:15
  184.8 3.8 %bitcast_add_fusion.3 = f32[768,512]{1,0:T(8,128)S(1)} fusion(f32[768,512,1]{1,0,2:T(8,128)} %fusion.29, f32[768,512,1]{1,0,2:T(8,128)} %fusion.21, f32[768,512,1]{1,0,2:T(8,128)} %fusion.75, bf16[2,128,512]{1,2,0:T(8,128)(2,1)S(1)} %get-tuple-element.93, bf16[2,256,256]{1,2,0:T(8,128)(2,1)S(1)} %copy-done.19, bf16[2,256,256]{1,2,0:T(8,128)(2,1)S(1)} %copy-done.18, ...), kind=kOutput, calls=%fused_computation.12 | convolution fusion | flops 818544640 | bytes 8912896 | tf_op jit(solution)/shard_map/mpc,mpd->cd/dot_general | solution.py:151
  189.2 1.8 copy-done
  192.0 1.9 collective-permute-done.32
  193.9 1.7 fusion.1
  195.7 1.7 collective-permute-start.33
  198.1 2.1 collective-permute-start.30
  200.2 3.6 %collective-permute-start.31 = (bf16[2,128,256]{2,1,0:T(8,128)(2,1)S(1)}, bf16[2,128,256]{2,1,0:T(8,128)(2,1)S(1)}, u32[]{:S(2)}, u32[]{:S(2)}) collective-permute-start(bf16[2,128,256]{2,1,0:T(8,128)(2,1)S(1)} %get-tuple-element.63), channel_id=1, source_target_pairs={{1,0},{2,1},{3,2},{4,3},{5,4},{6,5},{7,6},{8,7},{9,8},{10,9},{11,1... | collective-permute-start | bytes 393224 | tf_op jit(solution)/shard_map/ppermute | solution.py:15
  203.9 5.9 %collective-permute-done.33 = bf16[2,2,2,56,512]{4,3,2,1,0:T(8,128)(2,1)S(1)} collective-permute-done((bf16[2,2,2,56,512]{4,3,2,1,0:T(8,128)(2,1)S(1)}, bf16[2,2,2,56,512]{4,3,2,1,0:T(8,128)(2,1)S(1)}, u32[]{:S(2)}, u32[]{:S(2)}) %collective-permute-start.33) | collective-permute-done | bytes 458784 | tf_op jit(solution)/shard_map/ppermute | solution.py:199
  210.2 1.3 fusion.87
  211.6 5.4 %collective-permute-done.34 = bf16[2,2,56,512]{3,2,1,0:T(8,128)(2,1)S(1)} collective-permute-done((bf16[2,2,56,512]{3,2,1,0:T(8,128)(2,1)S(1)}, bf16[2,2,56,512]{3,2,1,0:T(8,128)(2,1)S(1)}, u32[]{:S(2)}, u32[]{:S(2)}) %collective-permute-start.34) | collective-permute-done | bytes 229408 | tf_op jit(solution)/shard_map/ppermute | solution.py:199
  217.5 6.1 %collective-permute-done.35 = bf16[2,56,512]{2,1,0:T(8,128)(2,1)S(1)} collective-permute-done((bf16[2,56,512]{2,1,0:T(8,128)(2,1)S(1)}, bf16[2,56,512]{2,1,0:T(8,128)(2,1)S(1)}, u32[]{:S(2)}, u32[]{:S(2)}) %collective-permute-start.35) | collective-permute-done | bytes 114720 | tf_op jit(solution)/shard_map/ppermute | solution.py:199
  223.6 3.4 %collective-permute-start.36 = (bf16[56,512]{1,0:T(8,128)(2,1)S(1)}, bf16[56,512]{1,0:T(8,128)(2,1)S(1)}, u32[]{:S(2)}, u32[]{:S(2)}) collective-permute-start(bf16[56,512]{1,0:T(8,128)(2,1)S(1)} %fusion.258), channel_id=1, source_target_pairs={{0,16},{1,17},{2,18},{3,19},{4,20},{5,21},{6,22},{7,23},{8,24},{9,... | collective-permute-start | bytes 172040 | tf_op jit(solution)/shard_map/ppermute | solution.py:199
  227.1 1.2 fusion.20
  228.3 1.1 collective-permute-done.36
  (192 shorter events, 33.7 us)
Async XLA Ops:
  0.6 8.3 %copy-start.3 = (bf16[1,2,512,256]{3,2,1,0:T(8,128)(2,1)S(1)}, bf16[1,2,512,256]{3,2,1,0:T(8,128)(2,1)}, u32[]{:S(2)}) copy-start(bf16[1,2,512,256]{3,2,1,0:T(8,128)(2,1)} %param.4) | copy-start | bytes 1572868
  1.7 7.3 %collective-permute-start = (bf16[2,128,256]{2,1,0:T(8,128)(2,1)S(1)}, bf16[2,128,256]{2,1,0:T(8,128)(2,1)S(1)}, u32[]{:S(2)}, u32[]{:S(2)}) collective-permute-start(bf16[2,128,256]{2,1,0:T(8,128)(2,1)S(1)} %get-tuple-element.131), channel_id=1, source_target_pairs={{0,1},{1,2},{2,3},{3,4},{4,5},{5,6},{6,7},{7,8},{8,9},{9,10},{10,1... | collective-permute-start | bytes 393224 | tf_op jit(solution)/shard_map/ppermute | solution.py:15
  3.6 7.2 %collective-permute-start.1 = (bf16[2,128,256]{2,1,0:T(8,128)(2,1)S(1)}, bf16[2,128,256]{2,1,0:T(8,128)(2,1)S(1)}, u32[]{:S(2)}, u32[]{:S(2)}) collective-permute-start(bf16[2,128,256]{2,1,0:T(8,128)(2,1)S(1)} %get-tuple-element.130), channel_id=1, source_target_pairs={{1,0},{2,1},{3,2},{4,3},{5,4},{6,5},{7,6},{8,7},{9,8},{10,9},{11,1... | collective-permute-start | bytes 393224 | tf_op jit(solution)/shard_map/ppermute | solution.py:15
  8.9 2.0 copy-start.4
  9.0 140.9 %copy-start.16 = (bf16[2,384,256]{2,1,0:T(8,128)(2,1)}, bf16[2,384,256]{2,1,0:T(8,128)(2,1)S(1)}, u32[]{:S(2)}) copy-start(bf16[2,384,256]{2,1,0:T(8,128)(2,1)S(1)} %get-tuple-element.128) | copy-start | bytes 1179652
  9.0 140.9 %copy-start.17 = (bf16[2,384,256]{2,1,0:T(8,128)(2,1)}, bf16[2,384,256]{2,1,0:T(8,128)(2,1)S(1)}, u32[]{:S(2)}) copy-start(bf16[2,384,256]{2,1,0:T(8,128)(2,1)S(1)} %get-tuple-element.129) | copy-start | bytes 1179652
  9.0 2.8 %copy-start.30 = (bf16[2,128,256]{2,1,0:T(8,128)(2,1)}, bf16[2,128,256]{2,1,0:T(8,128)(2,1)S(1)}, u32[]{:S(2)}) copy-start(bf16[2,128,256]{2,1,0:T(8,128)(2,1)S(1)} %collective-permute-done) | copy-start | bytes 393220
  12.7 16.4 %collective-permute-start.2 = (bf16[2,512,256]{2,1,0:T(8,128)(2,1)S(1)}, bf16[2,512,256]{2,1,0:T(8,128)(2,1)S(1)}, u32[]{:S(2)}, u32[]{:S(2)}) collective-permute-start(bf16[2,512,256]{2,1,0:T(8,128)(2,1)S(1)} %fusion.2), channel_id=1, source_target_pairs={{0,2},{1,3},{2,4},{3,5},{4,6},{5,7},{6,8},{7,9},{8,10},{9,11},{10,... | collective-permute-start | bytes 1572872 | tf_op jit(solution)/shard_map/ppermute | solution.py:15
  18.4 17.0 %collective-permute-start.3 = (bf16[2,512,256]{2,1,0:T(8,128)(2,1)S(1)}, bf16[2,512,256]{2,1,0:T(8,128)(2,1)S(1)}, u32[]{:S(2)}, u32[]{:S(2)}) collective-permute-start(bf16[2,512,256]{2,1,0:T(8,128)(2,1)S(1)} %fusion.2), channel_id=1, source_target_pairs={{2,0},{3,1},{4,2},{5,3},{6,4},{7,5},{8,6},{9,7},{10,8},{11,9},{12,... | collective-permute-start | bytes 1572872 | tf_op jit(solution)/shard_map/ppermute | solution.py:15
  29.6 6.4 %copy-start.10 = (bf16[2,512,256]{2,1,0:T(8,128)(2,1)S(1)}, bf16[2,512,256]{2,1,0:T(8,128)(2,1)}, u32[]{:S(2)}) copy-start(bf16[2,512,256]{2,1,0:T(8,128)(2,1)} %param.5) | copy-start | bytes 1572868
  37.8 14.0 %collective-permute-start.5 = (bf16[2,512,256]{2,1,0:T(8,128)(2,1)S(1)}, bf16[2,512,256]{2,1,0:T(8,128)(2,1)S(1)}, u32[]{:S(2)}, u32[]{:S(2)}) collective-permute-start(bf16[2,512,256]{2,1,0:T(8,128)(2,1)S(1)} %get-tuple-element.51), channel_id=1, source_target_pairs={{0,2},{1,3},{2,4},{3,5},{4,6},{5,7},{6,8},{7,9},{8,10},{9,11},{10,... | collective-permute-start | bytes 1572872 | tf_op jit(solution)/shard_map/ppermute | solution.py:15
  39.7 16.1 %collective-permute-start.4 = (bf16[2,512,256]{2,1,0:T(8,128)(2,1)S(1)}, bf16[2,512,256]{2,1,0:T(8,128)(2,1)S(1)}, u32[]{:S(2)}, u32[]{:S(2)}) collective-permute-start(bf16[2,512,256]{2,1,0:T(8,128)(2,1)S(1)} %get-tuple-element.50), channel_id=1, source_target_pairs={{2,0},{3,1},{4,2},{5,3},{6,4},{7,5},{8,6},{9,7},{10,8},{11,9},{12,... | collective-permute-start | bytes 1572872 | tf_op jit(solution)/shard_map/ppermute | solution.py:15
  57.8 8.0 %copy-start.31 = (bf16[2,128,256]{2,1,0:T(8,128)(2,1)S(1)}, bf16[2,128,256]{2,1,0:T(8,128)(2,1)}, u32[]{:S(2)}) copy-start(bf16[2,128,256]{2,1,0:T(8,128)(2,1)} %copy-done.30) | copy-start | bytes 393220
  57.8 10.2 %collective-permute-start.6 = (bf16[2,128,256]{2,1,0:T(8,128)(2,1)S(1)}, bf16[2,128,256]{2,1,0:T(8,128)(2,1)S(1)}, u32[]{:S(2)}, u32[]{:S(2)}) collective-permute-start(bf16[2,128,256]{2,1,0:T(8,128)(2,1)S(1)} %get-tuple-element.48), channel_id=1, source_target_pairs={{0,1},{1,2},{2,3},{3,4},{4,5},{5,6},{6,7},{7,8},{8,9},{9,10},{10,1... | collective-permute-start | bytes 393224 | tf_op jit(solution)/shard_map/ppermute | solution.py:15
  59.9 8.2 %collective-permute-start.7 = (bf16[2,128,256]{2,1,0:T(8,128)(2,1)S(1)}, bf16[2,128,256]{2,1,0:T(8,128)(2,1)S(1)}, u32[]{:S(2)}, u32[]{:S(2)}) collective-permute-start(bf16[2,128,256]{2,1,0:T(8,128)(2,1)S(1)} %get-tuple-element.49), channel_id=1, source_target_pairs={{1,0},{2,1},{3,2},{4,3},{5,4},{6,5},{7,6},{8,7},{9,8},{10,9},{11,1... | collective-permute-start | bytes 393224 | tf_op jit(solution)/shard_map/ppermute | solution.py:15
  64.5 9.7 %collective-permute-start.11 = (bf16[2,256,256]{2,1,0:T(8,128)(2,1)S(1)}, bf16[2,256,256]{2,1,0:T(8,128)(2,1)S(1)}, u32[]{:S(2)}, u32[]{:S(2)}) collective-permute-start(bf16[2,256,256]{2,1,0:T(8,128)(2,1)S(1)} %get-tuple-element.27), channel_id=1, source_target_pairs={{32,0},{64,32},{96,64},{33,1},{65,33},{97,65},{34,2},{66,34},{98,6... | collective-permute-start | bytes 786440 | tf_op jit(solution)/shard_map/ppermute | solution.py:15
  69.1 12.5 %collective-permute-start.8 = (bf16[2,256,256]{2,1,0:T(8,128)(2,1)S(1)}, bf16[2,256,256]{2,1,0:T(8,128)(2,1)S(1)}, u32[]{:S(2)}, u32[]{:S(2)}) collective-permute-start(bf16[2,256,256]{2,1,0:T(8,128)(2,1)S(1)} %pad_maximum_fusion.25), channel_id=1, source_target_pairs={{32,0},{64,32},{96,64},{33,1},{65,33},{97,65},{34,2},{66,34},{98,6... | collective-permute-start | bytes 786440 | tf_op jit(solution)/shard_map/ppermute | solution.py:15
  75.1 16.6 %collective-permute-start.13 = (bf16[2,256,256]{2,1,0:T(8,128)(2,1)S(1)}, bf16[2,256,256]{2,1,0:T(8,128)(2,1)S(1)}, u32[]{:S(2)}, u32[]{:S(2)}) collective-permute-start(bf16[2,256,256]{2,1,0:T(8,128)(2,1)S(1)} %get-tuple-element.91), channel_id=1, source_target_pairs={{0,2},{1,3},{2,4},{3,5},{4,6},{5,7},{6,8},{7,9},{8,10},{9,11},{10,... | collective-permute-start | bytes 786440 | tf_op jit(solution)/shard_map/ppermute | solution.py:15
  79.4 12.2 %collective-permute-start.12 = (bf16[2,256,256]{2,1,0:T(8,128)(2,1)S(1)}, bf16[2,256,256]{2,1,0:T(8,128)(2,1)S(1)}, u32[]{:S(2)}, u32[]{:S(2)}) collective-permute-start(bf16[2,256,256]{2,1,0:T(8,128)(2,1)S(1)} %get-tuple-element.90), channel_id=1, source_target_pairs={{2,0},{3,1},{4,2},{5,3},{6,4},{7,5},{8,6},{9,7},{10,8},{11,9},{12,... | collective-permute-start | bytes 786440 | tf_op jit(solution)/shard_map/ppermute | solution.py:15
  82.5 10.2 %collective-permute-start.10 = (bf16[2,256,256]{2,1,0:T(8,128)(2,1)S(1)}, bf16[2,256,256]{2,1,0:T(8,128)(2,1)S(1)}, u32[]{:S(2)}, u32[]{:S(2)}) collective-permute-start(bf16[2,256,256]{2,1,0:T(8,128)(2,1)S(1)} %get-tuple-element.89), channel_id=1, source_target_pairs={{0,2},{1,3},{2,4},{3,5},{4,6},{5,7},{6,8},{7,9},{8,10},{9,11},{10,... | collective-permute-start | bytes 786440 | tf_op jit(solution)/shard_map/ppermute | solution.py:15
  88.5 10.4 %collective-permute-start.9 = (bf16[2,256,256]{2,1,0:T(8,128)(2,1)S(1)}, bf16[2,256,256]{2,1,0:T(8,128)(2,1)S(1)}, u32[]{:S(2)}, u32[]{:S(2)}) collective-permute-start(bf16[2,256,256]{2,1,0:T(8,128)(2,1)S(1)} %get-tuple-element.88), channel_id=1, source_target_pairs={{2,0},{3,1},{4,2},{5,3},{6,4},{7,5},{8,6},{9,7},{10,8},{11,9},{12,... | collective-permute-start | bytes 786440 | tf_op jit(solution)/shard_map/ppermute | solution.py:15
  100.1 10.4 %collective-permute-start.14 = (bf16[2,128,256]{2,1,0:T(8,128)(2,1)S(1)}, bf16[2,128,256]{2,1,0:T(8,128)(2,1)S(1)}, u32[]{:S(2)}, u32[]{:S(2)}) collective-permute-start(bf16[2,128,256]{2,1,0:T(8,128)(2,1)S(1)} %get-tuple-element.82), channel_id=1, source_target_pairs={{0,1},{1,2},{2,3},{3,4},{4,5},{5,6},{6,7},{7,8},{8,9},{9,10},{10,1... | collective-permute-start | bytes 393224 | tf_op jit(solution)/shard_map/ppermute | solution.py:15
  102.0 8.5 %collective-permute-start.15 = (bf16[2,128,256]{2,1,0:T(8,128)(2,1)S(1)}, bf16[2,128,256]{2,1,0:T(8,128)(2,1)S(1)}, u32[]{:S(2)}, u32[]{:S(2)}) collective-permute-start(bf16[2,128,256]{2,1,0:T(8,128)(2,1)S(1)} %get-tuple-element.83), channel_id=1, source_target_pairs={{1,0},{2,1},{3,2},{4,3},{5,4},{6,5},{7,6},{8,7},{9,8},{10,9},{11,1... | collective-permute-start | bytes 393224 | tf_op jit(solution)/shard_map/ppermute | solution.py:15
  106.8 9.0 %collective-permute-start.19 = (bf16[2,256,256]{2,1,0:T(8,128)(2,1)S(1)}, bf16[2,256,256]{2,1,0:T(8,128)(2,1)S(1)}, u32[]{:S(2)}, u32[]{:S(2)}) collective-permute-start(bf16[2,256,256]{2,1,0:T(8,128)(2,1)S(1)} %get-tuple-element.9), channel_id=1, source_target_pairs={{32,0},{64,32},{96,64},{33,1},{65,33},{97,65},{34,2},{66,34},{98,6... | collective-permute-start | bytes 786440 | tf_op jit(solution)/shard_map/ppermute | solution.py:15
  111.5 11.6 %collective-permute-start.16 = (bf16[2,256,256]{2,1,0:T(8,128)(2,1)S(1)}, bf16[2,256,256]{2,1,0:T(8,128)(2,1)S(1)}, u32[]{:S(2)}, u32[]{:S(2)}) collective-permute-start(bf16[2,256,256]{2,1,0:T(8,128)(2,1)S(1)} %pad_maximum_fusion.26), channel_id=1, source_target_pairs={{32,0},{64,32},{96,64},{33,1},{65,33},{97,65},{34,2},{66,34},{98,6... | collective-permute-start | bytes 786440 | tf_op jit(solution)/shard_map/ppermute | solution.py:15
  116.7 16.9 %collective-permute-start.21 = (bf16[2,256,256]{2,1,0:T(8,128)(2,1)S(1)}, bf16[2,256,256]{2,1,0:T(8,128)(2,1)S(1)}, u32[]{:S(2)}, u32[]{:S(2)}) collective-permute-start(bf16[2,256,256]{2,1,0:T(8,128)(2,1)S(1)} %get-tuple-element.81), channel_id=1, source_target_pairs={{0,2},{1,3},{2,4},{3,5},{4,6},{5,7},{6,8},{7,9},{8,10},{9,11},{10,... | collective-permute-start | bytes 786440 | tf_op jit(solution)/shard_map/ppermute | solution.py:15
  121.2 12.4 %collective-permute-start.20 = (bf16[2,256,256]{2,1,0:T(8,128)(2,1)S(1)}, bf16[2,256,256]{2,1,0:T(8,128)(2,1)S(1)}, u32[]{:S(2)}, u32[]{:S(2)}) collective-permute-start(bf16[2,256,256]{2,1,0:T(8,128)(2,1)S(1)} %get-tuple-element.80), channel_id=1, source_target_pairs={{2,0},{3,1},{4,2},{5,3},{6,4},{7,5},{8,6},{9,7},{10,8},{11,9},{12,... | collective-permute-start | bytes 786440 | tf_op jit(solution)/shard_map/ppermute | solution.py:15
  124.1 10.5 %collective-permute-start.18 = (bf16[2,256,256]{2,1,0:T(8,128)(2,1)S(1)}, bf16[2,256,256]{2,1,0:T(8,128)(2,1)S(1)}, u32[]{:S(2)}, u32[]{:S(2)}) collective-permute-start(bf16[2,256,256]{2,1,0:T(8,128)(2,1)S(1)} %get-tuple-element.79), channel_id=1, source_target_pairs={{0,2},{1,3},{2,4},{3,5},{4,6},{5,7},{6,8},{7,9},{8,10},{9,11},{10,... | collective-permute-start | bytes 786440 | tf_op jit(solution)/shard_map/ppermute | solution.py:15
  130.2 10.4 %collective-permute-start.17 = (bf16[2,256,256]{2,1,0:T(8,128)(2,1)S(1)}, bf16[2,256,256]{2,1,0:T(8,128)(2,1)S(1)}, u32[]{:S(2)}, u32[]{:S(2)}) collective-permute-start(bf16[2,256,256]{2,1,0:T(8,128)(2,1)S(1)} %get-tuple-element.78), channel_id=1, source_target_pairs={{2,0},{3,1},{4,2},{5,3},{6,4},{7,5},{8,6},{9,7},{10,8},{11,9},{12,... | collective-permute-start | bytes 786440 | tf_op jit(solution)/shard_map/ppermute | solution.py:15
  141.7 10.7 %collective-permute-start.22 = (bf16[2,128,256]{2,1,0:T(8,128)(2,1)S(1)}, bf16[2,128,256]{2,1,0:T(8,128)(2,1)S(1)}, u32[]{:S(2)}, u32[]{:S(2)}) collective-permute-start(bf16[2,128,256]{2,1,0:T(8,128)(2,1)S(1)} %get-tuple-element.72), channel_id=1, source_target_pairs={{0,1},{1,2},{2,3},{3,4},{4,5},{5,6},{6,7},{7,8},{8,9},{9,10},{10,1... | collective-permute-start | bytes 393224 | tf_op jit(solution)/shard_map/ppermute | solution.py:15
  143.7 8.8 %collective-permute-start.23 = (bf16[2,128,256]{2,1,0:T(8,128)(2,1)S(1)}, bf16[2,128,256]{2,1,0:T(8,128)(2,1)S(1)}, u32[]{:S(2)}, u32[]{:S(2)}) collective-permute-start(bf16[2,128,256]{2,1,0:T(8,128)(2,1)S(1)} %get-tuple-element.73), channel_id=1, source_target_pairs={{1,0},{2,1},{3,2},{4,3},{5,4},{6,5},{7,6},{8,7},{9,8},{10,9},{11,1... | collective-permute-start | bytes 393224 | tf_op jit(solution)/shard_map/ppermute | solution.py:15
  148.4 8.9 %collective-permute-start.27 = (bf16[2,256,256]{2,1,0:T(8,128)(2,1)S(1)}, bf16[2,256,256]{2,1,0:T(8,128)(2,1)S(1)}, u32[]{:S(2)}, u32[]{:S(2)}) collective-permute-start(bf16[2,256,256]{2,1,0:T(8,128)(2,1)S(1)} %get-tuple-element.3), channel_id=1, source_target_pairs={{32,0},{64,32},{96,64},{33,1},{65,33},{97,65},{34,2},{66,34},{98,6... | collective-permute-start | bytes 786440 | tf_op jit(solution)/shard_map/ppermute | solution.py:15
  153.4 11.0 %collective-permute-start.24 = (bf16[2,256,256]{2,1,0:T(8,128)(2,1)S(1)}, bf16[2,256,256]{2,1,0:T(8,128)(2,1)S(1)}, u32[]{:S(2)}, u32[]{:S(2)}) collective-permute-start(bf16[2,256,256]{2,1,0:T(8,128)(2,1)S(1)} %pad_maximum_fusion.27), channel_id=1, source_target_pairs={{32,0},{64,32},{96,64},{33,1},{65,33},{97,65},{34,2},{66,34},{98,6... | collective-permute-start | bytes 786440 | tf_op jit(solution)/shard_map/ppermute | solution.py:15
  157.2 19.2 %copy-start.8 = (bf16[2,256,256]{2,1,0:T(8,128)(2,1)}, bf16[2,256,256]{2,1,0:T(8,128)(2,1)S(1)}, u32[]{:S(2)}) copy-start(bf16[2,256,256]{2,1,0:T(8,128)(2,1)S(1)} %collective-permute-done.27) | copy-start | bytes 786436
  158.1 18.3 %copy-start.5 = (f32[2,256,768]{2,1,0:T(8,128)}, f32[2,256,768]{2,1,0:T(8,128)S(1)}, u32[]{:S(2)}) copy-start(f32[2,256,768]{2,1,0:T(8,128)S(1)} %get-tuple-element.169) | copy-start | bytes 4718596
  158.2 18.2 %collective-permute-start.29 = (bf16[2,256,256]{2,1,0:T(8,128)(2,1)S(1)}, bf16[2,256,256]{2,1,0:T(8,128)(2,1)S(1)}, u32[]{:S(2)}, u32[]{:S(2)}) collective-permute-start(bf16[2,256,256]{2,1,0:T(8,128)(2,1)S(1)} %get-tuple-element.69), channel_id=1, source_target_pairs={{0,2},{1,3},{2,4},{3,5},{4,6},{5,7},{6,8},{7,9},{8,10},{9,11},{10,... | collective-permute-start | bytes 786440 | tf_op jit(solution)/shard_map/ppermute | solution.py:15
  162.5 13.8 %collective-permute-start.28 = (bf16[2,256,256]{2,1,0:T(8,128)(2,1)S(1)}, bf16[2,256,256]{2,1,0:T(8,128)(2,1)S(1)}, u32[]{:S(2)}, u32[]{:S(2)}) collective-permute-start(bf16[2,256,256]{2,1,0:T(8,128)(2,1)S(1)} %get-tuple-element.68), channel_id=1, source_target_pairs={{2,0},{3,1},{4,2},{5,3},{6,4},{7,5},{8,6},{9,7},{10,8},{11,9},{12,... | collective-permute-start | bytes 786440 | tf_op jit(solution)/shard_map/ppermute | solution.py:15
  165.5 12.1 %collective-permute-start.26 = (bf16[2,256,256]{2,1,0:T(8,128)(2,1)S(1)}, bf16[2,256,256]{2,1,0:T(8,128)(2,1)S(1)}, u32[]{:S(2)}, u32[]{:S(2)}) collective-permute-start(bf16[2,256,256]{2,1,0:T(8,128)(2,1)S(1)} %get-tuple-element.71), channel_id=1, source_target_pairs={{0,2},{1,3},{2,4},{3,5},{4,6},{5,7},{6,8},{7,9},{8,10},{9,11},{10,... | collective-permute-start | bytes 786440 | tf_op jit(solution)/shard_map/ppermute | solution.py:15
  171.6 10.4 %collective-permute-start.25 = (bf16[2,256,256]{2,1,0:T(8,128)(2,1)S(1)}, bf16[2,256,256]{2,1,0:T(8,128)(2,1)S(1)}, u32[]{:S(2)}, u32[]{:S(2)}) collective-permute-start(bf16[2,256,256]{2,1,0:T(8,128)(2,1)S(1)} %get-tuple-element.70), channel_id=1, source_target_pairs={{2,0},{3,1},{4,2},{5,3},{6,4},{7,5},{8,6},{9,7},{10,8},{11,9},{12,... | collective-permute-start | bytes 786440 | tf_op jit(solution)/shard_map/ppermute | solution.py:15
  176.4 6.5 %copy-start.26 = (bf16[2,256,256]{2,1,0:T(8,128)(2,1)}, bf16[2,256,256]{2,1,0:T(8,128)(2,1)S(1)}, u32[]{:S(2)}) copy-start(bf16[2,256,256]{2,1,0:T(8,128)(2,1)S(1)} %collective-permute-done.29) | copy-start | bytes 786436
  176.4 6.5 %copy-start.28 = (bf16[2,256,256]{2,1,0:T(8,128)(2,1)}, bf16[2,256,256]{2,1,0:T(8,128)(2,1)S(1)}, u32[]{:S(2)}) copy-start(bf16[2,256,256]{2,1,0:T(8,128)(2,1)S(1)} %collective-permute-done.28) | copy-start | bytes 786436
  184.8 3.8 %copy-start.15 = (f32[768,512]{1,0:T(8,128)S(1)}, f32[768,512]{1,0:T(8,128)}, u32[]{:S(2)}) copy-start(f32[768,512]{1,0:T(8,128)} %bitcast_add_fusion) | copy-start | bytes 4718596
  191.2 2.7 %collective-permute-start.32 = (bf16[2,2,2,2,56,512]{5,4,3,2,1,0:T(8,128)(2,1)S(1)}, bf16[2,2,2,2,56,512]{5,4,3,2,1,0:T(8,128)(2,1)}, u32[]{:S(2)}, u32[]{:S(2)}) collective-permute-start(bf16[2,2,2,2,56,512]{5,4,3,2,1,0:T(8,128)(2,1)S(1)} %fusion.70), channel_id=1, source_target_pairs={{0,1},{1,0},{2,3},{3,2},{4,5},{5,4},{6,7},{7,6},{8,9},{9,8},{10,11... | collective-permute-start | bytes 2752520 | tf_op jit(solution)/shard_map/ppermute | solution.py:199
  191.3 2.6 %copy-start.1 = (f32[2,2,2,2,2,56,512]{6,5,4,3,2,1,0:T(8,128)S(1)}, f32[2,2,2,2,2,56,512]{6,5,4,3,2,1,0:T(8,128)}, u32[]{:S(2)}) copy-start(f32[2,2,2,2,2,56,512]{6,5,4,3,2,1,0:T(8,128)} %copy-done) | copy-start | bytes 11010052
  192.0 5.5 %copy-start.7 = (bf16[2,256,256]{1,2,0:T(8,128)(2,1)S(1)}, bf16[2,256,256]{1,2,0:T(8,128)(2,1)}, u32[]{:S(2)}) copy-start(bf16[2,256,256]{1,2,0:T(8,128)(2,1)} %copy-done.6) | copy-start | bytes 786436
  195.7 14.0 %collective-permute-start.33 = (bf16[2,2,2,56,512]{4,3,2,1,0:T(8,128)(2,1)S(1)}, bf16[2,2,2,56,512]{4,3,2,1,0:T(8,128)(2,1)S(1)}, u32[]{:S(2)}, u32[]{:S(2)}) collective-permute-start(bf16[2,2,2,56,512]{4,3,2,1,0:T(8,128)(2,1)S(1)} %fusion.173), channel_id=1, source_target_pairs={{0,8},{1,9},{2,10},{3,11},{4,12},{5,13},{6,14},{7,15},{8,0},{9,1},... | collective-permute-start | bytes 1376264 | tf_op jit(solution)/shard_map/ppermute | solution.py:199
  198.1 12.1 %copy-start.9 = (bf16[2,256,256]{2,1,0:T(8,128)(2,1)S(1)}, bf16[2,256,256]{2,1,0:T(8,128)(2,1)}, u32[]{:S(2)}) copy-start(bf16[2,256,256]{2,1,0:T(8,128)(2,1)} %copy-done.8) | copy-start | bytes 786436
  198.1 12.1 %copy-start.27 = (bf16[2,256,256]{2,1,0:T(8,128)(2,1)S(1)}, bf16[2,256,256]{2,1,0:T(8,128)(2,1)}, u32[]{:S(2)}) copy-start(bf16[2,256,256]{2,1,0:T(8,128)(2,1)} %copy-done.26) | copy-start | bytes 786436
  198.1 12.1 %copy-start.29 = (bf16[2,256,256]{2,1,0:T(8,128)(2,1)S(1)}, bf16[2,256,256]{2,1,0:T(8,128)(2,1)}, u32[]{:S(2)}) copy-start(bf16[2,256,256]{2,1,0:T(8,128)(2,1)} %copy-done.28) | copy-start | bytes 786436
  198.1 19.2 %collective-permute-start.30 = (bf16[2,128,256]{2,1,0:T(8,128)(2,1)S(1)}, bf16[2,128,256]{2,1,0:T(8,128)(2,1)S(1)}, u32[]{:S(2)}, u32[]{:S(2)}) collective-permute-start(bf16[2,128,256]{2,1,0:T(8,128)(2,1)S(1)} %get-tuple-element.62), channel_id=1, source_target_pairs={{0,1},{1,2},{2,3},{3,4},{4,5},{5,6},{6,7},{7,8},{8,9},{9,10},{10,1... | collective-permute-start | bytes 393224 | tf_op jit(solution)/shard_map/ppermute | solution.py:15
  200.2 17.1 %collective-permute-start.31 = (bf16[2,128,256]{2,1,0:T(8,128)(2,1)S(1)}, bf16[2,128,256]{2,1,0:T(8,128)(2,1)S(1)}, u32[]{:S(2)}, u32[]{:S(2)}) collective-permute-start(bf16[2,128,256]{2,1,0:T(8,128)(2,1)S(1)} %get-tuple-element.63), channel_id=1, source_target_pairs={{1,0},{2,1},{3,2},{4,3},{5,4},{6,5},{7,6},{8,7},{9,8},{10,9},{11,1... | collective-permute-start | bytes 393224 | tf_op jit(solution)/shard_map/ppermute | solution.py:15
  210.1 6.9 %collective-permute-start.34 = (bf16[2,2,56,512]{3,2,1,0:T(8,128)(2,1)S(1)}, bf16[2,2,56,512]{3,2,1,0:T(8,128)(2,1)S(1)}, u32[]{:S(2)}, u32[]{:S(2)}) collective-permute-start(bf16[2,2,56,512]{3,2,1,0:T(8,128)(2,1)S(1)} %fusion.227), channel_id=1, source_target_pairs={{0,2},{1,3},{2,0},{3,1},{4,6},{5,7},{6,4},{7,5},{8,10},{9,11},{10,... | collective-permute-start | bytes 688136 | tf_op jit(solution)/shard_map/ppermute | solution.py:199
  210.2 7.1 %copy-start.14 = (f32[2,256,256]{2,1,0:T(8,128)S(1)}, f32[2,256,256]{2,1,0:T(8,128)}, u32[]{:S(2)}) copy-start(f32[2,256,256]{2,1,0:T(8,128)} %get-tuple-element.6) | copy-start | bytes 1572868
  217.1 10.0 %copy-start.11 = (f32[1,2,256,256]{3,2,1,0:T(8,128)S(1)}, f32[1,2,256,256]{3,2,1,0:T(8,128)}, u32[]{:S(2)}) copy-start(f32[1,2,256,256]{3,2,1,0:T(8,128)} %get-tuple-element.28) | copy-start | bytes 1572868
  217.1 9.9 %copy-start.12 = (f32[2,256,256]{2,1,0:T(8,128)S(1)}, f32[2,256,256]{2,1,0:T(8,128)}, u32[]{:S(2)}) copy-start(f32[2,256,256]{2,1,0:T(8,128)} %get-tuple-element.10) | copy-start | bytes 1572868
  217.1 9.9 %copy-start.13 = (f32[2,256,256]{2,1,0:T(8,128)S(1)}, f32[2,256,256]{2,1,0:T(8,128)}, u32[]{:S(2)}) copy-start(f32[2,256,256]{2,1,0:T(8,128)} %get-tuple-element.4) | copy-start | bytes 1572868
  217.1 9.9 %copy-start.20 = (f32[1,2,128,256]{3,2,1,0:T(8,128)S(1)}, f32[1,2,128,256]{3,2,1,0:T(8,128)}, u32[]{:S(2)}) copy-start(f32[1,2,128,256]{3,2,1,0:T(8,128)} %get-tuple-element.22) | copy-start | bytes 786436
  217.1 9.9 %copy-start.21 = (f32[1,2,128,256]{3,2,1,0:T(8,128)S(1)}, f32[1,2,128,256]{3,2,1,0:T(8,128)}, u32[]{:S(2)}) copy-start(f32[1,2,128,256]{3,2,1,0:T(8,128)} %get-tuple-element.25) | copy-start | bytes 786436
  217.1 9.9 %copy-start.22 = (f32[1,2,128,256]{3,2,1,0:T(8,128)S(1)}, f32[1,2,128,256]{3,2,1,0:T(8,128)}, u32[]{:S(2)}) copy-start(f32[1,2,128,256]{3,2,1,0:T(8,128)} %get-tuple-element.38) | copy-start | bytes 786436
  217.1 9.9 %copy-start.23 = (f32[1,2,128,256]{3,2,1,0:T(8,128)S(1)}, f32[1,2,128,256]{3,2,1,0:T(8,128)}, u32[]{:S(2)}) copy-start(f32[1,2,128,256]{3,2,1,0:T(8,128)} %get-tuple-element.45) | copy-start | bytes 786436
  217.2 9.9 %copy-start.24 = (f32[1,2,128,256]{3,2,1,0:T(8,128)S(1)}, f32[1,2,128,256]{3,2,1,0:T(8,128)}, u32[]{:S(2)}) copy-start(f32[1,2,128,256]{3,2,1,0:T(8,128)} %get-tuple-element.34) | copy-start | bytes 786436
  217.2 9.9 %copy-start.25 = (f32[1,2,128,256]{3,2,1,0:T(8,128)S(1)}, f32[1,2,128,256]{3,2,1,0:T(8,128)}, u32[]{:S(2)}) copy-start(f32[1,2,128,256]{3,2,1,0:T(8,128)} %get-tuple-element.43) | copy-start | bytes 786436
  217.2 6.4 %collective-permute-start.35 = (bf16[2,56,512]{2,1,0:T(8,128)(2,1)S(1)}, bf16[2,56,512]{2,1,0:T(8,128)(2,1)S(1)}, u32[]{:S(2)}, u32[]{:S(2)}) collective-permute-start(bf16[2,56,512]{2,1,0:T(8,128)(2,1)S(1)} %fusion.257), channel_id=1, source_target_pairs={{0,4},{1,5},{2,6},{3,7},{4,0},{5,1},{6,2},{7,3},{8,12},{9,13},{10,... | collective-permute-start | bytes 344072 | tf_op jit(solution)/shard_map/ppermute | solution.py:199
  223.6 5.8 %collective-permute-start.36 = (bf16[56,512]{1,0:T(8,128)(2,1)S(1)}, bf16[56,512]{1,0:T(8,128)(2,1)S(1)}, u32[]{:S(2)}, u32[]{:S(2)}) collective-permute-start(bf16[56,512]{1,0:T(8,128)(2,1)S(1)} %fusion.258), channel_id=1, source_target_pairs={{0,16},{1,17},{2,18},{3,19},{4,20},{5,21},{6,22},{7,23},{8,24},{9,... | collective-permute-start | bytes 172040 | tf_op jit(solution)/shard_map/ppermute | solution.py:199
  (5 other events, 5.7 us)

commit v11 on v10

--- a/solution.py
+++ b/solution.py
@@ -266,7 +266,7 @@
     out_all = jnp.concatenate(
         [acc.reshape(seq_count, out_rows, channels) for acc in out_acc], axis=1
     ).reshape(seq_count, depth * out_rows * channels // (2 * channels), 2 * channels)
-    (mine,) = halving_scatter([jnp.concatenate([conv_all, out_all], axis=1)], (0, 3, 1, 2, 4))
+    (mine,) = halving_scatter([jnp.concatenate([conv_all, out_all], axis=1)], (0, 1, 3, 4, 2))
     conv_grads = mine[: depth * conv_rows].reshape(1, depth, conv_rows, 2 * channels) * grad_scale
     out_grads = mine[depth * conv_rows :].reshape(1, depth, out_rows, channels) * grad_scale
     return (input_grads[None], conv_grads, out_grads)

time: 232 us -> 231 us (level)
  transfers between devices with their start and end apart: 37 -> 37, of which waited for: 15 -> 15; matrix products, arithmetic and copies ran while one was open for 16% -> 17% of each run, Pallas kernels for 0% -> 0%
where the time goes in v11:
time: 231 us; the launch traced here: 229 us
  starting transfers between devices  97.7 us (42%)
  waiting for transfers between devices  69.6 us (30%)
  matrix products  38.9 us (17%)
  other arithmetic  15.1 us (7%)
  local copies, waits for them, and re-layouts  5.88 us (3%)
    ppermute x32, starting transfers between devices, shifted(): lax.ppermute(value, axis, [(source, source + steps) for source in range(l...  92.4 us
    ppermute x32, waiting for transfers between devices, shifted(): lax.ppermute(value, axis, [(source, source + steps) for source in range(l...  50.5 us
    ppermute x5, waiting for transfers between devices, halving_scatter(): got = lax.ppermute(sends, 'seq', pairs)  19.1 us
    dot_general x3, matrix products, backward_near_pieces(): jnp.einsum('mpc,mpd->cd', taps, grad_pre, preferred_element_type=f32)  8.24 us
    dot_general x7, matrix products, mm(): return jnp.einsum('mpc,cd->mpd', a, b, preferred_element_type=jnp.float32)  5.75 us
    ppermute x5, starting transfers between devices, halving_scatter(): got = lax.ppermute(sends, 'seq', pairs)  5.34 us
  transfers between devices with their start and end apart: 37, of which 15 were waited for; matrix products, arithmetic and copies ran while one was open for 17% of the time, Pallas kernels for 0%

profile of v11, /device:TPU:24, one launch (start us, length us, event | category | flops | bytes accessed | tf_op | source)
XLA Modules:
  0.0 229.4 jit_solution(13412542090090781419)
XLA Ops:
  0.6 1.0 fusion.350
  1.7 1.9 collective-permute-start
  3.6 3.6 %collective-permute-start.1 = (bf16[2,128,256]{2,1,0:T(8,128)(2,1)S(1)}, bf16[2,128,256]{2,1,0:T(8,128)(2,1)S(1)}, u32[]{:S(2)}, u32[]{:S(2)}) collective-permute-start(bf16[2,128,256]{2,1,0:T(8,128)(2,1)S(1)} %get-tuple-element.130), channel_id=1, source_target_pairs={{1,0},{2,1},{3,2},{4,3},{5,4},{6,5},{7,6},{8,7},{9,8},{10,9},{11,1... | collective-permute-start | bytes 393224 | tf_op jit(solution)/shard_map/ppermute | solution.py:15
  7.3 1.6 fusion.215
  9.0 1.8 fusion.106
  12.7 5.6 %collective-permute-start.2 = (bf16[2,512,256]{2,1,0:T(8,128)(2,1)S(1)}, bf16[2,512,256]{2,1,0:T(8,128)(2,1)S(1)}, u32[]{:S(2)}, u32[]{:S(2)}) collective-permute-start(bf16[2,512,256]{2,1,0:T(8,128)(2,1)S(1)} %fusion.2), channel_id=1, source_target_pairs={{0,2},{1,3},{2,4},{3,5},{4,6},{5,7},{6,8},{7,9},{8,10},{9,11},{10,... | collective-permute-start | bytes 1572872 | tf_op jit(solution)/shard_map/ppermute | solution.py:15
  18.4 1.9 collective-permute-start.3
  20.8 8.2 %collective-permute-done.2 = bf16[2,512,256]{2,1,0:T(8,128)(2,1)S(1)} collective-permute-done((bf16[2,512,256]{2,1,0:T(8,128)(2,1)S(1)}, bf16[2,512,256]{2,1,0:T(8,128)(2,1)S(1)}, u32[]{:S(2)}, u32[]{:S(2)}) %collective-permute-start.2) | collective-permute-done | bytes 524320 | tf_op jit(solution)/shard_map/ppermute | solution.py:15
  29.6 5.8 %collective-permute-done.3 = bf16[2,512,256]{2,1,0:T(8,128)(2,1)S(1)} collective-permute-done((bf16[2,512,256]{2,1,0:T(8,128)(2,1)S(1)}, bf16[2,512,256]{2,1,0:T(8,128)(2,1)S(1)}, u32[]{:S(2)}, u32[]{:S(2)}) %collective-permute-start.3) | collective-permute-done | bytes 524320 | tf_op jit(solution)/shard_map/ppermute | solution.py:15
  37.8 1.9 collective-permute-start.5
  39.7 3.9 %collective-permute-start.4 = (bf16[2,512,256]{2,1,0:T(8,128)(2,1)S(1)}, bf16[2,512,256]{2,1,0:T(8,128)(2,1)S(1)}, u32[]{:S(2)}, u32[]{:S(2)}) collective-permute-start(bf16[2,512,256]{2,1,0:T(8,128)(2,1)S(1)} %get-tuple-element.50), channel_id=1, source_target_pairs={{2,0},{3,1},{4,2},{5,3},{6,4},{7,5},{8,6},{9,7},{10,8},{11,9},{12,... | collective-permute-start | bytes 1572872 | tf_op jit(solution)/shard_map/ppermute | solution.py:15
  45.1 6.7 %collective-permute-done.5 = bf16[2,512,256]{2,1,0:T(8,128)(2,1)S(1)} collective-permute-done((bf16[2,512,256]{2,1,0:T(8,128)(2,1)S(1)}, bf16[2,512,256]{2,1,0:T(8,128)(2,1)S(1)}, u32[]{:S(2)}, u32[]{:S(2)}) %collective-permute-start.5) | collective-permute-done | bytes 524320 | tf_op jit(solution)/shard_map/ppermute | solution.py:15
  51.8 4.0 %collective-permute-done.4 = bf16[2,512,256]{2,1,0:T(8,128)(2,1)S(1)} collective-permute-done((bf16[2,512,256]{2,1,0:T(8,128)(2,1)S(1)}, bf16[2,512,256]{2,1,0:T(8,128)(2,1)S(1)}, u32[]{:S(2)}, u32[]{:S(2)}) %collective-permute-start.4) | collective-permute-done | bytes 524320 | tf_op jit(solution)/shard_map/ppermute | solution.py:15
  57.8 2.1 collective-permute-start.6
  59.9 3.6 %collective-permute-start.7 = (bf16[2,128,256]{2,1,0:T(8,128)(2,1)S(1)}, bf16[2,128,256]{2,1,0:T(8,128)(2,1)S(1)}, u32[]{:S(2)}, u32[]{:S(2)}) collective-permute-start(bf16[2,128,256]{2,1,0:T(8,128)(2,1)S(1)} %get-tuple-element.49), channel_id=1, source_target_pairs={{1,0},{2,1},{3,2},{4,3},{5,4},{6,5},{7,6},{8,7},{9,8},{10,9},{11,1... | collective-permute-start | bytes 393224 | tf_op jit(solution)/shard_map/ppermute | solution.py:15
  64.5 1.3 collective-permute-start.11
  65.8 2.2 fusion.75
  69.1 1.3 collective-permute-start.8
  70.4 3.8 %collective-permute-done.11 = bf16[2,256,256]{2,1,0:T(8,128)(2,1)S(1)} collective-permute-done((bf16[2,256,256]{2,1,0:T(8,128)(2,1)S(1)}, bf16[2,256,256]{2,1,0:T(8,128)(2,1)S(1)}, u32[]{:S(2)}, u32[]{:S(2)}) %collective-permute-start.11) | collective-permute-done | bytes 262176 | tf_op jit(solution)/shard_map/ppermute | solution.py:15
  75.1 4.3 %collective-permute-start.13 = (bf16[2,256,256]{2,1,0:T(8,128)(2,1)S(1)}, bf16[2,256,256]{2,1,0:T(8,128)(2,1)S(1)}, u32[]{:S(2)}, u32[]{:S(2)}) collective-permute-start(bf16[2,256,256]{2,1,0:T(8,128)(2,1)S(1)} %get-tuple-element.91), channel_id=1, source_target_pairs={{0,2},{1,3},{2,4},{3,5},{4,6},{5,7},{6,8},{7,9},{8,10},{9,11},{10,... | collective-permute-start | bytes 786440 | tf_op jit(solution)/shard_map/ppermute | solution.py:15
  79.4 2.1 collective-permute-start.12
  82.5 6.0 %collective-permute-start.10 = (bf16[2,256,256]{2,1,0:T(8,128)(2,1)S(1)}, bf16[2,256,256]{2,1,0:T(8,128)(2,1)S(1)}, u32[]{:S(2)}, u32[]{:S(2)}) collective-permute-start(bf16[2,256,256]{2,1,0:T(8,128)(2,1)S(1)} %get-tuple-element.89), channel_id=1, source_target_pairs={{0,2},{1,3},{2,4},{3,5},{4,6},{5,7},{6,8},{7,9},{8,10},{9,11},{10,... | collective-permute-start | bytes 786440 | tf_op jit(solution)/shard_map/ppermute | solution.py:15
  88.5 1.9 collective-permute-start.9
  92.7 6.2 %collective-permute-done.9 = bf16[2,256,256]{2,1,0:T(8,128)(2,1)S(1)} collective-permute-done((bf16[2,256,256]{2,1,0:T(8,128)(2,1)S(1)}, bf16[2,256,256]{2,1,0:T(8,128)(2,1)S(1)}, u32[]{:S(2)}, u32[]{:S(2)}) %collective-permute-start.9) | collective-permute-done | bytes 262176 | tf_op jit(solution)/shard_map/ppermute | solution.py:15
  100.1 1.9 collective-permute-start.14
  102.0 3.6 %collective-permute-start.15 = (bf16[2,128,256]{2,1,0:T(8,128)(2,1)S(1)}, bf16[2,128,256]{2,1,0:T(8,128)(2,1)S(1)}, u32[]{:S(2)}, u32[]{:S(2)}) collective-permute-start(bf16[2,128,256]{2,1,0:T(8,128)(2,1)S(1)} %get-tuple-element.83), channel_id=1, source_target_pairs={{1,0},{2,1},{3,2},{4,3},{5,4},{6,5},{7,6},{8,7},{9,8},{10,9},{11,1... | collective-permute-start | bytes 393224 | tf_op jit(solution)/shard_map/ppermute | solution.py:15
  105.7 1.1 fusion.326
  106.8 1.3 collective-permute-start.19
  108.0 2.2 fusion.21
  111.5 1.3 collective-permute-start.16
  112.8 2.9 %collective-permute-done.19 = bf16[2,256,256]{2,1,0:T(8,128)(2,1)S(1)} collective-permute-done((bf16[2,256,256]{2,1,0:T(8,128)(2,1)S(1)}, bf16[2,256,256]{2,1,0:T(8,128)(2,1)S(1)}, u32[]{:S(2)}, u32[]{:S(2)}) %collective-permute-start.19) | collective-permute-done | bytes 262176 | tf_op jit(solution)/shard_map/ppermute | solution.py:15
  116.7 4.6 %collective-permute-start.21 = (bf16[2,256,256]{2,1,0:T(8,128)(2,1)S(1)}, bf16[2,256,256]{2,1,0:T(8,128)(2,1)S(1)}, u32[]{:S(2)}, u32[]{:S(2)}) collective-permute-start(bf16[2,256,256]{2,1,0:T(8,128)(2,1)S(1)} %get-tuple-element.81), channel_id=1, source_target_pairs={{0,2},{1,3},{2,4},{3,5},{4,6},{5,7},{6,8},{7,9},{8,10},{9,11},{10,... | collective-permute-start | bytes 786440 | tf_op jit(solution)/shard_map/ppermute | solution.py:15
  121.2 1.9 collective-permute-start.20
  124.1 6.0 %collective-permute-start.18 = (bf16[2,256,256]{2,1,0:T(8,128)(2,1)S(1)}, bf16[2,256,256]{2,1,0:T(8,128)(2,1)S(1)}, u32[]{:S(2)}, u32[]{:S(2)}) collective-permute-start(bf16[2,256,256]{2,1,0:T(8,128)(2,1)S(1)} %get-tuple-element.79), channel_id=1, source_target_pairs={{0,2},{1,3},{2,4},{3,5},{4,6},{5,7},{6,8},{7,9},{8,10},{9,11},{10,... | collective-permute-start | bytes 786440 | tf_op jit(solution)/shard_map/ppermute | solution.py:15
  130.2 1.9 collective-permute-start.17
  134.7 5.9 %collective-permute-done.17 = bf16[2,256,256]{2,1,0:T(8,128)(2,1)S(1)} collective-permute-done((bf16[2,256,256]{2,1,0:T(8,128)(2,1)S(1)}, bf16[2,256,256]{2,1,0:T(8,128)(2,1)S(1)}, u32[]{:S(2)}, u32[]{:S(2)}) %collective-permute-start.17) | collective-permute-done | bytes 262176 | tf_op jit(solution)/shard_map/ppermute | solution.py:15
  141.7 1.9 collective-permute-start.22
  143.7 3.6 %collective-permute-start.23 = (bf16[2,128,256]{2,1,0:T(8,128)(2,1)S(1)}, bf16[2,128,256]{2,1,0:T(8,128)(2,1)S(1)}, u32[]{:S(2)}, u32[]{:S(2)}) collective-permute-start(bf16[2,128,256]{2,1,0:T(8,128)(2,1)S(1)} %get-tuple-element.73), channel_id=1, source_target_pairs={{1,0},{2,1},{3,2},{4,3},{5,4},{6,5},{7,6},{8,7},{9,8},{10,9},{11,1... | collective-permute-start | bytes 393224 | tf_op jit(solution)/shard_map/ppermute | solution.py:15
  147.3 1.0 fusion.320
  148.4 1.5 collective-permute-start.27
  149.9 2.3 fusion.29
  153.4 1.3 collective-permute-start.24
  154.7 2.5 %collective-permute-done.27 = bf16[2,256,256]{2,1,0:T(8,128)(2,1)S(1)} collective-permute-done((bf16[2,256,256]{2,1,0:T(8,128)(2,1)S(1)}, bf16[2,256,256]{2,1,0:T(8,128)(2,1)S(1)}, u32[]{:S(2)}, u32[]{:S(2)}) %collective-permute-start.27) | collective-permute-done | bytes 262176 | tf_op jit(solution)/shard_map/ppermute | solution.py:15
  158.2 4.3 %collective-permute-start.29 = (bf16[2,256,256]{2,1,0:T(8,128)(2,1)S(1)}, bf16[2,256,256]{2,1,0:T(8,128)(2,1)S(1)}, u32[]{:S(2)}, u32[]{:S(2)}) collective-permute-start(bf16[2,256,256]{2,1,0:T(8,128)(2,1)S(1)} %get-tuple-element.69), channel_id=1, source_target_pairs={{0,2},{1,3},{2,4},{3,5},{4,6},{5,7},{6,8},{7,9},{8,10},{9,11},{10,... | collective-permute-start | bytes 786440 | tf_op jit(solution)/shard_map/ppermute | solution.py:15
  162.5 1.9 collective-permute-start.28
  165.5 6.0 %collective-permute-start.26 = (bf16[2,256,256]{2,1,0:T(8,128)(2,1)S(1)}, bf16[2,256,256]{2,1,0:T(8,128)(2,1)S(1)}, u32[]{:S(2)}, u32[]{:S(2)}) collective-permute-start(bf16[2,256,256]{2,1,0:T(8,128)(2,1)S(1)} %get-tuple-element.71), channel_id=1, source_target_pairs={{0,2},{1,3},{2,4},{3,5},{4,6},{5,7},{6,8},{7,9},{8,10},{9,11},{10,... | collective-permute-start | bytes 786440 | tf_op jit(solution)/shard_map/ppermute | solution.py:15
  171.6 1.9 collective-permute-start.25
  173.5 2.2 bitcast_add_fusion
  176.5 1.1 multiply_convert_fusion.5
  177.6 4.3 %collective-permute-done.25 = bf16[2,256,256]{2,1,0:T(8,128)(2,1)S(1)} collective-permute-done((bf16[2,256,256]{2,1,0:T(8,128)(2,1)S(1)}, bf16[2,256,256]{2,1,0:T(8,128)(2,1)S(1)}, u32[]{:S(2)}, u32[]{:S(2)}) %collective-permute-start.25) | collective-permute-done | bytes 262176 | tf_op jit(solution)/shard_map/ppermute | solution.py:15
  184.8 3.8 %bitcast_add_fusion.3 = f32[768,512]{1,0:T(8,128)S(1)} fusion(f32[768,512,1]{1,0,2:T(8,128)} %fusion.29, f32[768,512,1]{1,0,2:T(8,128)} %fusion.21, f32[768,512,1]{1,0,2:T(8,128)} %fusion.75, bf16[2,128,512]{1,2,0:T(8,128)(2,1)S(1)} %get-tuple-element.93, bf16[2,256,256]{1,2,0:T(8,128)(2,1)S(1)} %copy-done.19, bf16[2,256,256]{1,2,0:T(8,128)(2,1)S(1)} %copy-done.18, ...), kind=kOutput, calls=%fused_computation.12 | convolution fusion | flops 818544640 | bytes 8912896 | tf_op jit(solution)/shard_map/mpc,mpd->cd/dot_general | solution.py:151
  189.2 1.8 copy-done
  192.0 1.9 collective-permute-done.32
  193.9 1.7 fusion.1
  196.5 2.2 collective-permute-start.30
  198.7 3.5 %collective-permute-start.31 = (bf16[2,128,256]{2,1,0:T(8,128)(2,1)S(1)}, bf16[2,128,256]{2,1,0:T(8,128)(2,1)S(1)}, u32[]{:S(2)}, u32[]{:S(2)}) collective-permute-start(bf16[2,128,256]{2,1,0:T(8,128)(2,1)S(1)} %get-tuple-element.63), channel_id=1, source_target_pairs={{1,0},{2,1},{3,2},{4,3},{5,4},{6,5},{7,6},{8,7},{9,8},{10,9},{11,1... | collective-permute-start | bytes 393224 | tf_op jit(solution)/shard_map/ppermute | solution.py:15
  202.3 7.0 %collective-permute-done.33 = bf16[2,2,2,56,512]{4,3,2,1,0:T(8,128)(2,1)S(1)} collective-permute-done((bf16[2,2,2,56,512]{4,3,2,1,0:T(8,128)(2,1)S(1)}, bf16[2,2,2,56,512]{4,3,2,1,0:T(8,128)(2,1)S(1)}, u32[]{:S(2)}, u32[]{:S(2)}) %collective-permute-start.33) | collective-permute-done | bytes 458784 | tf_op jit(solution)/shard_map/ppermute | solution.py:199
  209.5 1.7 collective-permute-start.34
  211.2 1.3 fusion.87
  212.6 3.0 %collective-permute-done.34 = bf16[2,2,56,512]{3,2,1,0:T(8,128)(2,1)S(1)} collective-permute-done((bf16[2,2,56,512]{3,2,1,0:T(8,128)(2,1)S(1)}, bf16[2,2,56,512]{3,2,1,0:T(8,128)(2,1)S(1)}, u32[]{:S(2)}, u32[]{:S(2)}) %collective-permute-start.34) | collective-permute-done | bytes 229408 | tf_op jit(solution)/shard_map/ppermute | solution.py:199
  215.9 3.4 %collective-permute-start.35 = (bf16[2,56,512]{2,1,0:T(8,128)(2,1)S(1)}, bf16[2,56,512]{2,1,0:T(8,128)(2,1)S(1)}, u32[]{:S(2)}, u32[]{:S(2)}) collective-permute-start(bf16[2,56,512]{2,1,0:T(8,128)(2,1)S(1)} %fusion.255), channel_id=1, source_target_pairs={{0,16},{1,17},{2,18},{3,19},{4,20},{5,21},{6,22},{7,23},{8,24},{9,... | collective-permute-start | bytes 344072 | tf_op jit(solution)/shard_map/ppermute | solution.py:199
  219.4 2.9 %collective-permute-done.35 = bf16[2,56,512]{2,1,0:T(8,128)(2,1)S(1)} collective-permute-done((bf16[2,56,512]{2,1,0:T(8,128)(2,1)S(1)}, bf16[2,56,512]{2,1,0:T(8,128)(2,1)S(1)}, u32[]{:S(2)}, u32[]{:S(2)}) %collective-permute-start.35) | collective-permute-done | bytes 114720 | tf_op jit(solution)/shard_map/ppermute | solution.py:199
  222.5 1.2 fusion.20
  223.7 4.3 %collective-permute-done.36 = bf16[56,512]{1,0:T(8,128)(2,1)S(1)} collective-permute-done((bf16[56,512]{1,0:T(8,128)(2,1)S(1)}, bf16[56,512]{1,0:T(8,128)(2,1)S(1)}, u32[]{:S(2)}, u32[]{:S(2)}) %collective-permute-start.36) | collective-permute-done | bytes 57376 | tf_op jit(solution)/shard_map/ppermute | solution.py:199
  (192 shorter events, 33.7 us)
Async XLA Ops:
  0.6 8.3 %copy-start.3 = (bf16[1,2,512,256]{3,2,1,0:T(8,128)(2,1)S(1)}, bf16[1,2,512,256]{3,2,1,0:T(8,128)(2,1)}, u32[]{:S(2)}) copy-start(bf16[1,2,512,256]{3,2,1,0:T(8,128)(2,1)} %param.4) | copy-start | bytes 1572868
  1.7 7.3 %collective-permute-start = (bf16[2,128,256]{2,1,0:T(8,128)(2,1)S(1)}, bf16[2,128,256]{2,1,0:T(8,128)(2,1)S(1)}, u32[]{:S(2)}, u32[]{:S(2)}) collective-permute-start(bf16[2,128,256]{2,1,0:T(8,128)(2,1)S(1)} %get-tuple-element.131), channel_id=1, source_target_pairs={{0,1},{1,2},{2,3},{3,4},{4,5},{5,6},{6,7},{7,8},{8,9},{9,10},{10,1... | collective-permute-start | bytes 393224 | tf_op jit(solution)/shard_map/ppermute | solution.py:15
  3.6 7.2 %collective-permute-start.1 = (bf16[2,128,256]{2,1,0:T(8,128)(2,1)S(1)}, bf16[2,128,256]{2,1,0:T(8,128)(2,1)S(1)}, u32[]{:S(2)}, u32[]{:S(2)}) collective-permute-start(bf16[2,128,256]{2,1,0:T(8,128)(2,1)S(1)} %get-tuple-element.130), channel_id=1, source_target_pairs={{1,0},{2,1},{3,2},{4,3},{5,4},{6,5},{7,6},{8,7},{9,8},{10,9},{11,1... | collective-permute-start | bytes 393224 | tf_op jit(solution)/shard_map/ppermute | solution.py:15
  8.9 2.0 copy-start.4
  9.0 140.9 %copy-start.16 = (bf16[2,384,256]{2,1,0:T(8,128)(2,1)}, bf16[2,384,256]{2,1,0:T(8,128)(2,1)S(1)}, u32[]{:S(2)}) copy-start(bf16[2,384,256]{2,1,0:T(8,128)(2,1)S(1)} %get-tuple-element.128) | copy-start | bytes 1179652
  9.0 140.9 %copy-start.17 = (bf16[2,384,256]{2,1,0:T(8,128)(2,1)}, bf16[2,384,256]{2,1,0:T(8,128)(2,1)S(1)}, u32[]{:S(2)}) copy-start(bf16[2,384,256]{2,1,0:T(8,128)(2,1)S(1)} %get-tuple-element.129) | copy-start | bytes 1179652
  9.0 2.8 %copy-start.30 = (bf16[2,128,256]{2,1,0:T(8,128)(2,1)}, bf16[2,128,256]{2,1,0:T(8,128)(2,1)S(1)}, u32[]{:S(2)}) copy-start(bf16[2,128,256]{2,1,0:T(8,128)(2,1)S(1)} %collective-permute-done) | copy-start | bytes 393220
  12.7 16.4 %collective-permute-start.2 = (bf16[2,512,256]{2,1,0:T(8,128)(2,1)S(1)}, bf16[2,512,256]{2,1,0:T(8,128)(2,1)S(1)}, u32[]{:S(2)}, u32[]{:S(2)}) collective-permute-start(bf16[2,512,256]{2,1,0:T(8,128)(2,1)S(1)} %fusion.2), channel_id=1, source_target_pairs={{0,2},{1,3},{2,4},{3,5},{4,6},{5,7},{6,8},{7,9},{8,10},{9,11},{10,... | collective-permute-start | bytes 1572872 | tf_op jit(solution)/shard_map/ppermute | solution.py:15
  18.4 17.0 %collective-permute-start.3 = (bf16[2,512,256]{2,1,0:T(8,128)(2,1)S(1)}, bf16[2,512,256]{2,1,0:T(8,128)(2,1)S(1)}, u32[]{:S(2)}, u32[]{:S(2)}) collective-permute-start(bf16[2,512,256]{2,1,0:T(8,128)(2,1)S(1)} %fusion.2), channel_id=1, source_target_pairs={{2,0},{3,1},{4,2},{5,3},{6,4},{7,5},{8,6},{9,7},{10,8},{11,9},{12,... | collective-permute-start | bytes 1572872 | tf_op jit(solution)/shard_map/ppermute | solution.py:15
  29.6 6.4 %copy-start.10 = (bf16[2,512,256]{2,1,0:T(8,128)(2,1)S(1)}, bf16[2,512,256]{2,1,0:T(8,128)(2,1)}, u32[]{:S(2)}) copy-start(bf16[2,512,256]{2,1,0:T(8,128)(2,1)} %param.5) | copy-start | bytes 1572868
  37.8 14.0 %collective-permute-start.5 = (bf16[2,512,256]{2,1,0:T(8,128)(2,1)S(1)}, bf16[2,512,256]{2,1,0:T(8,128)(2,1)S(1)}, u32[]{:S(2)}, u32[]{:S(2)}) collective-permute-start(bf16[2,512,256]{2,1,0:T(8,128)(2,1)S(1)} %get-tuple-element.51), channel_id=1, source_target_pairs={{0,2},{1,3},{2,4},{3,5},{4,6},{5,7},{6,8},{7,9},{8,10},{9,11},{10,... | collective-permute-start | bytes 1572872 | tf_op jit(solution)/shard_map/ppermute | solution.py:15
  39.7 16.1 %collective-permute-start.4 = (bf16[2,512,256]{2,1,0:T(8,128)(2,1)S(1)}, bf16[2,512,256]{2,1,0:T(8,128)(2,1)S(1)}, u32[]{:S(2)}, u32[]{:S(2)}) collective-permute-start(bf16[2,512,256]{2,1,0:T(8,128)(2,1)S(1)} %get-tuple-element.50), channel_id=1, source_target_pairs={{2,0},{3,1},{4,2},{5,3},{6,4},{7,5},{8,6},{9,7},{10,8},{11,9},{12,... | collective-permute-start | bytes 1572872 | tf_op jit(solution)/shard_map/ppermute | solution.py:15
  57.8 8.0 %copy-start.31 = (bf16[2,128,256]{2,1,0:T(8,128)(2,1)S(1)}, bf16[2,128,256]{2,1,0:T(8,128)(2,1)}, u32[]{:S(2)}) copy-start(bf16[2,128,256]{2,1,0:T(8,128)(2,1)} %copy-done.30) | copy-start | bytes 393220
  57.8 10.2 %collective-permute-start.6 = (bf16[2,128,256]{2,1,0:T(8,128)(2,1)S(1)}, bf16[2,128,256]{2,1,0:T(8,128)(2,1)S(1)}, u32[]{:S(2)}, u32[]{:S(2)}) collective-permute-start(bf16[2,128,256]{2,1,0:T(8,128)(2,1)S(1)} %get-tuple-element.48), channel_id=1, source_target_pairs={{0,1},{1,2},{2,3},{3,4},{4,5},{5,6},{6,7},{7,8},{8,9},{9,10},{10,1... | collective-permute-start | bytes 393224 | tf_op jit(solution)/shard_map/ppermute | solution.py:15
  59.9 8.2 %collective-permute-start.7 = (bf16[2,128,256]{2,1,0:T(8,128)(2,1)S(1)}, bf16[2,128,256]{2,1,0:T(8,128)(2,1)S(1)}, u32[]{:S(2)}, u32[]{:S(2)}) collective-permute-start(bf16[2,128,256]{2,1,0:T(8,128)(2,1)S(1)} %get-tuple-element.49), channel_id=1, source_target_pairs={{1,0},{2,1},{3,2},{4,3},{5,4},{6,5},{7,6},{8,7},{9,8},{10,9},{11,1... | collective-permute-start | bytes 393224 | tf_op jit(solution)/shard_map/ppermute | solution.py:15
  64.5 9.7 %collective-permute-start.11 = (bf16[2,256,256]{2,1,0:T(8,128)(2,1)S(1)}, bf16[2,256,256]{2,1,0:T(8,128)(2,1)S(1)}, u32[]{:S(2)}, u32[]{:S(2)}) collective-permute-start(bf16[2,256,256]{2,1,0:T(8,128)(2,1)S(1)} %get-tuple-element.27), channel_id=1, source_target_pairs={{32,0},{64,32},{96,64},{33,1},{65,33},{97,65},{34,2},{66,34},{98,6... | collective-permute-start | bytes 786440 | tf_op jit(solution)/shard_map/ppermute | solution.py:15
  69.1 12.5 %collective-permute-start.8 = (bf16[2,256,256]{2,1,0:T(8,128)(2,1)S(1)}, bf16[2,256,256]{2,1,0:T(8,128)(2,1)S(1)}, u32[]{:S(2)}, u32[]{:S(2)}) collective-permute-start(bf16[2,256,256]{2,1,0:T(8,128)(2,1)S(1)} %pad_maximum_fusion.25), channel_id=1, source_target_pairs={{32,0},{64,32},{96,64},{33,1},{65,33},{97,65},{34,2},{66,34},{98,6... | collective-permute-start | bytes 786440 | tf_op jit(solution)/shard_map/ppermute | solution.py:15
  75.1 16.6 %collective-permute-start.13 = (bf16[2,256,256]{2,1,0:T(8,128)(2,1)S(1)}, bf16[2,256,256]{2,1,0:T(8,128)(2,1)S(1)}, u32[]{:S(2)}, u32[]{:S(2)}) collective-permute-start(bf16[2,256,256]{2,1,0:T(8,128)(2,1)S(1)} %get-tuple-element.91), channel_id=1, source_target_pairs={{0,2},{1,3},{2,4},{3,5},{4,6},{5,7},{6,8},{7,9},{8,10},{9,11},{10,... | collective-permute-start | bytes 786440 | tf_op jit(solution)/shard_map/ppermute | solution.py:15
  79.4 12.2 %collective-permute-start.12 = (bf16[2,256,256]{2,1,0:T(8,128)(2,1)S(1)}, bf16[2,256,256]{2,1,0:T(8,128)(2,1)S(1)}, u32[]{:S(2)}, u32[]{:S(2)}) collective-permute-start(bf16[2,256,256]{2,1,0:T(8,128)(2,1)S(1)} %get-tuple-element.90), channel_id=1, source_target_pairs={{2,0},{3,1},{4,2},{5,3},{6,4},{7,5},{8,6},{9,7},{10,8},{11,9},{12,... | collective-permute-start | bytes 786440 | tf_op jit(solution)/shard_map/ppermute | solution.py:15
  82.5 10.2 %collective-permute-start.10 = (bf16[2,256,256]{2,1,0:T(8,128)(2,1)S(1)}, bf16[2,256,256]{2,1,0:T(8,128)(2,1)S(1)}, u32[]{:S(2)}, u32[]{:S(2)}) collective-permute-start(bf16[2,256,256]{2,1,0:T(8,128)(2,1)S(1)} %get-tuple-element.89), channel_id=1, source_target_pairs={{0,2},{1,3},{2,4},{3,5},{4,6},{5,7},{6,8},{7,9},{8,10},{9,11},{10,... | collective-permute-start | bytes 786440 | tf_op jit(solution)/shard_map/ppermute | solution.py:15
  88.5 10.4 %collective-permute-start.9 = (bf16[2,256,256]{2,1,0:T(8,128)(2,1)S(1)}, bf16[2,256,256]{2,1,0:T(8,128)(2,1)S(1)}, u32[]{:S(2)}, u32[]{:S(2)}) collective-permute-start(bf16[2,256,256]{2,1,0:T(8,128)(2,1)S(1)} %get-tuple-element.88), channel_id=1, source_target_pairs={{2,0},{3,1},{4,2},{5,3},{6,4},{7,5},{8,6},{9,7},{10,8},{11,9},{12,... | collective-permute-start | bytes 786440 | tf_op jit(solution)/shard_map/ppermute | solution.py:15
  100.1 10.4 %collective-permute-start.14 = (bf16[2,128,256]{2,1,0:T(8,128)(2,1)S(1)}, bf16[2,128,256]{2,1,0:T(8,128)(2,1)S(1)}, u32[]{:S(2)}, u32[]{:S(2)}) collective-permute-start(bf16[2,128,256]{2,1,0:T(8,128)(2,1)S(1)} %get-tuple-element.82), channel_id=1, source_target_pairs={{0,1},{1,2},{2,3},{3,4},{4,5},{5,6},{6,7},{7,8},{8,9},{9,10},{10,1... | collective-permute-start | bytes 393224 | tf_op jit(solution)/shard_map/ppermute | solution.py:15
  102.0 8.5 %collective-permute-start.15 = (bf16[2,128,256]{2,1,0:T(8,128)(2,1)S(1)}, bf16[2,128,256]{2,1,0:T(8,128)(2,1)S(1)}, u32[]{:S(2)}, u32[]{:S(2)}) collective-permute-start(bf16[2,128,256]{2,1,0:T(8,128)(2,1)S(1)} %get-tuple-element.83), channel_id=1, source_target_pairs={{1,0},{2,1},{3,2},{4,3},{5,4},{6,5},{7,6},{8,7},{9,8},{10,9},{11,1... | collective-permute-start | bytes 393224 | tf_op jit(solution)/shard_map/ppermute | solution.py:15
  106.8 9.0 %collective-permute-start.19 = (bf16[2,256,256]{2,1,0:T(8,128)(2,1)S(1)}, bf16[2,256,256]{2,1,0:T(8,128)(2,1)S(1)}, u32[]{:S(2)}, u32[]{:S(2)}) collective-permute-start(bf16[2,256,256]{2,1,0:T(8,128)(2,1)S(1)} %get-tuple-element.9), channel_id=1, source_target_pairs={{32,0},{64,32},{96,64},{33,1},{65,33},{97,65},{34,2},{66,34},{98,6... | collective-permute-start | bytes 786440 | tf_op jit(solution)/shard_map/ppermute | solution.py:15
  111.5 11.6 %collective-permute-start.16 = (bf16[2,256,256]{2,1,0:T(8,128)(2,1)S(1)}, bf16[2,256,256]{2,1,0:T(8,128)(2,1)S(1)}, u32[]{:S(2)}, u32[]{:S(2)}) collective-permute-start(bf16[2,256,256]{2,1,0:T(8,128)(2,1)S(1)} %pad_maximum_fusion.26), channel_id=1, source_target_pairs={{32,0},{64,32},{96,64},{33,1},{65,33},{97,65},{34,2},{66,34},{98,6... | collective-permute-start | bytes 786440 | tf_op jit(solution)/shard_map/ppermute | solution.py:15
  116.7 16.9 %collective-permute-start.21 = (bf16[2,256,256]{2,1,0:T(8,128)(2,1)S(1)}, bf16[2,256,256]{2,1,0:T(8,128)(2,1)S(1)}, u32[]{:S(2)}, u32[]{:S(2)}) collective-permute-start(bf16[2,256,256]{2,1,0:T(8,128)(2,1)S(1)} %get-tuple-element.81), channel_id=1, source_target_pairs={{0,2},{1,3},{2,4},{3,5},{4,6},{5,7},{6,8},{7,9},{8,10},{9,11},{10,... | collective-permute-start | bytes 786440 | tf_op jit(solution)/shard_map/ppermute | solution.py:15
  121.2 12.4 %collective-permute-start.20 = (bf16[2,256,256]{2,1,0:T(8,128)(2,1)S(1)}, bf16[2,256,256]{2,1,0:T(8,128)(2,1)S(1)}, u32[]{:S(2)}, u32[]{:S(2)}) collective-permute-start(bf16[2,256,256]{2,1,0:T(8,128)(2,1)S(1)} %get-tuple-element.80), channel_id=1, source_target_pairs={{2,0},{3,1},{4,2},{5,3},{6,4},{7,5},{8,6},{9,7},{10,8},{11,9},{12,... | collective-permute-start | bytes 786440 | tf_op jit(solution)/shard_map/ppermute | solution.py:15
  124.1 10.5 %collective-permute-start.18 = (bf16[2,256,256]{2,1,0:T(8,128)(2,1)S(1)}, bf16[2,256,256]{2,1,0:T(8,128)(2,1)S(1)}, u32[]{:S(2)}, u32[]{:S(2)}) collective-permute-start(bf16[2,256,256]{2,1,0:T(8,128)(2,1)S(1)} %get-tuple-element.79), channel_id=1, source_target_pairs={{0,2},{1,3},{2,4},{3,5},{4,6},{5,7},{6,8},{7,9},{8,10},{9,11},{10,... | collective-permute-start | bytes 786440 | tf_op jit(solution)/shard_map/ppermute | solution.py:15
  130.2 10.4 %collective-permute-start.17 = (bf16[2,256,256]{2,1,0:T(8,128)(2,1)S(1)}, bf16[2,256,256]{2,1,0:T(8,128)(2,1)S(1)}, u32[]{:S(2)}, u32[]{:S(2)}) collective-permute-start(bf16[2,256,256]{2,1,0:T(8,128)(2,1)S(1)} %get-tuple-element.78), channel_id=1, source_target_pairs={{2,0},{3,1},{4,2},{5,3},{6,4},{7,5},{8,6},{9,7},{10,8},{11,9},{12,... | collective-permute-start | bytes 786440 | tf_op jit(solution)/shard_map/ppermute | solution.py:15
  141.7 10.7 %collective-permute-start.22 = (bf16[2,128,256]{2,1,0:T(8,128)(2,1)S(1)}, bf16[2,128,256]{2,1,0:T(8,128)(2,1)S(1)}, u32[]{:S(2)}, u32[]{:S(2)}) collective-permute-start(bf16[2,128,256]{2,1,0:T(8,128)(2,1)S(1)} %get-tuple-element.72), channel_id=1, source_target_pairs={{0,1},{1,2},{2,3},{3,4},{4,5},{5,6},{6,7},{7,8},{8,9},{9,10},{10,1... | collective-permute-start | bytes 393224 | tf_op jit(solution)/shard_map/ppermute | solution.py:15
  143.7 8.8 %collective-permute-start.23 = (bf16[2,128,256]{2,1,0:T(8,128)(2,1)S(1)}, bf16[2,128,256]{2,1,0:T(8,128)(2,1)S(1)}, u32[]{:S(2)}, u32[]{:S(2)}) collective-permute-start(bf16[2,128,256]{2,1,0:T(8,128)(2,1)S(1)} %get-tuple-element.73), channel_id=1, source_target_pairs={{1,0},{2,1},{3,2},{4,3},{5,4},{6,5},{7,6},{8,7},{9,8},{10,9},{11,1... | collective-permute-start | bytes 393224 | tf_op jit(solution)/shard_map/ppermute | solution.py:15
  148.4 8.9 %collective-permute-start.27 = (bf16[2,256,256]{2,1,0:T(8,128)(2,1)S(1)}, bf16[2,256,256]{2,1,0:T(8,128)(2,1)S(1)}, u32[]{:S(2)}, u32[]{:S(2)}) collective-permute-start(bf16[2,256,256]{2,1,0:T(8,128)(2,1)S(1)} %get-tuple-element.3), channel_id=1, source_target_pairs={{32,0},{64,32},{96,64},{33,1},{65,33},{97,65},{34,2},{66,34},{98,6... | collective-permute-start | bytes 786440 | tf_op jit(solution)/shard_map/ppermute | solution.py:15
  153.4 11.0 %collective-permute-start.24 = (bf16[2,256,256]{2,1,0:T(8,128)(2,1)S(1)}, bf16[2,256,256]{2,1,0:T(8,128)(2,1)S(1)}, u32[]{:S(2)}, u32[]{:S(2)}) collective-permute-start(bf16[2,256,256]{2,1,0:T(8,128)(2,1)S(1)} %pad_maximum_fusion.27), channel_id=1, source_target_pairs={{32,0},{64,32},{96,64},{33,1},{65,33},{97,65},{34,2},{66,34},{98,6... | collective-permute-start | bytes 786440 | tf_op jit(solution)/shard_map/ppermute | solution.py:15
  157.2 19.2 %copy-start.8 = (bf16[2,256,256]{2,1,0:T(8,128)(2,1)}, bf16[2,256,256]{2,1,0:T(8,128)(2,1)S(1)}, u32[]{:S(2)}) copy-start(bf16[2,256,256]{2,1,0:T(8,128)(2,1)S(1)} %collective-permute-done.27) | copy-start | bytes 786436
  158.1 18.3 %copy-start.5 = (f32[2,256,768]{2,1,0:T(8,128)}, f32[2,256,768]{2,1,0:T(8,128)S(1)}, u32[]{:S(2)}) copy-start(f32[2,256,768]{2,1,0:T(8,128)S(1)} %get-tuple-element.169) | copy-start | bytes 4718596
  158.2 18.2 %collective-permute-start.29 = (bf16[2,256,256]{2,1,0:T(8,128)(2,1)S(1)}, bf16[2,256,256]{2,1,0:T(8,128)(2,1)S(1)}, u32[]{:S(2)}, u32[]{:S(2)}) collective-permute-start(bf16[2,256,256]{2,1,0:T(8,128)(2,1)S(1)} %get-tuple-element.69), channel_id=1, source_target_pairs={{0,2},{1,3},{2,4},{3,5},{4,6},{5,7},{6,8},{7,9},{8,10},{9,11},{10,... | collective-permute-start | bytes 786440 | tf_op jit(solution)/shard_map/ppermute | solution.py:15
  162.5 13.8 %collective-permute-start.28 = (bf16[2,256,256]{2,1,0:T(8,128)(2,1)S(1)}, bf16[2,256,256]{2,1,0:T(8,128)(2,1)S(1)}, u32[]{:S(2)}, u32[]{:S(2)}) collective-permute-start(bf16[2,256,256]{2,1,0:T(8,128)(2,1)S(1)} %get-tuple-element.68), channel_id=1, source_target_pairs={{2,0},{3,1},{4,2},{5,3},{6,4},{7,5},{8,6},{9,7},{10,8},{11,9},{12,... | collective-permute-start | bytes 786440 | tf_op jit(solution)/shard_map/ppermute | solution.py:15
  165.5 12.1 %collective-permute-start.26 = (bf16[2,256,256]{2,1,0:T(8,128)(2,1)S(1)}, bf16[2,256,256]{2,1,0:T(8,128)(2,1)S(1)}, u32[]{:S(2)}, u32[]{:S(2)}) collective-permute-start(bf16[2,256,256]{2,1,0:T(8,128)(2,1)S(1)} %get-tuple-element.71), channel_id=1, source_target_pairs={{0,2},{1,3},{2,4},{3,5},{4,6},{5,7},{6,8},{7,9},{8,10},{9,11},{10,... | collective-permute-start | bytes 786440 | tf_op jit(solution)/shard_map/ppermute | solution.py:15
  171.6 10.4 %collective-permute-start.25 = (bf16[2,256,256]{2,1,0:T(8,128)(2,1)S(1)}, bf16[2,256,256]{2,1,0:T(8,128)(2,1)S(1)}, u32[]{:S(2)}, u32[]{:S(2)}) collective-permute-start(bf16[2,256,256]{2,1,0:T(8,128)(2,1)S(1)} %get-tuple-element.70), channel_id=1, source_target_pairs={{2,0},{3,1},{4,2},{5,3},{6,4},{7,5},{8,6},{9,7},{10,8},{11,9},{12,... | collective-permute-start | bytes 786440 | tf_op jit(solution)/shard_map/ppermute | solution.py:15
  176.4 6.5 %copy-start.26 = (bf16[2,256,256]{2,1,0:T(8,128)(2,1)}, bf16[2,256,256]{2,1,0:T(8,128)(2,1)S(1)}, u32[]{:S(2)}) copy-start(bf16[2,256,256]{2,1,0:T(8,128)(2,1)S(1)} %collective-permute-done.29) | copy-start | bytes 786436
  176.4 6.5 %copy-start.28 = (bf16[2,256,256]{2,1,0:T(8,128)(2,1)}, bf16[2,256,256]{2,1,0:T(8,128)(2,1)S(1)}, u32[]{:S(2)}) copy-start(bf16[2,256,256]{2,1,0:T(8,128)(2,1)S(1)} %collective-permute-done.28) | copy-start | bytes 786436
  184.8 3.8 %copy-start.15 = (f32[768,512]{1,0:T(8,128)S(1)}, f32[768,512]{1,0:T(8,128)}, u32[]{:S(2)}) copy-start(f32[768,512]{1,0:T(8,128)} %bitcast_add_fusion) | copy-start | bytes 4718596
  191.2 2.7 %collective-permute-start.32 = (bf16[2,2,2,2,56,512]{5,4,3,2,1,0:T(8,128)(2,1)S(1)}, bf16[2,2,2,2,56,512]{5,4,3,2,1,0:T(8,128)(2,1)}, u32[]{:S(2)}, u32[]{:S(2)}) collective-permute-start(bf16[2,2,2,2,56,512]{5,4,3,2,1,0:T(8,128)(2,1)S(1)} %fusion.70), channel_id=1, source_target_pairs={{0,1},{1,0},{2,3},{3,2},{4,5},{5,4},{6,7},{7,6},{8,9},{9,8},{10,11... | collective-permute-start | bytes 2752520 | tf_op jit(solution)/shard_map/ppermute | solution.py:199
  191.3 2.6 %copy-start.1 = (f32[2,2,2,2,2,56,512]{6,5,4,3,2,1,0:T(8,128)S(1)}, f32[2,2,2,2,2,56,512]{6,5,4,3,2,1,0:T(8,128)}, u32[]{:S(2)}) copy-start(f32[2,2,2,2,2,56,512]{6,5,4,3,2,1,0:T(8,128)} %copy-done) | copy-start | bytes 11010052
  192.0 3.8 %copy-start.7 = (bf16[2,256,256]{1,2,0:T(8,128)(2,1)S(1)}, bf16[2,256,256]{1,2,0:T(8,128)(2,1)}, u32[]{:S(2)}) copy-start(bf16[2,256,256]{1,2,0:T(8,128)(2,1)} %copy-done.6) | copy-start | bytes 786436
  195.7 13.5 %collective-permute-start.33 = (bf16[2,2,2,56,512]{4,3,2,1,0:T(8,128)(2,1)S(1)}, bf16[2,2,2,56,512]{4,3,2,1,0:T(8,128)(2,1)S(1)}, u32[]{:S(2)}, u32[]{:S(2)}) collective-permute-start(bf16[2,2,2,56,512]{4,3,2,1,0:T(8,128)(2,1)S(1)} %fusion.173), channel_id=1, source_target_pairs={{0,2},{1,3},{2,0},{3,1},{4,6},{5,7},{6,4},{7,5},{8,10},{9,11},{10,... | collective-permute-start | bytes 1376264 | tf_op jit(solution)/shard_map/ppermute | solution.py:199
  196.5 14.7 %copy-start.9 = (bf16[2,256,256]{2,1,0:T(8,128)(2,1)S(1)}, bf16[2,256,256]{2,1,0:T(8,128)(2,1)}, u32[]{:S(2)}) copy-start(bf16[2,256,256]{2,1,0:T(8,128)(2,1)} %copy-done.8) | copy-start | bytes 786436
  196.5 14.7 %copy-start.27 = (bf16[2,256,256]{2,1,0:T(8,128)(2,1)S(1)}, bf16[2,256,256]{2,1,0:T(8,128)(2,1)}, u32[]{:S(2)}) copy-start(bf16[2,256,256]{2,1,0:T(8,128)(2,1)} %copy-done.26) | copy-start | bytes 786436
  196.5 14.7 %copy-start.29 = (bf16[2,256,256]{2,1,0:T(8,128)(2,1)S(1)}, bf16[2,256,256]{2,1,0:T(8,128)(2,1)}, u32[]{:S(2)}) copy-start(bf16[2,256,256]{2,1,0:T(8,128)(2,1)} %copy-done.28) | copy-start | bytes 786436
  196.5 22.7 %collective-permute-start.30 = (bf16[2,128,256]{2,1,0:T(8,128)(2,1)S(1)}, bf16[2,128,256]{2,1,0:T(8,128)(2,1)S(1)}, u32[]{:S(2)}, u32[]{:S(2)}) collective-permute-start(bf16[2,128,256]{2,1,0:T(8,128)(2,1)S(1)} %get-tuple-element.62), channel_id=1, source_target_pairs={{0,1},{1,2},{2,3},{3,4},{4,5},{5,6},{6,7},{7,8},{8,9},{9,10},{10,1... | collective-permute-start | bytes 393224 | tf_op jit(solution)/shard_map/ppermute | solution.py:15
  198.7 20.5 %collective-permute-start.31 = (bf16[2,128,256]{2,1,0:T(8,128)(2,1)S(1)}, bf16[2,128,256]{2,1,0:T(8,128)(2,1)S(1)}, u32[]{:S(2)}, u32[]{:S(2)}) collective-permute-start(bf16[2,128,256]{2,1,0:T(8,128)(2,1)S(1)} %get-tuple-element.63), channel_id=1, source_target_pairs={{1,0},{2,1},{3,2},{4,3},{5,4},{6,5},{7,6},{8,7},{9,8},{10,9},{11,1... | collective-permute-start | bytes 393224 | tf_op jit(solution)/shard_map/ppermute | solution.py:15
  209.5 6.1 %collective-permute-start.34 = (bf16[2,2,56,512]{3,2,1,0:T(8,128)(2,1)S(1)}, bf16[2,2,56,512]{3,2,1,0:T(8,128)(2,1)S(1)}, u32[]{:S(2)}, u32[]{:S(2)}) collective-permute-start(bf16[2,2,56,512]{3,2,1,0:T(8,128)(2,1)S(1)} %fusion.227), channel_id=1, source_target_pairs={{0,8},{1,9},{2,10},{3,11},{4,12},{5,13},{6,14},{7,15},{8,0},{9,1},... | collective-permute-start | bytes 688136 | tf_op jit(solution)/shard_map/ppermute | solution.py:199
  211.2 8.0 %copy-start.14 = (f32[2,256,256]{2,1,0:T(8,128)S(1)}, f32[2,256,256]{2,1,0:T(8,128)}, u32[]{:S(2)}) copy-start(f32[2,256,256]{2,1,0:T(8,128)} %get-tuple-element.6) | copy-start | bytes 1572868
  215.7 6.7 %copy-start.11 = (f32[1,2,256,256]{3,2,1,0:T(8,128)S(1)}, f32[1,2,256,256]{3,2,1,0:T(8,128)}, u32[]{:S(2)}) copy-start(f32[1,2,256,256]{3,2,1,0:T(8,128)} %get-tuple-element.28) | copy-start | bytes 1572868
  215.8 6.7 %copy-start.12 = (f32[2,256,256]{2,1,0:T(8,128)S(1)}, f32[2,256,256]{2,1,0:T(8,128)}, u32[]{:S(2)}) copy-start(f32[2,256,256]{2,1,0:T(8,128)} %get-tuple-element.10) | copy-start | bytes 1572868
  215.8 6.7 %copy-start.13 = (f32[2,256,256]{2,1,0:T(8,128)S(1)}, f32[2,256,256]{2,1,0:T(8,128)}, u32[]{:S(2)}) copy-start(f32[2,256,256]{2,1,0:T(8,128)} %get-tuple-element.4) | copy-start | bytes 1572868
  215.8 6.7 %copy-start.20 = (f32[1,2,128,256]{3,2,1,0:T(8,128)S(1)}, f32[1,2,128,256]{3,2,1,0:T(8,128)}, u32[]{:S(2)}) copy-start(f32[1,2,128,256]{3,2,1,0:T(8,128)} %get-tuple-element.22) | copy-start | bytes 786436
  215.8 6.7 %copy-start.21 = (f32[1,2,128,256]{3,2,1,0:T(8,128)S(1)}, f32[1,2,128,256]{3,2,1,0:T(8,128)}, u32[]{:S(2)}) copy-start(f32[1,2,128,256]{3,2,1,0:T(8,128)} %get-tuple-element.25) | copy-start | bytes 786436
  215.8 6.7 %copy-start.22 = (f32[1,2,128,256]{3,2,1,0:T(8,128)S(1)}, f32[1,2,128,256]{3,2,1,0:T(8,128)}, u32[]{:S(2)}) copy-start(f32[1,2,128,256]{3,2,1,0:T(8,128)} %get-tuple-element.38) | copy-start | bytes 786436
  215.8 6.7 %copy-start.23 = (f32[1,2,128,256]{3,2,1,0:T(8,128)S(1)}, f32[1,2,128,256]{3,2,1,0:T(8,128)}, u32[]{:S(2)}) copy-start(f32[1,2,128,256]{3,2,1,0:T(8,128)} %get-tuple-element.45) | copy-start | bytes 786436
  215.8 6.7 %copy-start.24 = (f32[1,2,128,256]{3,2,1,0:T(8,128)S(1)}, f32[1,2,128,256]{3,2,1,0:T(8,128)}, u32[]{:S(2)}) copy-start(f32[1,2,128,256]{3,2,1,0:T(8,128)} %get-tuple-element.34) | copy-start | bytes 786436
  215.8 6.7 %copy-start.25 = (f32[1,2,128,256]{3,2,1,0:T(8,128)S(1)}, f32[1,2,128,256]{3,2,1,0:T(8,128)}, u32[]{:S(2)}) copy-start(f32[1,2,128,256]{3,2,1,0:T(8,128)} %get-tuple-element.43) | copy-start | bytes 786436
  215.9 6.4 %collective-permute-start.35 = (bf16[2,56,512]{2,1,0:T(8,128)(2,1)S(1)}, bf16[2,56,512]{2,1,0:T(8,128)(2,1)S(1)}, u32[]{:S(2)}, u32[]{:S(2)}) collective-permute-start(bf16[2,56,512]{2,1,0:T(8,128)(2,1)S(1)} %fusion.255), channel_id=1, source_target_pairs={{0,16},{1,17},{2,18},{3,19},{4,20},{5,21},{6,22},{7,23},{8,24},{9,... | collective-permute-start | bytes 344072 | tf_op jit(solution)/shard_map/ppermute | solution.py:199
  222.3 5.8 %collective-permute-start.36 = (bf16[56,512]{1,0:T(8,128)(2,1)S(1)}, bf16[56,512]{1,0:T(8,128)(2,1)S(1)}, u32[]{:S(2)}, u32[]{:S(2)}) collective-permute-start(bf16[56,512]{1,0:T(8,128)(2,1)S(1)} %fusion.256), channel_id=1, source_target_pairs={{0,4},{1,5},{2,6},{3,7},{4,0},{5,1},{6,2},{7,3},{8,12},{9,13},{10,... | collective-permute-start | bytes 172040 | tf_op jit(solution)/shard_map/ppermute | solution.py:199
  (5 other events, 5.7 us)

commit v12 on v8

--- a/solution.py
+++ b/solution.py
@@ -239,11 +239,13 @@
                 flowing, conv_term, out_term = backward_far(
                     flowing, stored[layer], conv_mat[layer], out_mat[layer], far_hops
                 )
-            elif layer == 0 and depth == 2 and step > 0:
+            elif layer == 0 and depth == 2 and 0 < step < section_count - 1:
                 flowing, conv_term, out_term = backward_near_pieces(
                     flowing, stored[layer], conv_mat[layer], out_mat[layer]
                 )
             else:
+                if isinstance(flowing, tuple):
+                    flowing = join_rows(flowing[0], flowing[1], NEAR)
                 flowing, conv_term, out_term = backward_layer(
                     flowing, stored[layer], conv_mat[layer], out_mat[layer], layer, far_hops
                 )

time: 231 us -> 235 us (1.017)
  waiting for transfers between devices: 69.6 us -> 72.6 us
    dot_general x2 -> x3, matrix products: 3.21 us -> 7.26 us  [backward_layer(): jnp.einsum('mpc,mpd->cd', taps, grad_pre, preferred_element_type=jnp.floa...]
    dot_general x3 -> x2, matrix products: 8.24 us -> 4.5 us  [backward_near_pieces(): jnp.einsum('mpc,mpd->cd', taps, grad_pre, preferred_element_type=f32)]
    ppermute x5, waiting for transfers between devices: 19.1 us -> 22.5 us  [halving_scatter(): got = lax.ppermute(sends, 'seq', pairs)]
    ppermute x5, starting transfers between devices: 5.34 us -> 2.4 us  [halving_scatter(): got = lax.ppermute(sends, 'seq', pairs)]
  transfers between devices with their start and end apart: 37 -> 37, of which waited for: 15 -> 15; matrix products, arithmetic and copies ran while one was open for 17% -> 16% of each run, Pallas kernels for 0% -> 0%
where the time goes in v12:
time: 235 us; the launch traced here: 234 us
  starting transfers between devices  95.8 us (41%)
  waiting for transfers between devices  72.6 us (31%)
  matrix products  41.2 us (18%)
  other arithmetic  16.4 us (7%)
  local copies, waits for them, and re-layouts  6.25 us (3%)
    ppermute x32, starting transfers between devices, shifted(): lax.ppermute(value, axis, [(source, source + steps) for source in range(l...  93.4 us
    ppermute x32, waiting for transfers between devices, shifted(): lax.ppermute(value, axis, [(source, source + steps) for source in range(l...  50.1 us
    ppermute x5, waiting for transfers between devices, halving_scatter(): got = lax.ppermute(sends, 'seq', pairs)  22.5 us
    dot_general x7, matrix products, mm(): return jnp.einsum('mpc,cd->mpd', a, b, preferred_element_type=jnp.float32)  8.01 us
    dot_general x3, matrix products, backward_layer(): jnp.einsum('mpc,mpd->cd', taps, grad_pre, preferred_element_type=jnp.floa...  7.26 us
  transfers between devices with their start and end apart: 37, of which 15 were waited for; matrix products, arithmetic and copies ran while one was open for 16% of the time, Pallas kernels for 0%

profile of v12, /device:TPU:24, one launch (start us, length us, event | category | flops | bytes accessed | tf_op | source)
XLA Modules:
  0.0 234.2 jit_solution(13828460177648621154)
XLA Ops:
  1.7 1.9 collective-permute-start
  3.6 3.6 %collective-permute-start.1 = (bf16[2,128,256]{2,1,0:T(8,128)(2,1)S(1)}, bf16[2,128,256]{2,1,0:T(8,128)(2,1)S(1)}, u32[]{:S(2)}, u32[]{:S(2)}) collective-permute-start(bf16[2,128,256]{2,1,0:T(8,128)(2,1)S(1)} %get-tuple-element.122), channel_id=1, source_target_pairs={{1,0},{2,1},{3,2},{4,3},{5,4},{6,5},{7,6},{8,7},{9,8},{10,9},{11,1... | collective-permute-start | bytes 393224 | tf_op jit(solution)/shard_map/ppermute | solution.py:15
  7.3 2.9 %fusion.197 = f32[2,512,512]{1,2,0:T(8,128)} fusion(bf16[1,2,3,256,512]{4,3,2,1,0:T(8,128)(2,1)} %param.6, bf16[1,2,512,256]{3,2,1,0:T(8,128)(2,1)} %param.4), kind=kOutput, calls=%fused_computation.309 | convolution fusion | flops 268435456 | bytes 2883584 | tf_op jit(solution)/shard_map/mpc,cd->mpd/dot_general | solution.py:32
  10.3 1.8 fusion.99
  12.2 1.4 add_add_fusion.1
  14.9 5.6 %collective-permute-start.2 = (bf16[2,512,256]{2,1,0:T(8,128)(2,1)S(1)}, bf16[2,512,256]{2,1,0:T(8,128)(2,1)S(1)}, u32[]{:S(2)}, u32[]{:S(2)}) collective-permute-start(bf16[2,512,256]{2,1,0:T(8,128)(2,1)S(1)} %fusion.2), channel_id=1, source_target_pairs={{0,2},{1,3},{2,4},{3,5},{4,6},{5,7},{6,8},{7,9},{8,10},{9,11},{10,... | collective-permute-start | bytes 1572872 | tf_op jit(solution)/shard_map/ppermute | solution.py:15
  20.7 1.9 collective-permute-start.3
  23.1 8.0 %collective-permute-done.2 = bf16[2,512,256]{2,1,0:T(8,128)(2,1)S(1)} collective-permute-done((bf16[2,512,256]{2,1,0:T(8,128)(2,1)S(1)}, bf16[2,512,256]{2,1,0:T(8,128)(2,1)S(1)}, u32[]{:S(2)}, u32[]{:S(2)}) %collective-permute-start.2) | collective-permute-done | bytes 524320 | tf_op jit(solution)/shard_map/ppermute | solution.py:15
  31.6 4.8 %collective-permute-done.3 = bf16[2,512,256]{2,1,0:T(8,128)(2,1)S(1)} collective-permute-done((bf16[2,512,256]{2,1,0:T(8,128)(2,1)S(1)}, bf16[2,512,256]{2,1,0:T(8,128)(2,1)S(1)}, u32[]{:S(2)}, u32[]{:S(2)}) %collective-permute-start.3) | collective-permute-done | bytes 524320 | tf_op jit(solution)/shard_map/ppermute | solution.py:15
  38.7 1.9 collective-permute-start.5
  40.7 3.9 %collective-permute-start.4 = (bf16[2,512,256]{2,1,0:T(8,128)(2,1)S(1)}, bf16[2,512,256]{2,1,0:T(8,128)(2,1)S(1)}, u32[]{:S(2)}, u32[]{:S(2)}) collective-permute-start(bf16[2,512,256]{2,1,0:T(8,128)(2,1)S(1)} %get-tuple-element.50), channel_id=1, source_target_pairs={{2,0},{3,1},{4,2},{5,3},{6,4},{7,5},{8,6},{9,7},{10,8},{11,9},{12,... | collective-permute-start | bytes 1572872 | tf_op jit(solution)/shard_map/ppermute | solution.py:15
  46.0 5.4 %collective-permute-done.5 = bf16[2,512,256]{2,1,0:T(8,128)(2,1)S(1)} collective-permute-done((bf16[2,512,256]{2,1,0:T(8,128)(2,1)S(1)}, bf16[2,512,256]{2,1,0:T(8,128)(2,1)S(1)}, u32[]{:S(2)}, u32[]{:S(2)}) %collective-permute-start.5) | collective-permute-done | bytes 524320 | tf_op jit(solution)/shard_map/ppermute | solution.py:15
  51.5 4.7 %collective-permute-done.4 = bf16[2,512,256]{2,1,0:T(8,128)(2,1)S(1)} collective-permute-done((bf16[2,512,256]{2,1,0:T(8,128)(2,1)S(1)}, bf16[2,512,256]{2,1,0:T(8,128)(2,1)S(1)}, u32[]{:S(2)}, u32[]{:S(2)}) %collective-permute-start.4) | collective-permute-done | bytes 524320 | tf_op jit(solution)/shard_map/ppermute | solution.py:15
  58.2 1.9 collective-permute-start.6
  60.1 3.6 %collective-permute-start.7 = (bf16[2,128,256]{2,1,0:T(8,128)(2,1)S(1)}, bf16[2,128,256]{2,1,0:T(8,128)(2,1)S(1)}, u32[]{:S(2)}, u32[]{:S(2)}) collective-permute-start(bf16[2,128,256]{2,1,0:T(8,128)(2,1)S(1)} %get-tuple-element.49), channel_id=1, source_target_pairs={{1,0},{2,1},{3,2},{4,3},{5,4},{6,5},{7,6},{8,7},{9,8},{10,9},{11,1... | collective-permute-start | bytes 393224 | tf_op jit(solution)/shard_map/ppermute | solution.py:15
  63.9 1.3 collective-permute-start.11
  65.2 2.2 fusion.69
  68.5 1.3 collective-permute-start.8
  69.8 4.3 %collective-permute-done.11 = bf16[2,256,256]{2,1,0:T(8,128)(2,1)S(1)} collective-permute-done((bf16[2,256,256]{2,1,0:T(8,128)(2,1)S(1)}, bf16[2,256,256]{2,1,0:T(8,128)(2,1)S(1)}, u32[]{:S(2)}, u32[]{:S(2)}) %collective-permute-start.11) | collective-permute-done | bytes 262176 | tf_op jit(solution)/shard_map/ppermute | solution.py:15
  75.1 5.5 %collective-permute-start.13 = (bf16[2,256,256]{2,1,0:T(8,128)(2,1)S(1)}, bf16[2,256,256]{2,1,0:T(8,128)(2,1)S(1)}, u32[]{:S(2)}, u32[]{:S(2)}) collective-permute-start(bf16[2,256,256]{2,1,0:T(8,128)(2,1)S(1)} %get-tuple-element.87), channel_id=1, source_target_pairs={{0,2},{1,3},{2,4},{3,5},{4,6},{5,7},{6,8},{7,9},{8,10},{9,11},{10,... | collective-permute-start | bytes 786440 | tf_op jit(solution)/shard_map/ppermute | solution.py:15
  80.6 2.1 collective-permute-start.12
  83.7 6.0 %collective-permute-start.10 = (bf16[2,256,256]{2,1,0:T(8,128)(2,1)S(1)}, bf16[2,256,256]{2,1,0:T(8,128)(2,1)S(1)}, u32[]{:S(2)}, u32[]{:S(2)}) collective-permute-start(bf16[2,256,256]{2,1,0:T(8,128)(2,1)S(1)} %get-tuple-element.85), channel_id=1, source_target_pairs={{0,2},{1,3},{2,4},{3,5},{4,6},{5,7},{6,8},{7,9},{8,10},{9,11},{10,... | collective-permute-start | bytes 786440 | tf_op jit(solution)/shard_map/ppermute | solution.py:15
  89.7 1.9 collective-permute-start.9
  93.9 6.2 %collective-permute-done.9 = bf16[2,256,256]{2,1,0:T(8,128)(2,1)S(1)} collective-permute-done((bf16[2,256,256]{2,1,0:T(8,128)(2,1)S(1)}, bf16[2,256,256]{2,1,0:T(8,128)(2,1)S(1)}, u32[]{:S(2)}, u32[]{:S(2)}) %collective-permute-start.9) | collective-permute-done | bytes 262176 | tf_op jit(solution)/shard_map/ppermute | solution.py:15
  101.3 1.9 collective-permute-start.14
  103.3 3.6 %collective-permute-start.15 = (bf16[2,128,256]{2,1,0:T(8,128)(2,1)S(1)}, bf16[2,128,256]{2,1,0:T(8,128)(2,1)S(1)}, u32[]{:S(2)}, u32[]{:S(2)}) collective-permute-start(bf16[2,128,256]{2,1,0:T(8,128)(2,1)S(1)} %get-tuple-element.79), channel_id=1, source_target_pairs={{1,0},{2,1},{3,2},{4,3},{5,4},{6,5},{7,6},{8,7},{9,8},{10,9},{11,1... | collective-permute-start | bytes 393224 | tf_op jit(solution)/shard_map/ppermute | solution.py:15
  106.9 1.1 fusion.305
  108.0 1.3 collective-permute-start.19
  109.3 2.2 fusion.21
  112.8 1.3 collective-permute-start.16
  114.1 2.9 %collective-permute-done.19 = bf16[2,256,256]{2,1,0:T(8,128)(2,1)S(1)} collective-permute-done((bf16[2,256,256]{2,1,0:T(8,128)(2,1)S(1)}, bf16[2,256,256]{2,1,0:T(8,128)(2,1)S(1)}, u32[]{:S(2)}, u32[]{:S(2)}) %collective-permute-start.19) | collective-permute-done | bytes 262176 | tf_op jit(solution)/shard_map/ppermute | solution.py:15
  117.9 4.5 %collective-permute-start.21 = (bf16[2,256,256]{2,1,0:T(8,128)(2,1)S(1)}, bf16[2,256,256]{2,1,0:T(8,128)(2,1)S(1)}, u32[]{:S(2)}, u32[]{:S(2)}) collective-permute-start(bf16[2,256,256]{2,1,0:T(8,128)(2,1)S(1)} %get-tuple-element.77), channel_id=1, source_target_pairs={{0,2},{1,3},{2,4},{3,5},{4,6},{5,7},{6,8},{7,9},{8,10},{9,11},{10,... | collective-permute-start | bytes 786440 | tf_op jit(solution)/shard_map/ppermute | solution.py:15
  122.5 1.9 collective-permute-start.20
  125.3 6.0 %collective-permute-start.18 = (bf16[2,256,256]{2,1,0:T(8,128)(2,1)S(1)}, bf16[2,256,256]{2,1,0:T(8,128)(2,1)S(1)}, u32[]{:S(2)}, u32[]{:S(2)}) collective-permute-start(bf16[2,256,256]{2,1,0:T(8,128)(2,1)S(1)} %get-tuple-element.75), channel_id=1, source_target_pairs={{0,2},{1,3},{2,4},{3,5},{4,6},{5,7},{6,8},{7,9},{8,10},{9,11},{10,... | collective-permute-start | bytes 786440 | tf_op jit(solution)/shard_map/ppermute | solution.py:15
  131.4 1.9 collective-permute-start.17
  135.9 5.9 %collective-permute-done.17 = bf16[2,256,256]{2,1,0:T(8,128)(2,1)S(1)} collective-permute-done((bf16[2,256,256]{2,1,0:T(8,128)(2,1)S(1)}, bf16[2,256,256]{2,1,0:T(8,128)(2,1)S(1)}, u32[]{:S(2)}, u32[]{:S(2)}) %collective-permute-start.17) | collective-permute-done | bytes 262176 | tf_op jit(solution)/shard_map/ppermute | solution.py:15
  143.0 1.9 collective-permute-start.22
  144.9 3.6 %collective-permute-start.23 = (bf16[2,128,256]{2,1,0:T(8,128)(2,1)S(1)}, bf16[2,128,256]{2,1,0:T(8,128)(2,1)S(1)}, u32[]{:S(2)}, u32[]{:S(2)}) collective-permute-start(bf16[2,128,256]{2,1,0:T(8,128)(2,1)S(1)} %get-tuple-element.69), channel_id=1, source_target_pairs={{1,0},{2,1},{3,2},{4,3},{5,4},{6,5},{7,6},{8,7},{9,8},{10,9},{11,1... | collective-permute-start | bytes 393224 | tf_op jit(solution)/shard_map/ppermute | solution.py:15
  149.6 1.5 collective-permute-start.27
  151.2 2.3 fusion.29
  154.7 1.3 collective-permute-start.24
  156.0 2.5 %collective-permute-done.27 = bf16[2,256,256]{2,1,0:T(8,128)(2,1)S(1)} collective-permute-done((bf16[2,256,256]{2,1,0:T(8,128)(2,1)S(1)}, bf16[2,256,256]{2,1,0:T(8,128)(2,1)S(1)}, u32[]{:S(2)}, u32[]{:S(2)}) %collective-permute-start.27) | collective-permute-done | bytes 262176 | tf_op jit(solution)/shard_map/ppermute | solution.py:15
  159.5 4.3 %collective-permute-start.29 = (bf16[2,256,256]{2,1,0:T(8,128)(2,1)S(1)}, bf16[2,256,256]{2,1,0:T(8,128)(2,1)S(1)}, u32[]{:S(2)}, u32[]{:S(2)}) collective-permute-start(bf16[2,256,256]{2,1,0:T(8,128)(2,1)S(1)} %get-tuple-element.65), channel_id=1, source_target_pairs={{0,2},{1,3},{2,4},{3,5},{4,6},{5,7},{6,8},{7,9},{8,10},{9,11},{10,... | collective-permute-start | bytes 786440 | tf_op jit(solution)/shard_map/ppermute | solution.py:15
  163.8 1.9 collective-permute-start.28
  166.8 6.0 %collective-permute-start.26 = (bf16[2,256,256]{2,1,0:T(8,128)(2,1)S(1)}, bf16[2,256,256]{2,1,0:T(8,128)(2,1)S(1)}, u32[]{:S(2)}, u32[]{:S(2)}) collective-permute-start(bf16[2,256,256]{2,1,0:T(8,128)(2,1)S(1)} %get-tuple-element.67), channel_id=1, source_target_pairs={{0,2},{1,3},{2,4},{3,5},{4,6},{5,7},{6,8},{7,9},{8,10},{9,11},{10,... | collective-permute-start | bytes 786440 | tf_op jit(solution)/shard_map/ppermute | solution.py:15
  172.8 1.9 collective-permute-start.25
  174.8 2.2 bitcast_add_fusion
  177.8 5.4 %collective-permute-done.25 = bf16[2,256,256]{2,1,0:T(8,128)(2,1)S(1)} collective-permute-done((bf16[2,256,256]{2,1,0:T(8,128)(2,1)S(1)}, bf16[2,256,256]{2,1,0:T(8,128)(2,1)S(1)}, u32[]{:S(2)}, u32[]{:S(2)}) %collective-permute-start.25) | collective-permute-done | bytes 262176 | tf_op jit(solution)/shard_map/ppermute | solution.py:15
  183.3 1.3 multiply_convert_fusion.1
  186.1 1.2 concatenate.275
  187.3 4.1 %bitcast_add_fusion.3 = f32[768,512]{1,0:T(8,128)S(1)} fusion(f32[768,512,1]{1,0,2:T(8,128)} %fusion.29, f32[768,512,1]{1,0,2:T(8,128)} %fusion.21, f32[768,512,1]{1,0,2:T(8,128)} %fusion.69, bf16[2,512,256]{1,2,0:T(8,128)(2,1)} %get-tuple-element.55, bf16[2,512,256]{1,2,0:T(8,128)(2,1)} %get-tuple-element.54, ...), kind=kOutput, calls=%fused_computation.12 | convolution fusion | flops 816447488 | bytes 8912896 | tf_op jit(solution)/shard_map/mpc,mpd->cd/dot_general | solution.py:62
  192.0 1.8 copy-done
  193.8 1.1 fusion.63
  194.9 2.8 %collective-permute-done.32 = bf16[2,2,2,2,56,512]{5,4,3,2,1,0:T(8,128)(2,1)} collective-permute-done((bf16[2,2,2,2,56,512]{5,4,3,2,1,0:T(8,128)(2,1)}, bf16[2,2,2,2,56,512]{5,4,3,2,1,0:T(8,128)(2,1)}, u32[]{:S(2)}, u32[]{:S(2)}) %collective-permute-start.32) | collective-permute-done | bytes 917536 | tf_op jit(solution)/shard_map/ppermute | solution.py:199
  197.7 2.8 %fusion.1 = f32[2,2,2,2,56,512]{5,4,3,2,1,0:T(8,128)S(1)} fusion(bf16[2,2,2,2,56,512]{5,4,3,2,1,0:T(8,128)(2,1)} %collective-permute-done.32, f32[2,2,2,2,2,56,512]{6,5,4,3,2,1,0:T(8,128)} %copy-done, pred[]{:T(512)S(6)} %eq.23), kind=kLoop, calls=%fused_computation.5 | loop fusion | flops 1376256 | bytes 6422529 | tf_op jit(solution)/shard_map/add | solution.py:201
  201.8 2.2 collective-permute-start.30
  204.0 3.5 %collective-permute-start.31 = (bf16[2,128,256]{2,1,0:T(8,128)(2,1)S(1)}, bf16[2,128,256]{2,1,0:T(8,128)(2,1)S(1)}, u32[]{:S(2)}, u32[]{:S(2)}) collective-permute-start(bf16[2,128,256]{2,1,0:T(8,128)(2,1)S(1)} %get-tuple-element.47), channel_id=1, source_target_pairs={{1,0},{2,1},{3,2},{4,3},{5,4},{6,5},{7,6},{8,7},{9,8},{10,9},{11,1... | collective-permute-start | bytes 393224 | tf_op jit(solution)/shard_map/ppermute | solution.py:15
  207.6 6.6 %collective-permute-done.33 = bf16[2,2,2,56,512]{4,3,2,1,0:T(8,128)(2,1)S(1)} collective-permute-done((bf16[2,2,2,56,512]{4,3,2,1,0:T(8,128)(2,1)S(1)}, bf16[2,2,2,56,512]{4,3,2,1,0:T(8,128)(2,1)S(1)}, u32[]{:S(2)}, u32[]{:S(2)}) %collective-permute-start.33) | collective-permute-done | bytes 458784 | tf_op jit(solution)/shard_map/ppermute | solution.py:199
  214.4 1.1 collective-permute-start.34
  215.5 1.3 fusion.80
  216.9 3.6 %collective-permute-done.34 = bf16[2,2,56,512]{3,2,1,0:T(8,128)(2,1)S(1)} collective-permute-done((bf16[2,2,56,512]{3,2,1,0:T(8,128)(2,1)S(1)}, bf16[2,2,56,512]{3,2,1,0:T(8,128)(2,1)S(1)}, u32[]{:S(2)}, u32[]{:S(2)}) %collective-permute-start.34) | collective-permute-done | bytes 229408 | tf_op jit(solution)/shard_map/ppermute | solution.py:199
  221.0 6.1 %collective-permute-done.35 = bf16[2,56,512]{2,1,0:T(8,128)(2,1)S(1)} collective-permute-done((bf16[2,56,512]{2,1,0:T(8,128)(2,1)S(1)}, bf16[2,56,512]{2,1,0:T(8,128)(2,1)S(1)}, u32[]{:S(2)}, u32[]{:S(2)}) %collective-permute-start.35) | collective-permute-done | bytes 114720 | tf_op jit(solution)/shard_map/ppermute | solution.py:199
  228.3 1.2 fusion.20
  229.5 3.4 %collective-permute-done.36 = bf16[56,512]{1,0:T(8,128)(2,1)S(1)} collective-permute-done((bf16[56,512]{1,0:T(8,128)(2,1)S(1)}, bf16[56,512]{1,0:T(8,128)(2,1)S(1)}, u32[]{:S(2)}, u32[]{:S(2)}) %collective-permute-start.36) | collective-permute-done | bytes 57376 | tf_op jit(solution)/shard_map/ppermute | solution.py:199
  (178 shorter events, 34.1 us)
Async XLA Ops:
  0.6 9.5 %copy-start.3 = (bf16[1,2,512,256]{3,2,1,0:T(8,128)(2,1)S(1)}, bf16[1,2,512,256]{3,2,1,0:T(8,128)(2,1)}, u32[]{:S(2)}) copy-start(bf16[1,2,512,256]{3,2,1,0:T(8,128)(2,1)} %param.4) | copy-start | bytes 1572868
  1.7 8.6 %collective-permute-start = (bf16[2,128,256]{2,1,0:T(8,128)(2,1)S(1)}, bf16[2,128,256]{2,1,0:T(8,128)(2,1)S(1)}, u32[]{:S(2)}, u32[]{:S(2)}) collective-permute-start(bf16[2,128,256]{2,1,0:T(8,128)(2,1)S(1)} %get-tuple-element.123), channel_id=1, source_target_pairs={{0,1},{1,2},{2,3},{3,4},{4,5},{5,6},{6,7},{7,8},{8,9},{9,10},{10,1... | collective-permute-start | bytes 393224 | tf_op jit(solution)/shard_map/ppermute | solution.py:15
  3.6 8.5 %collective-permute-start.1 = (bf16[2,128,256]{2,1,0:T(8,128)(2,1)S(1)}, bf16[2,128,256]{2,1,0:T(8,128)(2,1)S(1)}, u32[]{:S(2)}, u32[]{:S(2)}) collective-permute-start(bf16[2,128,256]{2,1,0:T(8,128)(2,1)S(1)} %get-tuple-element.122), channel_id=1, source_target_pairs={{1,0},{2,1},{3,2},{4,3},{5,4},{6,5},{7,6},{8,7},{9,8},{10,9},{11,1... | collective-permute-start | bytes 393224 | tf_op jit(solution)/shard_map/ppermute | solution.py:15
  10.2 2.0 copy-start.2
  10.2 140.9 %copy-start.12 = (bf16[2,384,256]{2,1,0:T(8,128)(2,1)}, bf16[2,384,256]{2,1,0:T(8,128)(2,1)S(1)}, u32[]{:S(2)}) copy-start(bf16[2,384,256]{2,1,0:T(8,128)(2,1)S(1)} %get-tuple-element.120) | copy-start | bytes 1179652
  10.2 140.9 %copy-start.13 = (bf16[2,384,256]{2,1,0:T(8,128)(2,1)}, bf16[2,384,256]{2,1,0:T(8,128)(2,1)S(1)}, u32[]{:S(2)}) copy-start(bf16[2,384,256]{2,1,0:T(8,128)(2,1)S(1)} %get-tuple-element.121) | copy-start | bytes 1179652
  10.3 55.0 %copy-start.24 = (bf16[2,128,256]{2,1,0:T(8,128)(2,1)}, bf16[2,128,256]{2,1,0:T(8,128)(2,1)S(1)}, u32[]{:S(2)}) copy-start(bf16[2,128,256]{2,1,0:T(8,128)(2,1)S(1)} %collective-permute-done) | copy-start | bytes 393220
  13.6 1.0 copy-start.1
  13.6 6.9 %copy-start.4 = (bf16[1,2,3,256,512]{4,3,2,1,0:T(8,128)(2,1)S(1)}, bf16[1,2,3,256,512]{4,3,2,1,0:T(8,128)(2,1)}, u32[]{:S(2)}) copy-start(bf16[1,2,3,256,512]{4,3,2,1,0:T(8,128)(2,1)} %param.6) | copy-start | bytes 4718596
  14.9 16.1 %collective-permute-start.2 = (bf16[2,512,256]{2,1,0:T(8,128)(2,1)S(1)}, bf16[2,512,256]{2,1,0:T(8,128)(2,1)S(1)}, u32[]{:S(2)}, u32[]{:S(2)}) collective-permute-start(bf16[2,512,256]{2,1,0:T(8,128)(2,1)S(1)} %fusion.2), channel_id=1, source_target_pairs={{0,2},{1,3},{2,4},{3,5},{4,6},{5,7},{6,8},{7,9},{8,10},{9,11},{10,... | collective-permute-start | bytes 1572872 | tf_op jit(solution)/shard_map/ppermute | solution.py:15
  20.7 15.7 %collective-permute-start.3 = (bf16[2,512,256]{2,1,0:T(8,128)(2,1)S(1)}, bf16[2,512,256]{2,1,0:T(8,128)(2,1)S(1)}, u32[]{:S(2)}, u32[]{:S(2)}) collective-permute-start(bf16[2,512,256]{2,1,0:T(8,128)(2,1)S(1)} %fusion.2), channel_id=1, source_target_pairs={{2,0},{3,1},{4,2},{5,3},{6,4},{7,5},{8,6},{9,7},{10,8},{11,9},{12,... | collective-permute-start | bytes 1572872 | tf_op jit(solution)/shard_map/ppermute | solution.py:15
  31.6 5.3 %copy-start.6 = (bf16[2,512,256]{2,1,0:T(8,128)(2,1)S(1)}, bf16[2,512,256]{2,1,0:T(8,128)(2,1)}, u32[]{:S(2)}) copy-start(bf16[2,512,256]{2,1,0:T(8,128)(2,1)} %param.5) | copy-start | bytes 1572868
  38.7 12.7 %collective-permute-start.5 = (bf16[2,512,256]{2,1,0:T(8,128)(2,1)S(1)}, bf16[2,512,256]{2,1,0:T(8,128)(2,1)S(1)}, u32[]{:S(2)}, u32[]{:S(2)}) collective-permute-start(bf16[2,512,256]{2,1,0:T(8,128)(2,1)S(1)} %get-tuple-element.51), channel_id=1, source_target_pairs={{0,2},{1,3},{2,4},{3,5},{4,6},{5,7},{6,8},{7,9},{8,10},{9,11},{10,... | collective-permute-start | bytes 1572872 | tf_op jit(solution)/shard_map/ppermute | solution.py:15
  40.7 15.5 %collective-permute-start.4 = (bf16[2,512,256]{2,1,0:T(8,128)(2,1)S(1)}, bf16[2,512,256]{2,1,0:T(8,128)(2,1)S(1)}, u32[]{:S(2)}, u32[]{:S(2)}) collective-permute-start(bf16[2,512,256]{2,1,0:T(8,128)(2,1)S(1)} %get-tuple-element.50), channel_id=1, source_target_pairs={{2,0},{3,1},{4,2},{5,3},{6,4},{7,5},{8,6},{9,7},{10,8},{11,9},{12,... | collective-permute-start | bytes 1572872 | tf_op jit(solution)/shard_map/ppermute | solution.py:15
  58.2 9.3 %collective-permute-start.6 = (bf16[2,128,256]{2,1,0:T(8,128)(2,1)S(1)}, bf16[2,128,256]{2,1,0:T(8,128)(2,1)S(1)}, u32[]{:S(2)}, u32[]{:S(2)}) collective-permute-start(bf16[2,128,256]{2,1,0:T(8,128)(2,1)S(1)} %get-tuple-element.48), channel_id=1, source_target_pairs={{0,1},{1,2},{2,3},{3,4},{4,5},{5,6},{6,7},{7,8},{8,9},{9,10},{10,1... | collective-permute-start | bytes 393224 | tf_op jit(solution)/shard_map/ppermute | solution.py:15
  60.1 7.4 %collective-permute-start.7 = (bf16[2,128,256]{2,1,0:T(8,128)(2,1)S(1)}, bf16[2,128,256]{2,1,0:T(8,128)(2,1)S(1)}, u32[]{:S(2)}, u32[]{:S(2)}) collective-permute-start(bf16[2,128,256]{2,1,0:T(8,128)(2,1)S(1)} %get-tuple-element.49), channel_id=1, source_target_pairs={{1,0},{2,1},{3,2},{4,3},{5,4},{6,5},{7,6},{8,7},{9,8},{10,9},{11,1... | collective-permute-start | bytes 393224 | tf_op jit(solution)/shard_map/ppermute | solution.py:15
  63.9 10.2 %collective-permute-start.11 = (bf16[2,256,256]{2,1,0:T(8,128)(2,1)S(1)}, bf16[2,256,256]{2,1,0:T(8,128)(2,1)S(1)}, u32[]{:S(2)}, u32[]{:S(2)}) collective-permute-start(bf16[2,256,256]{2,1,0:T(8,128)(2,1)S(1)} %get-tuple-element.25), channel_id=1, source_target_pairs={{32,0},{64,32},{96,64},{33,1},{65,33},{97,65},{34,2},{66,34},{98,6... | collective-permute-start | bytes 786440 | tf_op jit(solution)/shard_map/ppermute | solution.py:15
  68.5 14.2 %collective-permute-start.8 = (bf16[2,256,256]{2,1,0:T(8,128)(2,1)S(1)}, bf16[2,256,256]{2,1,0:T(8,128)(2,1)S(1)}, u32[]{:S(2)}, u32[]{:S(2)}) collective-permute-start(bf16[2,256,256]{2,1,0:T(8,128)(2,1)S(1)} %pad_maximum_fusion.27), channel_id=1, source_target_pairs={{32,0},{64,32},{96,64},{33,1},{65,33},{97,65},{34,2},{66,34},{98,6... | collective-permute-start | bytes 786440 | tf_op jit(solution)/shard_map/ppermute | solution.py:15
  75.1 17.8 %collective-permute-start.13 = (bf16[2,256,256]{2,1,0:T(8,128)(2,1)S(1)}, bf16[2,256,256]{2,1,0:T(8,128)(2,1)S(1)}, u32[]{:S(2)}, u32[]{:S(2)}) collective-permute-start(bf16[2,256,256]{2,1,0:T(8,128)(2,1)S(1)} %get-tuple-element.87), channel_id=1, source_target_pairs={{0,2},{1,3},{2,4},{3,5},{4,6},{5,7},{6,8},{7,9},{8,10},{9,11},{10,... | collective-permute-start | bytes 786440 | tf_op jit(solution)/shard_map/ppermute | solution.py:15
  80.6 12.2 %collective-permute-start.12 = (bf16[2,256,256]{2,1,0:T(8,128)(2,1)S(1)}, bf16[2,256,256]{2,1,0:T(8,128)(2,1)S(1)}, u32[]{:S(2)}, u32[]{:S(2)}) collective-permute-start(bf16[2,256,256]{2,1,0:T(8,128)(2,1)S(1)} %get-tuple-element.86), channel_id=1, source_target_pairs={{2,0},{3,1},{4,2},{5,3},{6,4},{7,5},{8,6},{9,7},{10,8},{11,9},{12,... | collective-permute-start | bytes 786440 | tf_op jit(solution)/shard_map/ppermute | solution.py:15
  83.7 10.2 %collective-permute-start.10 = (bf16[2,256,256]{2,1,0:T(8,128)(2,1)S(1)}, bf16[2,256,256]{2,1,0:T(8,128)(2,1)S(1)}, u32[]{:S(2)}, u32[]{:S(2)}) collective-permute-start(bf16[2,256,256]{2,1,0:T(8,128)(2,1)S(1)} %get-tuple-element.85), channel_id=1, source_target_pairs={{0,2},{1,3},{2,4},{3,5},{4,6},{5,7},{6,8},{7,9},{8,10},{9,11},{10,... | collective-permute-start | bytes 786440 | tf_op jit(solution)/shard_map/ppermute | solution.py:15
  89.7 10.4 %collective-permute-start.9 = (bf16[2,256,256]{2,1,0:T(8,128)(2,1)S(1)}, bf16[2,256,256]{2,1,0:T(8,128)(2,1)S(1)}, u32[]{:S(2)}, u32[]{:S(2)}) collective-permute-start(bf16[2,256,256]{2,1,0:T(8,128)(2,1)S(1)} %get-tuple-element.84), channel_id=1, source_target_pairs={{2,0},{3,1},{4,2},{5,3},{6,4},{7,5},{8,6},{9,7},{10,8},{11,9},{12,... | collective-permute-start | bytes 786440 | tf_op jit(solution)/shard_map/ppermute | solution.py:15
  101.3 8.0 %copy-start.25 = (bf16[2,128,256]{2,1,0:T(8,128)(2,1)S(1)}, bf16[2,128,256]{2,1,0:T(8,128)(2,1)}, u32[]{:S(2)}) copy-start(bf16[2,128,256]{2,1,0:T(8,128)(2,1)} %copy-done.24) | copy-start | bytes 393220
  101.3 10.5 %collective-permute-start.14 = (bf16[2,128,256]{2,1,0:T(8,128)(2,1)S(1)}, bf16[2,128,256]{2,1,0:T(8,128)(2,1)S(1)}, u32[]{:S(2)}, u32[]{:S(2)}) collective-permute-start(bf16[2,128,256]{2,1,0:T(8,128)(2,1)S(1)} %get-tuple-element.78), channel_id=1, source_target_pairs={{0,1},{1,2},{2,3},{3,4},{4,5},{5,6},{6,7},{7,8},{8,9},{9,10},{10,1... | collective-permute-start | bytes 393224 | tf_op jit(solution)/shard_map/ppermute | solution.py:15
  103.3 8.6 %collective-permute-start.15 = (bf16[2,128,256]{2,1,0:T(8,128)(2,1)S(1)}, bf16[2,128,256]{2,1,0:T(8,128)(2,1)S(1)}, u32[]{:S(2)}, u32[]{:S(2)}) collective-permute-start(bf16[2,128,256]{2,1,0:T(8,128)(2,1)S(1)} %get-tuple-element.79), channel_id=1, source_target_pairs={{1,0},{2,1},{3,2},{4,3},{5,4},{6,5},{7,6},{8,7},{9,8},{10,9},{11,1... | collective-permute-start | bytes 393224 | tf_op jit(solution)/shard_map/ppermute | solution.py:15
  108.0 9.0 %collective-permute-start.19 = (bf16[2,256,256]{2,1,0:T(8,128)(2,1)S(1)}, bf16[2,256,256]{2,1,0:T(8,128)(2,1)S(1)}, u32[]{:S(2)}, u32[]{:S(2)}) collective-permute-start(bf16[2,256,256]{2,1,0:T(8,128)(2,1)S(1)} %get-tuple-element.7), channel_id=1, source_target_pairs={{32,0},{64,32},{96,64},{33,1},{65,33},{97,65},{34,2},{66,34},{98,6... | collective-permute-start | bytes 786440 | tf_op jit(solution)/shard_map/ppermute | solution.py:15
  112.8 11.6 %collective-permute-start.16 = (bf16[2,256,256]{2,1,0:T(8,128)(2,1)S(1)}, bf16[2,256,256]{2,1,0:T(8,128)(2,1)S(1)}, u32[]{:S(2)}, u32[]{:S(2)}) collective-permute-start(bf16[2,256,256]{2,1,0:T(8,128)(2,1)S(1)} %pad_maximum_fusion.28), channel_id=1, source_target_pairs={{32,0},{64,32},{96,64},{33,1},{65,33},{97,65},{34,2},{66,34},{98,6... | collective-permute-start | bytes 786440 | tf_op jit(solution)/shard_map/ppermute | solution.py:15
  117.9 16.8 %collective-permute-start.21 = (bf16[2,256,256]{2,1,0:T(8,128)(2,1)S(1)}, bf16[2,256,256]{2,1,0:T(8,128)(2,1)S(1)}, u32[]{:S(2)}, u32[]{:S(2)}) collective-permute-start(bf16[2,256,256]{2,1,0:T(8,128)(2,1)S(1)} %get-tuple-element.77), channel_id=1, source_target_pairs={{0,2},{1,3},{2,4},{3,5},{4,6},{5,7},{6,8},{7,9},{8,10},{9,11},{10,... | collective-permute-start | bytes 786440 | tf_op jit(solution)/shard_map/ppermute | solution.py:15
  122.5 12.3 %collective-permute-start.20 = (bf16[2,256,256]{2,1,0:T(8,128)(2,1)S(1)}, bf16[2,256,256]{2,1,0:T(8,128)(2,1)S(1)}, u32[]{:S(2)}, u32[]{:S(2)}) collective-permute-start(bf16[2,256,256]{2,1,0:T(8,128)(2,1)S(1)} %get-tuple-element.76), channel_id=1, source_target_pairs={{2,0},{3,1},{4,2},{5,3},{6,4},{7,5},{8,6},{9,7},{10,8},{11,9},{12,... | collective-permute-start | bytes 786440 | tf_op jit(solution)/shard_map/ppermute | solution.py:15
  125.3 10.5 %collective-permute-start.18 = (bf16[2,256,256]{2,1,0:T(8,128)(2,1)S(1)}, bf16[2,256,256]{2,1,0:T(8,128)(2,1)S(1)}, u32[]{:S(2)}, u32[]{:S(2)}) collective-permute-start(bf16[2,256,256]{2,1,0:T(8,128)(2,1)S(1)} %get-tuple-element.75), channel_id=1, source_target_pairs={{0,2},{1,3},{2,4},{3,5},{4,6},{5,7},{6,8},{7,9},{8,10},{9,11},{10,... | collective-permute-start | bytes 786440 | tf_op jit(solution)/shard_map/ppermute | solution.py:15
  131.4 10.4 %collective-permute-start.17 = (bf16[2,256,256]{2,1,0:T(8,128)(2,1)S(1)}, bf16[2,256,256]{2,1,0:T(8,128)(2,1)S(1)}, u32[]{:S(2)}, u32[]{:S(2)}) collective-permute-start(bf16[2,256,256]{2,1,0:T(8,128)(2,1)S(1)} %get-tuple-element.74), channel_id=1, source_target_pairs={{2,0},{3,1},{4,2},{5,3},{6,4},{7,5},{8,6},{9,7},{10,8},{11,9},{12,... | collective-permute-start | bytes 786440 | tf_op jit(solution)/shard_map/ppermute | solution.py:15
  143.0 10.8 %collective-permute-start.22 = (bf16[2,128,256]{2,1,0:T(8,128)(2,1)S(1)}, bf16[2,128,256]{2,1,0:T(8,128)(2,1)S(1)}, u32[]{:S(2)}, u32[]{:S(2)}) collective-permute-start(bf16[2,128,256]{2,1,0:T(8,128)(2,1)S(1)} %get-tuple-element.68), channel_id=1, source_target_pairs={{0,1},{1,2},{2,3},{3,4},{4,5},{5,6},{6,7},{7,8},{8,9},{9,10},{10,1... | collective-permute-start | bytes 393224 | tf_op jit(solution)/shard_map/ppermute | solution.py:15
  144.9 8.9 %collective-permute-start.23 = (bf16[2,128,256]{2,1,0:T(8,128)(2,1)S(1)}, bf16[2,128,256]{2,1,0:T(8,128)(2,1)S(1)}, u32[]{:S(2)}, u32[]{:S(2)}) collective-permute-start(bf16[2,128,256]{2,1,0:T(8,128)(2,1)S(1)} %get-tuple-element.69), channel_id=1, source_target_pairs={{1,0},{2,1},{3,2},{4,3},{5,4},{6,5},{7,6},{8,7},{9,8},{10,9},{11,1... | collective-permute-start | bytes 393224 | tf_op jit(solution)/shard_map/ppermute | solution.py:15
  149.6 8.9 %collective-permute-start.27 = (bf16[2,256,256]{2,1,0:T(8,128)(2,1)S(1)}, bf16[2,256,256]{2,1,0:T(8,128)(2,1)S(1)}, u32[]{:S(2)}, u32[]{:S(2)}) collective-permute-start(bf16[2,256,256]{2,1,0:T(8,128)(2,1)S(1)} %get-tuple-element.3), channel_id=1, source_target_pairs={{32,0},{64,32},{96,64},{33,1},{65,33},{97,65},{34,2},{66,34},{98,6... | collective-permute-start | bytes 786440 | tf_op jit(solution)/shard_map/ppermute | solution.py:15
  154.7 11.0 %collective-permute-start.24 = (bf16[2,256,256]{2,1,0:T(8,128)(2,1)S(1)}, bf16[2,256,256]{2,1,0:T(8,128)(2,1)S(1)}, u32[]{:S(2)}, u32[]{:S(2)}) collective-permute-start(bf16[2,256,256]{2,1,0:T(8,128)(2,1)S(1)} %pad_maximum_fusion.29), channel_id=1, source_target_pairs={{32,0},{64,32},{96,64},{33,1},{65,33},{97,65},{34,2},{66,34},{98,6... | collective-permute-start | bytes 786440 | tf_op jit(solution)/shard_map/ppermute | solution.py:15
  159.4 18.3 %copy-start.5 = (f32[2,256,768]{2,1,0:T(8,128)}, f32[2,256,768]{2,1,0:T(8,128)S(1)}, u32[]{:S(2)}) copy-start(f32[2,256,768]{2,1,0:T(8,128)S(1)} %get-tuple-element.157) | copy-start | bytes 4718596
  159.5 18.2 %collective-permute-start.29 = (bf16[2,256,256]{2,1,0:T(8,128)(2,1)S(1)}, bf16[2,256,256]{2,1,0:T(8,128)(2,1)S(1)}, u32[]{:S(2)}, u32[]{:S(2)}) collective-permute-start(bf16[2,256,256]{2,1,0:T(8,128)(2,1)S(1)} %get-tuple-element.65), channel_id=1, source_target_pairs={{0,2},{1,3},{2,4},{3,5},{4,6},{5,7},{6,8},{7,9},{8,10},{9,11},{10,... | collective-permute-start | bytes 786440 | tf_op jit(solution)/shard_map/ppermute | solution.py:15
  163.8 13.9 %collective-permute-start.28 = (bf16[2,256,256]{2,1,0:T(8,128)(2,1)S(1)}, bf16[2,256,256]{2,1,0:T(8,128)(2,1)S(1)}, u32[]{:S(2)}, u32[]{:S(2)}) collective-permute-start(bf16[2,256,256]{2,1,0:T(8,128)(2,1)S(1)} %get-tuple-element.64), channel_id=1, source_target_pairs={{2,0},{3,1},{4,2},{5,3},{6,4},{7,5},{8,6},{9,7},{10,8},{11,9},{12,... | collective-permute-start | bytes 786440 | tf_op jit(solution)/shard_map/ppermute | solution.py:15
  166.8 11.0 %collective-permute-start.26 = (bf16[2,256,256]{2,1,0:T(8,128)(2,1)S(1)}, bf16[2,256,256]{2,1,0:T(8,128)(2,1)S(1)}, u32[]{:S(2)}, u32[]{:S(2)}) collective-permute-start(bf16[2,256,256]{2,1,0:T(8,128)(2,1)S(1)} %get-tuple-element.67), channel_id=1, source_target_pairs={{0,2},{1,3},{2,4},{3,5},{4,6},{5,7},{6,8},{7,9},{8,10},{9,11},{10,... | collective-permute-start | bytes 786440 | tf_op jit(solution)/shard_map/ppermute | solution.py:15
  172.8 10.4 %collective-permute-start.25 = (bf16[2,256,256]{2,1,0:T(8,128)(2,1)S(1)}, bf16[2,256,256]{2,1,0:T(8,128)(2,1)S(1)}, u32[]{:S(2)}, u32[]{:S(2)}) collective-permute-start(bf16[2,256,256]{2,1,0:T(8,128)(2,1)S(1)} %get-tuple-element.66), channel_id=1, source_target_pairs={{2,0},{3,1},{4,2},{5,3},{6,4},{7,5},{8,6},{9,7},{10,8},{11,9},{12,... | collective-permute-start | bytes 786440 | tf_op jit(solution)/shard_map/ppermute | solution.py:15
  177.6 7.0 %copy-start.20 = (bf16[2,256,256]{2,1,0:T(8,128)(2,1)}, bf16[2,256,256]{2,1,0:T(8,128)(2,1)S(1)}, u32[]{:S(2)}) copy-start(bf16[2,256,256]{2,1,0:T(8,128)(2,1)S(1)} %collective-permute-done.29) | copy-start | bytes 786436
  177.6 7.0 %copy-start.22 = (bf16[2,256,256]{2,1,0:T(8,128)(2,1)}, bf16[2,256,256]{2,1,0:T(8,128)(2,1)S(1)}, u32[]{:S(2)}) copy-start(bf16[2,256,256]{2,1,0:T(8,128)(2,1)S(1)} %collective-permute-done.28) | copy-start | bytes 786436
  184.9 2.4 %copy-start.26 = (bf16[2,128,256]{2,1,0:T(8,128)(2,1)S(1)}, bf16[2,128,256]{2,1,0:T(8,128)(2,1)}, u32[]{:S(2)}) copy-start(bf16[2,128,256]{2,1,0:T(8,128)(2,1)} %copy-done.24) | copy-start | bytes 393220
  187.3 4.1 %copy-start.11 = (f32[768,512]{1,0:T(8,128)S(1)}, f32[768,512]{1,0:T(8,128)}, u32[]{:S(2)}) copy-start(f32[768,512]{1,0:T(8,128)} %bitcast_add_fusion) | copy-start | bytes 4718596
  192.0 1.9 copy-start
  194.9 2.8 %collective-permute-start.32 = (bf16[2,2,2,2,56,512]{5,4,3,2,1,0:T(8,128)(2,1)}, bf16[2,2,2,2,56,512]{5,4,3,2,1,0:T(8,128)(2,1)}, u32[]{:S(2)}, u32[]{:S(2)}) collective-permute-start(bf16[2,2,2,2,56,512]{5,4,3,2,1,0:T(8,128)(2,1)} %fusion.63), channel_id=1, source_target_pairs={{0,1},{1,0},{2,3},{3,2},{4,5},{5,4},{6,7},{7,6},{8,9},{9,8},{10,11... | collective-permute-start | bytes 2752520 | tf_op jit(solution)/shard_map/ppermute | solution.py:199
  194.9 5.8 %copy-start.9 = (bf16[2,512,256]{1,2,0:T(8,128)(2,1)S(1)}, bf16[2,512,256]{1,2,0:T(8,128)(2,1)}, u32[]{:S(2)}) copy-start(bf16[2,512,256]{1,2,0:T(8,128)(2,1)} %get-tuple-element.54) | copy-start | bytes 1572868
  194.9 5.9 %copy-start.10 = (bf16[2,512,256]{1,2,0:T(8,128)(2,1)S(1)}, bf16[2,512,256]{1,2,0:T(8,128)(2,1)}, u32[]{:S(2)}) copy-start(bf16[2,512,256]{1,2,0:T(8,128)(2,1)} %get-tuple-element.55) | copy-start | bytes 1572868
  200.6 13.5 %collective-permute-start.33 = (bf16[2,2,2,56,512]{4,3,2,1,0:T(8,128)(2,1)S(1)}, bf16[2,2,2,56,512]{4,3,2,1,0:T(8,128)(2,1)S(1)}, u32[]{:S(2)}, u32[]{:S(2)}) collective-permute-start(bf16[2,2,2,56,512]{4,3,2,1,0:T(8,128)(2,1)S(1)} %fusion.157), channel_id=1, source_target_pairs={{0,2},{1,3},{2,0},{3,1},{4,6},{5,7},{6,4},{7,5},{8,10},{9,11},{10,... | collective-permute-start | bytes 1376264 | tf_op jit(solution)/shard_map/ppermute | solution.py:199
  201.8 13.7 %copy-start.21 = (bf16[2,256,256]{2,1,0:T(8,128)(2,1)S(1)}, bf16[2,256,256]{2,1,0:T(8,128)(2,1)}, u32[]{:S(2)}) copy-start(bf16[2,256,256]{2,1,0:T(8,128)(2,1)} %copy-done.20) | copy-start | bytes 786436
  201.8 13.7 %copy-start.23 = (bf16[2,256,256]{2,1,0:T(8,128)(2,1)S(1)}, bf16[2,256,256]{2,1,0:T(8,128)(2,1)}, u32[]{:S(2)}) copy-start(bf16[2,256,256]{2,1,0:T(8,128)(2,1)} %copy-done.22) | copy-start | bytes 786436
  201.8 19.0 %collective-permute-start.30 = (bf16[2,128,256]{2,1,0:T(8,128)(2,1)S(1)}, bf16[2,128,256]{2,1,0:T(8,128)(2,1)S(1)}, u32[]{:S(2)}, u32[]{:S(2)}) collective-permute-start(bf16[2,128,256]{2,1,0:T(8,128)(2,1)S(1)} %get-tuple-element.46), channel_id=1, source_target_pairs={{0,1},{1,2},{2,3},{3,4},{4,5},{5,6},{6,7},{7,8},{8,9},{9,10},{10,1... | collective-permute-start | bytes 393224 | tf_op jit(solution)/shard_map/ppermute | solution.py:15
  204.0 16.8 %collective-permute-start.31 = (bf16[2,128,256]{2,1,0:T(8,128)(2,1)S(1)}, bf16[2,128,256]{2,1,0:T(8,128)(2,1)S(1)}, u32[]{:S(2)}, u32[]{:S(2)}) collective-permute-start(bf16[2,128,256]{2,1,0:T(8,128)(2,1)S(1)} %get-tuple-element.47), channel_id=1, source_target_pairs={{1,0},{2,1},{3,2},{4,3},{5,4},{6,5},{7,6},{8,7},{9,8},{10,9},{11,1... | collective-permute-start | bytes 393224 | tf_op jit(solution)/shard_map/ppermute | solution.py:15
  214.4 6.1 %collective-permute-start.34 = (bf16[2,2,56,512]{3,2,1,0:T(8,128)(2,1)S(1)}, bf16[2,2,56,512]{3,2,1,0:T(8,128)(2,1)S(1)}, u32[]{:S(2)}, u32[]{:S(2)}) collective-permute-start(bf16[2,2,56,512]{3,2,1,0:T(8,128)(2,1)S(1)} %fusion.209), channel_id=1, source_target_pairs={{0,8},{1,9},{2,10},{3,11},{4,12},{5,13},{6,14},{7,15},{8,0},{9,1},... | collective-permute-start | bytes 688136 | tf_op jit(solution)/shard_map/ppermute | solution.py:199
  220.6 7.6 %copy-start.7 = (f32[2,256,256]{2,1,0:T(8,128)S(1)}, f32[2,256,256]{2,1,0:T(8,128)}, u32[]{:S(2)}) copy-start(f32[2,256,256]{2,1,0:T(8,128)} %get-tuple-element.8) | copy-start | bytes 1572868
  220.6 7.6 %copy-start.8 = (f32[2,256,256]{2,1,0:T(8,128)S(1)}, f32[2,256,256]{2,1,0:T(8,128)}, u32[]{:S(2)}) copy-start(f32[2,256,256]{2,1,0:T(8,128)} %get-tuple-element.4) | copy-start | bytes 1572868
  220.6 7.6 %copy-start.14 = (f32[1,2,128,256]{3,2,1,0:T(8,128)S(1)}, f32[1,2,128,256]{3,2,1,0:T(8,128)}, u32[]{:S(2)}) copy-start(f32[1,2,128,256]{3,2,1,0:T(8,128)} %get-tuple-element.20) | copy-start | bytes 786436
  220.6 7.6 %copy-start.15 = (f32[1,2,128,256]{3,2,1,0:T(8,128)S(1)}, f32[1,2,128,256]{3,2,1,0:T(8,128)}, u32[]{:S(2)}) copy-start(f32[1,2,128,256]{3,2,1,0:T(8,128)} %get-tuple-element.23) | copy-start | bytes 786436
  220.6 7.6 %copy-start.16 = (f32[1,2,128,256]{3,2,1,0:T(8,128)S(1)}, f32[1,2,128,256]{3,2,1,0:T(8,128)}, u32[]{:S(2)}) copy-start(f32[1,2,128,256]{3,2,1,0:T(8,128)} %get-tuple-element.38) | copy-start | bytes 786436
  220.7 7.6 %copy-start.17 = (f32[1,2,128,256]{3,2,1,0:T(8,128)S(1)}, f32[1,2,128,256]{3,2,1,0:T(8,128)}, u32[]{:S(2)}) copy-start(f32[1,2,128,256]{3,2,1,0:T(8,128)} %get-tuple-element.43) | copy-start | bytes 786436
  220.7 7.6 %copy-start.18 = (f32[1,2,128,256]{3,2,1,0:T(8,128)S(1)}, f32[1,2,128,256]{3,2,1,0:T(8,128)}, u32[]{:S(2)}) copy-start(f32[1,2,128,256]{3,2,1,0:T(8,128)} %get-tuple-element.34) | copy-start | bytes 786436
  220.7 7.6 %copy-start.19 = (f32[1,2,128,256]{3,2,1,0:T(8,128)S(1)}, f32[1,2,128,256]{3,2,1,0:T(8,128)}, u32[]{:S(2)}) copy-start(f32[1,2,128,256]{3,2,1,0:T(8,128)} %get-tuple-element.41) | copy-start | bytes 786436
  220.7 6.4 %collective-permute-start.35 = (bf16[2,56,512]{2,1,0:T(8,128)(2,1)S(1)}, bf16[2,56,512]{2,1,0:T(8,128)(2,1)S(1)}, u32[]{:S(2)}, u32[]{:S(2)}) collective-permute-start(bf16[2,56,512]{2,1,0:T(8,128)(2,1)S(1)} %fusion.237), channel_id=1, source_target_pairs={{0,4},{1,5},{2,6},{3,7},{4,0},{5,1},{6,2},{7,3},{8,12},{9,13},{10,... | collective-permute-start | bytes 344072 | tf_op jit(solution)/shard_map/ppermute | solution.py:199
  227.2 5.8 %collective-permute-start.36 = (bf16[56,512]{1,0:T(8,128)(2,1)S(1)}, bf16[56,512]{1,0:T(8,128)(2,1)S(1)}, u32[]{:S(2)}, u32[]{:S(2)}) collective-permute-start(bf16[56,512]{1,0:T(8,128)(2,1)S(1)} %fusion.238), channel_id=1, source_target_pairs={{0,16},{1,17},{2,18},{3,19},{4,20},{5,21},{6,22},{7,23},{8,24},{9,... | collective-permute-start | bytes 172040 | tf_op jit(solution)/shard_map/ppermute | solution.py:199
